TPU v7x, 32 devices: a whole 2x2x4 slice. The times are simulated.
32 devices in a mesh: basin: 8 (over z, y), band: 4 (over x, core).
Axes of the slice: x: 2, y: 2, z: 4, core: 2. Of those that a mesh axis runs over, the one named last changes fastest.
Arguments:
- precip: float32 [6144, 8, 128], P(('basin', 'band')), may hold values from 0.002 to 0.02
- soil_water: float32 [6144, 128], P(('basin', 'band')), may hold values from 0.1 to 1
- capacity: float32 [6144, 128], P(('basin', 'band')), may hold values from 0.1 to 1
- evap_rate: float32 [6144, 128], P(('basin', 'band')), may hold values from 0.01 to 0.1
- tile_dest: int32 [6144], P(('basin', 'band')), may hold values from 0 to 31, as said below
- tile_block: int32 [6144], P(('basin', 'band')), may hold values from 0 to 7
- trib_op: float32 [256, 128, 128], P(('basin', 'band')), may hold values from 0 to 1
- trib_keep: float32 [256, 128], P(('basin', 'band')), may hold values from 0.01 to 0.6
- trib_prev: float32 [256, 128], P(('basin', 'band')), may hold values from 0 to 0.5
- trib_river: int32 [256], P(('basin', 'band')), may hold values from 0 to 3, as said below
- trib_reach: int32 [256], P(('basin', 'band')), may hold values from 0 to 127
- main_op: float32 [4, 8, 128, 128], P('band', 'basin'), may hold values from 0 to 1
- main_keep: float32 [4, 8, 128], P('band', 'basin'), may hold values from 0.002 to 0.1
- main_prev: float32 [4, 8, 128], P('band', 'basin'), may hold values from 0 to 4
- head_inflow: float32 [4, 8], P('band'), may hold values from 0.5 to 2
Outputs:
- soil_final: float32 [6144, 128], P(('basin', 'band'))
- trib_final: float32 [256, 128], P(('basin', 'band'))
- main_flow: float32 [4, 8, 8, 128], P('band', 'basin')
Inputs may be any that keep to these rules, and one draw needn't show every extreme that they name: `tile_dest`: among the 192 tiles of one device, at most 12 name the same owner. `trib_river`: among the 8 tributary blocks of one device, at most 4 name the same river.
All inputs are finite; a program needn't handle non-finite values.
Results may differ from a plain program's by a relative error of at most 0.00016.
Values sent between devices are 32-bit elements; how exact they have to be, the bound alone decides.
No kernel may reach another device: no remote copies, remote signals or barrier semaphores. Data moves between devices by JAX's collectives and lax.ppermute only.
A program may use at most 64 MiB of HBM per device.

v0:
```python
import jax
import jax.numpy as jnp
from jax import lax
from jax.sharding import PartitionSpec as P


def entering(value, axis, join, neutral):
    count, mine = (lax.axis_size(axis), lax.axis_index(axis))
    pieces = jax.tree.map(lambda part: lax.all_gather(part, axis), value)
    running = jax.tree.map(
        lambda part, zero: jnp.full_like(part, 0) + jnp.asarray(zero, part.dtype), value, neutral
    )

    def turn(position, running):
        longer = join(running, jax.tree.map(lambda part: part[position], pieces))
        return jax.tree.map(lambda new, old: jnp.where(position < mine, new, old), longer, running)

    return lax.fori_loop(0, count - 1, turn, running)


def land_update(precip, soil_water, capacity, evap_rate):
    water = soil_water
    runoff_steps = []
    for sub_step in range(precip.shape[1]):
        rain_now = precip[:, sub_step]
        runoff_now = rain_now * water / (water + capacity)
        water = (1.0 - evap_rate) * water + rain_now - runoff_now
        runoff_steps.append(runoff_now)
    return (jnp.stack(runoff_steps, axis=1), water)


def route_series(mixed, keep, previous):
    flow = previous
    flows = []
    for sub_step in range(mixed.shape[-2]):
        flow = keep * flow + (1.0 - keep) * mixed[..., sub_step, :]
        flows.append(flow)
    return jnp.stack(flows, axis=-2)


def pack_slots(values, labels, targets, peer_count, slot_cap):
    entries = targets.shape[0]
    position = jnp.arange(entries, dtype=jnp.int32)
    earlier = (targets[:, None] == targets[None, :]) & (position[None, :] < position[:, None])
    ranking = jnp.sum(earlier.astype(jnp.int32), axis=1)
    target_slot = targets * slot_cap + ranking
    buffer = (
        jnp.zeros((peer_count * slot_cap, values.shape[1]), values.dtype)
        .at[target_slot]
        .set(values)
    )
    slot_labels = jnp.zeros((peer_count * slot_cap,), jnp.int32).at[target_slot].set(labels)
    return (buffer, slot_labels)


def compose(earlier, later):
    new_map = jnp.dot(later[0], earlier[0], precision=lax.Precision.HIGHEST)
    new_shift = jnp.dot(later[0], earlier[1], precision=lax.Precision.HIGHEST) + later[1]
    return (new_map, new_shift)


def local(
    precip,
    soil_water,
    capacity,
    evap_rate,
    tile_dest,
    tile_block,
    trib_op,
    trib_keep,
    trib_prev,
    trib_river,
    trib_reach,
    main_op,
    main_keep,
    main_prev,
    head_inflow,
):
    tile_count = precip.shape[0]
    sub_steps = precip.shape[1]
    reaches = precip.shape[2]
    blocks = trib_op.shape[0]
    chains = lax.axis_size("basin")
    rivers = lax.axis_size("band")
    shards = chains * rivers
    operator = main_op[0, 0]
    keep_main = main_keep[0, 0]
    decay = keep_main[reaches - 1]
    through = operator[reaches - 1, 0]
    transfer = jnp.zeros((sub_steps, sub_steps), jnp.float32)
    power = jnp.ones((), jnp.float32)
    for lag in range(sub_steps):
        transfer = transfer + power * jnp.eye(sub_steps, k=-lag, dtype=jnp.float32)
        power = power * decay
    transfer = transfer * (through * (1.0 - decay))
    runoff, water = land_update(precip, soil_water, capacity, evap_rate)
    tile_cap = max(2, 2 * tile_count // shards)
    buffer, slot_labels = pack_slots(
        runoff.reshape(tile_count, sub_steps * reaches), tile_block, tile_dest, shards, tile_cap
    )
    buffer = buffer.reshape(chains, rivers, tile_cap, sub_steps * reaches)
    slot_labels = slot_labels.reshape(chains, rivers, tile_cap)
    arrived, arrived_ids = (
        lax.all_to_all(
            lax.all_to_all(buffer, "basin", split_axis=0, concat_axis=0, tiled=True),
            "band",
            split_axis=1,
            concat_axis=1,
            tiled=True,
        ),
        lax.all_to_all(
            lax.all_to_all(slot_labels, "basin", split_axis=0, concat_axis=0, tiled=True),
            "band",
            split_axis=1,
            concat_axis=1,
            tiled=True,
        ),
    )
    received = arrived.reshape(-1, sub_steps * reaches)
    block_pick = (
        arrived_ids.reshape(-1)[:, None] == jnp.arange(blocks, dtype=jnp.int32)[None, :]
    ).astype(jnp.float32)
    lateral = jnp.einsum("sk,sx->kx", block_pick, received, precision=lax.Precision.HIGHEST)
    trib_mixed = jnp.einsum(
        "brc,btc->btr",
        trib_op,
        lateral.reshape(blocks, sub_steps, reaches),
        precision=lax.Precision.HIGHEST,
    )
    trib_flows = route_series(trib_mixed, trib_keep, trib_prev)
    outlet = trib_flows[:, :, reaches - 1]
    branch_cap = max(2, 2 * blocks // rivers)
    sent, sent_reach = pack_slots(outlet, trib_reach, trib_river, rivers, branch_cap)
    got, got_reach = (
        lax.all_to_all(
            sent.reshape(rivers, branch_cap, sub_steps),
            "band",
            split_axis=0,
            concat_axis=0,
            tiled=True,
        ),
        lax.all_to_all(
            sent_reach.reshape(rivers, branch_cap), "band", split_axis=0, concat_axis=0, tiled=True
        ),
    )
    reach_pick = (
        got_reach.reshape(-1)[:, None] == jnp.arange(reaches, dtype=jnp.int32)[None, :]
    ).astype(jnp.float32)
    branch_in = jnp.einsum(
        "sr,st->tr", reach_pick, got.reshape(-1, sub_steps), precision=lax.Precision.HIGHEST
    )
    main_mixed = jnp.einsum("rc,tc->tr", operator, branch_in, precision=lax.Precision.HIGHEST)
    base_flows = route_series(main_mixed, keep_main, main_prev[0, 0])
    own_exit = base_flows[:, reaches - 1]
    unit_map = jnp.eye(sub_steps, dtype=jnp.float32)
    no_shift = jnp.zeros((sub_steps,), jnp.float32)
    prefix_map, prefix_shift = entering(
        (transfer, own_exit), "basin", compose, (unit_map, no_shift)
    )
    entry = jnp.dot(prefix_map, head_inflow[0], precision=lax.Precision.HIGHEST) + prefix_shift
    fed_mixed = main_mixed + entry[:, None] * operator[:, 0][None, :]
    main_flows = route_series(fed_mixed, keep_main, main_prev[0, 0])
    return (water, trib_flows[:, sub_steps - 1], main_flows[None, None])


def solution(mesh):
    return jax.shard_map(
        local,
        mesh=mesh,
        in_specs=(
            P(("basin", "band"), None, None),
            P(("basin", "band"), None),
            P(("basin", "band"), None),
            P(("basin", "band"), None),
            P(("basin", "band")),
            P(("basin", "band")),
            P(("basin", "band"), None, None),
            P(("basin", "band"), None),
            P(("basin", "band"), None),
            P(("basin", "band")),
            P(("basin", "band")),
            P("band", "basin", None, None),
            P("band", "basin", None),
            P("band", "basin", None),
            P("band", None),
        ),
        out_specs=(
            P(("basin", "band"), None),
            P(("basin", "band"), None),
            P("band", "basin", None, None),
        ),
        check_vma=False,
    )
```

profile of v0, /device:TPU:0, one launch (start us, length us, event | category | flops | bytes accessed | tf_op | source)
XLA Modules:
  0.0 160.7 jit_solution(4654353818864081058)
XLA Ops:
  0.7 0.9 convert_reduce_fusion
  1.6 0.7 compare_select_fusion
  2.3 1.3 scatter_custom_fusion
  3.7 0.7 reshape.312
  4.4 7.3 %all-to-all-start = ((s32[8,4,12]{2,1,0:T(4,128)}), s32[8,4,12]{2,1,0:T(4,128)S(1)}, u32[]{:S(2)}, u32[]{:S(2)}) async-start(s32[8,4,12]{2,1,0:T(4,128)} %reshape.312), calls=%async_computation | async-start | bytes 32768 | tf_op jit(solution)/shard_map/all_to_all | solution.py:112
  11.7 4.1 %fusion.63 = (f32[192,1,128]{2,1,0:T(1,128)S(1)}, f32[192,1,128]{2,1,0:T(1,128)S(1)}, f32[192,1,128]{2,1,0:T(1,128)S(1)}, f32[192,1,128]{2,1,0:T(1,128)S(1)}, f3...) fusion(f32[192,8,128]{2,1,0:T(8,128)} %param.17), kind=kLoop, calls=%fused_computation.144 | loop fusion | bytes 1572864 | tf_op jit(solution)/shard_map/slice | solution.py:25
  16.0 0.1 bitcast_dynamic-update-slice_fusion.4
  16.4 2.5 %scatter_custom_fusion.1 = f32[384,1024]{1,0:T(8,128)} fusion(s32[192]{0:T(256)S(1)} %compare_select_fusion, f32[8,24,8,128]{3,2,1,0:T(8,128)S(1)} %bitcast.264, f32[]{:T(128)} %constant.60.clone.1), kind=kCustom, calls=%fused_computation.20 | custom fusion | bytes 2359300 | tf_op jit(solution)/shard_map/scatter | solution.py:50
  18.9 1.4 reshape.314
  20.3 2.2 %copy.110 = f32[8,4,12,1024]{3,1,2,0:T(4,128)} copy(f32[8,4,12,1024]{3,2,1,0:T(8,128)S(1)} %reshape.314) | data formatting | bytes 3145728 | tf_op jit(solution)/shard_map/reshape | solution.py:101
  22.5 6.1 %all-to-all-start.2 = ((f32[8,4,12,1024]{3,1,2,0:T(4,128)}), f32[8,4,12,1024]{3,1,2,0:T(4,128)S(1)}, u32[]{:S(2)}, u32[]{:S(2)}) async-start(f32[8,4,12,1024]{3,1,2,0:T(4,128)} %copy.110), calls=%async_computation.2 | async-start | bytes 3145728 | tf_op jit(solution)/shard_map/all_to_all | solution.py:105
  28.7 0.6 copy.107
  29.3 35.8 %all-to-all-done.2 = f32[8,4,12,1024]{3,1,2,0:T(4,128)S(1)} async-done(((f32[8,4,12,1024]{3,1,2,0:T(4,128)}), f32[8,4,12,1024]{3,1,2,0:T(4,128)S(1)}, u32[]{:S(2)}, u32[]{:S(2)}) %all-to-all-start.2) | async-done | bytes 1572896 | tf_op jit(solution)/shard_map/all_to_all | solution.py:105
  65.1 3.3 %all-to-all-start.1 = ((s32[8,4,12]{2,0,1:T(8,128)}), s32[8,4,12]{2,0,1:T(8,128)S(1)}, u32[]{:S(2)}, u32[]{:S(2)}) async-start(s32[8,4,12]{2,0,1:T(8,128)} %copy.107), calls=%async_computation.1 | async-start | bytes 32768 | tf_op jit(solution)/shard_map/all_to_all | solution.py:111
  68.4 0.2 convert_reduce_fusion.1
  68.6 2.1 %copy.111 = f32[8,4,12,1024]{3,0,2,1:T(8,128)} copy(f32[8,4,12,1024]{3,1,2,0:T(4,128)S(1)} %all-to-all-done.2) | data formatting | bytes 3145728 | tf_op jit(solution)/shard_map/all_to_all | solution.py:105
  70.6 1.5 all-to-all-done.1
  72.2 3.6 %all-to-all-start.3 = ((f32[8,4,12,1024]{3,0,2,1:T(8,128)}), f32[8,4,12,1024]{3,0,2,1:T(8,128)S(1)}, u32[]{:S(2)}, u32[]{:S(2)}) async-start(f32[8,4,12,1024]{3,0,2,1:T(8,128)} %copy.111), calls=%async_computation.3 | async-start | bytes 3145728 | tf_op jit(solution)/shard_map/all_to_all | solution.py:104
  75.8 0.7 scatter_custom_fusion.3
  76.5 0.7 all_to_all.26
  77.2 0.5 slice.158
  77.7 0.6 slice.129
  84.2 0.7 add_multiply_fusion
  84.9 30.4 %all_gather.7 = f32[8,8,8]{2,1,0:T(8,128)S(1)} all-gather(f32[1,8,8]{2,1,0:T(8,128)S(1)} %add_multiply_fusion), channel_id=1, replica_groups=mesh['basin'=8,'band'=4] {'basin'}, dimensions={0}, use_global_device_ids=true | all-gather | bytes 2304 | tf_op jit(solution)/shard_map/all_gather | solution.py:9
  115.3 0.1 slice_reduce_fusion
  115.4 0.7 add_subtract_fusion
  116.1 0.1 eq.142
  116.3 1.2 copy-done.2
  117.4 3.2 %all-to-all-start.5 = ((s32[4,1,4]{2,1,0:T(1,128)}), s32[4,1,4]{2,1,0:T(1,128)S(1)}, u32[]{:S(2)}, u32[]{:S(2)}) async-start(s32[4,1,4]{2,1,0:T(1,128)} %bitcast.40), calls=%async_computation.5 | async-start | bytes 4096 | tf_op jit(solution)/shard_map/all_to_all | solution.py:142
  120.7 2.4 %copy.112 = f32[8,4,12,1024]{3,2,1,0:T(8,128)S(1)} copy(f32[8,4,12,1024]{3,0,2,1:T(8,128)} %copy-done.2) | data formatting | bytes 3145728 | tf_op jit(solution)/shard_map/all_to_all | solution.py:104
  123.0 1.3 reshape.315
  124.4 1.9 %copy.113 = f32[1024,384]{1,0:T(8,128)S(1)} copy(f32[1024,384]{0,1:T(8,128)} %bitcast.246) | data formatting | bytes 3145728 | tf_op jit(solution)/shard_map/sk,sx->kx/dot_general | solution.py:123
  126.3 0.8 fusion.20
  127.1 0.9 fusion.17
  128.2 0.6 constant_dynamic-update-slice_fusion
  128.9 0.1 copy.122
  129.0 1.2 scatter_custom_fusion.2
  130.2 3.3 %all-to-all-start.4 = ((f32[4,4,8]{2,1,0:T(4,128)}), f32[4,4,8]{2,1,0:T(4,128)S(1)}, u32[]{:S(2)}, u32[]{:S(2)}) async-start(f32[4,4,8]{2,1,0:T(4,128)} %bitcast.38), calls=%async_computation.4 | async-start | bytes 16384 | tf_op jit(solution)/shard_map/all_to_all | solution.py:135
  133.5 0.6 dynamic-slice
  134.7 0.5 broadcast.431
  135.2 0.7 reduce.7
  136.0 1.3 all-to-all-done.4
  137.3 0.2 fusion.22
  137.5 0.2 fusion.49
  137.8 0.2 slice_reduce_fusion.1
  138.0 0.2 dynamic-update-slice
  138.2 19.5 %all-reduce = f32[64]{0:T(128)S(1)} all-reduce(f32[64]{0:T(128)S(1)} %dynamic-update-slice), channel_id=2, replica_groups=mesh['basin'=8,'band'=4] {'basin'}, use_global_device_ids=true, to_apply=%add | all-reduce | flops 64 | bytes 512
  157.8 2.0 %while.16 = (s32[]{:T(128)}, f32[8,8]{1,0:T(8,128)S(1)}, f32[8]{0:T(128)S(1)}, s32[]{:T(128)}, f32[8,8,8]{2,1,0:T(8,128)S(1)}, /*index=5*/f32[8,8]{1,0:T(8,128)S(1)}, s32[]{:T(128)}, s32[]{:T(128)}) while((s32[]{:T(128)}, f32[8,8]{1,0:T(8,128)S(1)}, f32[8]{0:T(128)S(1)}, s32[]{:T(128)}, f32[8,8,8]{2,1,0:T(8,128)S(1)}, ...), condition=%wide.region_7.8_spmd.clone, body=%wide.region_6.7_spmd.clone.sunk | while | flops 7012 | bytes 21460 | solution.py:18
  157.8 0.1 convolution_select_fusion.2
  157.9 0.1 fusion.80
  158.0 0.1 convolution_select_fusion.2
  158.2 0.1 fusion.80
  158.3 0.1 convolution_select_fusion.2
  158.5 0.1 fusion.80
  158.6 0.1 convolution_select_fusion.2
  158.8 0.1 fusion.80
  158.9 0.1 convolution_select_fusion.2
  159.1 0.1 fusion.80
  159.2 0.1 convolution_select_fusion.2
  159.4 0.1 fusion.80
  159.5 0.1 convolution_select_fusion.2
  159.6 0.1 fusion.80
  159.8 0.1 fusion.11
  160.0 0.6 stack.95
  (73 shorter events, 1.1 us)
Async XLA Ops:
  0.6 126.5 %copy-start = (f32[8,128,128]{2,1,0:T(8,128)S(1)}, f32[8,128,128]{2,1,0:T(8,128)}, u32[]{:S(2)}) copy-start(f32[8,128,128]{2,1,0:T(8,128)} %param.23) | copy-start | bytes 1572868
  0.6 15.2 %copy-start.1 = (f32[192,128]{1,0:T(8,128)S(1)}, f32[192,128]{1,0:T(8,128)}, u32[]{:S(2)}) copy-start(f32[192,128]{1,0:T(8,128)} %param.19) | copy-start | bytes 294916
  0.7 15.2 %copy-start.4 = (f32[192,128]{1,0:T(8,128)S(1)}, f32[192,128]{1,0:T(8,128)}, u32[]{:S(2)}) copy-start(f32[192,128]{1,0:T(8,128)} %param.18) | copy-start | bytes 294916
  0.7 15.2 %copy-start.3 = (f32[192,128]{1,0:T(8,128)S(1)}, f32[192,128]{1,0:T(8,128)}, u32[]{:S(2)}) copy-start(f32[192,128]{1,0:T(8,128)} %param.20) | copy-start | bytes 294916
  4.4 18.1 %all-to-all-start = ((s32[8,4,12]{2,1,0:T(4,128)}), s32[8,4,12]{2,1,0:T(4,128)S(1)}, u32[]{:S(2)}, u32[]{:S(2)}) async-start(s32[8,4,12]{2,1,0:T(4,128)} %reshape.312), calls=%async_computation | async-start | bytes 32768 | tf_op jit(solution)/shard_map/all_to_all | solution.py:112
  22.5 45.8 %copy-start.10 = (s32[8]{0:T(128)S(1)}, s32[8]{0:T(128)}, u32[]{:S(2)}) copy-start(s32[8]{0:T(128)} %param.26) | copy-start | bytes 100
  22.5 42.6 %all-to-all-start.2 = ((f32[8,4,12,1024]{3,1,2,0:T(4,128)}), f32[8,4,12,1024]{3,1,2,0:T(4,128)S(1)}, u32[]{:S(2)}, u32[]{:S(2)}) async-start(f32[8,4,12,1024]{3,1,2,0:T(4,128)} %copy.110), calls=%async_computation.2 | async-start | bytes 3145728 | tf_op jit(solution)/shard_map/all_to_all | solution.py:105
  65.1 7.1 %all-to-all-start.1 = ((s32[8,4,12]{2,0,1:T(8,128)}), s32[8,4,12]{2,0,1:T(8,128)S(1)}, u32[]{:S(2)}, u32[]{:S(2)}) async-start(s32[8,4,12]{2,0,1:T(8,128)} %copy.107), calls=%async_computation.1 | async-start | bytes 32768 | tf_op jit(solution)/shard_map/all_to_all | solution.py:111
  70.6 6.6 %copy-start.5 = (f32[1,1,128,128]{3,2,1,0:T(8,128)S(1)}, f32[1,1,128,128]{3,2,1,0:T(8,128)}, u32[]{:S(2)}) copy-start(f32[1,1,128,128]{3,2,1,0:T(8,128)} %param.28) | copy-start | bytes 196612
  70.6 7.1 %copy-start.8 = (f32[1,1,128]{2,1,0:T(1,128)S(1)}, f32[1,1,128]{2,1,0:T(1,128)}, u32[]{:S(2)}) copy-start(f32[1,1,128]{2,1,0:T(1,128)} %param.29) | copy-start | bytes 1540
  72.2 44.1 %all-to-all-start.3 = ((f32[8,4,12,1024]{3,0,2,1:T(8,128)}), f32[8,4,12,1024]{3,0,2,1:T(8,128)S(1)}, u32[]{:S(2)}, u32[]{:S(2)}) async-start(f32[8,4,12,1024]{3,0,2,1:T(8,128)} %copy.111), calls=%async_computation.3 | async-start | bytes 3145728 | tf_op jit(solution)/shard_map/all_to_all | solution.py:104
  116.3 1.2 copy-start.2
  117.4 12.8 %all-to-all-start.5 = ((s32[4,1,4]{2,1,0:T(1,128)}), s32[4,1,4]{2,1,0:T(1,128)S(1)}, u32[]{:S(2)}, u32[]{:S(2)}) async-start(s32[4,1,4]{2,1,0:T(1,128)} %bitcast.40), calls=%async_computation.5 | async-start | bytes 4096 | tf_op jit(solution)/shard_map/all_to_all | solution.py:142
  126.2 1.9 %copy-start.6 = (f32[8,128]{1,0:T(8,128)S(1)}, f32[8,128]{1,0:T(8,128)}, u32[]{:S(2)}) copy-start(f32[8,128]{1,0:T(8,128)} %param.24) | copy-start | bytes 12292
  126.2 1.9 %copy-start.7 = (f32[8,128]{1,0:T(8,128)S(1)}, f32[8,128]{1,0:T(8,128)}, u32[]{:S(2)}) copy-start(f32[8,128]{1,0:T(8,128)} %param.25) | copy-start | bytes 12292
  126.3 7.2 %copy-start.12 = (u32[32]{0:T(128)S(1)}, u32[32]{0:T(128)}, u32[]{:S(2)}) copy-start(u32[32]{0:T(128)} %constant.83) | copy-start | bytes 388
  126.3 11.4 %copy-start.9 = (f32[1,1,128]{2,1,0:T(1,128)S(1)}, f32[1,1,128]{2,1,0:T(1,128)}, u32[]{:S(2)}) copy-start(f32[1,1,128]{2,1,0:T(1,128)} %param.30) | copy-start | bytes 1540
  126.3 33.5 %copy-start.11 = (f32[1,8]{1,0:T(1,128)S(1)}, f32[1,8]{1,0:T(1,128)}, u32[]{:S(2)}) copy-start(f32[1,8]{1,0:T(1,128)} %param.31) | copy-start | bytes 100
  130.2 7.1 %all-to-all-start.4 = ((f32[4,4,8]{2,1,0:T(4,128)}), f32[4,4,8]{2,1,0:T(4,128)S(1)}, u32[]{:S(2)}, u32[]{:S(2)}) async-start(f32[4,4,8]{2,1,0:T(4,128)} %bitcast.38), calls=%async_computation.4 | async-start | bytes 16384 | tf_op jit(solution)/shard_map/all_to_all | solution.py:135
where the time goes:
time: 161 us
  blocking collectives  49.9 us (31%)
  waiting for transfers between devices  38.7 us (24%)
  local copies, waits for them, and re-layouts  28.2 us (18%)
  starting transfers between devices  26.7 us (17%)
  between operations  7.51 us (5%)
  other arithmetic  5.32 us (3%)
  matrix products  4.27 us (3%)
    all_to_all x1, waiting for transfers between devices, local(): lax.all_to_all(buffer, 'basin', split_axis=0, concat_axis=0, tiled=True)  35.8 us
    all_gather x1, blocking collectives, entering(): pieces = jax.tree.map(lambda part: lax.all_gather(part, axis), value)  30.4 us
    unnamed x1, blocking collectives  19.5 us
    all_to_all x1, starting transfers between devices, local(): lax.all_to_all(slot_labels, 'basin', split_axis=0, concat_axis=0, tiled=T...  7.28 us
    all_to_all x1, starting transfers between devices, local(): lax.all_to_all(buffer, 'basin', split_axis=0, concat_axis=0, tiled=True)  6.13 us
    slice x1, local copies, waits for them, and re-layouts, land_update(): rain_now = precip[:, sub_step]  4.11 us
    scatter x2, local copies, waits for them, and re-layouts, pack_slots(): buffer = jnp.zeros((peer_count * slot_cap, values.shape[1]), values.dtype...  3.65 us
    reshape x2, local copies, waits for them, and re-layouts, local(): buffer = buffer.reshape(chains, rivers, tile_cap, sub_steps * reaches)  3.63 us
  transfers between devices with their start and end apart: 6, of which 3 were waited for; matrix products, arithmetic and copies ran while one was open for 18% of the time, Pallas kernels for 0%

commit v1 on v0

v1 whole, which is shorter than its diff:
```python
import jax
import jax.numpy as jnp
from jax import lax
from jax.sharding import PartitionSpec as P


def land_update(precip, soil_water, capacity, evap_rate):
    water = soil_water
    runoff_steps = []
    for sub_step in range(precip.shape[1]):
        rain_now = precip[:, sub_step]
        runoff_now = rain_now * water / (water + capacity)
        water = (1.0 - evap_rate) * water + rain_now - runoff_now
        runoff_steps.append(runoff_now)
    return (jnp.stack(runoff_steps, axis=1), water)


def route_series(mixed, keep, previous):
    flow = previous
    flows = []
    for sub_step in range(mixed.shape[-2]):
        flow = keep * flow + (1.0 - keep) * mixed[..., sub_step, :]
        flows.append(flow)
    return jnp.stack(flows, axis=-2)


def pack_slots(values, labels, targets, peer_count, slot_cap):
    entries = targets.shape[0]
    position = jnp.arange(entries, dtype=jnp.int32)
    earlier = (targets[:, None] == targets[None, :]) & (position[None, :] < position[:, None])
    ranking = jnp.sum(earlier.astype(jnp.int32), axis=1)
    target_slot = targets * slot_cap + ranking
    buffer = (
        jnp.zeros((peer_count * slot_cap, values.shape[1]), values.dtype)
        .at[target_slot]
        .set(values)
    )
    slot_labels = jnp.zeros((peer_count * slot_cap,), jnp.int32).at[target_slot].set(labels)
    return (buffer, slot_labels)


def gather_lateral(runoff, tile_dest, tile_block, blocks, shards):
    tile_count, width = runoff.shape
    tile_cap = max(2, 2 * tile_count // shards)
    grid = ("basin", "band")
    if tile_cap >= blocks:
        block_ids = tile_dest * blocks + tile_block
        pick = (
            block_ids[None, :] == jnp.arange(shards * blocks, dtype=jnp.int32)[:, None]
        ).astype(jnp.float32)
        dense = jnp.dot(pick, runoff, precision=lax.Precision.HIGHEST)
        arrived = lax.all_to_all(
            dense.reshape(shards, blocks, width), grid, split_axis=0, concat_axis=0, tiled=True
        )
        return jnp.sum(arrived, axis=0)
    buffer, slot_labels = pack_slots(runoff, tile_block, tile_dest, shards, tile_cap)
    arrived = lax.all_to_all(
        buffer.reshape(shards, tile_cap, width), grid, split_axis=0, concat_axis=0, tiled=True
    )
    arrived_ids = lax.all_to_all(
        slot_labels.reshape(shards, tile_cap), grid, split_axis=0, concat_axis=0, tiled=True
    )
    block_pick = (
        arrived_ids.reshape(-1)[:, None] == jnp.arange(blocks, dtype=jnp.int32)[None, :]
    ).astype(jnp.float32)
    return jnp.einsum(
        "sk,sx->kx", block_pick, arrived.reshape(-1, width), precision=lax.Precision.HIGHEST
    )


def local(
    precip,
    soil_water,
    capacity,
    evap_rate,
    tile_dest,
    tile_block,
    trib_op,
    trib_keep,
    trib_prev,
    trib_river,
    trib_reach,
    main_op,
    main_keep,
    main_prev,
    head_inflow,
):
    tile_count = precip.shape[0]
    sub_steps = precip.shape[1]
    reaches = precip.shape[2]
    blocks = trib_op.shape[0]
    chains = lax.axis_size("basin")
    rivers = lax.axis_size("band")
    shards = chains * rivers
    grid = ("basin", "band")
    operator = main_op[0, 0]
    keep_main = main_keep[0, 0]
    prev_main = main_prev[0, 0]

    runoff, water = land_update(precip, soil_water, capacity, evap_rate)
    lateral = gather_lateral(
        runoff.reshape(tile_count, sub_steps * reaches), tile_dest, tile_block, blocks, shards
    )
    trib_mixed = jnp.einsum(
        "brc,btc->btr",
        trib_op,
        lateral.reshape(blocks, sub_steps, reaches),
        precision=lax.Precision.HIGHEST,
    )
    trib_flows = route_series(trib_mixed, trib_keep, trib_prev)
    outlet = trib_flows[:, :, reaches - 1]

    payload = jnp.concatenate(
        [
            outlet.reshape(-1),
            trib_river.astype(jnp.float32),
            trib_reach.astype(jnp.float32),
            operator[reaches - 1],
            keep_main[reaches - 1 :],
            prev_main[reaches - 1 :],
        ]
    )
    width = payload.shape[0]
    padded = -(-width // 128) * 128
    payload = jnp.pad(payload, (0, padded - width))
    every = lax.all_gather(payload, grid, axis=0, tiled=False)

    mine = lax.axis_index("band")
    me = lax.axis_index("basin")
    at = 0
    outlets = every[:, at : at + blocks * sub_steps].reshape(chains, rivers * blocks, sub_steps)
    at += blocks * sub_steps
    river_of = every[:, at : at + blocks].reshape(chains, rivers * blocks)
    at += blocks
    reach_of = every[:, at : at + blocks].reshape(chains, rivers * blocks)
    at += blocks
    exit_rows = lax.dynamic_index_in_dim(
        every[:, at : at + reaches].reshape(chains, rivers, reaches), mine, axis=1, keepdims=False
    )
    at += reaches
    keeps = lax.dynamic_index_in_dim(
        every[:, at].reshape(chains, rivers), mine, axis=1, keepdims=False
    )
    starts = lax.dynamic_index_in_dim(
        every[:, at + 1].reshape(chains, rivers), mine, axis=1, keepdims=False
    )

    joins = (river_of == mine.astype(jnp.float32))[:, :, None] & (
        reach_of[:, :, None] == jnp.arange(reaches, dtype=jnp.float32)[None, None, :]
    )
    weight = joins.astype(jnp.float32)
    branch_all = jnp.sum(weight[:, :, None, :] * outlets[:, :, :, None], axis=1)
    branch_exit = jnp.sum(branch_all * exit_rows[:, None, :], axis=2)

    flow = starts
    free_exit = []
    for sub_step in range(sub_steps):
        flow = keeps * flow + (1.0 - keeps) * branch_exit[:, sub_step]
        free_exit.append(flow)
    free_exit = jnp.stack(free_exit, axis=1)
    lag = jnp.arange(sub_steps)[:, None] - jnp.arange(sub_steps)[None, :]
    lag_f = jnp.maximum(lag, 0).astype(jnp.float32)
    response = jnp.where(
        lag[None] >= 0,
        (exit_rows[:, 0] * (1.0 - keeps))[:, None, None] * keeps[:, None, None] ** lag_f[None],
        0.0,
    )

    def advance(section, entry):
        moved = jnp.sum(response[section] * entry[None, :], axis=1) + free_exit[section]
        return jnp.where(section < me, moved, entry)

    entry = lax.fori_loop(0, chains, advance, head_inflow[0], unroll=chains <= 16)

    branch_in = lax.dynamic_index_in_dim(branch_all, me, axis=0, keepdims=False)
    first_reach = (jnp.arange(reaches) == 0).astype(jnp.float32)
    fed = branch_in + entry[:, None] * first_reach[None, :]
    main_mixed = jnp.einsum("rc,tc->tr", operator, fed, precision=lax.Precision.HIGHEST)
    main_flows = route_series(main_mixed, keep_main, prev_main)
    return (water, trib_flows[:, sub_steps - 1], main_flows[None, None])


def solution(mesh):
    return jax.shard_map(
        local,
        mesh=mesh,
        in_specs=(
            P(("basin", "band"), None, None),
            P(("basin", "band"), None),
            P(("basin", "band"), None),
            P(("basin", "band"), None),
            P(("basin", "band")),
            P(("basin", "band")),
            P(("basin", "band"), None, None),
            P(("basin", "band"), None),
            P(("basin", "band"), None),
            P(("basin", "band")),
            P(("basin", "band")),
            P("band", "basin", None, None),
            P("band", "basin", None),
            P("band", "basin", None),
            P("band", None),
        ),
        out_specs=(
            P(("basin", "band"), None),
            P(("basin", "band"), None),
            P("band", "basin", None, None),
        ),
        check_vma=False,
    )
```

time: 161 us -> 91.7 us (0.57)
  starting transfers between devices: 26.7 us -> 7.3 us
  waiting for transfers between devices: 38.7 us -> 22.2 us
  local copies, waits for them, and re-layouts: 28.2 us -> 14.5 us
  blocking collectives: 49.9 us -> 39.6 us
  between operations: 7.51 us -> 0.97 us
    unnamed x1 -> x0, blocking collectives: 19.5 us -> none
    all_to_all x6 -> x1, starting transfers between devices: 26.7 us -> 7.3 us  [gather_lateral(): lax.all_to_all(dense.reshape(shards, blocks, width), grid, split_axis=0,...]
    all_to_all x6 -> x1, waiting for transfers between devices: 38.7 us -> 22.2 us  [gather_lateral(): lax.all_to_all(dense.reshape(shards, blocks, width), grid, split_axis=0,...]
    all_gather x1, blocking collectives: 30.4 us -> 39.6 us  [local(): every = lax.all_gather(payload, grid, axis=0, tiled=False)]
    all_to_all x6 -> x0, local copies, waits for them, and re-layouts: 6.21 us -> none  [the longest x1 2.35 us: local(): lax.all_to_all(lax.all_to_all(buffer, 'basin', split_axis=0, concat_axis=...]
    scatter x4 -> x0, local copies, waits for them, and re-layouts: 5.73 us -> none  [the longest x2 3.65 us: pack_slots(): buffer = jnp.zeros((peer_count * slot_cap, values.shape[1]), values.dtype...]
    reshape x4 -> x1, local copies, waits for them, and re-layouts: 5.69 us -> 0.12 us  [local(): runoff.reshape(tile_count, sub_steps * reaches)]
    unnamed x29, local copies, waits for them, and re-layouts: 2.04 us -> 4.79 us
  transfers between devices with their start and end apart: 6 -> 1, of which waited for: 3 -> 1; matrix products, arithmetic and copies ran while one was open for 18% -> 2% of each run, Pallas kernels for 0% -> 0%
where the time goes in v1:
time: 91.7 us; the launch traced here: 91.3 us
  blocking collectives  39.6 us (43%)
  waiting for transfers between devices  22.2 us (24%)
  local copies, waits for them, and re-layouts  14.5 us (16%)
  starting transfers between devices  7.3 us (8%)
  other arithmetic  4.05 us (4%)
  matrix products  2.78 us (3%)
  between operations  0.97 us (1%)
    all_gather x1, blocking collectives, local(): every = lax.all_gather(payload, grid, axis=0, tiled=False)  39.6 us
    all_to_all x1, waiting for transfers between devices, gather_lateral(): lax.all_to_all(dense.reshape(shards, blocks, width), grid, split_axis=0,...  22.2 us
    all_to_all x1, starting transfers between devices, gather_lateral(): lax.all_to_all(dense.reshape(shards, blocks, width), grid, split_axis=0,...  7.3 us
    unnamed x29, local copies, waits for them, and re-layouts  4.79 us
    slice x1, local copies, waits for them, and re-layouts, land_update(): rain_now = precip[:, sub_step]  4.67 us
  transfers between devices with their start and end apart: 1, of which 1 were waited for; matrix products, arithmetic and copies ran while one was open for 2% of the time, Pallas kernels for 0%

profile of v1, /device:TPU:0, one launch (start us, length us, event | category | flops | bytes accessed | tf_op | source)
XLA Modules:
  0.0 91.3 jit_solution(9325385059556425519)
XLA Ops:
  0.6 0.0 copy-start
  0.7 0.0 copy-start.1
  0.7 0.0 copy-start.3
  0.7 4.7 %fusion.52 = (f32[192,1,128]{2,1,0:T(1,128)S(1)}, f32[192,1,128]{2,1,0:T(1,128)S(1)}, f32[192,1,128]{2,1,0:T(1,128)S(1)}, f32[192,1,128]{2,1,0:T(1,128)S(1)}, f3...) fusion(f32[192,8,128]{2,1,0:T(8,128)} %param.15), kind=kLoop, calls=%fused_computation.158 | loop fusion | bytes 1572864 | tf_op jit(solution)/shard_map/slice | solution.py:11
  5.4 0.9 copy-done.2
  6.3 0.1 bitcast_dynamic-update-slice_fusion.6
  6.3 0.1 bitcast_dynamic-update-slice_fusion.5
  6.4 0.1 bitcast_dynamic-update-slice_fusion.4
  6.5 0.1 bitcast_dynamic-update-slice_fusion.3
  6.6 0.1 bitcast_dynamic-update-slice_fusion.2
  6.7 0.1 bitcast_dynamic-update-slice_fusion.1
  6.7 0.1 bitcast_dynamic-update-slice_fusion
  6.8 0.5 copy.95
  7.3 0.0 copy-start.8
  7.3 0.1 reshape.283
  7.4 0.5 copy-done.8
  8.0 0.0 copy-done.9
  8.0 1.7 %fusion = f32[32,8,1024]{2,1,0:T(8,128)} fusion(f32[192,1024,1]{1,0,2:T(8,128)S(1)} %reshape.283, s32[32,8]{1,0:T(8,128)S(1)} %multiply_add_fusion, s32[192]{0:T(256)S(1)} %multiply_add_fusion.17), kind=kOutput, calls=%fused_computation.1 | convolution fusion | flops 604028928 | bytes 1836800 | tf_op jit(solution)/shard_map/dot_general | solution.py:51
  9.6 7.3 %all-to-all-start = ((f32[32,8,1024]{2,1,0:T(8,128)}), f32[32,8,1024]{2,1,0:T(8,128)S(1)}, u32[]{:S(2)}, u32[]{:S(2)}) async-start(f32[32,8,1024]{2,1,0:T(8,128)} %fusion), calls=%async_computation | async-start | bytes 2097152 | tf_op jit(solution)/shard_map/all_to_all | solution.py:52
  17.0 0.6 copy-done.12
  17.6 0.7 copy-done.13
  18.3 0.7 copy-done.10
  18.9 0.6 slice.154
  19.5 0.1 copy-done.11
  19.6 0.7 slice.156
  20.3 0.7 add_subtract_fusion
  21.0 22.2 %all-to-all-done = f32[32,8,1024]{2,1,0:T(8,128)S(1)} async-done(((f32[32,8,1024]{2,1,0:T(8,128)}), f32[32,8,1024]{2,1,0:T(8,128)S(1)}, u32[]{:S(2)}, u32[]{:S(2)}) %all-to-all-start) | async-done | bytes 1048608 | tf_op jit(solution)/shard_map/all_to_all | solution.py:52
  43.2 0.1 reduce_sum.113
  43.3 0.9 %fusion.8 = f32[8,8,128]{2,1,0:T(8,128)S(1)} fusion(f32[8,128,128]{2,1,0:T(8,128)S(1)} %copy-done, f32[1,8,8,128]{3,1,2,0:T(8,128)S(1)} %bitcast.301), kind=kOutput, calls=%fused_computation.42 | convolution fusion | flops 12582912 | bytes 589824 | tf_op jit(solution)/shard_map/brc,btc->btr/dot_general | solution.py:104
  44.2 0.7 copy-done.4
  44.9 0.0 copy-done.6
  45.0 0.6 constant_dynamic-update-slice_fusion
  45.6 0.1 slice.189
  45.7 0.1 copy.103
  45.8 0.1 reshape_squeeze.9
  45.9 1.4 %concatenate.3 = f32[210]{0:T(256)S(1)} concatenate(f32[64]{0:T(128)S(1)} %reshape_squeeze.9, f32[8]{0:T(128)S(1)} %convert_element_type.33, f32[8]{0:T(128)S(1)} %convert_element_type.34, f32[128]{0:T(128)S(1)} %slice_bitcast_fusion.8, f32[1]{0:T(128)} %bitcast.35, f32[1]{0:T(128)} %bitcast.36), dimensions={0} | concatenate | bytes 1680 | tf_op jit(solution)/shard_map/concatenate | solution.py:113
  47.3 39.6 %all-gather.1 = f32[32,1,256]{2,1,0:T(1,128)S(1)} all-gather(f32[1,1,256]{2,1,0:T(1,128)S(1)} %bitcast.324), channel_id=2, replica_groups=mesh['basin'=8,'band'=4] {'basin','band'}, dimensions={0}, use_global_device_ids=true | all-gather | bytes 33792 | tf_op jit(solution)/shard_map/all_gather | solution.py:126
  86.9 0.1 slice.191
  87.0 0.1 slice.193
  87.0 0.2 slice_reduce_fusion
  87.2 0.1 mul.522
  87.3 0.1 eq.75
  87.4 0.1 slice_compare_fusion
  87.5 0.1 eq.74
  87.6 0.1 reshape_squeeze.10
  87.6 0.1 reshape_squeeze.11
  87.7 0.1 fusion.5
  87.9 0.3 multiply_reduce_fusion
  88.2 0.1 multiply_reduce_fusion.1
  88.3 0.2 multiply_add_fusion.1
  88.5 0.1 multiply_select_fusion
  88.7 0.6 copy-done.7
  89.3 0.1 fusion.12
  89.4 0.1 stack.94
  89.5 0.1 fusion.14
  89.6 0.1 fusion.16
  89.8 0.1 fusion.18
  89.9 0.1 fusion.20
  90.0 0.1 fusion.22
  90.2 0.1 fusion.24
  90.3 0.1 fusion.26
  90.4 0.2 fusion.6
  90.6 0.1 fusion.43
  90.7 0.6 stack.95
  (44 shorter events, 0.3 us)
Async XLA Ops:
  0.6 42.6 %copy-start = (f32[8,128,128]{2,1,0:T(8,128)S(1)}, f32[8,128,128]{2,1,0:T(8,128)}, u32[]{:S(2)}) copy-start(f32[8,128,128]{2,1,0:T(8,128)} %param.21) | copy-start | bytes 1572868
  0.7 4.7 %copy-start.1 = (f32[192,128]{1,0:T(8,128)S(1)}, f32[192,128]{1,0:T(8,128)}, u32[]{:S(2)}) copy-start(f32[192,128]{1,0:T(8,128)} %param.17) | copy-start | bytes 294916
  0.7 4.7 %copy-start.3 = (f32[192,128]{1,0:T(8,128)S(1)}, f32[192,128]{1,0:T(8,128)}, u32[]{:S(2)}) copy-start(f32[192,128]{1,0:T(8,128)} %param.16) | copy-start | bytes 294916
  5.4 0.9 copy-start.2
  7.3 0.7 copy-start.8
  7.3 0.7 copy-start.9
  9.6 10.6 %copy-start.5 = (f32[1,1,128,128]{3,2,1,0:T(8,128)S(1)}, f32[1,1,128,128]{3,2,1,0:T(8,128)}, u32[]{:S(2)}) copy-start(f32[1,1,128,128]{3,2,1,0:T(8,128)} %param.26) | copy-start | bytes 196612
  9.6 33.5 %all-to-all-start = ((f32[32,8,1024]{2,1,0:T(8,128)}), f32[32,8,1024]{2,1,0:T(8,128)S(1)}, u32[]{:S(2)}, u32[]{:S(2)}) async-start(f32[32,8,1024]{2,1,0:T(8,128)} %fusion), calls=%async_computation | async-start | bytes 2097152 | tf_op jit(solution)/shard_map/all_to_all | solution.py:52
  16.9 0.7 copy-start.12
  17.6 0.7 copy-start.13
  18.3 0.7 copy-start.10
  18.9 0.7 copy-start.11
  44.2 0.7 copy-start.4
  44.2 0.7 copy-start.6
  88.7 0.7 copy-start.7

commit v2 on v1

--- a/solution.py
+++ b/solution.py
@@ -123,7 +123,9 @@
     width = payload.shape[0]
     padded = -(-width // 128) * 128
     payload = jnp.pad(payload, (0, padded - width))
-    every = lax.all_gather(payload, grid, axis=0, tiled=False)
+    every = lax.all_to_all(
+        jnp.broadcast_to(payload[None], (shards, padded)), grid, split_axis=0, concat_axis=0, tiled=True
+    )
 
     mine = lax.axis_index("band")
     me = lax.axis_index("basin")

time: 91.7 us -> 63.7 us (0.69)
  blocking collectives: 39.6 us -> 0 us
  waiting for transfers between devices: 22.2 us -> 29.4 us
  starting transfers between devices: 7.3 us -> 10.9 us
    all_gather x1 -> x0, blocking collectives: 39.6 us -> none  [local(): every = lax.all_gather(payload, grid, axis=0, tiled=False)]
    all_to_all x0 -> x1, waiting for transfers between devices: none -> 7.24 us  [local(): lax.all_to_all(jnp.broadcast_to(payload[None], (shards, padded)), grid, s...]
    all_to_all x0 -> x1, starting transfers between devices: none -> 3.62 us  [local(): lax.all_to_all(jnp.broadcast_to(payload[None], (shards, padded)), grid, s...]
  transfers between devices with their start and end apart: 1 -> 2, of which waited for: 1 -> 2; matrix products, arithmetic and copies ran while one was open for 2% -> 3% of each run, Pallas kernels for 0% -> 0%
where the time goes in v2:
time: 63.7 us; the launch traced here: 63.3 us
  waiting for transfers between devices  29.4 us (46%)
  local copies, waits for them, and re-layouts  15.1 us (24%)
  starting transfers between devices  10.9 us (17%)
  other arithmetic  4.05 us (6%)
  matrix products  2.78 us (4%)
  between operations  0.98 us (2%)
    all_to_all x1, waiting for transfers between devices, gather_lateral(): lax.all_to_all(dense.reshape(shards, blocks, width), grid, split_axis=0,...  22.2 us
    all_to_all x1, starting transfers between devices, gather_lateral(): lax.all_to_all(dense.reshape(shards, blocks, width), grid, split_axis=0,...  7.3 us
    all_to_all x1, waiting for transfers between devices, local(): lax.all_to_all(jnp.broadcast_to(payload[None], (shards, padded)), grid, s...  7.24 us
    unnamed x29, local copies, waits for them, and re-layouts  4.79 us
    slice x1, local copies, waits for them, and re-layouts, land_update(): rain_now = precip[:, sub_step]  4.67 us
    all_to_all x1, starting transfers between devices, local(): lax.all_to_all(jnp.broadcast_to(payload[None], (shards, padded)), grid, s...  3.62 us
    dot_general x1, matrix products, gather_lateral(): dense = jnp.dot(pick, runoff, precision=lax.Precision.HIGHEST)  1.65 us
    concatenate x1, local copies, waits for them, and re-layouts, local(): jnp.concatenate([outlet.reshape(-1), trib_river.astype(jnp.float32), trib...  1.42 us
  transfers between devices with their start and end apart: 2, of which 2 were waited for; matrix products, arithmetic and copies ran while one was open for 3% of the time, Pallas kernels for 0%

profile of v2, /device:TPU:0, one launch (start us, length us, event | category | flops | bytes accessed | tf_op | source)
XLA Modules:
  0.0 63.3 jit_solution(5736210271424722319)
XLA Ops:
  0.6 0.0 copy-start
  0.7 0.0 copy-start.1
  0.7 4.7 %fusion.52 = (f32[192,1,128]{2,1,0:T(1,128)S(1)}, f32[192,1,128]{2,1,0:T(1,128)S(1)}, f32[192,1,128]{2,1,0:T(1,128)S(1)}, f32[192,1,128]{2,1,0:T(1,128)S(1)}, f3...) fusion(f32[192,8,128]{2,1,0:T(8,128)} %param.15), kind=kLoop, calls=%fused_computation.158 | loop fusion | bytes 1572864 | tf_op jit(solution)/shard_map/slice | solution.py:11
  5.4 0.9 %copy-done.2 = f32[192,128]{1,0:T(8,128)S(1)} copy-done((f32[192,128]{1,0:T(8,128)S(1)}, f32[192,128]{1,0:T(8,128)}, u32[]{:S(2)}) %copy-start.2) | copy-done | bytes 98328
  6.3 0.1 bitcast_dynamic-update-slice_fusion.6
  6.3 0.1 bitcast_dynamic-update-slice_fusion.5
  6.4 0.1 bitcast_dynamic-update-slice_fusion.4
  6.5 0.1 bitcast_dynamic-update-slice_fusion.3
  6.6 0.1 bitcast_dynamic-update-slice_fusion.2
  6.7 0.1 bitcast_dynamic-update-slice_fusion.1
  6.7 0.1 bitcast_dynamic-update-slice_fusion
  6.8 0.5 copy.95
  7.3 0.1 reshape.285
  7.4 0.5 copy-done.8
  8.0 0.0 copy-done.9
  8.0 1.7 %fusion = f32[32,8,1024]{2,1,0:T(8,128)} fusion(f32[192,1024,1]{1,0,2:T(8,128)S(1)} %reshape.285, s32[32,8]{1,0:T(8,128)S(1)} %multiply_add_fusion, s32[192]{0:T(256)S(1)} %multiply_add_fusion.17), kind=kOutput, calls=%fused_computation.1 | convolution fusion | flops 604028928 | bytes 1836800 | tf_op jit(solution)/shard_map/dot_general | solution.py:51
  9.6 7.3 %all-to-all-start = ((f32[32,8,1024]{2,1,0:T(8,128)}), f32[32,8,1024]{2,1,0:T(8,128)S(1)}, u32[]{:S(2)}, u32[]{:S(2)}) async-start(f32[32,8,1024]{2,1,0:T(8,128)} %fusion), calls=%async_computation | async-start | bytes 2097152 | tf_op jit(solution)/shard_map/all_to_all | solution.py:52
  17.0 0.6 %copy-done.12 = s32[8]{0:T(128)S(1)} copy-done((s32[8]{0:T(128)S(1)}, s32[8]{0:T(128)}, u32[]{:S(2)}) %copy-start.12) | copy-done | bytes 56
  17.6 0.7 %copy-done.13 = s32[8]{0:T(128)S(1)} copy-done((s32[8]{0:T(128)S(1)}, s32[8]{0:T(128)}, u32[]{:S(2)}) %copy-start.13) | copy-done | bytes 56
  18.3 0.7 %copy-done.10 = f32[1,1,128]{2,1,0:T(1,128)S(1)} copy-done((f32[1,1,128]{2,1,0:T(1,128)S(1)}, f32[1,1,128]{2,1,0:T(1,128)}, u32[]{:S(2)}) %copy-start.10) | copy-done | bytes 536
  18.9 0.6 slice.154
  19.5 0.1 copy-done.11
  19.6 0.7 %slice.156 = f32[1,1,1]{2,1,0:T(1,128)} slice(f32[1,1,128]{2,1,0:T(1,128)S(1)} %copy-done.11), slice={[0:1], [0:1], [127:128]} | slice | bytes 8 | tf_op jit(solution)/shard_map/slice | solution.py:120
  20.3 0.7 %add_subtract_fusion = f32[192,128]{1,0:T(8,128)} fusion(f32[192,128]{1,0:T(8,128)S(1)} %bitcast.294, f32[192,128]{1,0:T(8,128)S(1)} %copy-done.2, f32[192,128]{1,0:T(8,128)S(1)} %copy-done.1, f32[192,128]{1,0:T(8,128)S(1)} %bitcast.288, f32[192,128]{1,0:T(8,128)S(1)} %get-tuple-element.30, f32[192,128]{1,0:T(8,128)S(1)} %bitcast.279), kind=kLoop, calls=%fused_computation.17 | loop fusion | flops 466944 | bytes 688128 | tf_op jit(solution)/shard_map/sub | solution.py:13
  21.0 22.2 %all-to-all-done = f32[32,8,1024]{2,1,0:T(8,128)S(1)} async-done(((f32[32,8,1024]{2,1,0:T(8,128)}), f32[32,8,1024]{2,1,0:T(8,128)S(1)}, u32[]{:S(2)}, u32[]{:S(2)}) %all-to-all-start) | async-done | bytes 1048608 | tf_op jit(solution)/shard_map/all_to_all | solution.py:52
  43.2 0.1 reduce_sum.113
  43.3 0.9 %fusion.8 = f32[8,8,128]{2,1,0:T(8,128)S(1)} fusion(f32[8,128,128]{2,1,0:T(8,128)S(1)} %copy-done, f32[1,8,8,128]{3,1,2,0:T(8,128)S(1)} %bitcast.300), kind=kOutput, calls=%fused_computation.42 | convolution fusion | flops 12582912 | bytes 589824 | tf_op jit(solution)/shard_map/brc,btc->btr/dot_general | solution.py:104
  44.2 0.7 %copy-done.4 = f32[8,128]{1,0:T(8,128)S(1)} copy-done((f32[8,128]{1,0:T(8,128)S(1)}, f32[8,128]{1,0:T(8,128)}, u32[]{:S(2)}) %copy-start.4) | copy-done | bytes 4120
  44.9 0.0 copy-done.6
  45.0 0.6 constant_dynamic-update-slice_fusion
  45.6 0.1 slice.189
  45.7 0.1 copy.103
  45.8 0.1 reshape_squeeze.9
  45.9 1.4 %concatenate.3 = f32[210]{0:T(256)S(1)} concatenate(f32[64]{0:T(128)S(1)} %reshape_squeeze.9, f32[8]{0:T(128)S(1)} %convert_element_type.33, f32[8]{0:T(128)S(1)} %convert_element_type.34, f32[128]{0:T(128)S(1)} %slice_bitcast_fusion.8, f32[1]{0:T(128)} %bitcast.35, f32[1]{0:T(128)} %bitcast.36), dimensions={0} | concatenate | bytes 1680 | tf_op jit(solution)/shard_map/concatenate | solution.py:113
  47.3 0.6 broadcast_in_dim.12
  47.9 3.6 %all-to-all-start.1 = ((f32[32,1,256]{2,1,0:T(1,128)}), f32[32,1,256]{2,1,0:T(1,128)S(1)}, u32[]{:S(2)}, u32[]{:S(2)}) async-start(f32[32,1,256]{2,1,0:T(1,128)} %broadcast_in_dim.12), calls=%async_computation.1 | async-start | bytes 65536 | tf_op jit(solution)/shard_map/all_to_all | solution.py:126
  51.6 7.2 %all-to-all-done.1 = f32[32,1,256]{2,1,0:T(1,128)S(1)} async-done(((f32[32,1,256]{2,1,0:T(1,128)}), f32[32,1,256]{2,1,0:T(1,128)S(1)}, u32[]{:S(2)}, u32[]{:S(2)}) %all-to-all-start.1) | async-done | bytes 32800 | tf_op jit(solution)/shard_map/all_to_all | solution.py:126
  58.8 0.1 slice.191
  58.9 0.1 slice.193
  59.0 0.2 slice_reduce_fusion
  59.1 0.1 mul.522
  59.2 0.1 eq.75
  59.3 0.1 slice_compare_fusion
  59.4 0.1 eq.74
  59.5 0.1 reshape_squeeze.10
  59.6 0.1 reshape_squeeze.11
  59.6 0.1 fusion.5
  59.8 0.3 multiply_reduce_fusion
  60.2 0.1 multiply_reduce_fusion.1
  60.2 0.2 multiply_add_fusion.1
  60.5 0.1 multiply_select_fusion
  60.6 0.6 %copy-done.7 = f32[1,8]{1,0:T(1,128)S(1)} copy-done((f32[1,8]{1,0:T(1,128)S(1)}, f32[1,8]{1,0:T(1,128)}, u32[]{:S(2)}) %copy-start.7) | copy-done | bytes 56
  61.2 0.1 fusion.12
  61.4 0.1 stack.94
  61.4 0.1 fusion.14
  61.6 0.1 fusion.16
  61.7 0.1 fusion.18
  61.8 0.1 fusion.20
  62.0 0.1 fusion.22
  62.1 0.1 fusion.24
  62.2 0.1 fusion.26
  62.4 0.2 fusion.6
  62.6 0.1 fusion.43
  62.6 0.6 stack.95
  (46 shorter events, 0.3 us)
Async XLA Ops:
  0.6 42.6 %copy-start = (f32[8,128,128]{2,1,0:T(8,128)S(1)}, f32[8,128,128]{2,1,0:T(8,128)}, u32[]{:S(2)}) copy-start(f32[8,128,128]{2,1,0:T(8,128)} %param.21) | copy-start | bytes 1572868
  0.7 4.7 %copy-start.1 = (f32[192,128]{1,0:T(8,128)S(1)}, f32[192,128]{1,0:T(8,128)}, u32[]{:S(2)}) copy-start(f32[192,128]{1,0:T(8,128)} %param.17) | copy-start | bytes 294916
  0.7 4.7 %copy-start.3 = (f32[192,128]{1,0:T(8,128)S(1)}, f32[192,128]{1,0:T(8,128)}, u32[]{:S(2)}) copy-start(f32[192,128]{1,0:T(8,128)} %param.16) | copy-start | bytes 294916
  5.4 0.9 %copy-start.2 = (f32[192,128]{1,0:T(8,128)S(1)}, f32[192,128]{1,0:T(8,128)}, u32[]{:S(2)}) copy-start(f32[192,128]{1,0:T(8,128)} %param.18) | copy-start | bytes 294916
  7.3 0.7 %copy-start.8 = (s32[192]{0:T(256)S(1)}, s32[192]{0:T(256)}, u32[]{:S(2)}) copy-start(s32[192]{0:T(256)} %param.20) | copy-start | bytes 2308
  7.3 0.7 %copy-start.9 = (s32[192]{0:T(256)S(1)}, s32[192]{0:T(256)}, u32[]{:S(2)}) copy-start(s32[192]{0:T(256)} %param.19) | copy-start | bytes 2308
  9.6 10.6 %copy-start.5 = (f32[1,1,128,128]{3,2,1,0:T(8,128)S(1)}, f32[1,1,128,128]{3,2,1,0:T(8,128)}, u32[]{:S(2)}) copy-start(f32[1,1,128,128]{3,2,1,0:T(8,128)} %param.26) | copy-start | bytes 196612
  9.6 33.5 %all-to-all-start = ((f32[32,8,1024]{2,1,0:T(8,128)}), f32[32,8,1024]{2,1,0:T(8,128)S(1)}, u32[]{:S(2)}, u32[]{:S(2)}) async-start(f32[32,8,1024]{2,1,0:T(8,128)} %fusion), calls=%async_computation | async-start | bytes 2097152 | tf_op jit(solution)/shard_map/all_to_all | solution.py:52
  16.9 0.7 %copy-start.12 = (s32[8]{0:T(128)S(1)}, s32[8]{0:T(128)}, u32[]{:S(2)}) copy-start(s32[8]{0:T(128)} %param.24) | copy-start | bytes 100
  17.6 0.7 %copy-start.13 = (s32[8]{0:T(128)S(1)}, s32[8]{0:T(128)}, u32[]{:S(2)}) copy-start(s32[8]{0:T(128)} %param.25) | copy-start | bytes 100
  18.3 0.7 %copy-start.10 = (f32[1,1,128]{2,1,0:T(1,128)S(1)}, f32[1,1,128]{2,1,0:T(1,128)}, u32[]{:S(2)}) copy-start(f32[1,1,128]{2,1,0:T(1,128)} %param.27) | copy-start | bytes 1540
  18.9 0.7 %copy-start.11 = (f32[1,1,128]{2,1,0:T(1,128)S(1)}, f32[1,1,128]{2,1,0:T(1,128)}, u32[]{:S(2)}) copy-start(f32[1,1,128]{2,1,0:T(1,128)} %param.28) | copy-start | bytes 1540
  44.2 0.7 %copy-start.4 = (f32[8,128]{1,0:T(8,128)S(1)}, f32[8,128]{1,0:T(8,128)}, u32[]{:S(2)}) copy-start(f32[8,128]{1,0:T(8,128)} %param.22) | copy-start | bytes 12292
  44.2 0.7 %copy-start.6 = (f32[8,128]{1,0:T(8,128)S(1)}, f32[8,128]{1,0:T(8,128)}, u32[]{:S(2)}) copy-start(f32[8,128]{1,0:T(8,128)} %param.23) | copy-start | bytes 12292
  47.9 10.9 %all-to-all-start.1 = ((f32[32,1,256]{2,1,0:T(1,128)}), f32[32,1,256]{2,1,0:T(1,128)S(1)}, u32[]{:S(2)}, u32[]{:S(2)}) async-start(f32[32,1,256]{2,1,0:T(1,128)} %broadcast_in_dim.12), calls=%async_computation.1 | async-start | bytes 65536 | tf_op jit(solution)/shard_map/all_to_all | solution.py:126
  60.6 0.7 %copy-start.7 = (f32[1,8]{1,0:T(1,128)S(1)}, f32[1,8]{1,0:T(1,128)}, u32[]{:S(2)}) copy-start(f32[1,8]{1,0:T(1,128)} %param.29) | copy-start | bytes 100

commit v3 on v2

--- a/solution.py
+++ b/solution.py
@@ -49,10 +49,7 @@
             block_ids[None, :] == jnp.arange(shards * blocks, dtype=jnp.int32)[:, None]
         ).astype(jnp.float32)
         dense = jnp.dot(pick, runoff, precision=lax.Precision.HIGHEST)
-        arrived = lax.all_to_all(
-            dense.reshape(shards, blocks, width), grid, split_axis=0, concat_axis=0, tiled=True
-        )
-        return jnp.sum(arrived, axis=0)
+        return lax.psum_scatter(dense, grid, scatter_dimension=0, tiled=True)
     buffer, slot_labels = pack_slots(runoff, tile_block, tile_dest, shards, tile_cap)
     arrived = lax.all_to_all(
         buffer.reshape(shards, tile_cap, width), grid, split_axis=0, concat_axis=0, tiled=True

time: 63.7 us -> 180 us (2.83)
  waiting for transfers between devices: 29.4 us -> 141 us
  between operations: 0.98 us -> 14.3 us
  starting transfers between devices: 10.9 us -> 2.6 us
    reduce_scatter x0 -> x1, waiting for transfers between devices: none -> 134 us  [gather_lateral(): return lax.psum_scatter(dense, grid, scatter_dimension=0, tiled=True)]
    all_to_all x1 -> x0, waiting for transfers between devices: 22.2 us -> none  [gather_lateral(): lax.all_to_all(dense.reshape(shards, blocks, width), grid, split_axis=0,...]
    all_to_all x1 -> x0, starting transfers between devices: 7.3 us -> none  [gather_lateral(): lax.all_to_all(dense.reshape(shards, blocks, width), grid, split_axis=0,...]
  transfers between devices with their start and end apart: 2 -> 2, of which waited for: 2 -> 2; matrix products, arithmetic and copies ran while one was open for 3% -> 1% of each run, Pallas kernels for 0% -> 0%
where the time goes in v3:
time: 180 us
  waiting for transfers between devices  141 us (78%)
  between operations  14.3 us (8%)
  local copies, waits for them, and re-layouts  13.9 us (8%)
  other arithmetic  3.99 us (2%)
  matrix products  3.53 us (2%)
  starting transfers between devices  2.6 us (1%)
    reduce_scatter x1, waiting for transfers between devices, gather_lateral(): return lax.psum_scatter(dense, grid, scatter_dimension=0, tiled=True)  134 us
    all_to_all x1, waiting for transfers between devices, local(): lax.all_to_all(jnp.broadcast_to(payload[None], (shards, padded)), grid, s...  7.24 us
    slice x1, local copies, waits for them, and re-layouts, land_update(): rain_now = precip[:, sub_step]  4.67 us
    unnamed x29, local copies, waits for them, and re-layouts  4.23 us
  transfers between devices with their start and end apart: 2, of which 2 were waited for; matrix products, arithmetic and copies ran while one was open for 1% of the time, Pallas kernels for 0%

profile of v3, /device:TPU:0, one launch (start us, length us, event | category | flops | bytes accessed | tf_op | source)
XLA Modules:
  0.0 179.8 jit_solution(7415428891907542670)
XLA Ops:
  7.2 0.0 copy-start
  7.2 0.0 reduce-scatter.2.cloned.1.call-start
  7.2 4.7 %fusion.51 = (f32[192,1,128]{2,1,0:T(1,128)S(1)}, f32[192,1,128]{2,1,0:T(1,128)S(1)}, f32[192,1,128]{2,1,0:T(1,128)S(1)}, f32[192,1,128]{2,1,0:T(1,128)S(1)}, f3...) fusion(f32[192,8,128]{2,1,0:T(8,128)} %param.15), kind=kLoop, calls=%fused_computation.157 | loop fusion | bytes 1572864 | tf_op jit(solution)/shard_map/slice | solution.py:11
  11.9 0.0 copy-start.2
  12.0 0.9 copy-done.2
  12.8 0.1 bitcast_dynamic-update-slice_fusion.6
  12.9 0.1 bitcast_dynamic-update-slice_fusion.5
  13.0 0.1 bitcast_dynamic-update-slice_fusion.4
  13.1 0.1 bitcast_dynamic-update-slice_fusion.3
  13.2 0.1 bitcast_dynamic-update-slice_fusion.2
  13.2 0.1 bitcast_dynamic-update-slice_fusion.1
  13.3 0.0 copy-start.8
  13.3 0.1 bitcast_dynamic-update-slice_fusion
  13.4 0.6 copy-done.8
  14.0 0.0 copy-done.9
  14.0 1.6 fusion
  15.6 0.0 reduce-scatter.2.cloned.1.call-update
  15.7 0.0 copy-start.10
  15.7 0.6 copy-done.10
  16.3 0.6 slice.154
  16.9 0.1 copy-done.11
  17.0 0.6 slice.156
  17.6 0.0 copy-done.12
  17.7 0.7 copy-done.13
  18.3 0.7 add_subtract_fusion
  19.1 134.2 %reduce-scatter.2.cloned.1.call-done = f32[8,1024]{1,0:T(8,128)} async-done(((f32[256,1024]{1,0:T(8,128)}), f32[8,1024]{1,0:T(8,128)}) %reduce-scatter.2.cloned.1.call-update) | async-done | bytes 32784 | tf_op jit(solution)/shard_map/reduce_scatter | solution.py:52
  153.3 1.7 fusion.8
  155.0 0.7 copy-done.4
  155.7 0.0 copy-done.6
  155.8 0.6 constant_dynamic-update-slice_fusion
  156.4 0.1 slice.189
  156.5 0.1 copy.107
  156.6 0.1 reshape_squeeze.9
  156.7 1.4 concatenate.3
  158.1 0.6 broadcast_in_dim.12
  158.7 2.6 %all-to-all-start = ((f32[32,1,256]{2,1,0:T(1,128)}), f32[32,1,256]{2,1,0:T(1,128)S(1)}, u32[]{:S(2)}, u32[]{:S(2)}) async-start(f32[32,1,256]{2,1,0:T(1,128)} %broadcast_in_dim.12), calls=%async_computation.1 | async-start | bytes 65536 | tf_op jit(solution)/shard_map/all_to_all | solution.py:123
  161.3 7.2 %all-to-all-done = f32[32,1,256]{2,1,0:T(1,128)S(1)} async-done(((f32[32,1,256]{2,1,0:T(1,128)}), f32[32,1,256]{2,1,0:T(1,128)S(1)}, u32[]{:S(2)}, u32[]{:S(2)}) %all-to-all-start) | async-done | bytes 32800 | tf_op jit(solution)/shard_map/all_to_all | solution.py:123
  168.5 0.1 slice.191
  168.6 0.1 slice.193
  168.7 0.2 slice_reduce_fusion
  168.8 0.1 eq.61
  168.9 0.1 slice_compare_fusion
  169.0 0.1 eq.60
  169.1 0.1 mul.522
  169.2 0.1 reshape_squeeze.10
  169.3 0.1 reshape_squeeze.11
  169.3 0.1 fusion.5
  169.5 0.3 multiply_reduce_fusion
  169.9 0.1 multiply_reduce_fusion.1
  169.9 0.2 multiply_add_fusion
  170.2 0.1 multiply_select_fusion
  170.3 0.6 copy-done.7
  170.9 0.1 fusion.11
  171.1 0.1 stack.94
  171.1 0.1 fusion.13
  171.3 0.1 fusion.15
  171.4 0.1 fusion.17
  171.5 0.1 fusion.19
  171.7 0.1 fusion.21
  171.8 0.1 fusion.23
  171.9 0.1 fusion.25
  172.1 0.2 fusion.6
  172.3 0.1 fusion.42
  172.3 0.6 stack.95
  (43 shorter events, 0.3 us)
Async XLA Ops:
  7.2 146.2 %copy-start = (f32[8,128,128]{2,1,0:T(8,128)S(1)}, f32[8,128,128]{2,1,0:T(8,128)}, u32[]{:S(2)}) copy-start(f32[8,128,128]{2,1,0:T(8,128)} %param.21) | copy-start | bytes 1572868
  7.2 4.7 %copy-start.3 = (f32[192,128]{1,0:T(8,128)S(1)}, f32[192,128]{1,0:T(8,128)}, u32[]{:S(2)}) copy-start(f32[192,128]{1,0:T(8,128)} %param.16) | copy-start | bytes 294916
  7.2 4.7 %copy-start.1 = (f32[192,128]{1,0:T(8,128)S(1)}, f32[192,128]{1,0:T(8,128)}, u32[]{:S(2)}) copy-start(f32[192,128]{1,0:T(8,128)} %param.17) | copy-start | bytes 294916
  7.2 146.1 %reduce-scatter.2.cloned.1.call-start = ((), (), s32[]{:S(2)}) async-start(), calls=%async_computation.2 | async-start | bytes 1081344 | tf_op jit(solution)/shard_map/reduce_scatter | solution.py:52
  11.9 0.9 copy-start.2
  13.3 0.7 copy-start.8
  13.3 0.7 copy-start.9
  15.6 2.7 %copy-start.5 = (f32[1,1,128,128]{3,2,1,0:T(8,128)S(1)}, f32[1,1,128,128]{3,2,1,0:T(8,128)}, u32[]{:S(2)}) copy-start(f32[1,1,128,128]{3,2,1,0:T(8,128)} %param.26) | copy-start | bytes 196612
  15.7 0.7 copy-start.10
  16.3 0.7 copy-start.11
  17.0 0.7 copy-start.12
  17.7 0.7 copy-start.13
  155.0 0.7 copy-start.4
  155.0 0.7 copy-start.6
  158.7 9.8 %all-to-all-start = ((f32[32,1,256]{2,1,0:T(1,128)}), f32[32,1,256]{2,1,0:T(1,128)S(1)}, u32[]{:S(2)}, u32[]{:S(2)}) async-start(f32[32,1,256]{2,1,0:T(1,128)} %broadcast_in_dim.12), calls=%async_computation.1 | async-start | bytes 65536 | tf_op jit(solution)/shard_map/all_to_all | solution.py:123
  170.3 0.7 copy-start.7
Sparse Core Ops, SparseCore 0:
  15.8 137.4 reduce-scatter.1

commit v4 on v2

--- a/solution.py
+++ b/solution.py
@@ -49,8 +49,13 @@
             block_ids[None, :] == jnp.arange(shards * blocks, dtype=jnp.int32)[:, None]
         ).astype(jnp.float32)
         dense = jnp.dot(pick, runoff, precision=lax.Precision.HIGHEST)
+        chains = lax.axis_size("basin")
+        rivers = shards // chains
+        across = lax.all_to_all(
+            dense.reshape(chains, rivers, blocks, width), "band", split_axis=1, concat_axis=1, tiled=True
+        )
         arrived = lax.all_to_all(
-            dense.reshape(shards, blocks, width), grid, split_axis=0, concat_axis=0, tiled=True
+            jnp.sum(across, axis=1), "basin", split_axis=0, concat_axis=0, tiled=True
         )
         return jnp.sum(arrived, axis=0)
     buffer, slot_labels = pack_slots(runoff, tile_block, tile_dest, shards, tile_cap)

time: 63.7 us -> 64.1 us (level)
  waiting for transfers between devices: 29.4 us -> 26.4 us
  starting transfers between devices: 10.9 us -> 13.6 us
  other arithmetic: 4.05 us -> 4.76 us
    all_to_all x1 -> x2, starting transfers between devices: 7.3 us -> 10.9 us  [the longest x1 6.69 us: gather_lateral(): lax.all_to_all(jnp.sum(across, axis=1), 'basin', split_axis=0, concat_axi...]
    all_to_all x1 -> x2, waiting for transfers between devices: 22.2 us -> 19.1 us  [the longest x1 11.2 us: gather_lateral(): lax.all_to_all(dense.reshape(chains, rivers, blocks, width), 'band', spli...]
    all_to_all x1, starting transfers between devices: 3.62 us -> 2.74 us  [local(): lax.all_to_all(jnp.broadcast_to(payload[None], (shards, padded)), grid, s...]
    reduce_sum x0 -> x1, other arithmetic: none -> 0.76 us  [gather_lateral(): jnp.sum(across, axis=1)]
  transfers between devices with their start and end apart: 2 -> 3, of which waited for: 2 -> 3; matrix products, arithmetic and copies ran while one was open for 3% -> 3% of each run, Pallas kernels for 0% -> 0%
where the time goes in v4:
time: 64.1 us; the launch traced here: 63.6 us
  waiting for transfers between devices  26.4 us (41%)
  local copies, waits for them, and re-layouts  15.1 us (24%)
  starting transfers between devices  13.6 us (21%)
  other arithmetic  4.76 us (7%)
  matrix products  2.78 us (4%)
  between operations  0.95 us (1%)
    all_to_all x1, waiting for transfers between devices, gather_lateral(): lax.all_to_all(dense.reshape(chains, rivers, blocks, width), 'band', spli...  11.2 us
    all_to_all x1, waiting for transfers between devices, gather_lateral(): lax.all_to_all(jnp.sum(across, axis=1), 'basin', split_axis=0, concat_axi...  7.97 us
    all_to_all x1, waiting for transfers between devices, local(): lax.all_to_all(jnp.broadcast_to(payload[None], (shards, padded)), grid, s...  7.24 us
    all_to_all x1, starting transfers between devices, gather_lateral(): lax.all_to_all(jnp.sum(across, axis=1), 'basin', split_axis=0, concat_axi...  6.69 us
    unnamed x29, local copies, waits for them, and re-layouts  4.79 us
    slice x1, local copies, waits for them, and re-layouts, land_update(): rain_now = precip[:, sub_step]  4.67 us
    all_to_all x1, starting transfers between devices, gather_lateral(): lax.all_to_all(dense.reshape(chains, rivers, blocks, width), 'band', spli...  4.21 us
    all_to_all x1, starting transfers between devices, local(): lax.all_to_all(jnp.broadcast_to(payload[None], (shards, padded)), grid, s...  2.74 us
  transfers between devices with their start and end apart: 3, of which 3 were waited for; matrix products, arithmetic and copies ran while one was open for 3% of the time, Pallas kernels for 0%

profile of v4, /device:TPU:0, one launch (start us, length us, event | category | flops | bytes accessed | tf_op | source)
XLA Modules:
  0.0 63.6 jit_solution(6043223051245361641)
XLA Ops:
  0.7 4.7 %fusion.49 = (f32[192,1,128]{2,1,0:T(1,128)S(1)}, f32[192,1,128]{2,1,0:T(1,128)S(1)}, f32[192,1,128]{2,1,0:T(1,128)S(1)}, f32[192,1,128]{2,1,0:T(1,128)S(1)}, f3...) fusion(f32[192,8,128]{2,1,0:T(8,128)} %param.15), kind=kLoop, calls=%fused_computation.156 | loop fusion | bytes 1572864 | tf_op jit(solution)/shard_map/slice | solution.py:11
  5.4 0.9 %copy-done.2 = f32[192,128]{1,0:T(8,128)S(1)} copy-done((f32[192,128]{1,0:T(8,128)S(1)}, f32[192,128]{1,0:T(8,128)}, u32[]{:S(2)}) %copy-start.2) | copy-done | bytes 98328
  6.3 0.1 bitcast_dynamic-update-slice_fusion.6
  6.3 0.1 bitcast_dynamic-update-slice_fusion.5
  6.4 0.1 bitcast_dynamic-update-slice_fusion.4
  6.5 0.1 bitcast_dynamic-update-slice_fusion.3
  6.6 0.1 bitcast_dynamic-update-slice_fusion.2
  6.7 0.1 bitcast_dynamic-update-slice_fusion.1
  6.7 0.1 bitcast_dynamic-update-slice_fusion
  6.8 0.5 copy.96
  7.3 0.1 reshape.289
  7.4 0.5 copy-done.8
  8.0 0.0 copy-done.9
  8.0 1.7 %fusion = f32[8,4,8,1024]{3,2,0,1:T(8,128)} fusion(f32[192,1024,1,1]{1,0,2,3:T(8,128)S(1)} %reshape.289, s32[8,4,8]{2,1,0:T(4,128)S(1)} %multiply_add_fusion, s32[192]{0:T(256)S(1)} %multiply_add_fusion.17), kind=kOutput, calls=%fused_computation.1 | convolution fusion | flops 604028928 | bytes 1836800 | tf_op jit(solution)/shard_map/dot_general | solution.py:51
  9.6 4.2 %all-to-all-start = ((f32[8,4,8,1024]{3,2,0,1:T(8,128)}), f32[8,4,8,1024]{3,2,0,1:T(8,128)S(1)}, u32[]{:S(2)}, u32[]{:S(2)}) async-start(f32[8,4,8,1024]{3,2,0,1:T(8,128)} %fusion), calls=%async_computation | async-start | bytes 2097152 | tf_op jit(solution)/shard_map/all_to_all | solution.py:54
  13.8 0.7 %copy-done.12 = s32[8]{0:T(128)S(1)} copy-done((s32[8]{0:T(128)S(1)}, s32[8]{0:T(128)}, u32[]{:S(2)}) %copy-start.12) | copy-done | bytes 56
  14.5 0.7 %copy-done.13 = s32[8]{0:T(128)S(1)} copy-done((s32[8]{0:T(128)S(1)}, s32[8]{0:T(128)}, u32[]{:S(2)}) %copy-start.13) | copy-done | bytes 56
  15.2 0.7 %copy-done.10 = f32[1,1,128]{2,1,0:T(1,128)S(1)} copy-done((f32[1,1,128]{2,1,0:T(1,128)S(1)}, f32[1,1,128]{2,1,0:T(1,128)}, u32[]{:S(2)}) %copy-start.10) | copy-done | bytes 536
  15.8 0.6 slice.154
  16.4 0.1 copy-done.11
  16.5 0.7 %slice.156 = f32[1,1,1]{2,1,0:T(1,128)} slice(f32[1,1,128]{2,1,0:T(1,128)S(1)} %copy-done.11), slice={[0:1], [0:1], [127:128]} | slice | bytes 8 | tf_op jit(solution)/shard_map/slice | solution.py:125
  17.1 11.2 %all-to-all-done = f32[8,4,8,1024]{3,2,0,1:T(8,128)S(1)} async-done(((f32[8,4,8,1024]{3,2,0,1:T(8,128)}), f32[8,4,8,1024]{3,2,0,1:T(8,128)S(1)}, u32[]{:S(2)}, u32[]{:S(2)}) %all-to-all-start) | async-done | bytes 1048608 | tf_op jit(solution)/shard_map/all_to_all | solution.py:54
  28.3 0.8 %reduce_sum.122 = f32[8,8,1024]{2,1,0:T(8,128)} reduce(f32[8,4,8,1024]{3,2,0,1:T(8,128)S(1)} %all-to-all-done, f32[]{:T(128)} %constant.18.clone.1), dimensions={1}, to_apply=%region_0.0 | reduce | flops 196608 | bytes 1310724 | tf_op jit(solution)/shard_map/reduce_sum | solution.py:58
  29.1 6.7 %all-to-all-start.1 = ((f32[8,8,1024]{2,1,0:T(8,128)}), f32[8,8,1024]{2,1,0:T(8,128)S(1)}, u32[]{:S(2)}, u32[]{:S(2)}) async-start(f32[8,8,1024]{2,1,0:T(8,128)} %reduce_sum.122), calls=%async_computation.1 | async-start | bytes 524288 | tf_op jit(solution)/shard_map/all_to_all | solution.py:57
  35.8 0.7 %add_subtract_fusion = f32[192,128]{1,0:T(8,128)} fusion(f32[192,128]{1,0:T(8,128)S(1)} %bitcast.291, f32[192,128]{1,0:T(8,128)S(1)} %copy-done.2, f32[192,128]{1,0:T(8,128)S(1)} %copy-done.1, f32[192,128]{1,0:T(8,128)S(1)} %bitcast.285, f32[192,128]{1,0:T(8,128)S(1)} %get-tuple-element.30, f32[192,128]{1,0:T(8,128)S(1)} %bitcast.276), kind=kLoop, calls=%fused_computation.16 | loop fusion | flops 466944 | bytes 688128 | tf_op jit(solution)/shard_map/sub | solution.py:13
  36.5 8.0 %all-to-all-done.1 = f32[8,8,1024]{2,1,0:T(8,128)S(1)} async-done(((f32[8,8,1024]{2,1,0:T(8,128)}), f32[8,8,1024]{2,1,0:T(8,128)S(1)}, u32[]{:S(2)}, u32[]{:S(2)}) %all-to-all-start.1) | async-done | bytes 262176 | tf_op jit(solution)/shard_map/all_to_all | solution.py:57
  44.5 0.9 %fusion.6 = f32[8,8,128]{2,1,0:T(8,128)S(1)} fusion(f32[8,128,128]{2,1,0:T(8,128)S(1)} %copy-done, f32[8,8,128]{2,0,1:T(8,128)S(1)} %bitcast.297), kind=kOutput, calls=%fused_computation.42 | convolution fusion | flops 12582912 | bytes 589824 | tf_op jit(solution)/shard_map/brc,btc->btr/dot_general | solution.py:109
  45.5 0.7 %copy-done.4 = f32[8,128]{1,0:T(8,128)S(1)} copy-done((f32[8,128]{1,0:T(8,128)S(1)}, f32[8,128]{1,0:T(8,128)}, u32[]{:S(2)}) %copy-start.4) | copy-done | bytes 4120
  46.1 0.0 copy-done.6
  46.2 0.6 constant_dynamic-update-slice_fusion
  46.8 0.1 slice.189
  46.9 0.1 copy.106
  47.0 0.1 reshape_squeeze.9
  47.1 1.4 %concatenate.3 = f32[210]{0:T(256)S(1)} concatenate(f32[64]{0:T(128)S(1)} %reshape_squeeze.9, f32[8]{0:T(128)S(1)} %convert_element_type.33, f32[8]{0:T(128)S(1)} %convert_element_type.34, f32[128]{0:T(128)S(1)} %slice_bitcast_fusion.8, f32[1]{0:T(128)} %bitcast.36, f32[1]{0:T(128)} %bitcast.37), dimensions={0} | concatenate | bytes 1680 | tf_op jit(solution)/shard_map/concatenate | solution.py:118
  48.6 0.6 broadcast_in_dim.12
  49.2 2.7 %all-to-all-start.2 = ((f32[32,1,256]{2,1,0:T(1,128)}), f32[32,1,256]{2,1,0:T(1,128)S(1)}, u32[]{:S(2)}, u32[]{:S(2)}) async-start(f32[32,1,256]{2,1,0:T(1,128)} %broadcast_in_dim.12), calls=%async_computation.2 | async-start | bytes 65536 | tf_op jit(solution)/shard_map/all_to_all | solution.py:131
  51.9 7.2 %all-to-all-done.2 = f32[32,1,256]{2,1,0:T(1,128)S(1)} async-done(((f32[32,1,256]{2,1,0:T(1,128)}), f32[32,1,256]{2,1,0:T(1,128)S(1)}, u32[]{:S(2)}, u32[]{:S(2)}) %all-to-all-start.2) | async-done | bytes 32800 | tf_op jit(solution)/shard_map/all_to_all | solution.py:131
  59.2 0.1 slice.191
  59.3 0.1 slice.193
  59.3 0.2 slice_reduce_fusion
  59.5 0.1 mul.522
  59.6 0.1 eq.84
  59.7 0.1 slice_compare_fusion
  59.8 0.1 eq.83
  59.9 0.1 reshape_squeeze.10
  59.9 0.1 reshape_squeeze.11
  60.0 0.1 fusion.3
  60.2 0.3 multiply_reduce_fusion
  60.5 0.1 multiply_reduce_fusion.1
  60.6 0.2 multiply_add_fusion.1
  60.8 0.1 multiply_select_fusion
  61.0 0.6 %copy-done.7 = f32[1,8]{1,0:T(1,128)S(1)} copy-done((f32[1,8]{1,0:T(1,128)S(1)}, f32[1,8]{1,0:T(1,128)}, u32[]{:S(2)}) %copy-start.7) | copy-done | bytes 56
  61.6 0.1 fusion.9
  61.7 0.1 stack.94
  61.8 0.1 fusion.11
  61.9 0.1 fusion.13
  62.1 0.1 fusion.15
  62.2 0.1 fusion.17
  62.3 0.1 fusion.19
  62.5 0.1 fusion.21
  62.6 0.1 fusion.23
  62.7 0.2 fusion.4
  62.9 0.1 fusion.40
  63.0 0.6 stack.95
  (49 shorter events, 0.3 us)
Async XLA Ops:
  0.6 43.9 %copy-start = (f32[8,128,128]{2,1,0:T(8,128)S(1)}, f32[8,128,128]{2,1,0:T(8,128)}, u32[]{:S(2)}) copy-start(f32[8,128,128]{2,1,0:T(8,128)} %param.21) | copy-start | bytes 1572868
  0.7 4.7 %copy-start.1 = (f32[192,128]{1,0:T(8,128)S(1)}, f32[192,128]{1,0:T(8,128)}, u32[]{:S(2)}) copy-start(f32[192,128]{1,0:T(8,128)} %param.17) | copy-start | bytes 294916
  0.7 4.7 %copy-start.3 = (f32[192,128]{1,0:T(8,128)S(1)}, f32[192,128]{1,0:T(8,128)}, u32[]{:S(2)}) copy-start(f32[192,128]{1,0:T(8,128)} %param.16) | copy-start | bytes 294916
  5.4 0.9 %copy-start.2 = (f32[192,128]{1,0:T(8,128)S(1)}, f32[192,128]{1,0:T(8,128)}, u32[]{:S(2)}) copy-start(f32[192,128]{1,0:T(8,128)} %param.18) | copy-start | bytes 294916
  7.3 0.7 %copy-start.8 = (s32[192]{0:T(256)S(1)}, s32[192]{0:T(256)}, u32[]{:S(2)}) copy-start(s32[192]{0:T(256)} %param.20) | copy-start | bytes 2308
  7.3 0.7 %copy-start.9 = (s32[192]{0:T(256)S(1)}, s32[192]{0:T(256)}, u32[]{:S(2)}) copy-start(s32[192]{0:T(256)} %param.19) | copy-start | bytes 2308
  9.6 18.7 %all-to-all-start = ((f32[8,4,8,1024]{3,2,0,1:T(8,128)}), f32[8,4,8,1024]{3,2,0,1:T(8,128)S(1)}, u32[]{:S(2)}, u32[]{:S(2)}) async-start(f32[8,4,8,1024]{3,2,0,1:T(8,128)} %fusion), calls=%async_computation | async-start | bytes 2097152 | tf_op jit(solution)/shard_map/all_to_all | solution.py:54
  13.8 0.7 %copy-start.12 = (s32[8]{0:T(128)S(1)}, s32[8]{0:T(128)}, u32[]{:S(2)}) copy-start(s32[8]{0:T(128)} %param.24) | copy-start | bytes 100
  14.5 0.7 %copy-start.13 = (s32[8]{0:T(128)S(1)}, s32[8]{0:T(128)}, u32[]{:S(2)}) copy-start(s32[8]{0:T(128)} %param.25) | copy-start | bytes 100
  15.2 0.7 %copy-start.10 = (f32[1,1,128]{2,1,0:T(1,128)S(1)}, f32[1,1,128]{2,1,0:T(1,128)}, u32[]{:S(2)}) copy-start(f32[1,1,128]{2,1,0:T(1,128)} %param.27) | copy-start | bytes 1540
  15.8 0.7 %copy-start.11 = (f32[1,1,128]{2,1,0:T(1,128)S(1)}, f32[1,1,128]{2,1,0:T(1,128)}, u32[]{:S(2)}) copy-start(f32[1,1,128]{2,1,0:T(1,128)} %param.28) | copy-start | bytes 1540
  29.1 6.7 %copy-start.5 = (f32[1,1,128,128]{3,2,1,0:T(8,128)S(1)}, f32[1,1,128,128]{3,2,1,0:T(8,128)}, u32[]{:S(2)}) copy-start(f32[1,1,128,128]{3,2,1,0:T(8,128)} %param.26) | copy-start | bytes 196612
  29.1 15.4 %all-to-all-start.1 = ((f32[8,8,1024]{2,1,0:T(8,128)}), f32[8,8,1024]{2,1,0:T(8,128)S(1)}, u32[]{:S(2)}, u32[]{:S(2)}) async-start(f32[8,8,1024]{2,1,0:T(8,128)} %reduce_sum.122), calls=%async_computation.1 | async-start | bytes 524288 | tf_op jit(solution)/shard_map/all_to_all | solution.py:57
  45.4 0.7 %copy-start.4 = (f32[8,128]{1,0:T(8,128)S(1)}, f32[8,128]{1,0:T(8,128)}, u32[]{:S(2)}) copy-start(f32[8,128]{1,0:T(8,128)} %param.22) | copy-start | bytes 12292
  45.4 0.7 %copy-start.6 = (f32[8,128]{1,0:T(8,128)S(1)}, f32[8,128]{1,0:T(8,128)}, u32[]{:S(2)}) copy-start(f32[8,128]{1,0:T(8,128)} %param.23) | copy-start | bytes 12292
  49.2 10.0 %all-to-all-start.2 = ((f32[32,1,256]{2,1,0:T(1,128)}), f32[32,1,256]{2,1,0:T(1,128)S(1)}, u32[]{:S(2)}, u32[]{:S(2)}) async-start(f32[32,1,256]{2,1,0:T(1,128)} %broadcast_in_dim.12), calls=%async_computation.2 | async-start | bytes 65536 | tf_op jit(solution)/shard_map/all_to_all | solution.py:131
  61.0 0.7 %copy-start.7 = (f32[1,8]{1,0:T(1,128)S(1)}, f32[1,8]{1,0:T(1,128)}, u32[]{:S(2)}) copy-start(f32[1,8]{1,0:T(1,128)} %param.29) | copy-start | bytes 100

commit v5 on v2

--- a/solution.py
+++ b/solution.py
@@ -68,7 +68,13 @@
     )
 
 
-def local(
+def spread(value, shards):
+    grid = ("basin", "band")
+    copies = jnp.broadcast_to(value[None], (shards,) + value.shape)
+    return lax.all_to_all(copies, grid, split_axis=0, concat_axis=0, tiled=True)
+
+
+def local_two_rounds(
     precip,
     soil_water,
     capacity,
@@ -182,6 +188,161 @@
     return (water, trib_flows[:, sub_steps - 1], main_flows[None, None])
 
 
+def local_one_round(
+    precip,
+    soil_water,
+    capacity,
+    evap_rate,
+    tile_dest,
+    tile_block,
+    trib_op,
+    trib_keep,
+    trib_prev,
+    trib_river,
+    trib_reach,
+    main_op,
+    main_keep,
+    main_prev,
+    head_inflow,
+):
+    tile_count = precip.shape[0]
+    sub_steps = precip.shape[1]
+    reaches = precip.shape[2]
+    blocks = trib_op.shape[0]
+    chains = lax.axis_size("basin")
+    rivers = lax.axis_size("band")
+    shards = chains * rivers
+    grid = ("basin", "band")
+    width = sub_steps * reaches
+    operator = main_op[0, 0]
+    keep_main = main_keep[0, 0]
+    prev_main = main_prev[0, 0]
+    last = reaches - 1
+
+    facts = jnp.concatenate(
+        [
+            trib_keep[:, last],
+            trib_prev[:, last],
+            trib_river.astype(jnp.float32),
+            trib_reach.astype(jnp.float32),
+            keep_main[last:],
+            prev_main[last:],
+        ]
+    )
+    facts = jnp.pad(facts, (0, reaches - facts.shape[0]))
+    static = jnp.concatenate([trib_op[:, last], facts[None], operator[last:]], axis=0)
+    everyone = spread(static, shards)
+
+    runoff, water = land_update(precip, soil_water, capacity, evap_rate)
+    runoff = runoff.reshape(tile_count, width)
+    block_ids = tile_dest * blocks + tile_block
+    pick = (
+        block_ids[None, :] == jnp.arange(shards * blocks, dtype=jnp.int32)[:, None]
+    ).astype(jnp.float32)
+    dense = jnp.dot(pick, runoff, precision=lax.Precision.HIGHEST)
+    exit_rows_all = everyone[:, :blocks].reshape(shards * blocks, reaches)
+    partial_exit = jnp.sum(
+        dense.reshape(shards * blocks, sub_steps, reaches) * exit_rows_all[:, None, :], axis=2
+    )
+    extra = -(-(shards * blocks * sub_steps) // width)
+    tail_rows = jnp.pad(partial_exit.reshape(-1), (0, extra * width - shards * blocks * sub_steps))
+    send = jnp.concatenate(
+        [
+            dense.reshape(shards, blocks, width),
+            jnp.broadcast_to(tail_rows.reshape(1, extra, width), (shards, extra, width)),
+        ],
+        axis=1,
+    )
+    arrived = jnp.sum(
+        lax.all_to_all(send, grid, split_axis=0, concat_axis=0, tiled=True), axis=0
+    )
+    lateral = arrived[:blocks]
+    exit_mix = arrived[blocks:].reshape(-1)[: shards * blocks * sub_steps].reshape(
+        shards * blocks, sub_steps
+    )
+
+    trib_mixed = jnp.einsum(
+        "brc,btc->btr",
+        trib_op,
+        lateral.reshape(blocks, sub_steps, reaches),
+        precision=lax.Precision.HIGHEST,
+    )
+    trib_flows = route_series(trib_mixed, trib_keep, trib_prev)
+
+    facts_all = everyone[:, blocks]
+    at = 0
+    keep_of = facts_all[:, at : at + blocks].reshape(-1)
+    at += blocks
+    prev_of = facts_all[:, at : at + blocks].reshape(-1)
+    at += blocks
+    river_of = facts_all[:, at : at + blocks].reshape(chains, rivers * blocks)
+    at += blocks
+    reach_of = facts_all[:, at : at + blocks].reshape(chains, rivers * blocks)
+    at += blocks
+    mine = lax.axis_index("band")
+    me = lax.axis_index("basin")
+    keeps = lax.dynamic_index_in_dim(
+        facts_all[:, at].reshape(chains, rivers), mine, axis=1, keepdims=False
+    )
+    starts = lax.dynamic_index_in_dim(
+        facts_all[:, at + 1].reshape(chains, rivers), mine, axis=1, keepdims=False
+    )
+    exit_rows = lax.dynamic_index_in_dim(
+        everyone[:, blocks + 1].reshape(chains, rivers, reaches), mine, axis=1, keepdims=False
+    )
+
+    flow = prev_of
+    outlet_steps = []
+    for sub_step in range(sub_steps):
+        flow = keep_of * flow + (1.0 - keep_of) * exit_mix[:, sub_step]
+        outlet_steps.append(flow)
+    outlets = jnp.stack(outlet_steps, axis=1).reshape(chains, rivers * blocks, sub_steps)
+
+    joins = (river_of == mine.astype(jnp.float32))[:, :, None] & (
+        reach_of[:, :, None] == jnp.arange(reaches, dtype=jnp.float32)[None, None, :]
+    )
+    weight = joins.astype(jnp.float32)
+    branch_all = jnp.sum(weight[:, :, None, :] * outlets[:, :, :, None], axis=1)
+    branch_exit = jnp.sum(branch_all * exit_rows[:, None, :], axis=2)
+
+    flow = starts
+    free_exit = []
+    for sub_step in range(sub_steps):
+        flow = keeps * flow + (1.0 - keeps) * branch_exit[:, sub_step]
+        free_exit.append(flow)
+    free_exit = jnp.stack(free_exit, axis=1)
+    lag = jnp.arange(sub_steps)[:, None] - jnp.arange(sub_steps)[None, :]
+    lag_f = jnp.maximum(lag, 0).astype(jnp.float32)
+    response = jnp.where(
+        lag[None] >= 0,
+        (exit_rows[:, 0] * (1.0 - keeps))[:, None, None] * keeps[:, None, None] ** lag_f[None],
+        0.0,
+    )
+
+    def advance(section, entry):
+        moved = jnp.sum(response[section] * entry[None, :], axis=1) + free_exit[section]
+        return jnp.where(section < me, moved, entry)
+
+    entry = lax.fori_loop(0, chains, advance, head_inflow[0], unroll=chains <= 16)
+
+    branch_in = lax.dynamic_index_in_dim(branch_all, me, axis=0, keepdims=False)
+    first_reach = (jnp.arange(reaches) == 0).astype(jnp.float32)
+    fed = branch_in + entry[:, None] * first_reach[None, :]
+    main_mixed = jnp.einsum("rc,tc->tr", operator, fed, precision=lax.Precision.HIGHEST)
+    main_flows = route_series(main_mixed, keep_main, prev_main)
+    return (water, trib_flows[:, sub_steps - 1], main_flows[None, None])
+
+
+def local(*args):
+    precip, trib_op = args[0], args[6]
+    tile_count, reaches = precip.shape[0], precip.shape[2]
+    blocks = trib_op.shape[0]
+    shards = lax.axis_size("basin") * lax.axis_size("band")
+    if max(2, 2 * tile_count // shards) >= blocks and 4 * blocks + 2 <= reaches:
+        return local_one_round(*args)
+    return local_two_rounds(*args)
+
+
 def solution(mesh):
     return jax.shard_map(
         local,

time: 63.7 us -> 92.9 us (1.46)
  waiting for transfers between devices: 29.4 us -> 51.8 us
  other arithmetic: 4.05 us -> 12 us
  matrix products: 2.78 us -> 1.78 us
    all_to_all x2, waiting for transfers between devices: 29.4 us -> 51.8 us  [the longest x1 47 us: local_one_round(): lax.all_to_all(send, grid, split_axis=0, concat_axis=0, tiled=True)]
    add x2 -> x10, other arithmetic: 0.2 us -> 4.86 us  [the longest x8 4.68 us: local_one_round(): flow = keep_of * flow + (1.0 - keep_of) * exit_mix[:, sub_step]]
    slice x8 -> x11, local copies, waits for them, and re-layouts: 1.77 us -> 5.59 us  [the longest x1 1.28 us: local_one_round(): prev_main[last:]]
    unnamed x29 -> x41, local copies, waits for them, and re-layouts: 4.79 us -> 1.16 us
    concatenate x0 -> x2, other arithmetic: none -> 1.61 us  [the longest x1 1.6 us: local_one_round(): jnp.concatenate([dense.reshape(shards, blocks, width), jnp.broadcast_to(t...]
    convert_element_type x5, other arithmetic: 0.16 us -> 1.46 us  [the longest x1 0.66 us: local_one_round(): trib_river.astype(jnp.float32)]
    dot_general x3, matrix products: 2.78 us -> 1.78 us  [the longest x1 0.92 us: local_one_round(): jnp.einsum('brc,btc->btr', trib_op, lateral.reshape(blocks, sub_steps, re...]
  transfers between devices with their start and end apart: 2 -> 2, of which waited for: 2 -> 2; matrix products, arithmetic and copies ran while one was open for 3% -> 8% of each run, Pallas kernels for 0% -> 0%
where the time goes in v5:
time: 92.9 us; the launch traced here: 92.4 us
  waiting for transfers between devices  51.8 us (56%)
  local copies, waits for them, and re-layouts  15.7 us (17%)
  other arithmetic  12 us (13%)
  starting transfers between devices  10 us (11%)
  matrix products  1.78 us (2%)
  between operations  1.12 us (1%)
    all_to_all x1, waiting for transfers between devices, local_one_round(): lax.all_to_all(send, grid, split_axis=0, concat_axis=0, tiled=True)  47 us
    all_to_all x1, starting transfers between devices, spread(): return lax.all_to_all(copies, grid, split_axis=0, concat_axis=0, tiled=True)  7.3 us
    all_to_all x1, waiting for transfers between devices, spread(): return lax.all_to_all(copies, grid, split_axis=0, concat_axis=0, tiled=True)  4.82 us
    add x8, other arithmetic, local_one_round(): flow = keep_of * flow + (1.0 - keep_of) * exit_mix[:, sub_step]  4.68 us
    slice x1, local copies, waits for them, and re-layouts, land_update(): rain_now = precip[:, sub_step]  4.09 us
    all_to_all x1, starting transfers between devices, local_one_round(): lax.all_to_all(send, grid, split_axis=0, concat_axis=0, tiled=True)  2.73 us
  transfers between devices with their start and end apart: 2, of which 2 were waited for; matrix products, arithmetic and copies ran while one was open for 8% of the time, Pallas kernels for 0%

profile of v5, /device:TPU:0, one launch (start us, length us, event | category | flops | bytes accessed | tf_op | source)
XLA Modules:
  0.0 92.4 jit_solution(14968878089689673158)
XLA Ops:
  0.7 1.3 %slice.196 = f32[1,1,1]{2,1,0:T(1,128)} slice(f32[1,1,128]{2,1,0:T(1,128)} %param.28), slice={[0:1], [0:1], [127:128]} | slice | bytes 8 | tf_op jit(solution)/shard_map/slice | solution.py:229
  1.9 1.2 %slice.194 = f32[1,1,1]{2,1,0:T(1,128)} slice(f32[1,1,128]{2,1,0:T(1,128)} %param.27), slice={[0:1], [0:1], [127:128]} | slice | bytes 8 | tf_op jit(solution)/shard_map/slice | solution.py:228
  3.2 0.7 convert_element_type.33
  3.8 0.7 convert_element_type.34
  4.5 0.7 slice_bitcast_fusion.10
  5.2 0.9 slice_reduce_fusion.3
  6.1 1.4 %concatenate.10 = f32[34]{0:T(128)S(1)} concatenate(f32[8]{0:T(128)S(1)} %get-tuple-element.65, f32[8]{0:T(128)S(1)} %get-tuple-element.64, f32[8]{0:T(128)S(1)} %convert_element_type.33, f32[8]{0:T(128)S(1)} %convert_element_type.34, f32[1]{0:T(128)} %bitcast.18, f32[1]{0:T(128)} %bitcast.19), dimensions={0} | concatenate | bytes 272 | tf_op jit(solution)/shard_map/concatenate | solution.py:222
  7.5 0.8 slice.191
  8.3 0.7 broadcast_in_dim.19
  9.0 7.3 %all-to-all-start = ((f32[32,10,128]{2,1,0:T(8,128)}), f32[32,10,128]{2,1,0:T(8,128)S(1)}, u32[]{:S(2)}, u32[]{:S(2)}) async-start(f32[32,10,128]{2,1,0:T(8,128)} %broadcast_in_dim.19), calls=%async_computation | async-start | bytes 524288 | tf_op jit(solution)/shard_map/all_to_all | solution.py:74
  16.3 4.1 %fusion.64 = (f32[192,1,128]{2,1,0:T(1,128)S(1)}, f32[192,1,128]{2,1,0:T(1,128)S(1)}, f32[192,1,128]{2,1,0:T(1,128)S(1)}, f32[192,1,128]{2,1,0:T(1,128)S(1)}, f3...) fusion(f32[192,8,128]{2,1,0:T(8,128)} %param.15), kind=kLoop, calls=%fused_computation.185 | loop fusion | bytes 1572864 | tf_op jit(solution)/shard_map/slice | solution.py:11
  20.5 0.1 bitcast_dynamic-update-slice_fusion.5
  20.6 0.1 bitcast_dynamic-update-slice_fusion.4
  21.0 0.2 copy-done.8
  21.2 0.6 fusion
  21.9 0.2 copy.134
  22.1 4.8 %all-to-all-done = f32[32,10,128]{2,1,0:T(8,128)S(1)} async-done(((f32[32,10,128]{2,1,0:T(8,128)}), f32[32,10,128]{2,1,0:T(8,128)S(1)}, u32[]{:S(2)}, u32[]{:S(2)}) %all-to-all-start) | async-done | bytes 163872 | tf_op jit(solution)/shard_map/all_to_all | solution.py:74
  26.9 0.3 multiply_reduce_fusion.1
  27.2 0.1 broadcast_in_dim.20
  27.4 1.6 %pad_maximum_fusion = f32[32,10,1024]{2,1,0:T(8,128)} fusion(f32[32,2,1024]{2,1,0:T(2,128)S(1)} %broadcast_in_dim.21, f32[32,8,1024]{2,1,0:T(8,128)S(1)} %bitcast.276), kind=kLoop, calls=%fused_computation | loop fusion | flops 327680 | bytes 2621440 | tf_op jit(solution)/shard_map/concatenate | solution.py:249
  29.0 2.7 %all-to-all-start.1 = ((f32[32,10,1024]{2,1,0:T(8,128)}), f32[32,10,1024]{2,1,0:T(8,128)S(1)}, u32[]{:S(2)}, u32[]{:S(2)}) async-start(f32[32,10,1024]{2,1,0:T(8,128)} %pad_maximum_fusion), calls=%async_computation.1 | async-start | bytes 4194304 | tf_op jit(solution)/shard_map/all_to_all | solution.py:257
  31.8 0.7 add_subtract_fusion
  32.6 0.2 slice_reduce_fusion
  32.9 0.1 eq.60
  33.1 0.1 fusion.68
  33.3 0.1 reshape.322
  33.4 0.1 reshape.323
  33.5 0.1 slice_reduce_fusion.2
  33.6 0.1 fusion.5
  33.7 47.0 %all-to-all-done.1 = f32[32,10,1024]{2,1,0:T(8,128)S(1)} async-done(((f32[32,10,1024]{2,1,0:T(8,128)}), f32[32,10,1024]{2,1,0:T(8,128)S(1)}, u32[]{:S(2)}, u32[]{:S(2)}) %all-to-all-start.1) | async-done | bytes 1310752 | tf_op jit(solution)/shard_map/all_to_all | solution.py:257
  80.7 0.1 reduce_sum.123
  80.9 0.9 fusion.8
  81.8 0.1 reshape_reshape.3
  82.0 0.3 fusion.66
  82.4 0.1 copy.131
  82.5 0.1 copy.130
  82.6 0.1 copy.129
  82.6 0.1 copy.128
  82.7 0.1 copy.127
  82.8 0.1 copy.126
  82.9 0.1 copy.125
  83.0 0.5 broadcast.318
  83.5 0.7 reduce.42
  84.2 0.7 reduce.41
  84.9 0.7 reduce.40
  85.5 0.7 reduce.39
  86.2 0.7 reduce.38
  86.9 0.7 reduce.37
  88.0 0.7 add_reduce_fusion
  88.9 0.1 copy.109
  89.0 0.3 multiply_reduce_fusion
  89.4 0.2 multiply_add_fusion
  89.6 0.1 multiply_select_fusion
  89.7 0.1 fusion.12
  89.9 0.1 fusion.14
  90.1 0.1 fusion.16
  90.2 0.1 fusion.18
  90.3 0.1 fusion.20
  90.5 0.1 fusion.22
  90.6 0.1 fusion.24
  90.7 0.1 fusion.26
  90.9 0.2 fusion.6
  91.2 0.6 multiply_add_fusion.8
  91.8 0.6 stack.95
  (76 shorter events, 2.0 us)
Async XLA Ops:
  0.6 19.7 %copy-start = (f32[192,128]{1,0:T(8,128)S(1)}, f32[192,128]{1,0:T(8,128)}, u32[]{:S(2)}) copy-start(f32[192,128]{1,0:T(8,128)} %param.17) | copy-start | bytes 294916
  0.6 19.7 %copy-start.2 = (f32[192,128]{1,0:T(8,128)S(1)}, f32[192,128]{1,0:T(8,128)}, u32[]{:S(2)}) copy-start(f32[192,128]{1,0:T(8,128)} %param.16) | copy-start | bytes 294916
  0.7 19.8 %copy-start.1 = (f32[192,128]{1,0:T(8,128)S(1)}, f32[192,128]{1,0:T(8,128)}, u32[]{:S(2)}) copy-start(f32[192,128]{1,0:T(8,128)} %param.18) | copy-start | bytes 294916
  9.0 17.9 %all-to-all-start = ((f32[32,10,128]{2,1,0:T(8,128)}), f32[32,10,128]{2,1,0:T(8,128)S(1)}, u32[]{:S(2)}, u32[]{:S(2)}) async-start(f32[32,10,128]{2,1,0:T(8,128)} %broadcast_in_dim.19), calls=%async_computation | async-start | bytes 524288 | tf_op jit(solution)/shard_map/all_to_all | solution.py:74
  20.5 0.7 copy-start.8
  20.5 0.7 copy-start.9
  29.0 51.7 %all-to-all-start.1 = ((f32[32,10,1024]{2,1,0:T(8,128)}), f32[32,10,1024]{2,1,0:T(8,128)S(1)}, u32[]{:S(2)}, u32[]{:S(2)}) async-start(f32[32,10,1024]{2,1,0:T(8,128)} %pad_maximum_fusion), calls=%async_computation.1 | async-start | bytes 4194304 | tf_op jit(solution)/shard_map/all_to_all | solution.py:257
  31.8 49.1 %copy-start.3 = (f32[8,128,128]{2,1,0:T(8,128)S(1)}, f32[8,128,128]{2,1,0:T(8,128)}, u32[]{:S(2)}) copy-start(f32[8,128,128]{2,1,0:T(8,128)} %param.21) | copy-start | bytes 1572868
  81.8 7.9 %copy-start.7 = (f32[1,8]{1,0:T(1,128)S(1)}, f32[1,8]{1,0:T(1,128)}, u32[]{:S(2)}) copy-start(f32[1,8]{1,0:T(1,128)} %param.29) | copy-start | bytes 100
  81.8 9.0 %copy-start.4 = (f32[1,1,128,128]{3,2,1,0:T(8,128)S(1)}, f32[1,1,128,128]{3,2,1,0:T(8,128)}, u32[]{:S(2)}) copy-start(f32[1,1,128,128]{3,2,1,0:T(8,128)} %param.26) | copy-start | bytes 196612
  82.0 9.1 %copy-start.10 = (f32[1,1,128]{2,1,0:T(1,128)S(1)}, f32[1,1,128]{2,1,0:T(1,128)}, u32[]{:S(2)}) copy-start(f32[1,1,128]{2,1,0:T(1,128)} %param.27) | copy-start | bytes 1540
  82.0 9.1 %copy-start.11 = (f32[1,1,128]{2,1,0:T(1,128)S(1)}, f32[1,1,128]{2,1,0:T(1,128)}, u32[]{:S(2)}) copy-start(f32[1,1,128]{2,1,0:T(1,128)} %param.28) | copy-start | bytes 1540
  82.0 9.2 %copy-start.5 = (f32[8,128]{1,0:T(8,128)S(1)}, f32[8,128]{1,0:T(8,128)}, u32[]{:S(2)}) copy-start(f32[8,128]{1,0:T(8,128)} %param.23) | copy-start | bytes 12292
  82.0 9.2 %copy-start.6 = (f32[8,128]{1,0:T(8,128)S(1)}, f32[8,128]{1,0:T(8,128)}, u32[]{:S(2)}) copy-start(f32[8,128]{1,0:T(8,128)} %param.22) | copy-start | bytes 12292

commit v6 on v3

--- a/solution.py
+++ b/solution.py
@@ -49,7 +49,12 @@
             block_ids[None, :] == jnp.arange(shards * blocks, dtype=jnp.int32)[:, None]
         ).astype(jnp.float32)
         dense = jnp.dot(pick, runoff, precision=lax.Precision.HIGHEST)
-        return lax.psum_scatter(dense, grid, scatter_dimension=0, tiled=True)
+        if not PAIRED or blocks % 2:
+            arrived = lax.all_to_all(
+                dense.reshape(shards, blocks, width), grid, split_axis=0, concat_axis=0, tiled=True
+            )
+            return jnp.sum(arrived, axis=0)
+        return pair_exchange(dense, blocks, shards)
     buffer, slot_labels = pack_slots(runoff, tile_block, tile_dest, shards, tile_cap)
     arrived = lax.all_to_all(
         buffer.reshape(shards, tile_cap, width), grid, split_axis=0, concat_axis=0, tiled=True
@@ -63,6 +68,27 @@
     return jnp.einsum(
         "sk,sx->kx", block_pick, arrived.reshape(-1, width), precision=lax.Precision.HIGHEST
     )
+
+
+def pair_exchange(dense, blocks, shards):
+    chains = lax.axis_size("basin")
+    rivers = lax.axis_size("band")
+    width = dense.shape[1]
+    half = blocks // 2
+    swap = [(m ^ 1, m) for m in range(rivers)]
+    core = lax.axis_index("band") % 2
+    parts = dense.reshape(chains, rivers // 2, 2, blocks, width)
+    keep_side = lax.dynamic_index_in_dim(parts, core, axis=2, keepdims=False)
+    give_side = lax.dynamic_index_in_dim(parts, 1 - core, axis=2, keepdims=False)
+    chip_sum = keep_side + lax.ppermute(give_side, "band", swap)
+    side = (jnp.arange(2) == core)[None, None, :, None, None]
+    send = jnp.where(side, chip_sum[:, :, None, :half], chip_sum[:, :, None, half:])
+    arrived = lax.all_to_all(
+        send.reshape(shards, half, width), ("basin", "band"), split_axis=0, concat_axis=0, tiled=True
+    ).reshape(chains, rivers // 2, 2, half, width)
+    same = jnp.sum(jnp.where(side, arrived, 0.0), axis=(0, 1, 2))
+    other = jnp.sum(jnp.where(side, 0.0, arrived), axis=(0, 1, 2))
+    return jnp.concatenate([same, lax.ppermute(other, "band", swap)], axis=0)
 
 
 def local(
@@ -179,7 +205,27 @@
     return (water, trib_flows[:, sub_steps - 1], main_flows[None, None])
 
 
+def cores_paired(mesh):
+    try:
+        grid = mesh.devices
+        if grid.ndim != 2 or grid.shape[1] % 2:
+            return False
+        for row in grid:
+            for m in range(0, len(row), 2):
+                a, b = row[m], row[m + 1]
+                if tuple(a.coords) != tuple(b.coords) or a.core_on_chip == b.core_on_chip:
+                    return False
+        return True
+    except AttributeError:
+        return False
+
+
+PAIRED = False
+
+
 def solution(mesh):
+    global PAIRED
+    PAIRED = cores_paired(mesh)
     return jax.shard_map(
         local,
         mesh=mesh,

time: 180 us -> 58.5 us (0.33)
  waiting for transfers between devices: 141 us -> 23.4 us
  between operations: 14.3 us -> 1.08 us
  starting transfers between devices: 2.6 us -> 11 us
    reduce_scatter x1 -> x0, waiting for transfers between devices: 134 us -> none  [gather_lateral(): return lax.psum_scatter(dense, grid, scatter_dimension=0, tiled=True)]
    all_to_all x0 -> x1, waiting for transfers between devices: none -> 14.8 us  [pair_exchange(): lax.all_to_all(send.reshape(shards, half, width), ('basin', 'band'), spli...]
    all_to_all x0 -> x1, starting transfers between devices: none -> 7.22 us  [pair_exchange(): lax.all_to_all(send.reshape(shards, half, width), ('basin', 'band'), spli...]
  transfers between devices with their start and end apart: 2 -> 4, of which waited for: 2 -> 3; matrix products, arithmetic and copies ran while one was open for 1% -> 4% of each run, Pallas kernels for 0% -> 0%
where the time goes in v6:
time: 58.5 us; the launch traced here: 58.1 us
  waiting for transfers between devices  23.4 us (40%)
  local copies, waits for them, and re-layouts  15.5 us (26%)
  starting transfers between devices  11 us (19%)
  other arithmetic  5.3 us (9%)
  matrix products  1.79 us (3%)
  between operations  1.08 us (2%)
    all_to_all x1, waiting for transfers between devices, pair_exchange(): lax.all_to_all(send.reshape(shards, half, width), ('basin', 'band'), spli...  14.8 us
    all_to_all x1, waiting for transfers between devices, local(): lax.all_to_all(jnp.broadcast_to(payload[None], (shards, padded)), grid, s...  7.24 us
    all_to_all x1, starting transfers between devices, pair_exchange(): lax.all_to_all(send.reshape(shards, half, width), ('basin', 'band'), spli...  7.22 us
    unnamed x29, local copies, waits for them, and re-layouts  4.92 us
    slice x1, local copies, waits for them, and re-layouts, land_update(): rain_now = precip[:, sub_step]  4.69 us
    all_to_all x1, starting transfers between devices, local(): lax.all_to_all(jnp.broadcast_to(payload[None], (shards, padded)), grid, s...  3.15 us
    concatenate x1, local copies, waits for them, and re-layouts, local(): jnp.concatenate([outlet.reshape(-1), trib_river.astype(jnp.float32), trib...  1.42 us
    ppermute x1, waiting for transfers between devices, pair_exchange(): chip_sum = keep_side + lax.ppermute(give_side, 'band', swap)  1.42 us
  transfers between devices with their start and end apart: 4, of which 3 were waited for; matrix products, arithmetic and copies ran while one was open for 4% of the time, Pallas kernels for 0%

profile of v6, /device:TPU:0, one launch (start us, length us, event | category | flops | bytes accessed | tf_op | source)
XLA Modules:
  0.0 58.1 jit_solution(339561300998592118)
XLA Ops:
  0.7 4.7 %fusion.53 = (f32[192,1,128]{2,1,0:T(1,128)S(1)}, f32[192,1,128]{2,1,0:T(1,128)S(1)}, f32[192,1,128]{2,1,0:T(1,128)S(1)}, f32[192,1,128]{2,1,0:T(1,128)S(1)}, f3...) fusion(f32[192,8,128]{2,1,0:T(8,128)} %param.15), kind=kLoop, calls=%fused_computation.166 | loop fusion | bytes 1572864 | tf_op jit(solution)/shard_map/slice | solution.py:11
  5.5 0.9 %copy-done.2 = f32[192,128]{1,0:T(8,128)S(1)} copy-done((f32[192,128]{1,0:T(8,128)S(1)}, f32[192,128]{1,0:T(8,128)}, u32[]{:S(2)}) %copy-start.2) | copy-done | bytes 98328
  6.4 0.1 bitcast_dynamic-update-slice_fusion.5
  6.4 0.1 bitcast_dynamic-update-slice_fusion.4
  6.6 0.1 bitcast_dynamic-update-slice_fusion.2
  6.8 0.1 bitcast_dynamic-update-slice_fusion
  6.8 0.5 copy.131
  7.3 0.1 reshape.306
  7.5 0.5 copy-done.9
  8.0 0.2 copy-done.8
  8.2 0.7 %fusion = f32[8,2,2,8,1024]{4,3,2,1,0:T(8,128)S(1)} fusion(f32[192,1024,1,1,1]{1,0,2,3,4:T(8,128)S(1)} %reshape.306, s32[8,2,2,8]{3,2,1,0:T(2,128)S(1)} %multiply_add_fusion, s32[192]{0:T(256)S(1)} %multiply_add_fusion.17), kind=kOutput, calls=%fused_computation.1 | convolution fusion | flops 604028928 | bytes 1836800 | tf_op jit(solution)/shard_map/dot_general | solution.py:51
  8.9 0.5 collective-permute-start
  9.4 0.1 broadcast_in_dim.67
  9.5 1.4 %collective-permute-done = f32[8,2,8,1024]{3,2,1,0:T(8,128)S(1)} collective-permute-done((f32[8,2,8,1024]{3,2,1,0:T(8,128)S(1)}, f32[8,2,8,1024]{3,2,1,0:T(8,128)S(1)}, u32[]{:S(2)}, u32[]{:S(2)}) %collective-permute-start) | collective-permute-done | bytes 524320 | tf_op jit(solution)/shard_map/ppermute | solution.py:83
  10.9 0.1 bitcast_add_fusion
  11.0 0.1 fusion.54
  11.1 0.9 %bitcast_select_fusion = f32[32,4,1024]{2,1,0:T(4,128)} fusion(f32[8,2,4,1024]{3,2,1,0:T(4,128)S(1)} %get-tuple-element.44, f32[8,2,4,1024]{3,2,1,0:T(4,128)S(1)} %get-tuple-element.43, pred[32]{0:T(512)(128)(4,1)S(1)} %broadcast_in_dim.67), kind=kLoop, calls=%fused_computation.3 | loop fusion | flops 131072 | bytes 1048608 | tf_op jit(solution)/shard_map/jit(_where)/select_n | solution.py:85
  12.1 7.2 %all-to-all-start = ((f32[32,4,1024]{2,1,0:T(4,128)}), f32[32,4,1024]{2,1,0:T(4,128)S(1)}, u32[]{:S(2)}, u32[]{:S(2)}) async-start(f32[32,4,1024]{2,1,0:T(4,128)} %bitcast_select_fusion), calls=%async_computation | async-start | bytes 1048576 | tf_op jit(solution)/shard_map/all_to_all | solution.py:86
  19.3 0.7 %add_subtract_fusion = f32[192,128]{1,0:T(8,128)} fusion(f32[192,128]{1,0:T(8,128)S(1)} %bitcast.305, f32[192,128]{1,0:T(8,128)S(1)} %copy-done.2, f32[192,128]{1,0:T(8,128)S(1)} %copy-done.1, f32[192,128]{1,0:T(8,128)S(1)} %bitcast.299, f32[192,128]{1,0:T(8,128)S(1)} %get-tuple-element.32, f32[192,128]{1,0:T(8,128)S(1)} %bitcast.290), kind=kLoop, calls=%fused_computation.23 | loop fusion | flops 466944 | bytes 688128 | tf_op jit(solution)/shard_map/sub | solution.py:13
  20.1 14.8 %all-to-all-done = f32[32,4,1024]{2,1,0:T(4,128)S(1)} async-done(((f32[32,4,1024]{2,1,0:T(4,128)}), f32[32,4,1024]{2,1,0:T(4,128)S(1)}, u32[]{:S(2)}, u32[]{:S(2)}) %all-to-all-start) | async-done | bytes 524320 | tf_op jit(solution)/shard_map/all_to_all | solution.py:86
  34.9 0.3 select_reduce_fusion.1
  35.1 0.1 collective-permute-start.1
  35.3 0.6 %copy-done.12 = s32[8]{0:T(128)S(1)} copy-done((s32[8]{0:T(128)S(1)}, s32[8]{0:T(128)}, u32[]{:S(2)}) %copy-start.12) | copy-done | bytes 56
  35.9 0.7 %copy-done.13 = s32[8]{0:T(128)S(1)} copy-done((s32[8]{0:T(128)S(1)}, s32[8]{0:T(128)}, u32[]{:S(2)}) %copy-start.13) | copy-done | bytes 56
  36.6 0.7 %copy-done.10 = f32[1,1,128]{2,1,0:T(1,128)S(1)} copy-done((f32[1,1,128]{2,1,0:T(1,128)S(1)}, f32[1,1,128]{2,1,0:T(1,128)}, u32[]{:S(2)}) %copy-start.10) | copy-done | bytes 536
  37.2 0.6 slice.162
  37.8 0.1 copy-done.11
  37.9 0.7 %slice.164 = f32[1,1,1]{2,1,0:T(1,128)} slice(f32[1,1,128]{2,1,0:T(1,128)S(1)} %copy-done.11), slice={[0:1], [0:1], [127:128]} | slice | bytes 8 | tf_op jit(solution)/shard_map/slice | solution.py:143
  38.6 0.9 %fusion.9 = f32[8,8,128]{2,1,0:T(8,128)S(1)} fusion(f32[8,128,128]{2,1,0:T(8,128)S(1)} %copy-done, f32[1,8,8,128]{3,1,2,0:T(8,128)S(1)} %maximum_bitcast_fusion), kind=kOutput, calls=%fused_computation.48 | convolution fusion | flops 12582912 | bytes 589824 | tf_op jit(solution)/shard_map/brc,btc->btr/dot_general | solution.py:127
  39.5 0.7 %copy-done.4 = f32[8,128]{1,0:T(8,128)S(1)} copy-done((f32[8,128]{1,0:T(8,128)S(1)}, f32[8,128]{1,0:T(8,128)}, u32[]{:S(2)}) %copy-start.4) | copy-done | bytes 4120
  40.3 0.6 %constant_dynamic-update-slice_fusion = (f32[8,8,128]{2,0,1:T(8,128)S(1)}, f32[8,128]{1,0:T(8,128)}) fusion(f32[8,8,128]{2,0,1:T(8,128)S(1)} %constant_dynamic-update-slice_fusion.1, f32[8,128]{1,0:T(8,128)S(1)} %bitcast.322, f32[8,128]{1,0:T(8,128)S(1)} %copy-done.4, f32[8,128]{1,0:T(8,128)S(1)} %bitcast.314, f32[8,128]{1,0:T(8,128)S(1)} %get-tuple-element.26), kind=kLoop, calls=%fused_computation.40 | loop fusion | flops 7168 | bytes 24576 | tf_op jit(solution)/shard_map/stack | solution.py:24
  40.9 0.1 slice.199
  41.0 0.1 copy.141
  41.1 0.1 reshape_squeeze.9
  41.2 1.4 %concatenate.7 = f32[210]{0:T(256)S(1)} concatenate(f32[64]{0:T(128)S(1)} %reshape_squeeze.9, f32[8]{0:T(128)S(1)} %convert_element_type.33, f32[8]{0:T(128)S(1)} %convert_element_type.34, f32[128]{0:T(128)S(1)} %slice_bitcast_fusion.8, f32[1]{0:T(128)} %bitcast.40, f32[1]{0:T(128)} %bitcast.41), dimensions={0} | concatenate | bytes 1680 | tf_op jit(solution)/shard_map/concatenate | solution.py:136
  42.6 0.6 %broadcast_in_dim.103 = f32[32,1,256]{2,1,0:T(1,128)} broadcast(f32[256]{0:T(256)S(1)} %pad.4), dimensions={2} | broadcast | bytes 33792 | tf_op jit(solution)/shard_map/broadcast_in_dim | solution.py:150
  43.2 3.2 %all-to-all-start.1 = ((f32[32,1,256]{2,1,0:T(1,128)}), f32[32,1,256]{2,1,0:T(1,128)S(1)}, u32[]{:S(2)}, u32[]{:S(2)}) async-start(f32[32,1,256]{2,1,0:T(1,128)} %broadcast_in_dim.103), calls=%async_computation.1 | async-start | bytes 65536 | tf_op jit(solution)/shard_map/all_to_all | solution.py:149
  46.4 7.2 %all-to-all-done.1 = f32[32,1,256]{2,1,0:T(1,128)S(1)} async-done(((f32[32,1,256]{2,1,0:T(1,128)}), f32[32,1,256]{2,1,0:T(1,128)S(1)}, u32[]{:S(2)}, u32[]{:S(2)}) %all-to-all-start.1) | async-done | bytes 32800 | tf_op jit(solution)/shard_map/all_to_all | solution.py:149
  53.7 0.1 slice.201
  53.7 0.1 slice.203
  53.8 0.2 slice_reduce_fusion
  54.0 0.1 mul.522
  54.1 0.1 eq.107
  54.2 0.1 slice_compare_fusion
  54.2 0.1 eq.106
  54.3 0.1 reshape_squeeze.10
  54.4 0.1 reshape_squeeze.11
  54.5 0.1 fusion.6
  54.6 0.3 multiply_reduce_fusion
  55.0 0.1 multiply_reduce_fusion.1
  55.1 0.2 multiply_add_fusion.1
  55.3 0.1 multiply_select_fusion
  55.4 0.6 %copy-done.7 = f32[1,8]{1,0:T(1,128)S(1)} copy-done((f32[1,8]{1,0:T(1,128)S(1)}, f32[1,8]{1,0:T(1,128)}, u32[]{:S(2)}) %copy-start.7) | copy-done | bytes 56
  56.1 0.1 fusion.13
  56.2 0.1 stack.94
  56.3 0.1 fusion.15
  56.4 0.1 fusion.17
  56.5 0.1 fusion.19
  56.7 0.1 fusion.21
  56.8 0.1 fusion.23
  56.9 0.1 fusion.25
  57.1 0.1 fusion.27
  57.2 0.2 fusion.7
  57.5 0.6 %stack.95 = f32[8,128]{1,0:T(8,128)} concatenate(f32[1,128]{1,0:T(1,128)S(1)} %get-tuple-element.14, f32[1,128]{1,0:T(1,128)S(1)} %get-tuple-element.13, f32[1,128]{1,0:T(1,128)S(1)} %get-tuple-element.12, f32[1,128]{1,0:T(1,128)S(1)} %get-tuple-element.11, f32[1,128]{1,0:T(1,128)S(1)} %get-tuple-element.10, f32[1,128]{1,0:T(1,128)S(1)} %get-tuple-element.9, ...), dimensions={0} | concatenate | bytes 8192 | tf_op jit(solution)/shard_map/stack | solution.py:24
  (58 shorter events, 0.6 us)
Async XLA Ops:
  0.6 37.9 %copy-start = (f32[8,128,128]{2,1,0:T(8,128)S(1)}, f32[8,128,128]{2,1,0:T(8,128)}, u32[]{:S(2)}) copy-start(f32[8,128,128]{2,1,0:T(8,128)} %param.21) | copy-start | bytes 1572868
  0.7 4.7 %copy-start.1 = (f32[192,128]{1,0:T(8,128)S(1)}, f32[192,128]{1,0:T(8,128)}, u32[]{:S(2)}) copy-start(f32[192,128]{1,0:T(8,128)} %param.17) | copy-start | bytes 294916
  0.7 4.7 %copy-start.3 = (f32[192,128]{1,0:T(8,128)S(1)}, f32[192,128]{1,0:T(8,128)}, u32[]{:S(2)}) copy-start(f32[192,128]{1,0:T(8,128)} %param.16) | copy-start | bytes 294916
  5.4 0.9 %copy-start.2 = (f32[192,128]{1,0:T(8,128)S(1)}, f32[192,128]{1,0:T(8,128)}, u32[]{:S(2)}) copy-start(f32[192,128]{1,0:T(8,128)} %param.18) | copy-start | bytes 294916
  7.3 0.7 %copy-start.9 = (s32[192]{0:T(256)S(1)}, s32[192]{0:T(256)}, u32[]{:S(2)}) copy-start(s32[192]{0:T(256)} %param.19) | copy-start | bytes 2308
  7.5 0.7 %copy-start.8 = (s32[192]{0:T(256)S(1)}, s32[192]{0:T(256)}, u32[]{:S(2)}) copy-start(s32[192]{0:T(256)} %param.20) | copy-start | bytes 2308
  8.9 2.1 %collective-permute-start = (f32[8,2,8,1024]{3,2,1,0:T(8,128)S(1)}, f32[8,2,8,1024]{3,2,1,0:T(8,128)S(1)}, u32[]{:S(2)}, u32[]{:S(2)}) collective-permute-start(f32[8,2,8,1024]{3,2,1,0:T(8,128)S(1)} %dynamic-slice_bitcast_fusion), channel_id=1, source_target_pairs={{1,0},{0,1},{3,2},{2,3},{5,4},{4,5},{7,6},{6,7},{9,8},{8,9},{11,10... | collective-permute-start | bytes 1572872 | tf_op jit(solution)/shard_map/ppermute | solution.py:83
  12.1 7.2 %copy-start.5 = (f32[1,1,128,128]{3,2,1,0:T(8,128)S(1)}, f32[1,1,128,128]{3,2,1,0:T(8,128)}, u32[]{:S(2)}) copy-start(f32[1,1,128,128]{3,2,1,0:T(8,128)} %param.26) | copy-start | bytes 196612
  12.1 22.8 %all-to-all-start = ((f32[32,4,1024]{2,1,0:T(4,128)}), f32[32,4,1024]{2,1,0:T(4,128)S(1)}, u32[]{:S(2)}, u32[]{:S(2)}) async-start(f32[32,4,1024]{2,1,0:T(4,128)} %bitcast_select_fusion), calls=%async_computation | async-start | bytes 1048576 | tf_op jit(solution)/shard_map/all_to_all | solution.py:86
  35.1 3.4 %collective-permute-start.1 = (f32[4,1024]{1,0:T(4,128)S(1)}, f32[4,1024]{1,0:T(4,128)S(1)}, u32[]{:S(2)}, u32[]{:S(2)}) collective-permute-start(f32[4,1024]{1,0:T(4,128)S(1)} %get-tuple-element.4), channel_id=1, source_target_pairs={{1,0},{0,1},{3,2},{2,3},{5,4},{4,5},{7,6},{6,7},{9,8},{8,9},{11,10... | collective-permute-start | bytes 49160 | tf_op jit(solution)/shard_map/ppermute | solution.py:91
  35.3 0.7 %copy-start.12 = (s32[8]{0:T(128)S(1)}, s32[8]{0:T(128)}, u32[]{:S(2)}) copy-start(s32[8]{0:T(128)} %param.24) | copy-start | bytes 100
  35.9 0.7 %copy-start.13 = (s32[8]{0:T(128)S(1)}, s32[8]{0:T(128)}, u32[]{:S(2)}) copy-start(s32[8]{0:T(128)} %param.25) | copy-start | bytes 100
  36.6 0.7 %copy-start.10 = (f32[1,1,128]{2,1,0:T(1,128)S(1)}, f32[1,1,128]{2,1,0:T(1,128)}, u32[]{:S(2)}) copy-start(f32[1,1,128]{2,1,0:T(1,128)} %param.27) | copy-start | bytes 1540
  37.2 0.7 %copy-start.11 = (f32[1,1,128]{2,1,0:T(1,128)S(1)}, f32[1,1,128]{2,1,0:T(1,128)}, u32[]{:S(2)}) copy-start(f32[1,1,128]{2,1,0:T(1,128)} %param.28) | copy-start | bytes 1540
  39.5 0.7 %copy-start.4 = (f32[8,128]{1,0:T(8,128)S(1)}, f32[8,128]{1,0:T(8,128)}, u32[]{:S(2)}) copy-start(f32[8,128]{1,0:T(8,128)} %param.22) | copy-start | bytes 12292
  39.5 0.7 %copy-start.6 = (f32[8,128]{1,0:T(8,128)S(1)}, f32[8,128]{1,0:T(8,128)}, u32[]{:S(2)}) copy-start(f32[8,128]{1,0:T(8,128)} %param.23) | copy-start | bytes 12292
  43.2 10.4 %all-to-all-start.1 = ((f32[32,1,256]{2,1,0:T(1,128)}), f32[32,1,256]{2,1,0:T(1,128)S(1)}, u32[]{:S(2)}, u32[]{:S(2)}) async-start(f32[32,1,256]{2,1,0:T(1,128)} %broadcast_in_dim.103), calls=%async_computation.1 | async-start | bytes 65536 | tf_op jit(solution)/shard_map/all_to_all | solution.py:149
  55.4 0.7 %copy-start.7 = (f32[1,8]{1,0:T(1,128)S(1)}, f32[1,8]{1,0:T(1,128)}, u32[]{:S(2)}) copy-start(f32[1,8]{1,0:T(1,128)} %param.29) | copy-start | bytes 100

commit v7 on v6

--- a/solution.py
+++ b/solution.py
@@ -133,42 +133,69 @@
     trib_flows = route_series(trib_mixed, trib_keep, trib_prev)
     outlet = trib_flows[:, :, reaches - 1]
 
-    payload = jnp.concatenate(
-        [
-            outlet.reshape(-1),
-            trib_river.astype(jnp.float32),
-            trib_reach.astype(jnp.float32),
-            operator[reaches - 1],
-            keep_main[reaches - 1 :],
-            prev_main[reaches - 1 :],
-        ]
-    )
-    width = payload.shape[0]
-    padded = -(-width // 128) * 128
-    payload = jnp.pad(payload, (0, padded - width))
-    every = lax.all_to_all(
-        jnp.broadcast_to(payload[None], (shards, padded)), grid, split_axis=0, concat_axis=0, tiled=True
-    )
-
     mine = lax.axis_index("band")
     me = lax.axis_index("basin")
-    at = 0
-    outlets = every[:, at : at + blocks * sub_steps].reshape(chains, rivers * blocks, sub_steps)
-    at += blocks * sub_steps
-    river_of = every[:, at : at + blocks].reshape(chains, rivers * blocks)
-    at += blocks
-    reach_of = every[:, at : at + blocks].reshape(chains, rivers * blocks)
-    at += blocks
-    exit_rows = lax.dynamic_index_in_dim(
-        every[:, at : at + reaches].reshape(chains, rivers, reaches), mine, axis=1, keepdims=False
-    )
-    at += reaches
-    keeps = lax.dynamic_index_in_dim(
-        every[:, at].reshape(chains, rivers), mine, axis=1, keepdims=False
-    )
-    starts = lax.dynamic_index_in_dim(
-        every[:, at + 1].reshape(chains, rivers), mine, axis=1, keepdims=False
-    )
+    spread_lanes = reaches // blocks
+    if reaches % blocks == 0 and sub_steps + 4 + spread_lanes <= reaches:
+        column = lambda value: jnp.broadcast_to(value.reshape(-1, 1), (blocks, 1))
+        tile = jnp.concatenate(
+            [
+                outlet,
+                column(trib_river.astype(jnp.float32)),
+                column(trib_reach.astype(jnp.float32)),
+                column(keep_main[reaches - 1]),
+                column(prev_main[reaches - 1]),
+                operator[reaches - 1].reshape(blocks, spread_lanes),
+            ],
+            axis=1,
+        )
+        tile = jnp.pad(tile, ((0, 0), (0, reaches - tile.shape[1])))
+        every = lax.all_to_all(
+            jnp.broadcast_to(tile[None], (shards,) + tile.shape), grid, split_axis=0, concat_axis=0, tiled=True
+        )
+        outlets = every[:, :, :sub_steps].reshape(chains, rivers * blocks, sub_steps)
+        river_of = every[:, :, sub_steps].reshape(chains, rivers * blocks)
+        reach_of = every[:, :, sub_steps + 1].reshape(chains, rivers * blocks)
+        facts = lax.dynamic_index_in_dim(
+            every.reshape(chains, rivers, blocks, reaches), mine, axis=1, keepdims=False
+        )
+        keeps = facts[:, 0, sub_steps + 2]
+        starts = facts[:, 0, sub_steps + 3]
+        exit_rows = facts[:, :, sub_steps + 4 : sub_steps + 4 + spread_lanes].reshape(chains, reaches)
+    else:
+        payload = jnp.concatenate(
+            [
+                outlet.reshape(-1),
+                trib_river.astype(jnp.float32),
+                trib_reach.astype(jnp.float32),
+                operator[reaches - 1],
+                keep_main[reaches - 1 :],
+                prev_main[reaches - 1 :],
+            ]
+        )
+        width = payload.shape[0]
+        padded = -(-width // 128) * 128
+        payload = jnp.pad(payload, (0, padded - width))
+        every = lax.all_to_all(
+            jnp.broadcast_to(payload[None], (shards, padded)), grid, split_axis=0, concat_axis=0, tiled=True
+        )
+        at = 0
+        outlets = every[:, at : at + blocks * sub_steps].reshape(chains, rivers * blocks, sub_steps)
+        at += blocks * sub_steps
+        river_of = every[:, at : at + blocks].reshape(chains, rivers * blocks)
+        at += blocks
+        reach_of = every[:, at : at + blocks].reshape(chains, rivers * blocks)
+        at += blocks
+        exit_rows = lax.dynamic_index_in_dim(
+            every[:, at : at + reaches].reshape(chains, rivers, reaches), mine, axis=1, keepdims=False
+        )
+        at += reaches
+        keeps = lax.dynamic_index_in_dim(
+            every[:, at].reshape(chains, rivers), mine, axis=1, keepdims=False
+        )
+        starts = lax.dynamic_index_in_dim(
+            every[:, at + 1].reshape(chains, rivers), mine, axis=1, keepdims=False
+        )
 
     joins = (river_of == mine.astype(jnp.float32))[:, :, None] & (
         reach_of[:, :, None] == jnp.arange(reaches, dtype=jnp.float32)[None, None, :]

time: 58.5 us -> 58.9 us (level)
  other arithmetic: 5.3 us -> 6.04 us
    concatenate x1, local copies, waits for them, and re-layouts: 1.42 us -> 0.08 us  [local(): jnp.concatenate([outlet, column(trib_river.astype(jnp.float32)), column(t...]
    broadcast_in_dim x1 -> x3, local copies, waits for them, and re-layouts: 0.62 us -> 1.95 us  [the longest x2 1.3 us: local(): column = lambda value: jnp.broadcast_to(value.reshape(-1, 1), (blocks, 1))]
    eq x1, other arithmetic: 0.08 us -> 0.7 us  [local(): river_of == mine.astype(jnp.float32)]
    slice x6 -> x5, local copies, waits for them, and re-layouts: 1.57 us -> 1.43 us  [the longest x1 0.58 us: local(): keep_main[reaches - 1]]
where the time goes in v7:
time: 58.9 us; the launch traced here: 58.4 us
  waiting for transfers between devices  23.1 us (39%)
  local copies, waits for them, and re-layouts  15.4 us (26%)
  starting transfers between devices  11 us (19%)
  other arithmetic  6.04 us (10%)
  matrix products  1.79 us (3%)
  between operations  1.08 us (2%)
    all_to_all x1, waiting for transfers between devices, pair_exchange(): lax.all_to_all(send.reshape(shards, half, width), ('basin', 'band'), spli...  14.2 us
    all_to_all x1, waiting for transfers between devices, local(): lax.all_to_all(jnp.broadcast_to(tile[None], (shards,) + tile.shape), grid...  7.47 us
    all_to_all x1, starting transfers between devices, pair_exchange(): lax.all_to_all(send.reshape(shards, half, width), ('basin', 'band'), spli...  7.22 us
    unnamed x29, local copies, waits for them, and re-layouts  4.9 us
    slice x1, local copies, waits for them, and re-layouts, land_update(): rain_now = precip[:, sub_step]  4.69 us
    all_to_all x1, starting transfers between devices, local(): lax.all_to_all(jnp.broadcast_to(tile[None], (shards,) + tile.shape), grid...  3.17 us
    ppermute x1, waiting for transfers between devices, pair_exchange(): chip_sum = keep_side + lax.ppermute(give_side, 'band', swap)  1.42 us
    broadcast_in_dim x2, local copies, waits for them, and re-layouts, local(): column = lambda value: jnp.broadcast_to(value.reshape(-1, 1), (blocks, 1))  1.3 us
  transfers between devices with their start and end apart: 4, of which 3 were waited for; matrix products, arithmetic and copies ran while one was open for 4% of the time, Pallas kernels for 0%

profile of v7, /device:TPU:0, one launch (start us, length us, event | category | flops | bytes accessed | tf_op | source)
XLA Modules:
  0.0 58.4 jit_solution(18388227256390911610)
XLA Ops:
  0.7 4.7 %fusion.53 = (f32[192,1,128]{2,1,0:T(1,128)S(1)}, f32[192,1,128]{2,1,0:T(1,128)S(1)}, f32[192,1,128]{2,1,0:T(1,128)S(1)}, f32[192,1,128]{2,1,0:T(1,128)S(1)}, f3...) fusion(f32[192,8,128]{2,1,0:T(8,128)} %param.15), kind=kLoop, calls=%fused_computation.165 | loop fusion | bytes 1572864 | tf_op jit(solution)/shard_map/slice | solution.py:11
  5.5 0.9 %copy-done.2 = f32[192,128]{1,0:T(8,128)S(1)} copy-done((f32[192,128]{1,0:T(8,128)S(1)}, f32[192,128]{1,0:T(8,128)}, u32[]{:S(2)}) %copy-start.2) | copy-done | bytes 98328
  6.4 0.1 bitcast_dynamic-update-slice_fusion.5
  6.4 0.1 bitcast_dynamic-update-slice_fusion.4
  6.6 0.1 bitcast_dynamic-update-slice_fusion.2
  6.8 0.1 bitcast_dynamic-update-slice_fusion
  6.8 0.5 copy.212
  7.3 0.1 reshape.350
  7.5 0.5 copy-done.9
  8.0 0.2 copy-done.8
  8.2 0.7 %fusion = f32[8,2,2,8,1024]{4,3,2,1,0:T(8,128)S(1)} fusion(f32[192,1024,1,1,1]{1,0,2,3,4:T(8,128)S(1)} %reshape.350, s32[8,2,2,8]{3,2,1,0:T(2,128)S(1)} %multiply_add_fusion, s32[192]{0:T(256)S(1)} %multiply_add_fusion.17), kind=kOutput, calls=%fused_computation.1 | convolution fusion | flops 604028928 | bytes 1836800 | tf_op jit(solution)/shard_map/dot_general | solution.py:51
  8.9 0.5 collective-permute-start
  9.4 0.1 broadcast_in_dim.108
  9.5 1.4 %collective-permute-done = f32[8,2,8,1024]{3,2,1,0:T(8,128)S(1)} collective-permute-done((f32[8,2,8,1024]{3,2,1,0:T(8,128)S(1)}, f32[8,2,8,1024]{3,2,1,0:T(8,128)S(1)}, u32[]{:S(2)}, u32[]{:S(2)}) %collective-permute-start) | collective-permute-done | bytes 524320 | tf_op jit(solution)/shard_map/ppermute | solution.py:83
  11.0 0.1 fusion.54
  11.1 0.9 %bitcast_select_fusion = f32[32,4,1024]{2,1,0:T(4,128)} fusion(f32[8,2,4,1024]{3,2,1,0:T(4,128)S(1)} %get-tuple-element.44, f32[8,2,4,1024]{3,2,1,0:T(4,128)S(1)} %get-tuple-element.43, pred[32]{0:T(512)(128)(4,1)S(1)} %broadcast_in_dim.108), kind=kLoop, calls=%fused_computation.3 | loop fusion | flops 131072 | bytes 1048608 | tf_op jit(solution)/shard_map/jit(_where)/select_n | solution.py:85
  12.1 7.2 %all-to-all-start = ((f32[32,4,1024]{2,1,0:T(4,128)}), f32[32,4,1024]{2,1,0:T(4,128)S(1)}, u32[]{:S(2)}, u32[]{:S(2)}) async-start(f32[32,4,1024]{2,1,0:T(4,128)} %bitcast_select_fusion), calls=%async_computation | async-start | bytes 1048576 | tf_op jit(solution)/shard_map/all_to_all | solution.py:86
  19.4 0.6 %copy-done.12 = s32[8]{0:T(128)S(1)} copy-done((s32[8]{0:T(128)S(1)}, s32[8]{0:T(128)}, u32[]{:S(2)}) %copy-start.12) | copy-done | bytes 56
  20.0 0.7 %copy-done.13 = s32[8]{0:T(128)S(1)} copy-done((s32[8]{0:T(128)S(1)}, s32[8]{0:T(128)}, u32[]{:S(2)}) %copy-start.13) | copy-done | bytes 56
  20.7 14.2 %all-to-all-done = f32[32,4,1024]{2,1,0:T(4,128)S(1)} async-done(((f32[32,4,1024]{2,1,0:T(4,128)}), f32[32,4,1024]{2,1,0:T(4,128)S(1)}, u32[]{:S(2)}, u32[]{:S(2)}) %all-to-all-start) | async-done | bytes 524320 | tf_op jit(solution)/shard_map/all_to_all | solution.py:86
  34.9 0.3 select_reduce_fusion.1
  35.2 0.1 copy.223
  35.3 0.1 copy.224
  35.4 0.6 copy-done.10
  36.0 0.6 slice.157
  36.6 0.6 slice.158
  37.2 0.1 reshape_squeeze.2
  37.3 0.9 %fusion.10 = f32[8,8,128]{2,1,0:T(8,128)S(1)} fusion(f32[8,128,128]{2,1,0:T(8,128)S(1)} %copy-done, f32[1,8,8,128]{3,1,2,0:T(8,128)S(1)} %maximum_bitcast_fusion), kind=kOutput, calls=%fused_computation.51 | convolution fusion | flops 12582912 | bytes 589824 | tf_op jit(solution)/shard_map/brc,btc->btr/dot_general | solution.py:127
  38.3 0.7 %copy-done.4 = f32[8,128]{1,0:T(8,128)S(1)} copy-done((f32[8,128]{1,0:T(8,128)S(1)}, f32[8,128]{1,0:T(8,128)}, u32[]{:S(2)}) %copy-start.4) | copy-done | bytes 4120
  39.0 0.6 %constant_dynamic-update-slice_fusion = (f32[8,8,128]{2,0,1:T(8,128)S(1)}, f32[8,128]{1,0:T(8,128)}) fusion(f32[8,8,128]{2,0,1:T(8,128)S(1)} %constant_dynamic-update-slice_fusion.1, f32[8,128]{1,0:T(8,128)S(1)} %bitcast.331, f32[8,128]{1,0:T(8,128)S(1)} %copy-done.4, f32[8,128]{1,0:T(8,128)S(1)} %bitcast.323, f32[8,128]{1,0:T(8,128)S(1)} %get-tuple-element.26), kind=kLoop, calls=%fused_computation.43 | loop fusion | flops 7168 | bytes 24576 | tf_op jit(solution)/shard_map/stack | solution.py:24
  39.6 0.1 slice.193
  39.7 0.1 copy.222
  39.9 0.7 %broadcast_in_dim.116 = f32[8,1]{1,0:T(8,128)S(1)} broadcast(f32[]{:T(128)} %bitcast.42), dimensions={} | broadcast | bytes 36 | tf_op jit(solution)/shard_map/broadcast_in_dim | solution.py:140
  40.5 0.6 %broadcast_in_dim.118 = f32[8,1]{1,0:T(8,128)S(1)} broadcast(f32[]{:T(128)} %bitcast.43), dimensions={} | broadcast | bytes 36 | tf_op jit(solution)/shard_map/broadcast_in_dim | solution.py:140
  41.2 0.1 concatenate.7
  41.3 0.7 %broadcast_in_dim.119 = f32[32,8,128]{2,1,0:T(8,128)} broadcast(f32[8,128]{1,0:T(8,128)S(1)} %pad.4), dimensions={1,2} | broadcast | bytes 135168 | tf_op jit(solution)/shard_map/broadcast_in_dim | solution.py:154
  41.9 3.2 %all-to-all-start.1 = ((f32[32,8,128]{2,1,0:T(8,128)}), f32[32,8,128]{2,1,0:T(8,128)S(1)}, u32[]{:S(2)}, u32[]{:S(2)}) async-start(f32[32,8,128]{2,1,0:T(8,128)} %broadcast_in_dim.119), calls=%async_computation.1 | async-start | bytes 262144 | tf_op jit(solution)/shard_map/all_to_all | solution.py:153
  45.1 0.7 %add_subtract_fusion = f32[192,128]{1,0:T(8,128)} fusion(f32[192,128]{1,0:T(8,128)S(1)} %bitcast.320, f32[192,128]{1,0:T(8,128)S(1)} %copy-done.2, f32[192,128]{1,0:T(8,128)S(1)} %copy-done.1, f32[192,128]{1,0:T(8,128)S(1)} %bitcast.314, f32[192,128]{1,0:T(8,128)S(1)} %get-tuple-element.32, f32[192,128]{1,0:T(8,128)S(1)} %bitcast.303), kind=kLoop, calls=%fused_computation.26 | loop fusion | flops 466944 | bytes 688128 | tf_op jit(solution)/shard_map/sub | solution.py:13
  45.8 7.5 %all-to-all-done.1 = f32[32,8,128]{2,1,0:T(8,128)S(1)} async-done(((f32[32,8,128]{2,1,0:T(8,128)}), f32[32,8,128]{2,1,0:T(8,128)S(1)}, u32[]{:S(2)}, u32[]{:S(2)}) %all-to-all-start.1) | async-done | bytes 131104 | tf_op jit(solution)/shard_map/all_to_all | solution.py:153
  53.3 0.2 slice_reduce_fusion
  53.6 0.7 %fusion.7 = pred[32,8]{1,0:T(8,128)(4,1)S(1)} fusion(f32[32,8,128]{2,1,0:T(8,128)S(1)} %all-to-all-done.1, f32[]{:T(128)S(6)} %convert_element_type.35), kind=kLoop, calls=%fused_computation.16 | loop fusion | flops 256 | bytes 1284 | tf_op jit(solution)/shard_map/eq | solution.py:200
  54.3 0.1 eq.106
  54.4 0.1 slice.197
  54.4 0.1 reshape.349
  54.5 0.1 copy.255
  54.6 0.1 copy.226
  54.7 0.2 multiply_reduce_fusion.2
  54.9 0.1 fusion.6
  55.1 0.3 multiply_reduce_fusion
  55.4 0.1 multiply_reduce_fusion.1
  55.5 0.1 multiply_select_fusion
  55.7 0.6 %copy-done.7 = f32[1,8]{1,0:T(1,128)S(1)} copy-done((f32[1,8]{1,0:T(1,128)S(1)}, f32[1,8]{1,0:T(1,128)}, u32[]{:S(2)}) %copy-start.7) | copy-done | bytes 56
  56.3 0.1 fusion.14
  56.4 0.1 multiply_add_fusion.1
  56.5 0.1 stack.94
  56.6 0.1 fusion.16
  56.7 0.1 fusion.18
  56.8 0.1 fusion.20
  57.0 0.1 fusion.22
  57.1 0.1 fusion.24
  57.2 0.1 fusion.26
  57.4 0.1 fusion.28
  57.5 0.2 fusion.8
  57.8 0.6 %stack.95 = f32[8,128]{1,0:T(8,128)} concatenate(f32[1,128]{1,0:T(1,128)S(1)} %get-tuple-element.14, f32[1,128]{1,0:T(1,128)S(1)} %get-tuple-element.13, f32[1,128]{1,0:T(1,128)S(1)} %get-tuple-element.12, f32[1,128]{1,0:T(1,128)S(1)} %get-tuple-element.11, f32[1,128]{1,0:T(1,128)S(1)} %get-tuple-element.10, f32[1,128]{1,0:T(1,128)S(1)} %get-tuple-element.9, ...), dimensions={0} | concatenate | bytes 8192 | tf_op jit(solution)/shard_map/stack | solution.py:24
  (59 shorter events, 0.9 us)
Async XLA Ops:
  0.6 36.7 %copy-start = (f32[8,128,128]{2,1,0:T(8,128)S(1)}, f32[8,128,128]{2,1,0:T(8,128)}, u32[]{:S(2)}) copy-start(f32[8,128,128]{2,1,0:T(8,128)} %param.21) | copy-start | bytes 1572868
  0.7 4.7 %copy-start.1 = (f32[192,128]{1,0:T(8,128)S(1)}, f32[192,128]{1,0:T(8,128)}, u32[]{:S(2)}) copy-start(f32[192,128]{1,0:T(8,128)} %param.17) | copy-start | bytes 294916
  0.7 4.7 %copy-start.3 = (f32[192,128]{1,0:T(8,128)S(1)}, f32[192,128]{1,0:T(8,128)}, u32[]{:S(2)}) copy-start(f32[192,128]{1,0:T(8,128)} %param.16) | copy-start | bytes 294916
  5.4 0.9 %copy-start.2 = (f32[192,128]{1,0:T(8,128)S(1)}, f32[192,128]{1,0:T(8,128)}, u32[]{:S(2)}) copy-start(f32[192,128]{1,0:T(8,128)} %param.18) | copy-start | bytes 294916
  7.3 0.7 %copy-start.9 = (s32[192]{0:T(256)S(1)}, s32[192]{0:T(256)}, u32[]{:S(2)}) copy-start(s32[192]{0:T(256)} %param.19) | copy-start | bytes 2308
  7.5 0.7 %copy-start.8 = (s32[192]{0:T(256)S(1)}, s32[192]{0:T(256)}, u32[]{:S(2)}) copy-start(s32[192]{0:T(256)} %param.20) | copy-start | bytes 2308
  8.9 2.1 %collective-permute-start = (f32[8,2,8,1024]{3,2,1,0:T(8,128)S(1)}, f32[8,2,8,1024]{3,2,1,0:T(8,128)S(1)}, u32[]{:S(2)}, u32[]{:S(2)}) collective-permute-start(f32[8,2,8,1024]{3,2,1,0:T(8,128)S(1)} %dynamic-slice_bitcast_fusion), channel_id=1, source_target_pairs={{1,0},{0,1},{3,2},{2,3},{5,4},{4,5},{7,6},{6,7},{9,8},{8,9},{11,10... | collective-permute-start | bytes 1572872 | tf_op jit(solution)/shard_map/ppermute | solution.py:83
  12.1 7.2 %copy-start.5 = (f32[1,1,128,128]{3,2,1,0:T(8,128)S(1)}, f32[1,1,128,128]{3,2,1,0:T(8,128)}, u32[]{:S(2)}) copy-start(f32[1,1,128,128]{3,2,1,0:T(8,128)} %param.26) | copy-start | bytes 196612
  12.1 22.8 %all-to-all-start = ((f32[32,4,1024]{2,1,0:T(4,128)}), f32[32,4,1024]{2,1,0:T(4,128)S(1)}, u32[]{:S(2)}, u32[]{:S(2)}) async-start(f32[32,4,1024]{2,1,0:T(4,128)} %bitcast_select_fusion), calls=%async_computation | async-start | bytes 1048576 | tf_op jit(solution)/shard_map/all_to_all | solution.py:86
  19.3 0.7 %copy-start.12 = (s32[8]{0:T(128)S(1)}, s32[8]{0:T(128)}, u32[]{:S(2)}) copy-start(s32[8]{0:T(128)} %param.24) | copy-start | bytes 100
  20.0 0.7 %copy-start.13 = (s32[8]{0:T(128)S(1)}, s32[8]{0:T(128)}, u32[]{:S(2)}) copy-start(s32[8]{0:T(128)} %param.25) | copy-start | bytes 100
  35.1 2.1 %collective-permute-start.1 = (f32[4,1024]{1,0:T(4,128)S(1)}, f32[4,1024]{1,0:T(4,128)S(1)}, u32[]{:S(2)}, u32[]{:S(2)}) collective-permute-start(f32[4,1024]{1,0:T(4,128)S(1)} %get-tuple-element.4), channel_id=1, source_target_pairs={{1,0},{0,1},{3,2},{2,3},{5,4},{4,5},{7,6},{6,7},{9,8},{8,9},{11,10... | collective-permute-start | bytes 49160 | tf_op jit(solution)/shard_map/ppermute | solution.py:91
  35.3 0.7 %copy-start.10 = (f32[1,1,128]{2,1,0:T(1,128)S(1)}, f32[1,1,128]{2,1,0:T(1,128)}, u32[]{:S(2)}) copy-start(f32[1,1,128]{2,1,0:T(1,128)} %param.27) | copy-start | bytes 1540
  36.0 0.7 %copy-start.11 = (f32[1,1,128]{2,1,0:T(1,128)S(1)}, f32[1,1,128]{2,1,0:T(1,128)}, u32[]{:S(2)}) copy-start(f32[1,1,128]{2,1,0:T(1,128)} %param.28) | copy-start | bytes 1540
  38.2 0.7 %copy-start.4 = (f32[8,128]{1,0:T(8,128)S(1)}, f32[8,128]{1,0:T(8,128)}, u32[]{:S(2)}) copy-start(f32[8,128]{1,0:T(8,128)} %param.22) | copy-start | bytes 12292
  38.2 0.7 %copy-start.6 = (f32[8,128]{1,0:T(8,128)S(1)}, f32[8,128]{1,0:T(8,128)}, u32[]{:S(2)}) copy-start(f32[8,128]{1,0:T(8,128)} %param.23) | copy-start | bytes 12292
  41.9 11.4 %all-to-all-start.1 = ((f32[32,8,128]{2,1,0:T(8,128)}), f32[32,8,128]{2,1,0:T(8,128)S(1)}, u32[]{:S(2)}, u32[]{:S(2)}) async-start(f32[32,8,128]{2,1,0:T(8,128)} %broadcast_in_dim.119), calls=%async_computation.1 | async-start | bytes 262144 | tf_op jit(solution)/shard_map/all_to_all | solution.py:153
  55.6 0.7 %copy-start.7 = (f32[1,8]{1,0:T(1,128)S(1)}, f32[1,8]{1,0:T(1,128)}, u32[]{:S(2)}) copy-start(f32[1,8]{1,0:T(1,128)} %param.29) | copy-start | bytes 100

commit v8 on v7

--- a/solution.py
+++ b/solution.py
@@ -137,19 +137,20 @@
     me = lax.axis_index("basin")
     spread_lanes = reaches // blocks
     if reaches % blocks == 0 and sub_steps + 4 + spread_lanes <= reaches:
-        column = lambda value: jnp.broadcast_to(value.reshape(-1, 1), (blocks, 1))
-        tile = jnp.concatenate(
-            [
-                outlet,
-                column(trib_river.astype(jnp.float32)),
-                column(trib_reach.astype(jnp.float32)),
-                column(keep_main[reaches - 1]),
-                column(prev_main[reaches - 1]),
-                operator[reaches - 1].reshape(blocks, spread_lanes),
-            ],
-            axis=1,
-        )
-        tile = jnp.pad(tile, ((0, 0), (0, reaches - tile.shape[1])))
+        lane = lax.broadcasted_iota(jnp.int32, (blocks, reaches), 1)
+        tile = jnp.pad(outlet, ((0, 0), (0, reaches - sub_steps)))
+        columns = (
+            trib_river.astype(jnp.float32)[:, None],
+            trib_reach.astype(jnp.float32)[:, None],
+            keep_main[reaches - 1 :][None, :],
+            prev_main[reaches - 1 :][None, :],
+        )
+        for offset, value in enumerate(columns):
+            tile = tile + jnp.where(lane == sub_steps + offset, value, 0.0)
+        spread_row = operator[reaches - 1].reshape(blocks, spread_lanes)
+        tile = tile + jnp.pad(
+            spread_row, ((0, 0), (sub_steps + 4, reaches - sub_steps - 4 - spread_lanes))
+        )
         every = lax.all_to_all(
             jnp.broadcast_to(tile[None], (shards,) + tile.shape), grid, split_axis=0, concat_axis=0, tiled=True
         )

time: 58.9 us -> 58.1 us (0.986)
  local copies, waits for them, and re-layouts: 15.4 us -> 13.2 us
  other arithmetic: 6.04 us -> 7.42 us
    broadcast_in_dim x2 -> x0, local copies, waits for them, and re-layouts: 1.3 us -> none  [local(): column = lambda value: jnp.broadcast_to(value.reshape(-1, 1), (blocks, 1))]
    select_n x0 -> x1, other arithmetic: none -> 1.3 us  [local(): tile = tile + jnp.where(lane == sub_steps + offset, value, 0.0)]
    unnamed x29, local copies, waits for them, and re-layouts: 4.9 us -> 4.27 us
  transfers between devices with their start and end apart: 4 -> 4, of which waited for: 3 -> 3; matrix products, arithmetic and copies ran while one was open for 4% -> 6% of each run, Pallas kernels for 0% -> 0%
where the time goes in v8:
time: 58.1 us; the launch traced here: 57.6 us
  waiting for transfers between devices  23.1 us (40%)
  local copies, waits for them, and re-layouts  13.2 us (23%)
  starting transfers between devices  11 us (19%)
  other arithmetic  7.42 us (13%)
  matrix products  1.79 us (3%)
  between operations  1.07 us (2%)
    all_to_all x1, waiting for transfers between devices, pair_exchange(): lax.all_to_all(send.reshape(shards, half, width), ('basin', 'band'), spli...  14.2 us
    all_to_all x1, waiting for transfers between devices, local(): lax.all_to_all(jnp.broadcast_to(tile[None], (shards,) + tile.shape), grid...  7.47 us
    all_to_all x1, starting transfers between devices, pair_exchange(): lax.all_to_all(send.reshape(shards, half, width), ('basin', 'band'), spli...  7.22 us
    slice x1, local copies, waits for them, and re-layouts, land_update(): rain_now = precip[:, sub_step]  4.69 us
    unnamed x29, local copies, waits for them, and re-layouts  4.27 us
    all_to_all x1, starting transfers between devices, local(): lax.all_to_all(jnp.broadcast_to(tile[None], (shards,) + tile.shape), grid...  3.17 us
    ppermute x1, waiting for transfers between devices, pair_exchange(): chip_sum = keep_side + lax.ppermute(give_side, 'band', swap)  1.42 us
    select_n x1, other arithmetic, local(): tile = tile + jnp.where(lane == sub_steps + offset, value, 0.0)  1.3 us
  transfers between devices with their start and end apart: 4, of which 3 were waited for; matrix products, arithmetic and copies ran while one was open for 6% of the time, Pallas kernels for 0%

profile of v8, /device:TPU:0, one launch (start us, length us, event | category | flops | bytes accessed | tf_op | source)
XLA Modules:
  0.0 57.6 jit_solution(5447256582358551453)
XLA Ops:
  0.7 4.7 %fusion.53 = (f32[192,1,128]{2,1,0:T(1,128)S(1)}, f32[192,1,128]{2,1,0:T(1,128)S(1)}, f32[192,1,128]{2,1,0:T(1,128)S(1)}, f32[192,1,128]{2,1,0:T(1,128)S(1)}, f3...) fusion(f32[192,8,128]{2,1,0:T(8,128)} %param.15), kind=kLoop, calls=%fused_computation.168 | loop fusion | bytes 1572864 | tf_op jit(solution)/shard_map/slice | solution.py:11
  5.5 0.9 %copy-done.2 = f32[192,128]{1,0:T(8,128)S(1)} copy-done((f32[192,128]{1,0:T(8,128)S(1)}, f32[192,128]{1,0:T(8,128)}, u32[]{:S(2)}) %copy-start.2) | copy-done | bytes 98328
  6.4 0.1 bitcast_dynamic-update-slice_fusion.5
  6.4 0.1 bitcast_dynamic-update-slice_fusion.4
  6.6 0.1 bitcast_dynamic-update-slice_fusion.2
  6.8 0.1 bitcast_dynamic-update-slice_fusion
  6.8 0.5 copy.200
  7.3 0.1 reshape.340
  7.5 0.5 copy-done.9
  8.0 0.2 copy-done.8
  8.2 0.7 %fusion = f32[8,2,2,8,1024]{4,3,2,1,0:T(8,128)S(1)} fusion(f32[192,1024,1,1,1]{1,0,2,3,4:T(8,128)S(1)} %reshape.340, s32[8,2,2,8]{3,2,1,0:T(2,128)S(1)} %multiply_add_fusion, s32[192]{0:T(256)S(1)} %multiply_add_fusion.17), kind=kOutput, calls=%fused_computation.1 | convolution fusion | flops 604028928 | bytes 1836800 | tf_op jit(solution)/shard_map/dot_general | solution.py:51
  8.9 0.5 collective-permute-start
  9.4 0.1 broadcast_in_dim.138
  9.5 1.4 %collective-permute-done = f32[8,2,8,1024]{3,2,1,0:T(8,128)S(1)} collective-permute-done((f32[8,2,8,1024]{3,2,1,0:T(8,128)S(1)}, f32[8,2,8,1024]{3,2,1,0:T(8,128)S(1)}, u32[]{:S(2)}, u32[]{:S(2)}) %collective-permute-start) | collective-permute-done | bytes 524320 | tf_op jit(solution)/shard_map/ppermute | solution.py:83
  10.9 0.1 bitcast_add_fusion
  11.0 0.1 fusion.54
  11.1 0.9 %bitcast_select_fusion = f32[32,4,1024]{2,1,0:T(4,128)} fusion(f32[8,2,4,1024]{3,2,1,0:T(4,128)S(1)} %get-tuple-element.44, f32[8,2,4,1024]{3,2,1,0:T(4,128)S(1)} %get-tuple-element.43, pred[32]{0:T(512)(128)(4,1)S(1)} %broadcast_in_dim.138), kind=kLoop, calls=%fused_computation.3 | loop fusion | flops 131072 | bytes 1048608 | tf_op jit(solution)/shard_map/jit(_where)/select_n | solution.py:85
  12.1 7.2 %all-to-all-start = ((f32[32,4,1024]{2,1,0:T(4,128)}), f32[32,4,1024]{2,1,0:T(4,128)S(1)}, u32[]{:S(2)}, u32[]{:S(2)}) async-start(f32[32,4,1024]{2,1,0:T(4,128)} %bitcast_select_fusion), calls=%async_computation | async-start | bytes 1048576 | tf_op jit(solution)/shard_map/all_to_all | solution.py:86
  19.3 0.6 %slice.158 = f32[1,1,1]{2,1,0:T(1,128)} slice(f32[1,1,128]{2,1,0:T(1,128)S(1)} %copy-done.11), slice={[0:1], [0:1], [127:128]} | slice | bytes 8 | tf_op jit(solution)/shard_map/slice | solution.py:146
  19.9 0.1 copy-done.10
  20.0 0.6 %slice.157 = f32[1,1,1]{2,1,0:T(1,128)} slice(f32[1,1,128]{2,1,0:T(1,128)S(1)} %copy-done.10), slice={[0:1], [0:1], [127:128]} | slice | bytes 8 | tf_op jit(solution)/shard_map/slice | solution.py:145
  20.6 14.2 %all-to-all-done = f32[32,4,1024]{2,1,0:T(4,128)S(1)} async-done(((f32[32,4,1024]{2,1,0:T(4,128)}), f32[32,4,1024]{2,1,0:T(4,128)S(1)}, u32[]{:S(2)}, u32[]{:S(2)}) %all-to-all-start) | async-done | bytes 524320 | tf_op jit(solution)/shard_map/all_to_all | solution.py:86
  34.9 0.3 select_reduce_fusion.1
  35.1 0.1 collective-permute-start.1
  35.2 1.3 %compare_select_fusion = (f32[128]{0:T(128)S(1)}, f32[128]{0:T(128)S(1)}) fusion(f32[]{:T(128)} %bitcast.41, f32[]{:T(128)} %bitcast.40), kind=kLoop, calls=%fused_computation.111 | loop fusion | flops 512 | bytes 1032 | tf_op jit(solution)/shard_map/jit(_where)/select_n | solution.py:149
  36.5 0.1 reshape_squeeze.4
  36.6 0.6 copy-done.12
  37.2 0.7 %copy-done.13 = s32[8]{0:T(128)S(1)} copy-done((s32[8]{0:T(128)S(1)}, s32[8]{0:T(128)}, u32[]{:S(2)}) %copy-start.13) | copy-done | bytes 56
  37.9 0.9 %fusion.10 = f32[8,8,128]{2,1,0:T(8,128)S(1)} fusion(f32[8,128,128]{2,1,0:T(8,128)S(1)} %copy-done, f32[1,8,8,128]{3,1,2,0:T(8,128)S(1)} %maximum_bitcast_fusion), kind=kOutput, calls=%fused_computation.51 | convolution fusion | flops 12582912 | bytes 589824 | tf_op jit(solution)/shard_map/brc,btc->btr/dot_general | solution.py:127
  38.8 0.7 %copy-done.4 = f32[8,128]{1,0:T(8,128)S(1)} copy-done((f32[8,128]{1,0:T(8,128)S(1)}, f32[8,128]{1,0:T(8,128)}, u32[]{:S(2)}) %copy-start.4) | copy-done | bytes 4120
  39.6 0.6 %constant_dynamic-update-slice_fusion = (f32[8,8,128]{2,0,1:T(8,128)S(1)}, f32[8,128]{1,0:T(8,128)}) fusion(f32[8,8,128]{2,0,1:T(8,128)S(1)} %constant_dynamic-update-slice_fusion.1, f32[8,128]{1,0:T(8,128)S(1)} %bitcast.326, f32[8,128]{1,0:T(8,128)S(1)} %copy-done.4, f32[8,128]{1,0:T(8,128)S(1)} %bitcast.319, f32[8,128]{1,0:T(8,128)S(1)} %get-tuple-element.26), kind=kLoop, calls=%fused_computation.43 | loop fusion | flops 7168 | bytes 24576 | tf_op jit(solution)/shard_map/stack | solution.py:24
  40.2 0.1 slice.193
  40.3 0.1 copy.210
  40.4 0.1 pad_add_fusion
  40.5 0.7 %broadcast_in_dim.153 = f32[32,8,128]{2,1,0:T(8,128)} broadcast(f32[8,128]{1,0:T(8,128)S(1)} %pad_add_fusion), dimensions={1,2} | broadcast | bytes 135168 | tf_op jit(solution)/shard_map/broadcast_in_dim | solution.py:155
  41.1 3.2 %all-to-all-start.1 = ((f32[32,8,128]{2,1,0:T(8,128)}), f32[32,8,128]{2,1,0:T(8,128)S(1)}, u32[]{:S(2)}, u32[]{:S(2)}) async-start(f32[32,8,128]{2,1,0:T(8,128)} %broadcast_in_dim.153), calls=%async_computation.1 | async-start | bytes 262144 | tf_op jit(solution)/shard_map/all_to_all | solution.py:154
  44.4 0.7 %add_subtract_fusion = f32[192,128]{1,0:T(8,128)} fusion(f32[192,128]{1,0:T(8,128)S(1)} %bitcast.316, f32[192,128]{1,0:T(8,128)S(1)} %copy-done.2, f32[192,128]{1,0:T(8,128)S(1)} %copy-done.1, f32[192,128]{1,0:T(8,128)S(1)} %bitcast.310, f32[192,128]{1,0:T(8,128)S(1)} %get-tuple-element.32, f32[192,128]{1,0:T(8,128)S(1)} %bitcast.299), kind=kLoop, calls=%fused_computation.26 | loop fusion | flops 466944 | bytes 688128 | tf_op jit(solution)/shard_map/sub | solution.py:13
  45.1 7.5 %all-to-all-done.1 = f32[32,8,128]{2,1,0:T(8,128)S(1)} async-done(((f32[32,8,128]{2,1,0:T(8,128)}), f32[32,8,128]{2,1,0:T(8,128)S(1)}, u32[]{:S(2)}, u32[]{:S(2)}) %all-to-all-start.1) | async-done | bytes 131104 | tf_op jit(solution)/shard_map/all_to_all | solution.py:154
  52.6 0.2 slice_reduce_fusion
  52.7 0.1 eq.143
  52.8 0.7 %fusion.7 = pred[32,8]{1,0:T(8,128)(4,1)S(1)} fusion(f32[32,8,128]{2,1,0:T(8,128)S(1)} %all-to-all-done.1, f32[]{:T(128)S(6)} %convert_element_type.37), kind=kLoop, calls=%fused_computation.16 | loop fusion | flops 256 | bytes 1284 | tf_op jit(solution)/shard_map/eq | solution.py:201
  53.5 0.1 eq.142
  53.6 0.1 slice.197
  53.7 0.1 reshape.339
  53.8 0.1 copy.241
  53.8 0.1 copy.212
  53.9 0.2 multiply_reduce_fusion.2
  54.2 0.1 fusion.6
  54.3 0.3 multiply_reduce_fusion
  54.7 0.1 multiply_reduce_fusion.1
  54.8 0.1 multiply_select_fusion
  54.9 0.6 %copy-done.7 = f32[1,8]{1,0:T(1,128)S(1)} copy-done((f32[1,8]{1,0:T(1,128)S(1)}, f32[1,8]{1,0:T(1,128)}, u32[]{:S(2)}) %copy-start.7) | copy-done | bytes 56
  55.5 0.1 fusion.14
  55.7 0.1 multiply_add_fusion.1
  55.7 0.1 stack.94
  55.8 0.1 fusion.16
  56.0 0.1 fusion.18
  56.1 0.1 fusion.20
  56.2 0.1 fusion.22
  56.3 0.1 fusion.24
  56.5 0.1 fusion.26
  56.6 0.1 fusion.28
  56.7 0.2 fusion.8
  57.0 0.6 %stack.95 = f32[8,128]{1,0:T(8,128)} concatenate(f32[1,128]{1,0:T(1,128)S(1)} %get-tuple-element.14, f32[1,128]{1,0:T(1,128)S(1)} %get-tuple-element.13, f32[1,128]{1,0:T(1,128)S(1)} %get-tuple-element.12, f32[1,128]{1,0:T(1,128)S(1)} %get-tuple-element.11, f32[1,128]{1,0:T(1,128)S(1)} %get-tuple-element.10, f32[1,128]{1,0:T(1,128)S(1)} %get-tuple-element.9, ...), dimensions={0} | concatenate | bytes 8192 | tf_op jit(solution)/shard_map/stack | solution.py:24
  (56 shorter events, 0.6 us)
Async XLA Ops:
  0.6 37.2 %copy-start = (f32[8,128,128]{2,1,0:T(8,128)S(1)}, f32[8,128,128]{2,1,0:T(8,128)}, u32[]{:S(2)}) copy-start(f32[8,128,128]{2,1,0:T(8,128)} %param.21) | copy-start | bytes 1572868
  0.7 4.7 %copy-start.1 = (f32[192,128]{1,0:T(8,128)S(1)}, f32[192,128]{1,0:T(8,128)}, u32[]{:S(2)}) copy-start(f32[192,128]{1,0:T(8,128)} %param.17) | copy-start | bytes 294916
  0.7 4.7 %copy-start.3 = (f32[192,128]{1,0:T(8,128)S(1)}, f32[192,128]{1,0:T(8,128)}, u32[]{:S(2)}) copy-start(f32[192,128]{1,0:T(8,128)} %param.16) | copy-start | bytes 294916
  5.4 0.9 %copy-start.2 = (f32[192,128]{1,0:T(8,128)S(1)}, f32[192,128]{1,0:T(8,128)}, u32[]{:S(2)}) copy-start(f32[192,128]{1,0:T(8,128)} %param.18) | copy-start | bytes 294916
  7.3 0.7 %copy-start.9 = (s32[192]{0:T(256)S(1)}, s32[192]{0:T(256)}, u32[]{:S(2)}) copy-start(s32[192]{0:T(256)} %param.19) | copy-start | bytes 2308
  7.5 0.7 %copy-start.8 = (s32[192]{0:T(256)S(1)}, s32[192]{0:T(256)}, u32[]{:S(2)}) copy-start(s32[192]{0:T(256)} %param.20) | copy-start | bytes 2308
  8.9 2.1 %collective-permute-start = (f32[8,2,8,1024]{3,2,1,0:T(8,128)S(1)}, f32[8,2,8,1024]{3,2,1,0:T(8,128)S(1)}, u32[]{:S(2)}, u32[]{:S(2)}) collective-permute-start(f32[8,2,8,1024]{3,2,1,0:T(8,128)S(1)} %dynamic-slice_bitcast_fusion), channel_id=1, source_target_pairs={{1,0},{0,1},{3,2},{2,3},{5,4},{4,5},{7,6},{6,7},{9,8},{8,9},{11,10... | collective-permute-start | bytes 1572872 | tf_op jit(solution)/shard_map/ppermute | solution.py:83
  12.1 7.2 %copy-start.11 = (f32[1,1,128]{2,1,0:T(1,128)S(1)}, f32[1,1,128]{2,1,0:T(1,128)}, u32[]{:S(2)}) copy-start(f32[1,1,128]{2,1,0:T(1,128)} %param.28) | copy-start | bytes 1540
  12.1 8.5 %copy-start.5 = (f32[1,1,128,128]{3,2,1,0:T(8,128)S(1)}, f32[1,1,128,128]{3,2,1,0:T(8,128)}, u32[]{:S(2)}) copy-start(f32[1,1,128,128]{3,2,1,0:T(8,128)} %param.26) | copy-start | bytes 196612
  12.1 22.8 %all-to-all-start = ((f32[32,4,1024]{2,1,0:T(4,128)}), f32[32,4,1024]{2,1,0:T(4,128)S(1)}, u32[]{:S(2)}, u32[]{:S(2)}) async-start(f32[32,4,1024]{2,1,0:T(4,128)} %bitcast_select_fusion), calls=%async_computation | async-start | bytes 1048576 | tf_op jit(solution)/shard_map/all_to_all | solution.py:86
  19.3 0.7 %copy-start.10 = (f32[1,1,128]{2,1,0:T(1,128)S(1)}, f32[1,1,128]{2,1,0:T(1,128)}, u32[]{:S(2)}) copy-start(f32[1,1,128]{2,1,0:T(1,128)} %param.27) | copy-start | bytes 1540
  35.1 2.7 %collective-permute-start.1 = (f32[4,1024]{1,0:T(4,128)S(1)}, f32[4,1024]{1,0:T(4,128)S(1)}, u32[]{:S(2)}, u32[]{:S(2)}) collective-permute-start(f32[4,1024]{1,0:T(4,128)S(1)} %get-tuple-element.4), channel_id=1, source_target_pairs={{1,0},{0,1},{3,2},{2,3},{5,4},{4,5},{7,6},{6,7},{9,8},{8,9},{11,10... | collective-permute-start | bytes 49160 | tf_op jit(solution)/shard_map/ppermute | solution.py:91
  36.5 0.7 %copy-start.12 = (s32[8]{0:T(128)S(1)}, s32[8]{0:T(128)}, u32[]{:S(2)}) copy-start(s32[8]{0:T(128)} %param.25) | copy-start | bytes 100
  37.2 0.7 %copy-start.13 = (s32[8]{0:T(128)S(1)}, s32[8]{0:T(128)}, u32[]{:S(2)}) copy-start(s32[8]{0:T(128)} %param.24) | copy-start | bytes 100
  38.8 0.7 %copy-start.4 = (f32[8,128]{1,0:T(8,128)S(1)}, f32[8,128]{1,0:T(8,128)}, u32[]{:S(2)}) copy-start(f32[8,128]{1,0:T(8,128)} %param.22) | copy-start | bytes 12292
  38.8 0.7 %copy-start.6 = (f32[8,128]{1,0:T(8,128)S(1)}, f32[8,128]{1,0:T(8,128)}, u32[]{:S(2)}) copy-start(f32[8,128]{1,0:T(8,128)} %param.23) | copy-start | bytes 12292
  41.1 11.4 %all-to-all-start.1 = ((f32[32,8,128]{2,1,0:T(8,128)}), f32[32,8,128]{2,1,0:T(8,128)S(1)}, u32[]{:S(2)}, u32[]{:S(2)}) async-start(f32[32,8,128]{2,1,0:T(8,128)} %broadcast_in_dim.153), calls=%async_computation.1 | async-start | bytes 262144 | tf_op jit(solution)/shard_map/all_to_all | solution.py:154
  54.9 0.7 %copy-start.7 = (f32[1,8]{1,0:T(1,128)S(1)}, f32[1,8]{1,0:T(1,128)}, u32[]{:S(2)}) copy-start(f32[1,8]{1,0:T(1,128)} %param.29) | copy-start | bytes 100

commit v9 on v8

--- a/solution.py
+++ b/solution.py
@@ -131,7 +131,12 @@
         precision=lax.Precision.HIGHEST,
     )
     trib_flows = route_series(trib_mixed, trib_keep, trib_prev)
-    outlet = trib_flows[:, :, reaches - 1]
+    exit_mixed = jnp.sum(
+        lateral.reshape(blocks, sub_steps, reaches) * trib_op[:, reaches - 1][:, None, :], axis=2
+    )
+    outlet = route_series(
+        exit_mixed[:, :, None], trib_keep[:, reaches - 1 :], trib_prev[:, reaches - 1 :]
+    )[:, :, 0]
 
     mine = lax.axis_index("band")
     me = lax.axis_index("basin")

time: 58.1 us -> 55.9 us (0.962)
  waiting for transfers between devices: 23.1 us -> 21.2 us
  local copies, waits for them, and re-layouts: 13.2 us -> 12.6 us
    all_to_all x1, waiting for transfers between devices: 14.2 us -> 12.2 us  [pair_exchange(): lax.all_to_all(send.reshape(shards, half, width), ('basin', 'band'), spli...]
    add x1 -> x4, other arithmetic: 0.06 us -> 1.06 us  [route_series(): flow = keep * flow + (1.0 - keep) * mixed[..., sub_step, :]]
    another operation x1 -> x0, other arithmetic: 0.6 us -> none  [route_series(): return jnp.stack(flows, axis=-2)]
    unnamed x29 -> x36, local copies, waits for them, and re-layouts: 4.27 us -> 3.73 us
  transfers between devices with their start and end apart: 4 -> 4, of which waited for: 3 -> 3; matrix products, arithmetic and copies ran while one was open for 6% -> 7% of each run, Pallas kernels for 0% -> 0%
where the time goes in v9:
time: 55.9 us; the launch traced here: 55.5 us
  waiting for transfers between devices  21.2 us (38%)
  local copies, waits for them, and re-layouts  12.6 us (23%)
  starting transfers between devices  11 us (20%)
  other arithmetic  7.86 us (14%)
  matrix products  1.79 us (3%)
  between operations  1.09 us (2%)
    all_to_all x1, waiting for transfers between devices, pair_exchange(): lax.all_to_all(send.reshape(shards, half, width), ('basin', 'band'), spli...  12.2 us
    all_to_all x1, waiting for transfers between devices, local(): lax.all_to_all(jnp.broadcast_to(tile[None], (shards,) + tile.shape), grid...  7.58 us
    all_to_all x1, starting transfers between devices, pair_exchange(): lax.all_to_all(send.reshape(shards, half, width), ('basin', 'band'), spli...  7.22 us
    slice x1, local copies, waits for them, and re-layouts, land_update(): rain_now = precip[:, sub_step]  4.69 us
    unnamed x36, local copies, waits for them, and re-layouts  3.73 us
    all_to_all x1, starting transfers between devices, local(): lax.all_to_all(jnp.broadcast_to(tile[None], (shards,) + tile.shape), grid...  3.15 us
    ppermute x1, waiting for transfers between devices, pair_exchange(): chip_sum = keep_side + lax.ppermute(give_side, 'band', swap)  1.42 us
    select_n x1, other arithmetic, local(): tile = tile + jnp.where(lane == sub_steps + offset, value, 0.0)  1.3 us
  transfers between devices with their start and end apart: 4, of which 3 were waited for; matrix products, arithmetic and copies ran while one was open for 7% of the time, Pallas kernels for 0%

profile of v9, /device:TPU:0, one launch (start us, length us, event | category | flops | bytes accessed | tf_op | source)
XLA Modules:
  0.0 55.5 jit_solution(17319205498812797583)
XLA Ops:
  0.7 4.7 %fusion.81 = (f32[192,1,128]{2,1,0:T(1,128)S(1)}, f32[192,1,128]{2,1,0:T(1,128)S(1)}, f32[192,1,128]{2,1,0:T(1,128)S(1)}, f32[192,1,128]{2,1,0:T(1,128)S(1)}, f3...) fusion(f32[192,8,128]{2,1,0:T(8,128)} %param.15), kind=kLoop, calls=%fused_computation.201 | loop fusion | bytes 1572864 | tf_op jit(solution)/shard_map/slice | solution.py:11
  5.4 0.9 %copy-done.1 = f32[192,128]{1,0:T(8,128)S(1)} copy-done((f32[192,128]{1,0:T(8,128)S(1)}, f32[192,128]{1,0:T(8,128)}, u32[]{:S(2)}) %copy-start.1) | copy-done | bytes 98328
  6.3 0.1 bitcast_dynamic-update-slice_fusion.5
  6.4 0.1 bitcast_dynamic-update-slice_fusion.4
  6.6 0.1 bitcast_dynamic-update-slice_fusion.2
  6.7 0.1 bitcast_dynamic-update-slice_fusion
  6.8 0.5 copy.216
  7.3 0.1 reshape.341
  7.5 0.5 copy-done.9
  8.0 0.2 copy-done.8
  8.1 0.7 %fusion = f32[8,2,2,8,1024]{4,3,2,1,0:T(8,128)S(1)} fusion(f32[192,1024,1,1,1]{1,0,2,3,4:T(8,128)S(1)} %reshape.341, s32[8,2,2,8]{3,2,1,0:T(2,128)S(1)} %multiply_add_fusion, s32[192]{0:T(256)S(1)} %multiply_add_fusion.10), kind=kOutput, calls=%fused_computation.1 | convolution fusion | flops 604028928 | bytes 1836800 | tf_op jit(solution)/shard_map/dot_general | solution.py:51
  8.9 0.5 collective-permute-start
  9.4 0.1 broadcast_in_dim.141
  9.5 1.4 %collective-permute-done = f32[8,2,8,1024]{3,2,1,0:T(8,128)S(1)} collective-permute-done((f32[8,2,8,1024]{3,2,1,0:T(8,128)S(1)}, f32[8,2,8,1024]{3,2,1,0:T(8,128)S(1)}, u32[]{:S(2)}, u32[]{:S(2)}) %collective-permute-start) | collective-permute-done | bytes 524320 | tf_op jit(solution)/shard_map/ppermute | solution.py:83
  10.9 0.1 bitcast_add_fusion
  11.0 0.1 fusion.82
  11.1 0.9 %bitcast_select_fusion = f32[32,4,1024]{2,1,0:T(4,128)} fusion(f32[8,2,4,1024]{3,2,1,0:T(4,128)S(1)} %get-tuple-element.48, f32[8,2,4,1024]{3,2,1,0:T(4,128)S(1)} %get-tuple-element.47, pred[32]{0:T(512)(128)(4,1)S(1)} %broadcast_in_dim.141), kind=kLoop, calls=%fused_computation.3 | loop fusion | flops 131072 | bytes 1048608 | tf_op jit(solution)/shard_map/jit(_where)/select_n | solution.py:85
  12.1 7.2 %all-to-all-start = ((f32[32,4,1024]{2,1,0:T(4,128)}), f32[32,4,1024]{2,1,0:T(4,128)S(1)}, u32[]{:S(2)}, u32[]{:S(2)}) async-start(f32[32,4,1024]{2,1,0:T(4,128)} %bitcast_select_fusion), calls=%async_computation | async-start | bytes 1048576 | tf_op jit(solution)/shard_map/all_to_all | solution.py:86
  19.3 0.6 %slice.198 = f32[1,1,1]{2,1,0:T(1,128)} slice(f32[1,1,128]{2,1,0:T(1,128)S(1)} %copy-done.11), slice={[0:1], [0:1], [127:128]} | slice | bytes 8 | tf_op jit(solution)/shard_map/slice | solution.py:151
  20.0 0.6 %slice.197 = f32[1,1,1]{2,1,0:T(1,128)} slice(f32[1,1,128]{2,1,0:T(1,128)S(1)} %copy-done.10), slice={[0:1], [0:1], [127:128]} | slice | bytes 8 | tf_op jit(solution)/shard_map/slice | solution.py:150
  20.6 1.3 %compare_select_fusion = (f32[128]{0:T(128)S(1)}, f32[128]{0:T(128)S(1)}) fusion(f32[]{:T(128)} %bitcast.43, f32[]{:T(128)} %bitcast.42), kind=kLoop, calls=%fused_computation.141 | loop fusion | flops 512 | bytes 1032 | tf_op jit(solution)/shard_map/jit(_where)/select_n | solution.py:154
  21.9 0.7 %add_subtract_fusion = f32[192,128]{1,0:T(8,128)} fusion(f32[192,128]{1,0:T(8,128)S(1)} %bitcast.372, f32[192,128]{1,0:T(8,128)S(1)} %copy-done.1, f32[192,128]{1,0:T(8,128)S(1)} %copy-done, f32[192,128]{1,0:T(8,128)S(1)} %bitcast.366, f32[192,128]{1,0:T(8,128)S(1)} %get-tuple-element.36, f32[192,128]{1,0:T(8,128)S(1)} %bitcast.355), kind=kLoop, calls=%fused_computation.26 | loop fusion | flops 466944 | bytes 688128 | tf_op jit(solution)/shard_map/sub | solution.py:13
  22.6 12.2 %all-to-all-done = f32[32,4,1024]{2,1,0:T(4,128)S(1)} async-done(((f32[32,4,1024]{2,1,0:T(4,128)}), f32[32,4,1024]{2,1,0:T(4,128)S(1)}, u32[]{:S(2)}, u32[]{:S(2)}) %all-to-all-start) | async-done | bytes 524320 | tf_op jit(solution)/shard_map/all_to_all | solution.py:86
  34.8 0.3 select_reduce_fusion.1
  35.1 0.1 collective-permute-start.1
  35.2 0.1 reshape_squeeze.4
  35.3 0.6 %copy-done.12 = s32[8]{0:T(128)S(1)} copy-done((s32[8]{0:T(128)S(1)}, s32[8]{0:T(128)}, u32[]{:S(2)}) %copy-start.12) | copy-done | bytes 56
  36.0 0.7 %copy-done.13 = s32[8]{0:T(128)S(1)} copy-done((s32[8]{0:T(128)S(1)}, s32[8]{0:T(128)}, u32[]{:S(2)}) %copy-start.13) | copy-done | bytes 56
  36.7 0.9 %fusion.10 = f32[8,8,128]{2,1,0:T(8,128)S(1)} fusion(f32[8,128,128]{2,1,0:T(8,128)S(1)} %copy-done.3, f32[1,8,8,128]{3,1,2,0:T(8,128)S(1)} %maximum_bitcast_fusion), kind=kOutput, calls=%fused_computation.52 | convolution fusion | flops 12582912 | bytes 589824 | tf_op jit(solution)/shard_map/brc,btc->btr/dot_general | solution.py:127
  37.6 0.1 fusion.12
  37.7 0.1 fusion.33
  37.8 0.3 fusion.32
  38.2 0.1 copy.234
  38.3 0.1 pad_add_fusion
  38.3 0.6 %broadcast_in_dim.157 = f32[32,8,128]{2,1,0:T(8,128)} broadcast(f32[8,128]{1,0:T(8,128)S(1)} %pad_add_fusion), dimensions={1,2} | broadcast | bytes 135168 | tf_op jit(solution)/shard_map/broadcast_in_dim | solution.py:160
  39.0 3.2 %all-to-all-start.1 = ((f32[32,8,128]{2,1,0:T(8,128)}), f32[32,8,128]{2,1,0:T(8,128)S(1)}, u32[]{:S(2)}, u32[]{:S(2)}) async-start(f32[32,8,128]{2,1,0:T(8,128)} %broadcast_in_dim.157), calls=%async_computation.1 | async-start | bytes 262144 | tf_op jit(solution)/shard_map/all_to_all | solution.py:159
  42.2 0.6 %multiply_add_fusion.9 = f32[8,128]{1,0:T(8,128)} fusion(f32[8,128]{1,0:T(8,128)S(1)} %bitcast.386, f32[8,128]{1,0:T(8,128)S(1)} %copy-done.5, f32[8,128]{1,0:T(8,128)S(1)} %bitcast.387, f32[8,128]{1,0:T(8,128)S(1)} %bitcast.385, f32[8,128]{1,0:T(8,128)S(1)} %bitcast.384, f32[8,128]{1,0:T(8,128)S(1)} %bitcast.383, f32[8,128]{1,0:T(8,128)S(1)} %bitcast.382, ...), kind=kLoop, calls=%fused_computation.119 | loop fusion | flops 25600 | bytes 45056 | tf_op jit(solution)/shard_map/add | solution.py:22
  42.8 7.6 %all-to-all-done.1 = f32[32,8,128]{2,1,0:T(8,128)S(1)} async-done(((f32[32,8,128]{2,1,0:T(8,128)}), f32[32,8,128]{2,1,0:T(8,128)S(1)}, u32[]{:S(2)}, u32[]{:S(2)}) %all-to-all-start.1) | async-done | bytes 131104 | tf_op jit(solution)/shard_map/all_to_all | solution.py:159
  50.4 0.2 slice_reduce_fusion
  50.6 0.1 eq.143
  50.6 0.7 %fusion.7 = pred[32,8]{1,0:T(8,128)(4,1)S(1)} fusion(f32[32,8,128]{2,1,0:T(8,128)S(1)} %all-to-all-done.1, f32[]{:T(128)S(6)} %convert_element_type.37), kind=kLoop, calls=%fused_computation.16 | loop fusion | flops 256 | bytes 1284 | tf_op jit(solution)/shard_map/eq | solution.py:206
  51.3 0.1 eq.142
  51.4 0.1 slice.236
  51.5 0.1 reshape.340
  51.6 0.1 copy.265
  51.7 0.1 copy.236
  51.8 0.2 multiply_reduce_fusion.2
  52.0 0.1 fusion.6
  52.2 0.3 multiply_reduce_fusion
  52.5 0.1 multiply_reduce_fusion.1
  52.6 0.1 multiply_select_fusion
  52.7 0.6 %copy-done.7 = f32[1,8]{1,0:T(1,128)S(1)} copy-done((f32[1,8]{1,0:T(1,128)S(1)}, f32[1,8]{1,0:T(1,128)}, u32[]{:S(2)}) %copy-start.7) | copy-done | bytes 56
  53.4 0.1 fusion.15
  53.5 0.1 multiply_add_fusion.1
  53.6 0.1 stack.94
  53.7 0.1 fusion.17
  53.8 0.1 fusion.19
  53.9 0.1 fusion.21
  54.0 0.1 fusion.23
  54.2 0.1 fusion.25
  54.3 0.1 fusion.27
  54.4 0.1 fusion.29
  54.6 0.2 fusion.8
  54.9 0.6 %stack.95 = f32[8,128]{1,0:T(8,128)} concatenate(f32[1,128]{1,0:T(1,128)S(1)} %get-tuple-element.22, f32[1,128]{1,0:T(1,128)S(1)} %get-tuple-element.21, f32[1,128]{1,0:T(1,128)S(1)} %get-tuple-element.20, f32[1,128]{1,0:T(1,128)S(1)} %get-tuple-element.19, f32[1,128]{1,0:T(1,128)S(1)} %get-tuple-element.18, f32[1,128]{1,0:T(1,128)S(1)} %get-tuple-element.17, ...), dimensions={0} | concatenate | bytes 8192 | tf_op jit(solution)/shard_map/stack | solution.py:24
  (60 shorter events, 0.7 us)
Async XLA Ops:
  0.7 4.7 %copy-start = (f32[192,128]{1,0:T(8,128)S(1)}, f32[192,128]{1,0:T(8,128)}, u32[]{:S(2)}) copy-start(f32[192,128]{1,0:T(8,128)} %param.17) | copy-start | bytes 294916
  0.7 4.7 %copy-start.2 = (f32[192,128]{1,0:T(8,128)S(1)}, f32[192,128]{1,0:T(8,128)}, u32[]{:S(2)}) copy-start(f32[192,128]{1,0:T(8,128)} %param.16) | copy-start | bytes 294916
  5.4 0.9 %copy-start.1 = (f32[192,128]{1,0:T(8,128)S(1)}, f32[192,128]{1,0:T(8,128)}, u32[]{:S(2)}) copy-start(f32[192,128]{1,0:T(8,128)} %param.18) | copy-start | bytes 294916
  7.3 0.7 %copy-start.9 = (s32[192]{0:T(256)S(1)}, s32[192]{0:T(256)}, u32[]{:S(2)}) copy-start(s32[192]{0:T(256)} %param.19) | copy-start | bytes 2308
  7.4 0.7 %copy-start.8 = (s32[192]{0:T(256)S(1)}, s32[192]{0:T(256)}, u32[]{:S(2)}) copy-start(s32[192]{0:T(256)} %param.20) | copy-start | bytes 2308
  8.9 2.1 %collective-permute-start = (f32[8,2,8,1024]{3,2,1,0:T(8,128)S(1)}, f32[8,2,8,1024]{3,2,1,0:T(8,128)S(1)}, u32[]{:S(2)}, u32[]{:S(2)}) collective-permute-start(f32[8,2,8,1024]{3,2,1,0:T(8,128)S(1)} %dynamic-slice_bitcast_fusion), channel_id=1, source_target_pairs={{1,0},{0,1},{3,2},{2,3},{5,4},{4,5},{7,6},{6,7},{9,8},{8,9},{11,10... | collective-permute-start | bytes 1572872 | tf_op jit(solution)/shard_map/ppermute | solution.py:83
  12.1 7.2 %copy-start.11 = (f32[1,1,128]{2,1,0:T(1,128)S(1)}, f32[1,1,128]{2,1,0:T(1,128)}, u32[]{:S(2)}) copy-start(f32[1,1,128]{2,1,0:T(1,128)} %param.28) | copy-start | bytes 1540
  12.1 9.8 %copy-start.4 = (f32[1,1,128,128]{3,2,1,0:T(8,128)S(1)}, f32[1,1,128,128]{3,2,1,0:T(8,128)}, u32[]{:S(2)}) copy-start(f32[1,1,128,128]{3,2,1,0:T(8,128)} %param.26) | copy-start | bytes 196612
  12.1 22.8 %all-to-all-start = ((f32[32,4,1024]{2,1,0:T(4,128)}), f32[32,4,1024]{2,1,0:T(4,128)S(1)}, u32[]{:S(2)}, u32[]{:S(2)}) async-start(f32[32,4,1024]{2,1,0:T(4,128)} %bitcast_select_fusion), calls=%async_computation | async-start | bytes 1048576 | tf_op jit(solution)/shard_map/all_to_all | solution.py:86
  19.3 0.7 %copy-start.10 = (f32[1,1,128]{2,1,0:T(1,128)S(1)}, f32[1,1,128]{2,1,0:T(1,128)}, u32[]{:S(2)}) copy-start(f32[1,1,128]{2,1,0:T(1,128)} %param.27) | copy-start | bytes 1540
  21.9 13.4 %copy-start.3 = (f32[8,128,128]{2,1,0:T(8,128)S(1)}, f32[8,128,128]{2,1,0:T(8,128)}, u32[]{:S(2)}) copy-start(f32[8,128,128]{2,1,0:T(8,128)} %param.21) | copy-start | bytes 1572868
  35.1 1.5 %collective-permute-start.1 = (f32[4,1024]{1,0:T(4,128)S(1)}, f32[4,1024]{1,0:T(4,128)S(1)}, u32[]{:S(2)}, u32[]{:S(2)}) collective-permute-start(f32[4,1024]{1,0:T(4,128)S(1)} %get-tuple-element.4), channel_id=1, source_target_pairs={{1,0},{0,1},{3,2},{2,3},{5,4},{4,5},{7,6},{6,7},{9,8},{8,9},{11,10... | collective-permute-start | bytes 49160 | tf_op jit(solution)/shard_map/ppermute | solution.py:91
  35.3 0.7 %copy-start.12 = (s32[8]{0:T(128)S(1)}, s32[8]{0:T(128)}, u32[]{:S(2)}) copy-start(s32[8]{0:T(128)} %param.25) | copy-start | bytes 100
  36.0 0.7 %copy-start.13 = (s32[8]{0:T(128)S(1)}, s32[8]{0:T(128)}, u32[]{:S(2)}) copy-start(s32[8]{0:T(128)} %param.24) | copy-start | bytes 100
  36.7 1.0 %copy-start.5 = (f32[8,128]{1,0:T(8,128)S(1)}, f32[8,128]{1,0:T(8,128)}, u32[]{:S(2)}) copy-start(f32[8,128]{1,0:T(8,128)} %param.22) | copy-start | bytes 12292
  36.7 1.0 %copy-start.6 = (f32[8,128]{1,0:T(8,128)S(1)}, f32[8,128]{1,0:T(8,128)}, u32[]{:S(2)}) copy-start(f32[8,128]{1,0:T(8,128)} %param.23) | copy-start | bytes 12292
  39.0 11.4 %all-to-all-start.1 = ((f32[32,8,128]{2,1,0:T(8,128)}), f32[32,8,128]{2,1,0:T(8,128)S(1)}, u32[]{:S(2)}, u32[]{:S(2)}) async-start(f32[32,8,128]{2,1,0:T(8,128)} %broadcast_in_dim.157), calls=%async_computation.1 | async-start | bytes 262144 | tf_op jit(solution)/shard_map/all_to_all | solution.py:159
  52.7 0.7 %copy-start.7 = (f32[1,8]{1,0:T(1,128)S(1)}, f32[1,8]{1,0:T(1,128)}, u32[]{:S(2)}) copy-start(f32[1,8]{1,0:T(1,128)} %param.29) | copy-start | bytes 100

commit v10 on v9

--- a/solution.py
+++ b/solution.py
@@ -143,19 +143,20 @@
     spread_lanes = reaches // blocks
     if reaches % blocks == 0 and sub_steps + 4 + spread_lanes <= reaches:
         lane = lax.broadcasted_iota(jnp.int32, (blocks, reaches), 1)
-        tile = jnp.pad(outlet, ((0, 0), (0, reaches - sub_steps)))
         columns = (
             trib_river.astype(jnp.float32)[:, None],
             trib_reach.astype(jnp.float32)[:, None],
             keep_main[reaches - 1 :][None, :],
             prev_main[reaches - 1 :][None, :],
         )
+        spread_row = operator[reaches - 1].reshape(blocks, spread_lanes)
+        static_tile = jnp.pad(
+            spread_row, ((0, 0), (sub_steps + 4, reaches - sub_steps - 4 - spread_lanes))
+        )
         for offset, value in enumerate(columns):
-            tile = tile + jnp.where(lane == sub_steps + offset, value, 0.0)
-        spread_row = operator[reaches - 1].reshape(blocks, spread_lanes)
-        tile = tile + jnp.pad(
-            spread_row, ((0, 0), (sub_steps + 4, reaches - sub_steps - 4 - spread_lanes))
-        )
+            static_tile = static_tile + jnp.where(lane == sub_steps + offset, value, 0.0)
+        static_tile = lax.optimization_barrier(static_tile)
+        tile = jnp.pad(outlet, ((0, 0), (0, reaches - sub_steps))) + static_tile
         every = lax.all_to_all(
             jnp.broadcast_to(tile[None], (shards,) + tile.shape), grid, split_axis=0, concat_axis=0, tiled=True
         )

time: 55.9 us -> 55.4 us (level)
    all_to_all x1, waiting for transfers between devices: 12.2 us -> 10.8 us  [pair_exchange(): lax.all_to_all(send.reshape(shards, half, width), ('basin', 'band'), spli...]
    ppermute x1, waiting for transfers between devices: 0.01 us -> 1.11 us  [pair_exchange(): return jnp.concatenate([same, lax.ppermute(other, 'band', swap)], axis=0)]
  transfers between devices with their start and end apart: 4 -> 4, of which waited for: 3 -> 4; matrix products, arithmetic and copies ran while one was open for 7% -> 8% of each run, Pallas kernels for 0% -> 0%
where the time goes in v10:
time: 55.4 us; the launch traced here: 55.1 us
  waiting for transfers between devices  20.9 us (38%)
  local copies, waits for them, and re-layouts  12.6 us (23%)
  starting transfers between devices  10.9 us (20%)
  other arithmetic  7.87 us (14%)
  matrix products  1.79 us (3%)
  between operations  1.08 us (2%)
    all_to_all x1, waiting for transfers between devices, pair_exchange(): lax.all_to_all(send.reshape(shards, half, width), ('basin', 'band'), spli...  10.8 us
    all_to_all x1, waiting for transfers between devices, local(): lax.all_to_all(jnp.broadcast_to(tile[None], (shards,) + tile.shape), grid...  7.58 us
    all_to_all x1, starting transfers between devices, pair_exchange(): lax.all_to_all(send.reshape(shards, half, width), ('basin', 'band'), spli...  7.22 us
    slice x1, local copies, waits for them, and re-layouts, land_update(): rain_now = precip[:, sub_step]  4.69 us
    unnamed x36, local copies, waits for them, and re-layouts  3.73 us
    all_to_all x1, starting transfers between devices, local(): lax.all_to_all(jnp.broadcast_to(tile[None], (shards,) + tile.shape), grid...  3.08 us
    ppermute x1, waiting for transfers between devices, pair_exchange(): chip_sum = keep_side + lax.ppermute(give_side, 'band', swap)  1.42 us
    select_n x1, other arithmetic, local(): jnp.where(lane == sub_steps + offset, value, 0.0)  1.3 us
  transfers between devices with their start and end apart: 4, of which 4 were waited for; matrix products, arithmetic and copies ran while one was open for 8% of the time, Pallas kernels for 0%

profile of v10, /device:TPU:0, one launch (start us, length us, event | category | flops | bytes accessed | tf_op | source)
XLA Modules:
  0.0 55.1 jit_solution(9195027195104507150)
XLA Ops:
  0.7 4.7 %fusion.81 = (f32[192,1,128]{2,1,0:T(1,128)S(1)}, f32[192,1,128]{2,1,0:T(1,128)S(1)}, f32[192,1,128]{2,1,0:T(1,128)S(1)}, f32[192,1,128]{2,1,0:T(1,128)S(1)}, f3...) fusion(f32[192,8,128]{2,1,0:T(8,128)} %param.15), kind=kLoop, calls=%fused_computation.202 | loop fusion | bytes 1572864 | tf_op jit(solution)/shard_map/slice | solution.py:11
  5.4 0.9 %copy-done.1 = f32[192,128]{1,0:T(8,128)S(1)} copy-done((f32[192,128]{1,0:T(8,128)S(1)}, f32[192,128]{1,0:T(8,128)}, u32[]{:S(2)}) %copy-start.1) | copy-done | bytes 98328
  6.3 0.1 bitcast_dynamic-update-slice_fusion.5
  6.4 0.1 bitcast_dynamic-update-slice_fusion.4
  6.6 0.1 bitcast_dynamic-update-slice_fusion.2
  6.7 0.1 bitcast_dynamic-update-slice_fusion
  6.8 0.5 copy.216
  7.3 0.1 reshape.341
  7.5 0.5 copy-done.9
  8.0 0.2 copy-done.8
  8.1 0.7 %fusion = f32[8,2,2,8,1024]{4,3,2,1,0:T(8,128)S(1)} fusion(f32[192,1024,1,1,1]{1,0,2,3,4:T(8,128)S(1)} %reshape.341, s32[8,2,2,8]{3,2,1,0:T(2,128)S(1)} %multiply_add_fusion, s32[192]{0:T(256)S(1)} %multiply_add_fusion.10), kind=kOutput, calls=%fused_computation.1 | convolution fusion | flops 604028928 | bytes 1836800 | tf_op jit(solution)/shard_map/dot_general | solution.py:51
  8.9 0.5 collective-permute-start
  9.4 0.1 broadcast_in_dim.141
  9.5 1.4 %collective-permute-done = f32[8,2,8,1024]{3,2,1,0:T(8,128)S(1)} collective-permute-done((f32[8,2,8,1024]{3,2,1,0:T(8,128)S(1)}, f32[8,2,8,1024]{3,2,1,0:T(8,128)S(1)}, u32[]{:S(2)}, u32[]{:S(2)}) %collective-permute-start) | collective-permute-done | bytes 524320 | tf_op jit(solution)/shard_map/ppermute | solution.py:83
  11.0 0.1 fusion.82
  11.1 0.9 %bitcast_select_fusion = f32[32,4,1024]{2,1,0:T(4,128)} fusion(f32[8,2,4,1024]{3,2,1,0:T(4,128)S(1)} %get-tuple-element.48, f32[8,2,4,1024]{3,2,1,0:T(4,128)S(1)} %get-tuple-element.47, pred[32]{0:T(512)(128)(4,1)S(1)} %broadcast_in_dim.141), kind=kLoop, calls=%fused_computation.3 | loop fusion | flops 131072 | bytes 1048608 | tf_op jit(solution)/shard_map/jit(_where)/select_n | solution.py:85
  12.1 7.2 %all-to-all-start = ((f32[32,4,1024]{2,1,0:T(4,128)}), f32[32,4,1024]{2,1,0:T(4,128)S(1)}, u32[]{:S(2)}, u32[]{:S(2)}) async-start(f32[32,4,1024]{2,1,0:T(4,128)} %bitcast_select_fusion), calls=%async_computation | async-start | bytes 1048576 | tf_op jit(solution)/shard_map/all_to_all | solution.py:86
  19.3 0.1 reshape_squeeze.4
  19.4 0.6 %copy-done.11 = f32[1,1,128]{2,1,0:T(1,128)S(1)} copy-done((f32[1,1,128]{2,1,0:T(1,128)S(1)}, f32[1,1,128]{2,1,0:T(1,128)}, u32[]{:S(2)}) %copy-start.11) | copy-done | bytes 536
  20.0 0.6 %slice.199 = f32[1,1,1]{2,1,0:T(1,128)} slice(f32[1,1,128]{2,1,0:T(1,128)S(1)} %copy-done.11), slice={[0:1], [0:1], [127:128]} | slice | bytes 8 | tf_op jit(solution)/shard_map/slice | solution.py:150
  20.6 0.1 copy-done.10
  20.6 0.6 %slice.198 = f32[1,1,1]{2,1,0:T(1,128)} slice(f32[1,1,128]{2,1,0:T(1,128)S(1)} %copy-done.10), slice={[0:1], [0:1], [127:128]} | slice | bytes 8 | tf_op jit(solution)/shard_map/slice | solution.py:149
  21.2 0.1 copy-done.12
  21.3 0.7 %copy-done.13 = s32[8]{0:T(128)S(1)} copy-done((s32[8]{0:T(128)S(1)}, s32[8]{0:T(128)}, u32[]{:S(2)}) %copy-start.13) | copy-done | bytes 56
  22.0 1.3 %compare_select_fusion = (f32[128]{0:T(128)S(1)}, f32[128]{0:T(128)S(1)}) fusion(f32[]{:T(128)} %bitcast.43, f32[]{:T(128)} %bitcast.42), kind=kLoop, calls=%fused_computation.142 | loop fusion | flops 512 | bytes 1032 | tf_op jit(solution)/shard_map/jit(_where)/select_n | solution.py:157
  23.3 0.1 add_add_fusion
  23.4 0.7 %add_subtract_fusion = f32[192,128]{1,0:T(8,128)} fusion(f32[192,128]{1,0:T(8,128)S(1)} %bitcast.372, f32[192,128]{1,0:T(8,128)S(1)} %copy-done.1, f32[192,128]{1,0:T(8,128)S(1)} %copy-done, f32[192,128]{1,0:T(8,128)S(1)} %bitcast.366, f32[192,128]{1,0:T(8,128)S(1)} %get-tuple-element.36, f32[192,128]{1,0:T(8,128)S(1)} %bitcast.355), kind=kLoop, calls=%fused_computation.26 | loop fusion | flops 466944 | bytes 688128 | tf_op jit(solution)/shard_map/sub | solution.py:13
  24.1 10.8 %all-to-all-done = f32[32,4,1024]{2,1,0:T(4,128)S(1)} async-done(((f32[32,4,1024]{2,1,0:T(4,128)}), f32[32,4,1024]{2,1,0:T(4,128)S(1)}, u32[]{:S(2)}, u32[]{:S(2)}) %all-to-all-start) | async-done | bytes 524320 | tf_op jit(solution)/shard_map/all_to_all | solution.py:86
  34.8 0.3 select_reduce_fusion.1
  35.3 1.1 %collective-permute-done.1 = f32[4,1024]{1,0:T(4,128)S(1)} collective-permute-done((f32[4,1024]{1,0:T(4,128)S(1)}, f32[4,1024]{1,0:T(4,128)S(1)}, u32[]{:S(2)}, u32[]{:S(2)}) %collective-permute-start.1) | collective-permute-done | bytes 16416 | tf_op jit(solution)/shard_map/ppermute | solution.py:91
  36.4 0.9 %fusion.10 = f32[8,8,128]{2,1,0:T(8,128)S(1)} fusion(f32[8,128,128]{2,1,0:T(8,128)S(1)} %copy-done.3, f32[1,8,8,128]{3,1,2,0:T(8,128)S(1)} %maximum_bitcast_fusion), kind=kOutput, calls=%fused_computation.52 | convolution fusion | flops 12582912 | bytes 589824 | tf_op jit(solution)/shard_map/brc,btc->btr/dot_general | solution.py:127
  37.3 0.1 fusion.12
  37.4 0.1 fusion.33
  37.5 0.3 fusion.32
  38.0 0.6 %broadcast_in_dim.157 = f32[32,8,128]{2,1,0:T(8,128)} broadcast(f32[8,128]{1,0:T(8,128)S(1)} %pad_add_fusion), dimensions={1,2} | broadcast | bytes 135168 | tf_op jit(solution)/shard_map/broadcast_in_dim | solution.py:161
  38.7 3.1 %all-to-all-start.1 = ((f32[32,8,128]{2,1,0:T(8,128)}), f32[32,8,128]{2,1,0:T(8,128)S(1)}, u32[]{:S(2)}, u32[]{:S(2)}) async-start(f32[32,8,128]{2,1,0:T(8,128)} %broadcast_in_dim.157), calls=%async_computation.1 | async-start | bytes 262144 | tf_op jit(solution)/shard_map/all_to_all | solution.py:160
  41.8 0.6 %multiply_add_fusion.9 = f32[8,128]{1,0:T(8,128)} fusion(f32[8,128]{1,0:T(8,128)S(1)} %bitcast.386, f32[8,128]{1,0:T(8,128)S(1)} %copy-done.5, f32[8,128]{1,0:T(8,128)S(1)} %bitcast.387, f32[8,128]{1,0:T(8,128)S(1)} %bitcast.385, f32[8,128]{1,0:T(8,128)S(1)} %bitcast.384, f32[8,128]{1,0:T(8,128)S(1)} %bitcast.383, f32[8,128]{1,0:T(8,128)S(1)} %bitcast.382, ...), kind=kLoop, calls=%fused_computation.120 | loop fusion | flops 25600 | bytes 45056 | tf_op jit(solution)/shard_map/add | solution.py:22
  42.4 7.6 %all-to-all-done.1 = f32[32,8,128]{2,1,0:T(8,128)S(1)} async-done(((f32[32,8,128]{2,1,0:T(8,128)}), f32[32,8,128]{2,1,0:T(8,128)S(1)}, u32[]{:S(2)}, u32[]{:S(2)}) %all-to-all-start.1) | async-done | bytes 131104 | tf_op jit(solution)/shard_map/all_to_all | solution.py:160
  50.0 0.2 slice_reduce_fusion
  50.2 0.1 eq.143
  50.2 0.7 %fusion.7 = pred[32,8]{1,0:T(8,128)(4,1)S(1)} fusion(f32[32,8,128]{2,1,0:T(8,128)S(1)} %all-to-all-done.1, f32[]{:T(128)S(6)} %convert_element_type.37), kind=kLoop, calls=%fused_computation.16 | loop fusion | flops 256 | bytes 1284 | tf_op jit(solution)/shard_map/eq | solution.py:207
  50.9 0.1 eq.142
  51.0 0.1 slice.236
  51.1 0.1 reshape.340
  51.2 0.1 copy.265
  51.3 0.1 copy.236
  51.4 0.2 multiply_reduce_fusion.2
  51.6 0.1 fusion.6
  51.7 0.3 multiply_reduce_fusion
  52.1 0.1 multiply_reduce_fusion.1
  52.2 0.1 multiply_select_fusion
  52.3 0.6 %copy-done.7 = f32[1,8]{1,0:T(1,128)S(1)} copy-done((f32[1,8]{1,0:T(1,128)S(1)}, f32[1,8]{1,0:T(1,128)}, u32[]{:S(2)}) %copy-start.7) | copy-done | bytes 56
  53.0 0.1 fusion.15
  53.1 0.1 multiply_add_fusion.1
  53.2 0.1 stack.94
  53.2 0.1 fusion.17
  53.4 0.1 fusion.19
  53.5 0.1 fusion.21
  53.6 0.1 fusion.23
  53.8 0.1 fusion.25
  53.9 0.1 fusion.27
  54.0 0.1 fusion.29
  54.2 0.2 fusion.8
  54.4 0.6 %stack.95 = f32[8,128]{1,0:T(8,128)} concatenate(f32[1,128]{1,0:T(1,128)S(1)} %get-tuple-element.22, f32[1,128]{1,0:T(1,128)S(1)} %get-tuple-element.21, f32[1,128]{1,0:T(1,128)S(1)} %get-tuple-element.20, f32[1,128]{1,0:T(1,128)S(1)} %get-tuple-element.19, f32[1,128]{1,0:T(1,128)S(1)} %get-tuple-element.18, f32[1,128]{1,0:T(1,128)S(1)} %get-tuple-element.17, ...), dimensions={0} | concatenate | bytes 8192 | tf_op jit(solution)/shard_map/stack | solution.py:24
  (61 shorter events, 0.8 us)
Async XLA Ops:
  0.7 4.7 %copy-start = (f32[192,128]{1,0:T(8,128)S(1)}, f32[192,128]{1,0:T(8,128)}, u32[]{:S(2)}) copy-start(f32[192,128]{1,0:T(8,128)} %param.17) | copy-start | bytes 294916
  0.7 4.7 %copy-start.2 = (f32[192,128]{1,0:T(8,128)S(1)}, f32[192,128]{1,0:T(8,128)}, u32[]{:S(2)}) copy-start(f32[192,128]{1,0:T(8,128)} %param.16) | copy-start | bytes 294916
  5.4 0.9 %copy-start.1 = (f32[192,128]{1,0:T(8,128)S(1)}, f32[192,128]{1,0:T(8,128)}, u32[]{:S(2)}) copy-start(f32[192,128]{1,0:T(8,128)} %param.18) | copy-start | bytes 294916
  7.3 0.7 %copy-start.9 = (s32[192]{0:T(256)S(1)}, s32[192]{0:T(256)}, u32[]{:S(2)}) copy-start(s32[192]{0:T(256)} %param.19) | copy-start | bytes 2308
  7.4 0.7 %copy-start.8 = (s32[192]{0:T(256)S(1)}, s32[192]{0:T(256)}, u32[]{:S(2)}) copy-start(s32[192]{0:T(256)} %param.20) | copy-start | bytes 2308
  8.9 2.1 %collective-permute-start = (f32[8,2,8,1024]{3,2,1,0:T(8,128)S(1)}, f32[8,2,8,1024]{3,2,1,0:T(8,128)S(1)}, u32[]{:S(2)}, u32[]{:S(2)}) collective-permute-start(f32[8,2,8,1024]{3,2,1,0:T(8,128)S(1)} %dynamic-slice_bitcast_fusion), channel_id=1, source_target_pairs={{1,0},{0,1},{3,2},{2,3},{5,4},{4,5},{7,6},{6,7},{9,8},{8,9},{11,10... | collective-permute-start | bytes 1572872 | tf_op jit(solution)/shard_map/ppermute | solution.py:83
  12.1 7.2 %copy-start.4 = (f32[1,1,128,128]{3,2,1,0:T(8,128)S(1)}, f32[1,1,128,128]{3,2,1,0:T(8,128)}, u32[]{:S(2)}) copy-start(f32[1,1,128,128]{3,2,1,0:T(8,128)} %param.26) | copy-start | bytes 196612
  12.1 22.8 %all-to-all-start = ((f32[32,4,1024]{2,1,0:T(4,128)}), f32[32,4,1024]{2,1,0:T(4,128)S(1)}, u32[]{:S(2)}, u32[]{:S(2)}) async-start(f32[32,4,1024]{2,1,0:T(4,128)} %bitcast_select_fusion), calls=%async_computation | async-start | bytes 1048576 | tf_op jit(solution)/shard_map/all_to_all | solution.py:86
  19.3 0.7 %copy-start.11 = (f32[1,1,128]{2,1,0:T(1,128)S(1)}, f32[1,1,128]{2,1,0:T(1,128)}, u32[]{:S(2)}) copy-start(f32[1,1,128]{2,1,0:T(1,128)} %param.28) | copy-start | bytes 1540
  20.0 0.7 %copy-start.10 = (f32[1,1,128]{2,1,0:T(1,128)S(1)}, f32[1,1,128]{2,1,0:T(1,128)}, u32[]{:S(2)}) copy-start(f32[1,1,128]{2,1,0:T(1,128)} %param.27) | copy-start | bytes 1540
  20.6 0.7 %copy-start.12 = (s32[8]{0:T(128)S(1)}, s32[8]{0:T(128)}, u32[]{:S(2)}) copy-start(s32[8]{0:T(128)} %param.25) | copy-start | bytes 100
  21.3 0.7 %copy-start.13 = (s32[8]{0:T(128)S(1)}, s32[8]{0:T(128)}, u32[]{:S(2)}) copy-start(s32[8]{0:T(128)} %param.24) | copy-start | bytes 100
  23.4 11.9 %copy-start.3 = (f32[8,128,128]{2,1,0:T(8,128)S(1)}, f32[8,128,128]{2,1,0:T(8,128)}, u32[]{:S(2)}) copy-start(f32[8,128,128]{2,1,0:T(8,128)} %param.21) | copy-start | bytes 1572868
  35.1 1.2 %collective-permute-start.1 = (f32[4,1024]{1,0:T(4,128)S(1)}, f32[4,1024]{1,0:T(4,128)S(1)}, u32[]{:S(2)}, u32[]{:S(2)}) collective-permute-start(f32[4,1024]{1,0:T(4,128)S(1)} %get-tuple-element.4), channel_id=1, source_target_pairs={{1,0},{0,1},{3,2},{2,3},{5,4},{4,5},{7,6},{6,7},{9,8},{8,9},{11,10... | collective-permute-start | bytes 49160 | tf_op jit(solution)/shard_map/ppermute | solution.py:91
  36.4 1.0 %copy-start.5 = (f32[8,128]{1,0:T(8,128)S(1)}, f32[8,128]{1,0:T(8,128)}, u32[]{:S(2)}) copy-start(f32[8,128]{1,0:T(8,128)} %param.22) | copy-start | bytes 12292
  36.4 1.0 %copy-start.6 = (f32[8,128]{1,0:T(8,128)S(1)}, f32[8,128]{1,0:T(8,128)}, u32[]{:S(2)}) copy-start(f32[8,128]{1,0:T(8,128)} %param.23) | copy-start | bytes 12292
  38.7 11.3 %all-to-all-start.1 = ((f32[32,8,128]{2,1,0:T(8,128)}), f32[32,8,128]{2,1,0:T(8,128)S(1)}, u32[]{:S(2)}, u32[]{:S(2)}) async-start(f32[32,8,128]{2,1,0:T(8,128)} %broadcast_in_dim.157), calls=%async_computation.1 | async-start | bytes 262144 | tf_op jit(solution)/shard_map/all_to_all | solution.py:160
  52.3 0.7 %copy-start.7 = (f32[1,8]{1,0:T(1,128)S(1)}, f32[1,8]{1,0:T(1,128)}, u32[]{:S(2)}) copy-start(f32[1,8]{1,0:T(1,128)} %param.29) | copy-start | bytes 100

commit v11 on v10

--- a/solution.py
+++ b/solution.py
@@ -1,7 +1,7 @@
 import jax
 import jax.numpy as jnp
 from jax import lax
-from jax.sharding import PartitionSpec as P
+from jax.sharding import Mesh, PartitionSpec as P
 
 
 def land_update(precip, soil_water, capacity, evap_rate):
@@ -42,7 +42,7 @@
 def gather_lateral(runoff, tile_dest, tile_block, blocks, shards):
     tile_count, width = runoff.shape
     tile_cap = max(2, 2 * tile_count // shards)
-    grid = ("basin", "band")
+    grid = GRID
     if tile_cap >= blocks:
         block_ids = tile_dest * blocks + tile_block
         pick = (
@@ -72,23 +72,17 @@
 
 def pair_exchange(dense, blocks, shards):
     chains = lax.axis_size("basin")
-    rivers = lax.axis_size("band")
+    across = lax.axis_size("x")
     width = dense.shape[1]
-    half = blocks // 2
-    swap = [(m ^ 1, m) for m in range(rivers)]
-    core = lax.axis_index("band") % 2
-    parts = dense.reshape(chains, rivers // 2, 2, blocks, width)
+    core = lax.axis_index("core")
+    parts = dense.reshape(chains, across, 2, blocks, width)
     keep_side = lax.dynamic_index_in_dim(parts, core, axis=2, keepdims=False)
     give_side = lax.dynamic_index_in_dim(parts, 1 - core, axis=2, keepdims=False)
-    chip_sum = keep_side + lax.ppermute(give_side, "band", swap)
-    side = (jnp.arange(2) == core)[None, None, :, None, None]
-    send = jnp.where(side, chip_sum[:, :, None, :half], chip_sum[:, :, None, half:])
+    chip_sum = keep_side + lax.ppermute(give_side, "core", [(0, 1), (1, 0)])
     arrived = lax.all_to_all(
-        send.reshape(shards, half, width), ("basin", "band"), split_axis=0, concat_axis=0, tiled=True
-    ).reshape(chains, rivers // 2, 2, half, width)
-    same = jnp.sum(jnp.where(side, arrived, 0.0), axis=(0, 1, 2))
-    other = jnp.sum(jnp.where(side, 0.0, arrived), axis=(0, 1, 2))
-    return jnp.concatenate([same, lax.ppermute(other, "band", swap)], axis=0)
+        chip_sum.reshape(chains * across, blocks, width), ("basin", "x"), split_axis=0, concat_axis=0, tiled=True
+    )
+    return jnp.sum(arrived, axis=0)
 
 
 def local(
@@ -113,9 +107,9 @@
     reaches = precip.shape[2]
     blocks = trib_op.shape[0]
     chains = lax.axis_size("basin")
-    rivers = lax.axis_size("band")
+    rivers = lax.axis_size(BAND)
     shards = chains * rivers
-    grid = ("basin", "band")
+    grid = GRID
     operator = main_op[0, 0]
     keep_main = main_keep[0, 0]
     prev_main = main_prev[0, 0]
@@ -138,7 +132,7 @@
         exit_mixed[:, :, None], trib_keep[:, reaches - 1 :], trib_prev[:, reaches - 1 :]
     )[:, :, 0]
 
-    mine = lax.axis_index("band")
+    mine = lax.axis_index(BAND)
     me = lax.axis_index("basin")
     spread_lanes = reaches // blocks
     if reaches % blocks == 0 and sub_steps + 4 + spread_lanes <= reaches:
@@ -255,35 +249,43 @@
 
 
 PAIRED = False
+BAND = "band"
+GRID = ("basin", "band")
 
 
 def solution(mesh):
-    global PAIRED
+    global PAIRED, BAND, GRID
     PAIRED = cores_paired(mesh)
+    if PAIRED:
+        grid = mesh.devices
+        mesh = Mesh(grid.reshape(grid.shape[0], grid.shape[1] // 2, 2), ("basin", "x", "core"))
+        BAND, GRID = ("x", "core"), ("basin", "x", "core")
+    else:
+        BAND, GRID = "band", ("basin", "band")
     return jax.shard_map(
         local,
         mesh=mesh,
         in_specs=(
-            P(("basin", "band"), None, None),
-            P(("basin", "band"), None),
-            P(("basin", "band"), None),
-            P(("basin", "band"), None),
-            P(("basin", "band")),
-            P(("basin", "band")),
-            P(("basin", "band"), None, None),
-            P(("basin", "band"), None),
-            P(("basin", "band"), None),
-            P(("basin", "band")),
-            P(("basin", "band")),
-            P("band", "basin", None, None),
-            P("band", "basin", None),
-            P("band", "basin", None),
-            P("band", None),
+            P(GRID, None, None),
+            P(GRID, None),
+            P(GRID, None),
+            P(GRID, None),
+            P(GRID),
+            P(GRID),
+            P(GRID, None, None),
+            P(GRID, None),
+            P(GRID, None),
+            P(GRID),
+            P(GRID),
+            P(BAND, "basin", None, None),
+            P(BAND, "basin", None),
+            P(BAND, "basin", None),
+            P(BAND, None),
         ),
         out_specs=(
-            P(("basin", "band"), None),
-            P(("basin", "band"), None),
-            P("band", "basin", None, None),
+            P(GRID, None),
+            P(GRID, None),
+            P(BAND, "basin", None, None),
         ),
         check_vma=False,
     )

time: 55.4 us -> 55.7 us (level)
  starting transfers between devices: 10.9 us -> 11.8 us
    ppermute x2 -> x1, waiting for transfers between devices: 2.53 us -> 0.01 us  [pair_exchange(): chip_sum = keep_side + lax.ppermute(give_side, 'core', [(0, 1), (1, 0)])]
    all_to_all x1, waiting for transfers between devices: 10.8 us -> 13 us  [pair_exchange(): lax.all_to_all(chip_sum.reshape(chains * across, blocks, width), ('basin'...]
    all_to_all x1, starting transfers between devices: 7.22 us -> 8.44 us  [pair_exchange(): lax.all_to_all(chip_sum.reshape(chains * across, blocks, width), ('basin'...]
    select_n x1 -> x0, other arithmetic: 0.95 us -> none  [pair_exchange(): jnp.where(side, chip_sum[:, :, None, :half], chip_sum[:, :, None, half:])]
    add x1, other arithmetic: 0.07 us -> 0.85 us  [pair_exchange(): chip_sum = keep_side + lax.ppermute(give_side, 'core', [(0, 1), (1, 0)])]
  transfers between devices with their start and end apart: 4 -> 3, of which waited for: 4 -> 2; matrix products, arithmetic and copies ran while one was open for 8% -> 7% of each run, Pallas kernels for 0% -> 0%
where the time goes in v11:
time: 55.7 us; the launch traced here: 55.2 us
  waiting for transfers between devices  20.5 us (37%)
  local copies, waits for them, and re-layouts  12.6 us (23%)
  starting transfers between devices  11.8 us (21%)
  other arithmetic  7.44 us (13%)
  matrix products  1.79 us (3%)
  between operations  1.01 us (2%)
    all_to_all x1, waiting for transfers between devices, pair_exchange(): lax.all_to_all(chip_sum.reshape(chains * across, blocks, width), ('basin'...  13 us
    all_to_all x1, starting transfers between devices, pair_exchange(): lax.all_to_all(chip_sum.reshape(chains * across, blocks, width), ('basin'...  8.44 us
    all_to_all x1, waiting for transfers between devices, local(): lax.all_to_all(jnp.broadcast_to(tile[None], (shards,) + tile.shape), grid...  7.58 us
    slice x1, local copies, waits for them, and re-layouts, land_update(): rain_now = precip[:, sub_step]  4.69 us
    unnamed x36, local copies, waits for them, and re-layouts  3.98 us
    all_to_all x1, starting transfers between devices, local(): lax.all_to_all(jnp.broadcast_to(tile[None], (shards,) + tile.shape), grid...  2.88 us
    select_n x1, other arithmetic, local(): jnp.where(lane == sub_steps + offset, value, 0.0)  1.3 us
  transfers between devices with their start and end apart: 3, of which 2 were waited for; matrix products, arithmetic and copies ran while one was open for 7% of the time, Pallas kernels for 0%

profile of v11, /device:TPU:0, one launch (start us, length us, event | category | flops | bytes accessed | tf_op | source)
XLA Modules:
  0.0 55.2 jit_solution(17740345125713505177)
XLA Ops:
  0.7 4.7 %fusion.81 = (f32[192,1,128]{2,1,0:T(1,128)S(1)}, f32[192,1,128]{2,1,0:T(1,128)S(1)}, f32[192,1,128]{2,1,0:T(1,128)S(1)}, f32[192,1,128]{2,1,0:T(1,128)S(1)}, f3...) fusion(f32[192,8,128]{2,1,0:T(8,128)} %param.15), kind=kLoop, calls=%fused_computation.197 | loop fusion | bytes 1572864 | tf_op jit(solution)/shard_map/slice | solution.py:11
  5.4 0.9 %copy-done.1 = f32[192,128]{1,0:T(8,128)S(1)} copy-done((f32[192,128]{1,0:T(8,128)S(1)}, f32[192,128]{1,0:T(8,128)}, u32[]{:S(2)}) %copy-start.1) | copy-done | bytes 98328
  6.3 0.1 bitcast_dynamic-update-slice_fusion.6
  6.3 0.1 bitcast_dynamic-update-slice_fusion.5
  6.4 0.1 bitcast_dynamic-update-slice_fusion.4
  6.5 0.1 bitcast_dynamic-update-slice_fusion.3
  6.6 0.1 bitcast_dynamic-update-slice_fusion.2
  6.7 0.1 bitcast_dynamic-update-slice_fusion
  6.8 0.5 copy.177
  7.3 0.1 reshape.332
  7.4 0.5 copy-done.9
  8.0 0.1 copy-done.8
  8.1 0.7 %fusion = f32[8,2,2,8,1024]{4,3,2,1,0:T(8,128)S(1)} fusion(f32[192,1024,1,1,1]{1,0,2,3,4:T(8,128)S(1)} %reshape.332, s32[8,2,2,8]{3,2,1,0:T(2,128)S(1)} %multiply_add_fusion, s32[192]{0:T(256)S(1)} %multiply_add_fusion.10), kind=kOutput, calls=%fused_computation.1 | convolution fusion | flops 604028928 | bytes 1836800 | tf_op jit(solution)/shard_map/dot_general | solution.py:51
  8.9 0.5 collective-permute-start
  9.4 0.3 copy-done.4
  9.7 0.1 reshape_squeeze.4
  9.7 0.6 %copy-done.11 = f32[1,1,128]{2,1,0:T(1,128)S(1)} copy-done((f32[1,1,128]{2,1,0:T(1,128)S(1)}, f32[1,1,128]{2,1,0:T(1,128)}, u32[]{:S(2)}) %copy-start.11) | copy-done | bytes 536
  10.3 0.6 %slice.191 = f32[1,1,1]{2,1,0:T(1,128)} slice(f32[1,1,128]{2,1,0:T(1,128)S(1)} %copy-done.11), slice={[0:1], [0:1], [127:128]} | slice | bytes 8 | tf_op jit(solution)/shard_map/slice | solution.py:144
  10.9 0.1 copy-done.10
  11.0 0.6 %slice.190 = f32[1,1,1]{2,1,0:T(1,128)} slice(f32[1,1,128]{2,1,0:T(1,128)S(1)} %copy-done.10), slice={[0:1], [0:1], [127:128]} | slice | bytes 8 | tf_op jit(solution)/shard_map/slice | solution.py:143
  11.5 0.1 copy-done.12
  11.6 0.7 %copy-done.13 = s32[8]{0:T(128)S(1)} copy-done((s32[8]{0:T(128)S(1)}, s32[8]{0:T(128)}, u32[]{:S(2)}) %copy-start.13) | copy-done | bytes 56
  12.3 0.8 %bitcast_add_fusion = f32[8,2,8,1024]{3,2,1,0:T(8,128)} fusion(f32[8,2,8,1024]{3,2,1,0:T(8,128)S(1)} %collective-permute-done, f32[8,2,2,8,1024]{4,3,2,1,0:T(8,128)S(1)} %fusion, s32[]{:T(128)S(6)} %select_n.173), kind=kLoop, calls=%fused_computation.3 | loop fusion | flops 131072 | bytes 1572868 | tf_op jit(solution)/shard_map/add | solution.py:81
  13.1 8.4 %all-to-all-start = ((f32[16,8,1024]{2,1,0:T(8,128)}), f32[16,8,1024]{2,1,0:T(8,128)S(1)}, u32[]{:S(2)}, u32[]{:S(2)}) async-start(f32[16,8,1024]{2,1,0:T(8,128)} %bitcast.19), calls=%async_computation | async-start | bytes 1048576 | tf_op jit(solution)/shard_map/all_to_all | solution.py:82
  21.6 1.3 %compare_select_fusion = (f32[128]{0:T(128)S(1)}, f32[128]{0:T(128)S(1)}) fusion(f32[]{:T(128)} %bitcast.42, f32[]{:T(128)} %bitcast.41), kind=kLoop, calls=%fused_computation.138 | loop fusion | flops 512 | bytes 1032 | tf_op jit(solution)/shard_map/jit(_where)/select_n | solution.py:151
  22.9 0.1 add_add_fusion
  23.0 0.7 %add_subtract_fusion = f32[192,128]{1,0:T(8,128)} fusion(f32[192,128]{1,0:T(8,128)S(1)} %bitcast.368, f32[192,128]{1,0:T(8,128)S(1)} %copy-done.1, f32[192,128]{1,0:T(8,128)S(1)} %copy-done, f32[192,128]{1,0:T(8,128)S(1)} %bitcast.362, f32[192,128]{1,0:T(8,128)S(1)} %get-tuple-element.34, f32[192,128]{1,0:T(8,128)S(1)} %bitcast.351), kind=kLoop, calls=%fused_computation.23 | loop fusion | flops 466944 | bytes 688128 | tf_op jit(solution)/shard_map/sub | solution.py:13
  23.8 13.0 %all-to-all-done = f32[16,8,1024]{2,1,0:T(8,128)S(1)} async-done(((f32[16,8,1024]{2,1,0:T(8,128)}), f32[16,8,1024]{2,1,0:T(8,128)S(1)}, u32[]{:S(2)}, u32[]{:S(2)}) %all-to-all-start) | async-done | bytes 524320 | tf_op jit(solution)/shard_map/all_to_all | solution.py:82
  36.8 0.9 %fusion.10 = f32[8,8,128]{2,1,0:T(8,128)S(1)} fusion(f32[8,128,128]{2,1,0:T(8,128)S(1)} %copy-done.3, f32[1,8,8,128]{3,1,2,0:T(8,128)S(1)} %bitcast.371), kind=kOutput, calls=%fused_computation.49 | convolution fusion | flops 12582912 | bytes 589824 | tf_op jit(solution)/shard_map/brc,btc->btr/dot_general | solution.py:121
  37.7 0.1 fusion.12
  37.8 0.1 fusion.33
  37.9 0.3 fusion.32
  38.3 0.1 copy.193
  38.4 0.6 %broadcast_in_dim.96 = f32[32,8,128]{2,1,0:T(8,128)} broadcast(f32[8,128]{1,0:T(8,128)S(1)} %pad_add_fusion), dimensions={1,2} | broadcast | bytes 135168 | tf_op jit(solution)/shard_map/broadcast_in_dim | solution.py:155
  39.0 2.9 %all-to-all-start.1 = ((f32[32,8,128]{2,1,0:T(8,128)}), f32[32,8,128]{2,1,0:T(8,128)S(1)}, u32[]{:S(2)}, u32[]{:S(2)}) async-start(f32[32,8,128]{2,1,0:T(8,128)} %broadcast_in_dim.96), calls=%async_computation.1 | async-start | bytes 262144 | tf_op jit(solution)/shard_map/all_to_all | solution.py:154
  41.9 0.6 %multiply_add_fusion.9 = f32[8,128]{1,0:T(8,128)} fusion(f32[8,128]{1,0:T(8,128)S(1)} %bitcast.384, f32[8,128]{1,0:T(8,128)S(1)} %copy-done.5, f32[8,128]{1,0:T(8,128)S(1)} %bitcast.385, f32[8,128]{1,0:T(8,128)S(1)} %bitcast.383, f32[8,128]{1,0:T(8,128)S(1)} %bitcast.382, f32[8,128]{1,0:T(8,128)S(1)} %bitcast.381, f32[8,128]{1,0:T(8,128)S(1)} %bitcast.380, ...), kind=kLoop, calls=%fused_computation.116 | loop fusion | flops 25600 | bytes 45056 | tf_op jit(solution)/shard_map/add | solution.py:22
  42.6 7.6 %all-to-all-done.1 = f32[32,8,128]{2,1,0:T(8,128)S(1)} async-done(((f32[32,8,128]{2,1,0:T(8,128)}), f32[32,8,128]{2,1,0:T(8,128)S(1)}, u32[]{:S(2)}, u32[]{:S(2)}) %all-to-all-start.1) | async-done | bytes 131104 | tf_op jit(solution)/shard_map/all_to_all | solution.py:154
  50.1 0.2 slice_reduce_fusion
  50.3 0.1 eq.129
  50.4 0.7 %fusion.7 = pred[32,8]{1,0:T(8,128)(4,1)S(1)} fusion(f32[32,8,128]{2,1,0:T(8,128)S(1)} %all-to-all-done.1, f32[]{:T(128)S(6)} %convert_element_type.37), kind=kLoop, calls=%fused_computation.13 | loop fusion | flops 256 | bytes 1284 | tf_op jit(solution)/shard_map/eq | solution.py:201
  51.1 0.1 eq.128
  51.2 0.1 slice.226
  51.3 0.1 reshape.331
  51.3 0.1 copy.222
  51.4 0.1 copy.195
  51.5 0.2 multiply_reduce_fusion.2
  51.8 0.1 fusion.6
  51.9 0.3 multiply_reduce_fusion
  52.3 0.1 multiply_reduce_fusion.1
  52.3 0.1 multiply_select_fusion
  52.5 0.6 %copy-done.7 = f32[1,8]{1,0:T(1,128)S(1)} copy-done((f32[1,8]{1,0:T(1,128)S(1)}, f32[1,8]{1,0:T(1,128)}, u32[]{:S(2)}) %copy-start.7) | copy-done | bytes 56
  53.1 0.1 fusion.15
  53.2 0.1 multiply_add_fusion.1
  53.3 0.1 stack.94
  53.4 0.1 fusion.17
  53.5 0.1 fusion.19
  53.7 0.1 fusion.21
  53.8 0.1 fusion.23
  53.9 0.1 fusion.25
  54.0 0.1 fusion.27
  54.2 0.1 fusion.29
  54.3 0.2 fusion.8
  54.5 0.1 fusion.67
  54.6 0.6 %stack.95 = f32[8,128]{1,0:T(8,128)} concatenate(f32[1,128]{1,0:T(1,128)S(1)} %get-tuple-element.20, f32[1,128]{1,0:T(1,128)S(1)} %get-tuple-element.19, f32[1,128]{1,0:T(1,128)S(1)} %get-tuple-element.18, f32[1,128]{1,0:T(1,128)S(1)} %get-tuple-element.17, f32[1,128]{1,0:T(1,128)S(1)} %get-tuple-element.16, f32[1,128]{1,0:T(1,128)S(1)} %get-tuple-element.15, ...), dimensions={0} | concatenate | bytes 8192 | tf_op jit(solution)/shard_map/stack | solution.py:24
  (53 shorter events, 0.5 us)
Async XLA Ops:
  0.6 4.7 %copy-start = (f32[192,128]{1,0:T(8,128)S(1)}, f32[192,128]{1,0:T(8,128)}, u32[]{:S(2)}) copy-start(f32[192,128]{1,0:T(8,128)} %param.17) | copy-start | bytes 294916
  0.7 4.7 %copy-start.2 = (f32[192,128]{1,0:T(8,128)S(1)}, f32[192,128]{1,0:T(8,128)}, u32[]{:S(2)}) copy-start(f32[192,128]{1,0:T(8,128)} %param.16) | copy-start | bytes 294916
  5.4 0.9 %copy-start.1 = (f32[192,128]{1,0:T(8,128)S(1)}, f32[192,128]{1,0:T(8,128)}, u32[]{:S(2)}) copy-start(f32[192,128]{1,0:T(8,128)} %param.18) | copy-start | bytes 294916
  7.3 0.7 %copy-start.9 = (s32[192]{0:T(256)S(1)}, s32[192]{0:T(256)}, u32[]{:S(2)}) copy-start(s32[192]{0:T(256)} %param.19) | copy-start | bytes 2308
  7.4 0.7 %copy-start.8 = (s32[192]{0:T(256)S(1)}, s32[192]{0:T(256)}, u32[]{:S(2)}) copy-start(s32[192]{0:T(256)} %param.20) | copy-start | bytes 2308
  8.8 0.8 %copy-start.4 = (f32[1,1,128,128]{3,2,1,0:T(8,128)S(1)}, f32[1,1,128,128]{3,2,1,0:T(8,128)}, u32[]{:S(2)}) copy-start(f32[1,1,128,128]{3,2,1,0:T(8,128)} %param.26) | copy-start | bytes 196612
  8.9 3.4 %collective-permute-start = (f32[8,2,8,1024]{3,2,1,0:T(8,128)S(1)}, f32[8,2,8,1024]{3,2,1,0:T(8,128)S(1)}, u32[]{:S(2)}, u32[]{:S(2)}) collective-permute-start(f32[8,2,8,1024]{3,2,1,0:T(8,128)S(1)} %dynamic-slice_bitcast_fusion), channel_id=1, source_target_pairs={{0,1},{1,0},{2,3},{3,2},{4,5},{5,4},{6,7},{7,6},{8,9},{9,8},{10,11... | collective-permute-start | bytes 1572872 | tf_op jit(solution)/shard_map/ppermute | solution.py:81
  9.6 0.7 %copy-start.11 = (f32[1,1,128]{2,1,0:T(1,128)S(1)}, f32[1,1,128]{2,1,0:T(1,128)}, u32[]{:S(2)}) copy-start(f32[1,1,128]{2,1,0:T(1,128)} %param.28) | copy-start | bytes 1540
  10.3 0.7 %copy-start.10 = (f32[1,1,128]{2,1,0:T(1,128)S(1)}, f32[1,1,128]{2,1,0:T(1,128)}, u32[]{:S(2)}) copy-start(f32[1,1,128]{2,1,0:T(1,128)} %param.27) | copy-start | bytes 1540
  11.0 0.7 %copy-start.12 = (s32[8]{0:T(128)S(1)}, s32[8]{0:T(128)}, u32[]{:S(2)}) copy-start(s32[8]{0:T(128)} %param.25) | copy-start | bytes 100
  11.6 0.7 %copy-start.13 = (s32[8]{0:T(128)S(1)}, s32[8]{0:T(128)}, u32[]{:S(2)}) copy-start(s32[8]{0:T(128)} %param.24) | copy-start | bytes 100
  13.1 9.9 %copy-start.3 = (f32[8,128,128]{2,1,0:T(8,128)S(1)}, f32[8,128,128]{2,1,0:T(8,128)}, u32[]{:S(2)}) copy-start(f32[8,128,128]{2,1,0:T(8,128)} %param.21) | copy-start | bytes 1572868
  13.1 23.6 %all-to-all-start = ((f32[16,8,1024]{2,1,0:T(8,128)}), f32[16,8,1024]{2,1,0:T(8,128)S(1)}, u32[]{:S(2)}, u32[]{:S(2)}) async-start(f32[16,8,1024]{2,1,0:T(8,128)} %bitcast.19), calls=%async_computation | async-start | bytes 1048576 | tf_op jit(solution)/shard_map/all_to_all | solution.py:82
  36.8 1.0 %copy-start.5 = (f32[8,128]{1,0:T(8,128)S(1)}, f32[8,128]{1,0:T(8,128)}, u32[]{:S(2)}) copy-start(f32[8,128]{1,0:T(8,128)} %param.22) | copy-start | bytes 12292
  36.8 1.0 %copy-start.6 = (f32[8,128]{1,0:T(8,128)S(1)}, f32[8,128]{1,0:T(8,128)}, u32[]{:S(2)}) copy-start(f32[8,128]{1,0:T(8,128)} %param.23) | copy-start | bytes 12292
  39.0 11.1 %all-to-all-start.1 = ((f32[32,8,128]{2,1,0:T(8,128)}), f32[32,8,128]{2,1,0:T(8,128)S(1)}, u32[]{:S(2)}, u32[]{:S(2)}) async-start(f32[32,8,128]{2,1,0:T(8,128)} %broadcast_in_dim.96), calls=%async_computation.1 | async-start | bytes 262144 | tf_op jit(solution)/shard_map/all_to_all | solution.py:154
  52.5 0.7 %copy-start.7 = (f32[1,8]{1,0:T(1,128)S(1)}, f32[1,8]{1,0:T(1,128)}, u32[]{:S(2)}) copy-start(f32[1,8]{1,0:T(1,128)} %param.29) | copy-start | bytes 100

commit v12 on v11

--- a/solution.py
+++ b/solution.py
@@ -13,6 +13,17 @@
         water = (1.0 - evap_rate) * water + rain_now - runoff_now
         runoff_steps.append(runoff_now)
     return (jnp.stack(runoff_steps, axis=1), water)
+
+
+def land_update_t(precip_t, soil_water, capacity, evap_rate):
+    water = soil_water
+    runoff_steps = []
+    for sub_step in range(precip_t.shape[0]):
+        rain_now = precip_t[sub_step]
+        runoff_now = rain_now * water / (water + capacity)
+        water = (1.0 - evap_rate) * water + rain_now - runoff_now
+        runoff_steps.append(runoff_now)
+    return (jnp.stack(runoff_steps, axis=0), water)
 
 
 def route_series(mixed, keep, previous):
@@ -39,8 +50,9 @@
     return (buffer, slot_labels)
 
 
-def gather_lateral(runoff, tile_dest, tile_block, blocks, shards):
-    tile_count, width = runoff.shape
+def gather_lateral(runoff_t, tile_dest, tile_block, blocks, shards):
+    sub_steps, tile_count, reaches = runoff_t.shape
+    width = sub_steps * reaches
     tile_cap = max(2, 2 * tile_count // shards)
     grid = GRID
     if tile_cap >= blocks:
@@ -48,13 +60,16 @@
         pick = (
             block_ids[None, :] == jnp.arange(shards * blocks, dtype=jnp.int32)[:, None]
         ).astype(jnp.float32)
-        dense = jnp.dot(pick, runoff, precision=lax.Precision.HIGHEST)
+        dense = jnp.einsum(
+            "gk,tkc->gtc", pick, runoff_t, precision=lax.Precision.HIGHEST
+        ).reshape(shards * blocks, width)
         if not PAIRED or blocks % 2:
             arrived = lax.all_to_all(
                 dense.reshape(shards, blocks, width), grid, split_axis=0, concat_axis=0, tiled=True
             )
             return jnp.sum(arrived, axis=0)
         return pair_exchange(dense, blocks, shards)
+    runoff = jnp.transpose(runoff_t, (1, 0, 2)).reshape(tile_count, width)
     buffer, slot_labels = pack_slots(runoff, tile_block, tile_dest, shards, tile_cap)
     arrived = lax.all_to_all(
         buffer.reshape(shards, tile_cap, width), grid, split_axis=0, concat_axis=0, tiled=True
@@ -114,10 +129,8 @@
     keep_main = main_keep[0, 0]
     prev_main = main_prev[0, 0]
 
-    runoff, water = land_update(precip, soil_water, capacity, evap_rate)
-    lateral = gather_lateral(
-        runoff.reshape(tile_count, sub_steps * reaches), tile_dest, tile_block, blocks, shards
-    )
+    runoff_t, water = land_update_t(jnp.transpose(precip, (1, 0, 2)), soil_water, capacity, evap_rate)
+    lateral = gather_lateral(runoff_t, tile_dest, tile_block, blocks, shards)
     trib_mixed = jnp.einsum(
         "brc,btc->btr",
         trib_op,

time: 55.7 us -> 52.5 us (0.943)
  local copies, waits for them, and re-layouts: 12.6 us -> 9.37 us
    slice x1 -> x0, local copies, waits for them, and re-layouts: 4.69 us -> none  [land_update(): rain_now = precip[:, sub_step]]
    unnamed x36 -> x37, local copies, waits for them, and re-layouts: 3.98 us -> 5.25 us
    dot_general x0 -> x1, local copies, waits for them, and re-layouts: none -> 0.61 us  [gather_lateral(): jnp.einsum('gk,tkc->gtc', pick, runoff_t, precision=lax.Precision.HIGHEST)]
  transfers between devices with their start and end apart: 3 -> 3, of which waited for: 2 -> 2; matrix products, arithmetic and copies ran while one was open for 7% -> 8% of each run, Pallas kernels for 0% -> 0%
where the time goes in v12:
time: 52.5 us; the launch traced here: 52.1 us
  waiting for transfers between devices  20.6 us (39%)
  starting transfers between devices  11.8 us (22%)
  local copies, waits for them, and re-layouts  9.37 us (18%)
  other arithmetic  7.45 us (14%)
  matrix products  1.83 us (3%)
  between operations  1 us (2%)
    all_to_all x1, waiting for transfers between devices, pair_exchange(): lax.all_to_all(chip_sum.reshape(chains * across, blocks, width), ('basin'...  13 us
    all_to_all x1, starting transfers between devices, pair_exchange(): lax.all_to_all(chip_sum.reshape(chains * across, blocks, width), ('basin'...  8.44 us
    all_to_all x1, waiting for transfers between devices, local(): lax.all_to_all(jnp.broadcast_to(tile[None], (shards,) + tile.shape), grid...  7.58 us
    unnamed x37, local copies, waits for them, and re-layouts  5.25 us
    all_to_all x1, starting transfers between devices, local(): lax.all_to_all(jnp.broadcast_to(tile[None], (shards,) + tile.shape), grid...  2.88 us
    select_n x1, other arithmetic, local(): jnp.where(lane == sub_steps + offset, value, 0.0)  1.3 us
    add x4, other arithmetic, route_series(): flow = keep * flow + (1.0 - keep) * mixed[..., sub_step, :]  1.06 us
  transfers between devices with their start and end apart: 3, of which 2 were waited for; matrix products, arithmetic and copies ran while one was open for 8% of the time, Pallas kernels for 0%

profile of v12, /device:TPU:0, one launch (start us, length us, event | category | flops | bytes accessed | tf_op | source)
XLA Modules:
  0.0 52.1 jit_solution(12014995679736512554)
XLA Ops:
  0.7 1.3 %copy.178 = f32[192,8,128]{2,0,1:T(8,128)S(1)} copy(f32[192,8,128]{2,1,0:T(8,128)} %param.15) | data formatting | bytes 1572864 | tf_op args[0]
  2.0 0.9 %copy-done.1 = f32[192,128]{1,0:T(8,128)S(1)} copy-done((f32[192,128]{1,0:T(8,128)S(1)}, f32[192,128]{1,0:T(8,128)}, u32[]{:S(2)}) %copy-start.1) | copy-done | bytes 98328
  2.9 0.1 bitcast_dynamic-update-slice_fusion.6
  3.0 0.1 bitcast_dynamic-update-slice_fusion.5
  3.0 0.1 bitcast_dynamic-update-slice_fusion.4
  3.1 0.1 bitcast_dynamic-update-slice_fusion.3
  3.3 0.1 bitcast_dynamic-update-slice_fusion.2
  3.3 0.1 bitcast_dynamic-update-slice_fusion.1
  3.4 0.1 bitcast_dynamic-update-slice_fusion
  3.5 0.6 %copy-done.8 = s32[192]{0:T(256)S(1)} copy-done((s32[192]{0:T(256)S(1)}, s32[192]{0:T(256)}, u32[]{:S(2)}) %copy-start.8) | copy-done | bytes 792
  4.1 0.7 %fusion.1 = f32[256,8,128]{2,0,1:T(8,128)S(1)} fusion(f32[8,192,128]{2,1,0:T(8,128)S(1)} %bitcast_dynamic-update-slice_fusion, s32[192]{0:T(256)S(1)} %multiply_add_fusion.9), kind=kOutput, calls=%fused_computation.6 | convolution fusion | flops 604028928 | bytes 1835776 | tf_op jit(solution)/shard_map/gk,tkc->gtc/dot_general | solution.py:63
  4.8 0.6 %copy.134 = f32[256,8,128]{2,1,0:T(8,128)S(1)} copy(f32[256,8,128]{2,0,1:T(8,128)S(1)} %fusion.1) | data formatting | bytes 2097152 | tf_op jit(solution)/shard_map/gk,tkc->gtc/dot_general | solution.py:63
  5.5 0.2 reshape_reshape.3
  5.7 0.5 collective-permute-start
  6.2 0.3 copy-done.4
  6.5 0.1 reshape_squeeze.4
  6.6 0.6 %copy-done.11 = f32[1,1,128]{2,1,0:T(1,128)S(1)} copy-done((f32[1,1,128]{2,1,0:T(1,128)S(1)}, f32[1,1,128]{2,1,0:T(1,128)}, u32[]{:S(2)}) %copy-start.11) | copy-done | bytes 536
  7.1 0.6 %slice.191 = f32[1,1,1]{2,1,0:T(1,128)} slice(f32[1,1,128]{2,1,0:T(1,128)S(1)} %copy-done.11), slice={[0:1], [0:1], [127:128]} | slice | bytes 8 | tf_op jit(solution)/shard_map/slice | solution.py:157
  7.7 0.1 copy-done.10
  7.8 0.6 %slice.190 = f32[1,1,1]{2,1,0:T(1,128)} slice(f32[1,1,128]{2,1,0:T(1,128)S(1)} %copy-done.10), slice={[0:1], [0:1], [127:128]} | slice | bytes 8 | tf_op jit(solution)/shard_map/slice | solution.py:156
  8.4 0.1 copy-done.12
  8.5 0.7 %copy-done.13 = s32[8]{0:T(128)S(1)} copy-done((s32[8]{0:T(128)S(1)}, s32[8]{0:T(128)}, u32[]{:S(2)}) %copy-start.13) | copy-done | bytes 56
  9.1 0.8 %bitcast_add_fusion = f32[8,2,8,1024]{3,2,1,0:T(8,128)} fusion(f32[8,2,8,1024]{3,2,1,0:T(8,128)S(1)} %collective-permute-done, f32[8,2,2,8,1024]{4,3,2,1,0:T(8,128)S(1)} %reshape_reshape.3, s32[]{:T(128)S(6)} %select_n.173), kind=kLoop, calls=%fused_computation.2 | loop fusion | flops 131072 | bytes 1572868 | tf_op jit(solution)/shard_map/add | solution.py:96
  10.0 8.4 %all-to-all-start = ((f32[16,8,1024]{2,1,0:T(8,128)}), f32[16,8,1024]{2,1,0:T(8,128)S(1)}, u32[]{:S(2)}, u32[]{:S(2)}) async-start(f32[16,8,1024]{2,1,0:T(8,128)} %bitcast.20), calls=%async_computation | async-start | bytes 1048576 | tf_op jit(solution)/shard_map/all_to_all | solution.py:97
  18.4 1.3 %compare_select_fusion = (f32[128]{0:T(128)S(1)}, f32[128]{0:T(128)S(1)}) fusion(f32[]{:T(128)} %bitcast.43, f32[]{:T(128)} %bitcast.42), kind=kLoop, calls=%fused_computation.145 | loop fusion | flops 512 | bytes 1032 | tf_op jit(solution)/shard_map/jit(_where)/select_n | solution.py:164
  19.7 0.1 add_add_fusion
  19.9 0.7 %add_subtract_fusion = f32[192,128]{1,0:T(8,128)} fusion(f32[8,192,128]{2,1,0:T(8,128)S(1)} %bitcast.446, f32[192,128]{1,0:T(8,128)S(1)} %copy-done.1, f32[192,128]{1,0:T(8,128)S(1)} %copy-done, f32[192,128]{1,0:T(8,128)S(1)} %get-tuple-element.34), kind=kLoop, calls=%fused_computation.31 | loop fusion | flops 319488 | bytes 589824 | tf_op jit(solution)/shard_map/sub | solution.py:24
  20.6 13.0 %all-to-all-done = f32[16,8,1024]{2,1,0:T(8,128)S(1)} async-done(((f32[16,8,1024]{2,1,0:T(8,128)}), f32[16,8,1024]{2,1,0:T(8,128)S(1)}, u32[]{:S(2)}, u32[]{:S(2)}) %all-to-all-start) | async-done | bytes 524320 | tf_op jit(solution)/shard_map/all_to_all | solution.py:97
  33.6 0.9 %fusion.9 = f32[8,8,128]{2,1,0:T(8,128)S(1)} fusion(f32[8,128,128]{2,1,0:T(8,128)S(1)} %copy-done.3, f32[1,8,8,128]{3,1,2,0:T(8,128)S(1)} %bitcast.451), kind=kOutput, calls=%fused_computation.57 | convolution fusion | flops 12582912 | bytes 589824 | tf_op jit(solution)/shard_map/brc,btc->btr/dot_general | solution.py:134
  34.5 0.1 fusion.11
  34.6 0.1 fusion.32
  34.7 0.3 fusion.31
  35.1 0.1 copy.150
  35.2 0.6 %broadcast_in_dim.96 = f32[32,8,128]{2,1,0:T(8,128)} broadcast(f32[8,128]{1,0:T(8,128)S(1)} %pad_add_fusion), dimensions={1,2} | broadcast | bytes 135168 | tf_op jit(solution)/shard_map/broadcast_in_dim | solution.py:168
  35.9 2.9 %all-to-all-start.1 = ((f32[32,8,128]{2,1,0:T(8,128)}), f32[32,8,128]{2,1,0:T(8,128)S(1)}, u32[]{:S(2)}, u32[]{:S(2)}) async-start(f32[32,8,128]{2,1,0:T(8,128)} %broadcast_in_dim.96), calls=%async_computation.1 | async-start | bytes 262144 | tf_op jit(solution)/shard_map/all_to_all | solution.py:167
  38.8 0.6 %multiply_add_fusion.8 = f32[8,128]{1,0:T(8,128)} fusion(f32[8,128]{1,0:T(8,128)S(1)} %bitcast.464, f32[8,128]{1,0:T(8,128)S(1)} %copy-done.5, f32[8,128]{1,0:T(8,128)S(1)} %bitcast.465, f32[8,128]{1,0:T(8,128)S(1)} %bitcast.463, f32[8,128]{1,0:T(8,128)S(1)} %bitcast.462, f32[8,128]{1,0:T(8,128)S(1)} %bitcast.461, f32[8,128]{1,0:T(8,128)S(1)} %bitcast.460, ...), kind=kLoop, calls=%fused_computation.123 | loop fusion | flops 25600 | bytes 45056 | tf_op jit(solution)/shard_map/add | solution.py:33
  39.4 7.6 %all-to-all-done.1 = f32[32,8,128]{2,1,0:T(8,128)S(1)} async-done(((f32[32,8,128]{2,1,0:T(8,128)}), f32[32,8,128]{2,1,0:T(8,128)S(1)}, u32[]{:S(2)}, u32[]{:S(2)}) %all-to-all-start.1) | async-done | bytes 131104 | tf_op jit(solution)/shard_map/all_to_all | solution.py:167
  47.0 0.2 slice_reduce_fusion
  47.2 0.1 eq.97
  47.2 0.7 %fusion.5 = pred[32,8]{1,0:T(8,128)(4,1)S(1)} fusion(f32[32,8,128]{2,1,0:T(8,128)S(1)} %all-to-all-done.1, f32[]{:T(128)S(6)} %convert_element_type.37), kind=kLoop, calls=%fused_computation.12 | loop fusion | flops 256 | bytes 1284 | tf_op jit(solution)/shard_map/eq | solution.py:214
  47.9 0.1 eq.96
  48.0 0.1 slice.234
  48.1 0.1 reshape.300
  48.2 0.1 copy.170
  48.3 0.1 copy.152
  48.4 0.2 multiply_reduce_fusion.2
  48.6 0.1 fusion.4
  48.8 0.3 multiply_reduce_fusion
  49.1 0.1 multiply_reduce_fusion.1
  49.2 0.1 multiply_select_fusion
  49.3 0.6 %copy-done.7 = f32[1,8]{1,0:T(1,128)S(1)} copy-done((f32[1,8]{1,0:T(1,128)S(1)}, f32[1,8]{1,0:T(1,128)}, u32[]{:S(2)}) %copy-start.7) | copy-done | bytes 56
  50.0 0.1 fusion.14
  50.1 0.1 multiply_add_fusion
  50.2 0.1 stack.94
  50.3 0.1 fusion.16
  50.4 0.1 fusion.18
  50.5 0.1 fusion.20
  50.6 0.1 fusion.22
  50.8 0.1 fusion.24
  50.9 0.1 fusion.26
  51.0 0.1 fusion.28
  51.2 0.2 fusion.7
  51.4 0.1 fusion.66
  51.4 0.6 %stack.95 = f32[8,128]{1,0:T(8,128)} concatenate(f32[1,128]{1,0:T(1,128)S(1)} %get-tuple-element.20, f32[1,128]{1,0:T(1,128)S(1)} %get-tuple-element.19, f32[1,128]{1,0:T(1,128)S(1)} %get-tuple-element.18, f32[1,128]{1,0:T(1,128)S(1)} %get-tuple-element.17, f32[1,128]{1,0:T(1,128)S(1)} %get-tuple-element.16, f32[1,128]{1,0:T(1,128)S(1)} %get-tuple-element.15, ...), dimensions={0} | concatenate | bytes 8192 | tf_op jit(solution)/shard_map/stack | solution.py:35
  (52 shorter events, 0.4 us)
Async XLA Ops:
  0.6 1.3 %copy-start = (f32[192,128]{1,0:T(8,128)S(1)}, f32[192,128]{1,0:T(8,128)}, u32[]{:S(2)}) copy-start(f32[192,128]{1,0:T(8,128)} %param.17) | copy-start | bytes 294916
  0.6 1.3 %copy-start.2 = (f32[192,128]{1,0:T(8,128)S(1)}, f32[192,128]{1,0:T(8,128)}, u32[]{:S(2)}) copy-start(f32[192,128]{1,0:T(8,128)} %param.16) | copy-start | bytes 294916
  2.0 0.9 %copy-start.1 = (f32[192,128]{1,0:T(8,128)S(1)}, f32[192,128]{1,0:T(8,128)}, u32[]{:S(2)}) copy-start(f32[192,128]{1,0:T(8,128)} %param.18) | copy-start | bytes 294916
  3.4 0.7 %copy-start.8 = (s32[192]{0:T(256)S(1)}, s32[192]{0:T(256)}, u32[]{:S(2)}) copy-start(s32[192]{0:T(256)} %param.20) | copy-start | bytes 2308
  3.4 0.7 %copy-start.9 = (s32[192]{0:T(256)S(1)}, s32[192]{0:T(256)}, u32[]{:S(2)}) copy-start(s32[192]{0:T(256)} %param.19) | copy-start | bytes 2308
  5.6 0.8 %copy-start.4 = (f32[1,1,128,128]{3,2,1,0:T(8,128)S(1)}, f32[1,1,128,128]{3,2,1,0:T(8,128)}, u32[]{:S(2)}) copy-start(f32[1,1,128,128]{3,2,1,0:T(8,128)} %param.26) | copy-start | bytes 196612
  5.7 3.4 %collective-permute-start = (f32[8,2,8,1024]{3,2,1,0:T(8,128)S(1)}, f32[8,2,8,1024]{3,2,1,0:T(8,128)S(1)}, u32[]{:S(2)}, u32[]{:S(2)}) collective-permute-start(f32[8,2,8,1024]{3,2,1,0:T(8,128)S(1)} %dynamic-slice_bitcast_fusion), channel_id=1, source_target_pairs={{0,1},{1,0},{2,3},{3,2},{4,5},{5,4},{6,7},{7,6},{8,9},{9,8},{10,11... | collective-permute-start | bytes 1572872 | tf_op jit(solution)/shard_map/ppermute | solution.py:96
  6.5 0.7 %copy-start.11 = (f32[1,1,128]{2,1,0:T(1,128)S(1)}, f32[1,1,128]{2,1,0:T(1,128)}, u32[]{:S(2)}) copy-start(f32[1,1,128]{2,1,0:T(1,128)} %param.28) | copy-start | bytes 1540
  7.1 0.7 %copy-start.10 = (f32[1,1,128]{2,1,0:T(1,128)S(1)}, f32[1,1,128]{2,1,0:T(1,128)}, u32[]{:S(2)}) copy-start(f32[1,1,128]{2,1,0:T(1,128)} %param.27) | copy-start | bytes 1540
  7.8 0.7 %copy-start.12 = (s32[8]{0:T(128)S(1)}, s32[8]{0:T(128)}, u32[]{:S(2)}) copy-start(s32[8]{0:T(128)} %param.25) | copy-start | bytes 100
  8.5 0.7 %copy-start.13 = (s32[8]{0:T(128)S(1)}, s32[8]{0:T(128)}, u32[]{:S(2)}) copy-start(s32[8]{0:T(128)} %param.24) | copy-start | bytes 100
  10.0 9.9 %copy-start.3 = (f32[8,128,128]{2,1,0:T(8,128)S(1)}, f32[8,128,128]{2,1,0:T(8,128)}, u32[]{:S(2)}) copy-start(f32[8,128,128]{2,1,0:T(8,128)} %param.21) | copy-start | bytes 1572868
  10.0 23.6 %all-to-all-start = ((f32[16,8,1024]{2,1,0:T(8,128)}), f32[16,8,1024]{2,1,0:T(8,128)S(1)}, u32[]{:S(2)}, u32[]{:S(2)}) async-start(f32[16,8,1024]{2,1,0:T(8,128)} %bitcast.20), calls=%async_computation | async-start | bytes 1048576 | tf_op jit(solution)/shard_map/all_to_all | solution.py:97
  33.6 1.0 %copy-start.5 = (f32[8,128]{1,0:T(8,128)S(1)}, f32[8,128]{1,0:T(8,128)}, u32[]{:S(2)}) copy-start(f32[8,128]{1,0:T(8,128)} %param.22) | copy-start | bytes 12292
  33.6 1.0 %copy-start.6 = (f32[8,128]{1,0:T(8,128)S(1)}, f32[8,128]{1,0:T(8,128)}, u32[]{:S(2)}) copy-start(f32[8,128]{1,0:T(8,128)} %param.23) | copy-start | bytes 12292
  35.9 11.1 %all-to-all-start.1 = ((f32[32,8,128]{2,1,0:T(8,128)}), f32[32,8,128]{2,1,0:T(8,128)S(1)}, u32[]{:S(2)}, u32[]{:S(2)}) async-start(f32[32,8,128]{2,1,0:T(8,128)} %broadcast_in_dim.96), calls=%async_computation.1 | async-start | bytes 262144 | tf_op jit(solution)/shard_map/all_to_all | solution.py:167
  49.3 0.7 %copy-start.7 = (f32[1,8]{1,0:T(1,128)S(1)}, f32[1,8]{1,0:T(1,128)}, u32[]{:S(2)}) copy-start(f32[1,8]{1,0:T(1,128)} %param.29) | copy-start | bytes 100

commit v13 on v12

--- a/solution.py
+++ b/solution.py
@@ -162,7 +162,6 @@
         )
         for offset, value in enumerate(columns):
             static_tile = static_tile + jnp.where(lane == sub_steps + offset, value, 0.0)
-        static_tile = lax.optimization_barrier(static_tile)
         tile = jnp.pad(outlet, ((0, 0), (0, reaches - sub_steps))) + static_tile
         every = lax.all_to_all(
             jnp.broadcast_to(tile[None], (shards,) + tile.shape), grid, split_axis=0, concat_axis=0, tiled=True

time: 52.5 us -> 51.4 us (0.979)
  waiting for transfers between devices: 20.6 us -> 19.7 us
    all_to_all x1, waiting for transfers between devices: 13 us -> 10.6 us  [pair_exchange(): lax.all_to_all(chip_sum.reshape(chains * across, blocks, width), ('basin'...]
    ppermute x1, waiting for transfers between devices: 0.01 us -> 1.54 us  [pair_exchange(): chip_sum = keep_side + lax.ppermute(give_side, 'core', [(0, 1), (1, 0)])]
  transfers between devices with their start and end apart: 3 -> 3, of which waited for: 2 -> 3; matrix products, arithmetic and copies ran while one was open for 8% -> 8% of each run, Pallas kernels for 0% -> 0%
where the time goes in v13:
time: 51.4 us; the launch traced here: 51 us
  waiting for transfers between devices  19.7 us (38%)
  starting transfers between devices  11.8 us (23%)
  local copies, waits for them, and re-layouts  9.18 us (18%)
  other arithmetic  7.44 us (14%)
  matrix products  1.83 us (4%)
  between operations  1.01 us (2%)
    all_to_all x1, waiting for transfers between devices, pair_exchange(): lax.all_to_all(chip_sum.reshape(chains * across, blocks, width), ('basin'...  10.6 us
    all_to_all x1, starting transfers between devices, pair_exchange(): lax.all_to_all(chip_sum.reshape(chains * across, blocks, width), ('basin'...  8.37 us
    all_to_all x1, waiting for transfers between devices, local(): lax.all_to_all(jnp.broadcast_to(tile[None], (shards,) + tile.shape), grid...  7.58 us
    unnamed x37, local copies, waits for them, and re-layouts  5.07 us
    all_to_all x1, starting transfers between devices, local(): lax.all_to_all(jnp.broadcast_to(tile[None], (shards,) + tile.shape), grid...  2.92 us
    ppermute x1, waiting for transfers between devices, pair_exchange(): chip_sum = keep_side + lax.ppermute(give_side, 'core', [(0, 1), (1, 0)])  1.54 us
    select_n x1, other arithmetic, local(): jnp.where(lane == sub_steps + offset, value, 0.0)  1.3 us
    add x4, other arithmetic, route_series(): flow = keep * flow + (1.0 - keep) * mixed[..., sub_step, :]  1.06 us
  transfers between devices with their start and end apart: 3, of which 3 were waited for; matrix products, arithmetic and copies ran while one was open for 8% of the time, Pallas kernels for 0%

profile of v13, /device:TPU:0, one launch (start us, length us, event | category | flops | bytes accessed | tf_op | source)
XLA Modules:
  0.0 51.0 jit_solution(17954218434961394676)
XLA Ops:
  0.7 1.3 %copy.178 = f32[192,8,128]{2,0,1:T(8,128)S(1)} copy(f32[192,8,128]{2,1,0:T(8,128)} %param.15) | data formatting | bytes 1572864 | tf_op args[0]
  2.0 0.9 %copy-done.1 = f32[192,128]{1,0:T(8,128)S(1)} copy-done((f32[192,128]{1,0:T(8,128)S(1)}, f32[192,128]{1,0:T(8,128)}, u32[]{:S(2)}) %copy-start.1) | copy-done | bytes 98328
  2.9 0.1 bitcast_dynamic-update-slice_fusion.6
  3.0 0.1 bitcast_dynamic-update-slice_fusion.5
  3.0 0.1 bitcast_dynamic-update-slice_fusion.4
  3.1 0.1 bitcast_dynamic-update-slice_fusion.3
  3.3 0.1 bitcast_dynamic-update-slice_fusion.2
  3.3 0.1 bitcast_dynamic-update-slice_fusion.1
  3.4 0.1 bitcast_dynamic-update-slice_fusion
  3.5 0.6 %copy-done.8 = s32[192]{0:T(256)S(1)} copy-done((s32[192]{0:T(256)S(1)}, s32[192]{0:T(256)}, u32[]{:S(2)}) %copy-start.8) | copy-done | bytes 792
  4.1 0.7 %fusion.1 = f32[256,8,128]{2,0,1:T(8,128)S(1)} fusion(f32[8,192,128]{2,1,0:T(8,128)S(1)} %bitcast_dynamic-update-slice_fusion, s32[192]{0:T(256)S(1)} %multiply_add_fusion.9), kind=kOutput, calls=%fused_computation.6 | convolution fusion | flops 604028928 | bytes 1835776 | tf_op jit(solution)/shard_map/gk,tkc->gtc/dot_general | solution.py:63
  4.8 0.6 %copy.134 = f32[256,8,128]{2,1,0:T(8,128)S(1)} copy(f32[256,8,128]{2,0,1:T(8,128)S(1)} %fusion.1) | data formatting | bytes 2097152 | tf_op jit(solution)/shard_map/gk,tkc->gtc/dot_general | solution.py:63
  5.5 0.2 reshape_reshape.3
  5.7 0.5 %collective-permute-start = (f32[8,2,8,1024]{3,2,1,0:T(8,128)S(1)}, f32[8,2,8,1024]{3,2,1,0:T(8,128)S(1)}, u32[]{:S(2)}, u32[]{:S(2)}) collective-permute-start(f32[8,2,8,1024]{3,2,1,0:T(8,128)S(1)} %dynamic-slice_bitcast_fusion), channel_id=1, source_target_pairs={{0,1},{1,0},{2,3},{3,2},{4,5},{5,4},{6,7},{7,6},{8,9},{9,8},{10,11... | collective-permute-start | bytes 1572872 | tf_op jit(solution)/shard_map/ppermute | solution.py:96
  6.2 1.5 %collective-permute-done = f32[8,2,8,1024]{3,2,1,0:T(8,128)S(1)} collective-permute-done((f32[8,2,8,1024]{3,2,1,0:T(8,128)S(1)}, f32[8,2,8,1024]{3,2,1,0:T(8,128)S(1)}, u32[]{:S(2)}, u32[]{:S(2)}) %collective-permute-start) | collective-permute-done | bytes 524320 | tf_op jit(solution)/shard_map/ppermute | solution.py:96
  7.7 0.8 %bitcast_add_fusion = f32[8,2,8,1024]{3,2,1,0:T(8,128)} fusion(f32[8,2,8,1024]{3,2,1,0:T(8,128)S(1)} %collective-permute-done, f32[8,2,2,8,1024]{4,3,2,1,0:T(8,128)S(1)} %reshape_reshape.3, s32[]{:T(128)S(6)} %select_n.173), kind=kLoop, calls=%fused_computation.2 | loop fusion | flops 131072 | bytes 1572868 | tf_op jit(solution)/shard_map/add | solution.py:96
  8.6 8.4 %all-to-all-start = ((f32[16,8,1024]{2,1,0:T(8,128)}), f32[16,8,1024]{2,1,0:T(8,128)S(1)}, u32[]{:S(2)}, u32[]{:S(2)}) async-start(f32[16,8,1024]{2,1,0:T(8,128)} %bitcast.20), calls=%async_computation | async-start | bytes 1048576 | tf_op jit(solution)/shard_map/all_to_all | solution.py:97
  17.0 0.1 reshape_squeeze.4
  17.1 0.6 %copy-done.11 = f32[1,1,128]{2,1,0:T(1,128)S(1)} copy-done((f32[1,1,128]{2,1,0:T(1,128)S(1)}, f32[1,1,128]{2,1,0:T(1,128)}, u32[]{:S(2)}) %copy-start.11) | copy-done | bytes 536
  17.8 0.6 %slice.191 = f32[1,1,1]{2,1,0:T(1,128)} slice(f32[1,1,128]{2,1,0:T(1,128)S(1)} %copy-done.11), slice={[0:1], [0:1], [127:128]} | slice | bytes 8 | tf_op jit(solution)/shard_map/slice | solution.py:157
  18.3 0.1 copy-done.10
  18.4 0.6 %slice.190 = f32[1,1,1]{2,1,0:T(1,128)} slice(f32[1,1,128]{2,1,0:T(1,128)S(1)} %copy-done.10), slice={[0:1], [0:1], [127:128]} | slice | bytes 8 | tf_op jit(solution)/shard_map/slice | solution.py:156
  19.0 0.1 copy-done.12
  19.1 0.7 %copy-done.13 = s32[8]{0:T(128)S(1)} copy-done((s32[8]{0:T(128)S(1)}, s32[8]{0:T(128)}, u32[]{:S(2)}) %copy-start.13) | copy-done | bytes 56
  19.8 1.3 %compare_select_fusion = (f32[128]{0:T(128)S(1)}, f32[128]{0:T(128)S(1)}) fusion(f32[]{:T(128)} %bitcast.43, f32[]{:T(128)} %bitcast.42), kind=kLoop, calls=%fused_computation.144 | loop fusion | flops 512 | bytes 1032 | tf_op jit(solution)/shard_map/jit(_where)/select_n | solution.py:164
  21.1 0.7 %add_subtract_fusion = f32[192,128]{1,0:T(8,128)} fusion(f32[8,192,128]{2,1,0:T(8,128)S(1)} %bitcast.446, f32[192,128]{1,0:T(8,128)S(1)} %copy-done.1, f32[192,128]{1,0:T(8,128)S(1)} %copy-done, f32[192,128]{1,0:T(8,128)S(1)} %get-tuple-element.34), kind=kLoop, calls=%fused_computation.31 | loop fusion | flops 319488 | bytes 589824 | tf_op jit(solution)/shard_map/sub | solution.py:24
  21.8 10.6 %all-to-all-done = f32[16,8,1024]{2,1,0:T(8,128)S(1)} async-done(((f32[16,8,1024]{2,1,0:T(8,128)}), f32[16,8,1024]{2,1,0:T(8,128)S(1)}, u32[]{:S(2)}, u32[]{:S(2)}) %all-to-all-start) | async-done | bytes 524320 | tf_op jit(solution)/shard_map/all_to_all | solution.py:97
  32.4 0.9 %fusion.9 = f32[8,8,128]{2,1,0:T(8,128)S(1)} fusion(f32[8,128,128]{2,1,0:T(8,128)S(1)} %copy-done.3, f32[1,8,8,128]{3,1,2,0:T(8,128)S(1)} %bitcast.451), kind=kOutput, calls=%fused_computation.57 | convolution fusion | flops 12582912 | bytes 589824 | tf_op jit(solution)/shard_map/brc,btc->btr/dot_general | solution.py:134
  33.3 0.1 fusion.11
  33.4 0.1 fusion.32
  33.5 0.3 fusion.31
  33.9 0.1 copy.150
  34.0 0.1 add_add_fusion
  34.1 0.6 %broadcast_in_dim.96 = f32[32,8,128]{2,1,0:T(8,128)} broadcast(f32[8,128]{1,0:T(8,128)S(1)} %add_add_fusion), dimensions={1,2} | broadcast | bytes 135168 | tf_op jit(solution)/shard_map/broadcast_in_dim | solution.py:167
  34.7 2.9 %all-to-all-start.1 = ((f32[32,8,128]{2,1,0:T(8,128)}), f32[32,8,128]{2,1,0:T(8,128)S(1)}, u32[]{:S(2)}, u32[]{:S(2)}) async-start(f32[32,8,128]{2,1,0:T(8,128)} %broadcast_in_dim.96), calls=%async_computation.1 | async-start | bytes 262144 | tf_op jit(solution)/shard_map/all_to_all | solution.py:166
  37.7 0.6 %multiply_add_fusion.8 = f32[8,128]{1,0:T(8,128)} fusion(f32[8,128]{1,0:T(8,128)S(1)} %bitcast.464, f32[8,128]{1,0:T(8,128)S(1)} %copy-done.5, f32[8,128]{1,0:T(8,128)S(1)} %bitcast.465, f32[8,128]{1,0:T(8,128)S(1)} %bitcast.463, f32[8,128]{1,0:T(8,128)S(1)} %bitcast.462, f32[8,128]{1,0:T(8,128)S(1)} %bitcast.461, f32[8,128]{1,0:T(8,128)S(1)} %bitcast.460, ...), kind=kLoop, calls=%fused_computation.122 | loop fusion | flops 25600 | bytes 45056 | tf_op jit(solution)/shard_map/add | solution.py:33
  38.3 7.6 %all-to-all-done.1 = f32[32,8,128]{2,1,0:T(8,128)S(1)} async-done(((f32[32,8,128]{2,1,0:T(8,128)}), f32[32,8,128]{2,1,0:T(8,128)S(1)}, u32[]{:S(2)}, u32[]{:S(2)}) %all-to-all-start.1) | async-done | bytes 131104 | tf_op jit(solution)/shard_map/all_to_all | solution.py:166
  45.9 0.2 slice_reduce_fusion
  46.1 0.1 eq.97
  46.1 0.7 %fusion.5 = pred[32,8]{1,0:T(8,128)(4,1)S(1)} fusion(f32[32,8,128]{2,1,0:T(8,128)S(1)} %all-to-all-done.1, f32[]{:T(128)S(6)} %convert_element_type.37), kind=kLoop, calls=%fused_computation.12 | loop fusion | flops 256 | bytes 1284 | tf_op jit(solution)/shard_map/eq | solution.py:213
  46.8 0.1 eq.96
  46.9 0.1 slice.234
  47.0 0.1 reshape.300
  47.1 0.1 copy.170
  47.2 0.1 copy.152
  47.3 0.2 multiply_reduce_fusion.2
  47.5 0.1 fusion.4
  47.7 0.3 multiply_reduce_fusion
  48.0 0.1 multiply_reduce_fusion.1
  48.1 0.1 multiply_select_fusion
  48.2 0.6 %copy-done.7 = f32[1,8]{1,0:T(1,128)S(1)} copy-done((f32[1,8]{1,0:T(1,128)S(1)}, f32[1,8]{1,0:T(1,128)}, u32[]{:S(2)}) %copy-start.7) | copy-done | bytes 56
  48.9 0.1 fusion.14
  49.0 0.1 multiply_add_fusion
  49.1 0.1 stack.94
  49.2 0.1 fusion.16
  49.3 0.1 fusion.18
  49.4 0.1 fusion.20
  49.5 0.1 fusion.22
  49.7 0.1 fusion.24
  49.8 0.1 fusion.26
  49.9 0.1 fusion.28
  50.1 0.2 fusion.7
  50.3 0.1 fusion.66
  50.4 0.6 %stack.95 = f32[8,128]{1,0:T(8,128)} concatenate(f32[1,128]{1,0:T(1,128)S(1)} %get-tuple-element.20, f32[1,128]{1,0:T(1,128)S(1)} %get-tuple-element.19, f32[1,128]{1,0:T(1,128)S(1)} %get-tuple-element.18, f32[1,128]{1,0:T(1,128)S(1)} %get-tuple-element.17, f32[1,128]{1,0:T(1,128)S(1)} %get-tuple-element.16, f32[1,128]{1,0:T(1,128)S(1)} %get-tuple-element.15, ...), dimensions={0} | concatenate | bytes 8192 | tf_op jit(solution)/shard_map/stack | solution.py:35
  (51 shorter events, 0.4 us)
Async XLA Ops:
  0.6 1.3 %copy-start = (f32[192,128]{1,0:T(8,128)S(1)}, f32[192,128]{1,0:T(8,128)}, u32[]{:S(2)}) copy-start(f32[192,128]{1,0:T(8,128)} %param.17) | copy-start | bytes 294916
  0.6 1.3 %copy-start.2 = (f32[192,128]{1,0:T(8,128)S(1)}, f32[192,128]{1,0:T(8,128)}, u32[]{:S(2)}) copy-start(f32[192,128]{1,0:T(8,128)} %param.16) | copy-start | bytes 294916
  2.0 0.9 %copy-start.1 = (f32[192,128]{1,0:T(8,128)S(1)}, f32[192,128]{1,0:T(8,128)}, u32[]{:S(2)}) copy-start(f32[192,128]{1,0:T(8,128)} %param.18) | copy-start | bytes 294916
  3.4 0.7 %copy-start.8 = (s32[192]{0:T(256)S(1)}, s32[192]{0:T(256)}, u32[]{:S(2)}) copy-start(s32[192]{0:T(256)} %param.20) | copy-start | bytes 2308
  3.4 0.7 %copy-start.9 = (s32[192]{0:T(256)S(1)}, s32[192]{0:T(256)}, u32[]{:S(2)}) copy-start(s32[192]{0:T(256)} %param.19) | copy-start | bytes 2308
  5.7 2.1 %collective-permute-start = (f32[8,2,8,1024]{3,2,1,0:T(8,128)S(1)}, f32[8,2,8,1024]{3,2,1,0:T(8,128)S(1)}, u32[]{:S(2)}, u32[]{:S(2)}) collective-permute-start(f32[8,2,8,1024]{3,2,1,0:T(8,128)S(1)} %dynamic-slice_bitcast_fusion), channel_id=1, source_target_pairs={{0,1},{1,0},{2,3},{3,2},{4,5},{5,4},{6,7},{7,6},{8,9},{9,8},{10,11... | collective-permute-start | bytes 1572872 | tf_op jit(solution)/shard_map/ppermute | solution.py:96
  8.6 8.4 %copy-start.4 = (f32[1,1,128,128]{3,2,1,0:T(8,128)S(1)}, f32[1,1,128,128]{3,2,1,0:T(8,128)}, u32[]{:S(2)}) copy-start(f32[1,1,128,128]{3,2,1,0:T(8,128)} %param.26) | copy-start | bytes 196612
  8.6 8.5 %copy-start.3 = (f32[8,128,128]{2,1,0:T(8,128)S(1)}, f32[8,128,128]{2,1,0:T(8,128)}, u32[]{:S(2)}) copy-start(f32[8,128,128]{2,1,0:T(8,128)} %param.21) | copy-start | bytes 1572868
  8.6 23.8 %all-to-all-start = ((f32[16,8,1024]{2,1,0:T(8,128)}), f32[16,8,1024]{2,1,0:T(8,128)S(1)}, u32[]{:S(2)}, u32[]{:S(2)}) async-start(f32[16,8,1024]{2,1,0:T(8,128)} %bitcast.20), calls=%async_computation | async-start | bytes 1048576 | tf_op jit(solution)/shard_map/all_to_all | solution.py:97
  17.1 0.7 %copy-start.11 = (f32[1,1,128]{2,1,0:T(1,128)S(1)}, f32[1,1,128]{2,1,0:T(1,128)}, u32[]{:S(2)}) copy-start(f32[1,1,128]{2,1,0:T(1,128)} %param.28) | copy-start | bytes 1540
  17.8 0.7 %copy-start.10 = (f32[1,1,128]{2,1,0:T(1,128)S(1)}, f32[1,1,128]{2,1,0:T(1,128)}, u32[]{:S(2)}) copy-start(f32[1,1,128]{2,1,0:T(1,128)} %param.27) | copy-start | bytes 1540
  18.4 0.7 %copy-start.12 = (s32[8]{0:T(128)S(1)}, s32[8]{0:T(128)}, u32[]{:S(2)}) copy-start(s32[8]{0:T(128)} %param.25) | copy-start | bytes 100
  19.1 0.7 %copy-start.13 = (s32[8]{0:T(128)S(1)}, s32[8]{0:T(128)}, u32[]{:S(2)}) copy-start(s32[8]{0:T(128)} %param.24) | copy-start | bytes 100
  32.4 1.0 %copy-start.5 = (f32[8,128]{1,0:T(8,128)S(1)}, f32[8,128]{1,0:T(8,128)}, u32[]{:S(2)}) copy-start(f32[8,128]{1,0:T(8,128)} %param.22) | copy-start | bytes 12292
  32.4 1.0 %copy-start.6 = (f32[8,128]{1,0:T(8,128)S(1)}, f32[8,128]{1,0:T(8,128)}, u32[]{:S(2)}) copy-start(f32[8,128]{1,0:T(8,128)} %param.23) | copy-start | bytes 12292
  34.7 11.2 %all-to-all-start.1 = ((f32[32,8,128]{2,1,0:T(8,128)}), f32[32,8,128]{2,1,0:T(8,128)S(1)}, u32[]{:S(2)}, u32[]{:S(2)}) async-start(f32[32,8,128]{2,1,0:T(8,128)} %broadcast_in_dim.96), calls=%async_computation.1 | async-start | bytes 262144 | tf_op jit(solution)/shard_map/all_to_all | solution.py:166
  48.2 0.7 %copy-start.7 = (f32[1,8]{1,0:T(1,128)S(1)}, f32[1,8]{1,0:T(1,128)}, u32[]{:S(2)}) copy-start(f32[1,8]{1,0:T(1,128)} %param.29) | copy-start | bytes 100

commit v14 on v13

--- a/solution.py
+++ b/solution.py
@@ -1,6 +1,10 @@
+import functools
+
 import jax
 import jax.numpy as jnp
 from jax import lax
+from jax.experimental import pallas as pl
+from jax.experimental.pallas import tpu as pltpu
 from jax.sharding import Mesh, PartitionSpec as P
 
 
@@ -24,6 +28,36 @@
         water = (1.0 - evap_rate) * water + rain_now - runoff_now
         runoff_steps.append(runoff_now)
     return (jnp.stack(runoff_steps, axis=0), water)
+
+
+def land_kernel(sub_steps, rain_ref, soil_ref, capacity_ref, evap_ref, runoff_ref, water_ref):
+    tiles = soil_ref.shape[0]
+    water = soil_ref[...]
+    capacity = capacity_ref[...]
+    evap_rate = evap_ref[...]
+    for sub_step in range(sub_steps):
+        rain_now = rain_ref[pl.ds(sub_step, tiles, stride=sub_steps), :]
+        runoff_now = rain_now * water / (water + capacity)
+        water = (1.0 - evap_rate) * water + rain_now - runoff_now
+        runoff_ref[sub_step] = runoff_now
+    water_ref[...] = water
+
+
+def land_update_kernel(precip, soil_water, capacity, evap_rate):
+    tiles, sub_steps, reaches = precip.shape
+    vmem = pl.BlockSpec(memory_space=pltpu.VMEM)
+    return pl.pallas_call(
+        functools.partial(land_kernel, sub_steps),
+        out_shape=(
+            jax.ShapeDtypeStruct((sub_steps, tiles, reaches), precip.dtype),
+            jax.ShapeDtypeStruct((tiles, reaches), precip.dtype),
+        ),
+        in_specs=[vmem] * 4,
+        out_specs=(vmem, vmem),
+        cost_estimate=pl.CostEstimate(
+            flops=10 * precip.size, transcendentals=0, bytes_accessed=4 * (2 * precip.size + 4 * soil_water.size)
+        ),
+    )(precip.reshape(tiles * sub_steps, reaches), soil_water, capacity, evap_rate)
 
 
 def route_series(mixed, keep, previous):
@@ -129,7 +163,7 @@
     keep_main = main_keep[0, 0]
     prev_main = main_prev[0, 0]
 
-    runoff_t, water = land_update_t(jnp.transpose(precip, (1, 0, 2)), soil_water, capacity, evap_rate)
+    runoff_t, water = land_update_kernel(precip, soil_water, capacity, evap_rate)
     lateral = gather_lateral(runoff_t, tile_dest, tile_block, blocks, shards)
     trib_mixed = jnp.einsum(
         "brc,btc->btr",

time: 51.4 us -> 52.8 us (1.027)
  Pallas kernels: 0 us -> 2.38 us
  local copies, waits for them, and re-layouts: 9.18 us -> 7.04 us
  matrix products: 1.83 us -> 2.96 us
  waiting for transfers between devices: 19.7 us -> 20.4 us
  other arithmetic: 7.44 us -> 6.83 us
    pallas_call x0 -> x1, Pallas kernels: none -> 2.38 us  [land_update_kernel(): pl.pallas_call(functools.partial(land_kernel, sub_steps), out_shape=(jax....]
    unnamed x37 -> x28, local copies, waits for them, and re-layouts: 5.07 us -> 2.92 us
    dot_general x1, matrix products: 0.7 us -> 1.83 us  [gather_lateral(): jnp.einsum('gk,tkc->gtc', pick, runoff_t, precision=lax.Precision.HIGHEST)]
    all_to_all x1, waiting for transfers between devices: 10.6 us -> 11.3 us  [pair_exchange(): lax.all_to_all(chip_sum.reshape(chains * across, blocks, width), ('basin'...]
    sub x1 -> x0, other arithmetic: 0.7 us -> none  [land_update_t(): water = (1.0 - evap_rate) * water + rain_now - runoff_now]
    add x1, other arithmetic: 0.01 us -> 0.68 us  [gather_lateral(): block_ids = tile_dest * blocks + tile_block]
    unnamed x7 -> x0, other arithmetic: 0.53 us -> none
  transfers between devices with their start and end apart: 3 -> 3, of which waited for: 3 -> 3; matrix products, arithmetic and copies ran while one was open for 8% -> 6% of each run, Pallas kernels for 0% -> 0%
where the time goes in v14:
time: 52.8 us; the launch traced here: 52.3 us
  waiting for transfers between devices  20.4 us (39%)
  starting transfers between devices  11.8 us (22%)
  local copies, waits for them, and re-layouts  7.04 us (13%)
  other arithmetic  6.83 us (13%)
  matrix products  2.96 us (6%)
  Pallas kernels  2.38 us (5%)
  between operations  0.93 us (2%)
    all_to_all x1, waiting for transfers between devices, pair_exchange(): lax.all_to_all(chip_sum.reshape(chains * across, blocks, width), ('basin'...  11.3 us
    all_to_all x1, starting transfers between devices, pair_exchange(): lax.all_to_all(chip_sum.reshape(chains * across, blocks, width), ('basin'...  8.36 us
    all_to_all x1, waiting for transfers between devices, local(): lax.all_to_all(jnp.broadcast_to(tile[None], (shards,) + tile.shape), grid...  7.58 us
    unnamed x28, local copies, waits for them, and re-layouts  2.92 us
    all_to_all x1, starting transfers between devices, local(): lax.all_to_all(jnp.broadcast_to(tile[None], (shards,) + tile.shape), grid...  2.92 us
    pallas_call x1, Pallas kernels, land_update_kernel(): pl.pallas_call(functools.partial(land_kernel, sub_steps), out_shape=(jax....  2.38 us
    dot_general x1, matrix products, gather_lateral(): jnp.einsum('gk,tkc->gtc', pick, runoff_t, precision=lax.Precision.HIGHEST)  1.83 us
    ppermute x1, waiting for transfers between devices, pair_exchange(): chip_sum = keep_side + lax.ppermute(give_side, 'core', [(0, 1), (1, 0)])  1.54 us
  transfers between devices with their start and end apart: 3, of which 3 were waited for; matrix products, arithmetic and copies ran while one was open for 6% of the time, Pallas kernels for 0%

profile of v14, /device:TPU:0, one launch (start us, length us, event | category | flops | bytes accessed | tf_op | source)
XLA Modules:
  0.0 52.3 jit_solution(10153696161012531476)
XLA Ops:
  0.6 0.0 copy-start.5
  0.6 0.7 %copy-done.5 = s32[192]{0:T(256)S(1)} copy-done((s32[192]{0:T(256)S(1)}, s32[192]{0:T(256)}, u32[]{:S(2)}) %copy-start.5) | copy-done | bytes 792
  1.3 0.7 %multiply_add_fusion.9 = s32[192]{0:T(256)S(1)} fusion(s32[192]{0:T(256)S(1)} %copy-done.5, s32[192]{0:T(256)} %param.19), kind=kLoop, calls=%fused_computation.114 | loop fusion | flops 384 | bytes 2304 | tf_op jit(solution)/shard_map/add | solution.py:93
  2.0 2.4 %shard_map.166 = (f32[8,192,128]{2,1,0:T(8,128)}, f32[192,128]{1,0:T(8,128)}) custom-call(f32[1536,128]{1,0:T(8,128)} %bitcast.308, f32[192,128]{1,0:T(8,128)} %soil_ref.1, f32[192,128]{1,0:T(8,128)} %capacity_ref.1, f32[192,128]{1,0:T(8,128)} %evap_ref.1), custom_call_target="tpu_custom_call" | custom-call | flops 1966080 | bytes 1966080 | tf_op jit(solution)/shard_map/pallas_call | solution.py:49
  4.4 1.8 %fusion.1 = f32[256,8,128]{2,0,1:T(8,128)S(1)} fusion(f32[8,192,128]{2,1,0:T(8,128)} %get-tuple-element.6, s32[192]{0:T(256)S(1)} %multiply_add_fusion.9), kind=kOutput, calls=%fused_computation.5 | convolution fusion | flops 604028928 | bytes 1835776 | tf_op jit(solution)/shard_map/gk,tkc->gtc/dot_general | solution.py:97
  6.2 0.6 %copy.128 = f32[256,8,128]{2,1,0:T(8,128)S(1)} copy(f32[256,8,128]{2,0,1:T(8,128)S(1)} %fusion.1) | data formatting | bytes 2097152 | tf_op jit(solution)/shard_map/gk,tkc->gtc/dot_general | solution.py:97
  6.8 0.2 reshape_reshape.3
  7.1 0.5 collective-permute-start
  7.6 1.5 %collective-permute-done = f32[8,2,8,1024]{3,2,1,0:T(8,128)S(1)} collective-permute-done((f32[8,2,8,1024]{3,2,1,0:T(8,128)S(1)}, f32[8,2,8,1024]{3,2,1,0:T(8,128)S(1)}, u32[]{:S(2)}, u32[]{:S(2)}) %collective-permute-start) | collective-permute-done | bytes 524320 | tf_op jit(solution)/shard_map/ppermute | solution.py:130
  9.1 0.8 %bitcast_add_fusion = f32[8,2,8,1024]{3,2,1,0:T(8,128)} fusion(f32[8,2,8,1024]{3,2,1,0:T(8,128)S(1)} %collective-permute-done, f32[8,2,2,8,1024]{4,3,2,1,0:T(8,128)S(1)} %reshape_reshape.3, s32[]{:T(128)S(6)} %select_n.173), kind=kLoop, calls=%fused_computation.1 | loop fusion | flops 131072 | bytes 1572868 | tf_op jit(solution)/shard_map/add | solution.py:130
  10.0 8.4 %all-to-all-start = ((f32[16,8,1024]{2,1,0:T(8,128)}), f32[16,8,1024]{2,1,0:T(8,128)S(1)}, u32[]{:S(2)}, u32[]{:S(2)}) async-start(f32[16,8,1024]{2,1,0:T(8,128)} %bitcast.4), calls=%async_computation | async-start | bytes 1048576 | tf_op jit(solution)/shard_map/all_to_all | solution.py:131
  18.4 0.0 copy-done.1
  18.4 0.1 reshape_squeeze.4
  18.5 0.0 copy-done
  18.5 0.6 %copy-done.7 = f32[1,1,128]{2,1,0:T(1,128)S(1)} copy-done((f32[1,1,128]{2,1,0:T(1,128)S(1)}, f32[1,1,128]{2,1,0:T(1,128)}, u32[]{:S(2)}) %copy-start.7) | copy-done | bytes 536
  19.1 0.6 %slice.159 = f32[1,1,1]{2,1,0:T(1,128)} slice(f32[1,1,128]{2,1,0:T(1,128)S(1)} %copy-done.7), slice={[0:1], [0:1], [127:128]} | slice | bytes 8 | tf_op jit(solution)/shard_map/slice | solution.py:191
  19.7 0.1 copy-done.6
  19.8 0.6 %slice.158 = f32[1,1,1]{2,1,0:T(1,128)} slice(f32[1,1,128]{2,1,0:T(1,128)S(1)} %copy-done.6), slice={[0:1], [0:1], [127:128]} | slice | bytes 8 | tf_op jit(solution)/shard_map/slice | solution.py:190
  20.4 0.1 copy-done.8
  20.5 0.7 %copy-done.9 = s32[8]{0:T(128)S(1)} copy-done((s32[8]{0:T(128)S(1)}, s32[8]{0:T(128)}, u32[]{:S(2)}) %copy-start.9) | copy-done | bytes 56
  21.1 1.3 %compare_select_fusion = (f32[128]{0:T(128)S(1)}, f32[128]{0:T(128)S(1)}) fusion(f32[]{:T(128)} %bitcast.27, f32[]{:T(128)} %bitcast.26), kind=kLoop, calls=%fused_computation.111 | loop fusion | flops 512 | bytes 1032 | tf_op jit(solution)/shard_map/jit(_where)/select_n | solution.py:198
  22.4 11.3 %all-to-all-done = f32[16,8,1024]{2,1,0:T(8,128)S(1)} async-done(((f32[16,8,1024]{2,1,0:T(8,128)}), f32[16,8,1024]{2,1,0:T(8,128)S(1)}, u32[]{:S(2)}, u32[]{:S(2)}) %all-to-all-start) | async-done | bytes 524320 | tf_op jit(solution)/shard_map/all_to_all | solution.py:131
  33.8 0.0 copy-start.2
  33.8 0.0 copy-start.3
  33.8 0.9 %fusion.9 = f32[8,8,128]{2,1,0:T(8,128)S(1)} fusion(f32[8,128,128]{2,1,0:T(8,128)S(1)} %copy-done, f32[1,8,8,128]{3,1,2,0:T(8,128)S(1)} %bitcast.311), kind=kOutput, calls=%fused_computation.16 | convolution fusion | flops 12582912 | bytes 589824 | tf_op jit(solution)/shard_map/brc,btc->btr/dot_general | solution.py:168
  34.7 0.1 fusion.11
  34.8 0.0 copy-done.2
  34.8 0.0 copy-done.3
  34.8 0.1 fusion.32
  34.9 0.3 fusion.31
  35.3 0.1 copy.144
  35.4 0.1 add_add_fusion
  35.5 0.6 %broadcast_in_dim.96 = f32[32,8,128]{2,1,0:T(8,128)} broadcast(f32[8,128]{1,0:T(8,128)S(1)} %add_add_fusion), dimensions={1,2} | broadcast | bytes 135168 | tf_op jit(solution)/shard_map/broadcast_in_dim | solution.py:201
  36.1 2.9 %all-to-all-start.1 = ((f32[32,8,128]{2,1,0:T(8,128)}), f32[32,8,128]{2,1,0:T(8,128)S(1)}, u32[]{:S(2)}, u32[]{:S(2)}) async-start(f32[32,8,128]{2,1,0:T(8,128)} %broadcast_in_dim.96), calls=%async_computation.1 | async-start | bytes 262144 | tf_op jit(solution)/shard_map/all_to_all | solution.py:200
  39.1 0.6 %multiply_add_fusion.8 = f32[8,128]{1,0:T(8,128)} fusion(f32[8,128]{1,0:T(8,128)S(1)} %bitcast.324, f32[8,128]{1,0:T(8,128)S(1)} %copy-done.2, f32[8,128]{1,0:T(8,128)S(1)} %bitcast.325, f32[8,128]{1,0:T(8,128)S(1)} %bitcast.323, f32[8,128]{1,0:T(8,128)S(1)} %bitcast.322, f32[8,128]{1,0:T(8,128)S(1)} %bitcast.321, f32[8,128]{1,0:T(8,128)S(1)} %bitcast.320, ...), kind=kLoop, calls=%fused_computation.89 | loop fusion | flops 25600 | bytes 45056 | tf_op jit(solution)/shard_map/add | solution.py:67
  39.7 7.6 %all-to-all-done.1 = f32[32,8,128]{2,1,0:T(8,128)S(1)} async-done(((f32[32,8,128]{2,1,0:T(8,128)}), f32[32,8,128]{2,1,0:T(8,128)S(1)}, u32[]{:S(2)}, u32[]{:S(2)}) %all-to-all-start.1) | async-done | bytes 131104 | tf_op jit(solution)/shard_map/all_to_all | solution.py:200
  47.3 0.2 slice_reduce_fusion
  47.4 0.1 eq.97
  47.5 0.7 %fusion.5 = pred[32,8]{1,0:T(8,128)(4,1)S(1)} fusion(f32[32,8,128]{2,1,0:T(8,128)S(1)} %all-to-all-done.1, f32[]{:T(128)S(6)} %convert_element_type.37), kind=kLoop, calls=%fused_computation.11 | loop fusion | flops 256 | bytes 1284 | tf_op jit(solution)/shard_map/eq | solution.py:247
  48.2 0.1 eq.96
  48.3 0.1 slice.194
  48.4 0.1 reshape.304
  48.5 0.1 copy.164
  48.6 0.1 copy.146
  48.6 0.2 multiply_reduce_fusion.2
  48.9 0.1 fusion.4
  49.0 0.3 multiply_reduce_fusion
  49.4 0.1 multiply_reduce_fusion.1
  49.5 0.1 multiply_select_fusion
  49.6 0.0 copy-start.4
  49.6 0.6 %copy-done.4 = f32[1,8]{1,0:T(1,128)S(1)} copy-done((f32[1,8]{1,0:T(1,128)S(1)}, f32[1,8]{1,0:T(1,128)}, u32[]{:S(2)}) %copy-start.4) | copy-done | bytes 56
  50.2 0.1 fusion.14
  50.4 0.1 multiply_add_fusion
  50.4 0.1 stack.58
  50.5 0.1 fusion.16
  50.7 0.1 fusion.18
  50.8 0.1 fusion.20
  50.9 0.1 fusion.22
  51.0 0.1 fusion.24
  51.2 0.1 fusion.26
  51.3 0.1 fusion.28
  51.4 0.2 fusion.7
  51.7 0.1 fusion.66
  51.7 0.6 %stack.59 = f32[8,128]{1,0:T(8,128)} concatenate(f32[1,128]{1,0:T(1,128)S(1)} %get-tuple-element.24, f32[1,128]{1,0:T(1,128)S(1)} %get-tuple-element.23, f32[1,128]{1,0:T(1,128)S(1)} %get-tuple-element.22, f32[1,128]{1,0:T(1,128)S(1)} %get-tuple-element.21, f32[1,128]{1,0:T(1,128)S(1)} %get-tuple-element.20, f32[1,128]{1,0:T(1,128)S(1)} %get-tuple-element.19, ...), dimensions={0} | concatenate | bytes 8192 | tf_op jit(solution)/shard_map/stack | solution.py:69
  (34 shorter events, 0.3 us)
Async XLA Ops:
  0.6 0.7 %copy-start.5 = (s32[192]{0:T(256)S(1)}, s32[192]{0:T(256)}, u32[]{:S(2)}) copy-start(s32[192]{0:T(256)} %param.20) | copy-start | bytes 2308
  7.1 2.1 %collective-permute-start = (f32[8,2,8,1024]{3,2,1,0:T(8,128)S(1)}, f32[8,2,8,1024]{3,2,1,0:T(8,128)S(1)}, u32[]{:S(2)}, u32[]{:S(2)}) collective-permute-start(f32[8,2,8,1024]{3,2,1,0:T(8,128)S(1)} %dynamic-slice_bitcast_fusion), channel_id=1, source_target_pairs={{0,1},{1,0},{2,3},{3,2},{4,5},{5,4},{6,7},{7,6},{8,9},{9,8},{10,11... | collective-permute-start | bytes 1572872 | tf_op jit(solution)/shard_map/ppermute | solution.py:130
  10.0 8.4 %copy-start.1 = (f32[1,1,128,128]{3,2,1,0:T(8,128)S(1)}, f32[1,1,128,128]{3,2,1,0:T(8,128)}, u32[]{:S(2)}) copy-start(f32[1,1,128,128]{3,2,1,0:T(8,128)} %param.26) | copy-start | bytes 196612
  10.0 8.5 %copy-start = (f32[8,128,128]{2,1,0:T(8,128)S(1)}, f32[8,128,128]{2,1,0:T(8,128)}, u32[]{:S(2)}) copy-start(f32[8,128,128]{2,1,0:T(8,128)} %param.21) | copy-start | bytes 1572868
  10.0 23.8 %all-to-all-start = ((f32[16,8,1024]{2,1,0:T(8,128)}), f32[16,8,1024]{2,1,0:T(8,128)S(1)}, u32[]{:S(2)}, u32[]{:S(2)}) async-start(f32[16,8,1024]{2,1,0:T(8,128)} %bitcast.4), calls=%async_computation | async-start | bytes 1048576 | tf_op jit(solution)/shard_map/all_to_all | solution.py:131
  18.5 0.7 %copy-start.7 = (f32[1,1,128]{2,1,0:T(1,128)S(1)}, f32[1,1,128]{2,1,0:T(1,128)}, u32[]{:S(2)}) copy-start(f32[1,1,128]{2,1,0:T(1,128)} %param.28) | copy-start | bytes 1540
  19.1 0.7 %copy-start.6 = (f32[1,1,128]{2,1,0:T(1,128)S(1)}, f32[1,1,128]{2,1,0:T(1,128)}, u32[]{:S(2)}) copy-start(f32[1,1,128]{2,1,0:T(1,128)} %param.27) | copy-start | bytes 1540
  19.8 0.7 %copy-start.8 = (s32[8]{0:T(128)S(1)}, s32[8]{0:T(128)}, u32[]{:S(2)}) copy-start(s32[8]{0:T(128)} %param.25) | copy-start | bytes 100
  20.4 0.7 %copy-start.9 = (s32[8]{0:T(128)S(1)}, s32[8]{0:T(128)}, u32[]{:S(2)}) copy-start(s32[8]{0:T(128)} %param.24) | copy-start | bytes 100
  33.8 1.0 %copy-start.2 = (f32[8,128]{1,0:T(8,128)S(1)}, f32[8,128]{1,0:T(8,128)}, u32[]{:S(2)}) copy-start(f32[8,128]{1,0:T(8,128)} %param.22) | copy-start | bytes 12292
  33.8 1.0 %copy-start.3 = (f32[8,128]{1,0:T(8,128)S(1)}, f32[8,128]{1,0:T(8,128)}, u32[]{:S(2)}) copy-start(f32[8,128]{1,0:T(8,128)} %param.23) | copy-start | bytes 12292
  36.1 11.2 %all-to-all-start.1 = ((f32[32,8,128]{2,1,0:T(8,128)}), f32[32,8,128]{2,1,0:T(8,128)S(1)}, u32[]{:S(2)}, u32[]{:S(2)}) async-start(f32[32,8,128]{2,1,0:T(8,128)} %broadcast_in_dim.96), calls=%async_computation.1 | async-start | bytes 262144 | tf_op jit(solution)/shard_map/all_to_all | solution.py:200
  49.6 0.7 %copy-start.4 = (f32[1,8]{1,0:T(1,128)S(1)}, f32[1,8]{1,0:T(1,128)}, u32[]{:S(2)}) copy-start(f32[1,8]{1,0:T(1,128)} %param.29) | copy-start | bytes 100

commit v15 on v13

--- a/solution.py
+++ b/solution.py
@@ -60,6 +60,8 @@
         pick = (
             block_ids[None, :] == jnp.arange(shards * blocks, dtype=jnp.int32)[:, None]
         ).astype(jnp.float32)
+        if PAIRED:
+            return pair_exchange(runoff_t, block_ids, blocks, shards)
         dense = jnp.einsum(
             "gk,tkc->gtc", pick, runoff_t, precision=lax.Precision.HIGHEST
         ).reshape(shards * blocks, width)
@@ -85,18 +87,23 @@
     )
 
 
-def pair_exchange(dense, blocks, shards):
+def pair_exchange(runoff_t, block_ids, blocks, shards):
     chains = lax.axis_size("basin")
     across = lax.axis_size("x")
-    width = dense.shape[1]
+    sub_steps, tile_count, reaches = runoff_t.shape
+    width = sub_steps * reaches
     core = lax.axis_index("core")
-    parts = dense.reshape(chains, across, 2, blocks, width)
-    keep_side = lax.dynamic_index_in_dim(parts, core, axis=2, keepdims=False)
-    give_side = lax.dynamic_index_in_dim(parts, 1 - core, axis=2, keepdims=False)
-    chip_sum = keep_side + lax.ppermute(give_side, "core", [(0, 1), (1, 0)])
-    arrived = lax.all_to_all(
-        chip_sum.reshape(chains * across, blocks, width), ("basin", "x"), split_axis=0, concat_axis=0, tiled=True
-    )
+    owners = jnp.arange(chains * across, dtype=jnp.int32)[:, None] * 2
+    slots = jnp.arange(blocks, dtype=jnp.int32)[None, :]
+
+    def side_sums(side):
+        wanted = ((owners + side) * blocks + slots).reshape(-1)
+        pick = (block_ids[None, :] == wanted[:, None]).astype(jnp.float32)
+        return jnp.einsum("gk,tkc->gtc", pick, runoff_t, precision=lax.Precision.HIGHEST)
+
+    moved = lax.ppermute(side_sums(1 - core), "core", [(0, 1), (1, 0)])
+    chip_sum = (side_sums(core) + moved).reshape(chains * across, blocks, width)
+    arrived = lax.all_to_all(chip_sum, ("basin", "x"), split_axis=0, concat_axis=0, tiled=True)
     return jnp.sum(arrived, axis=0)
 
 

time: 51.4 us -> 51.4 us (level)
  other arithmetic: 7.44 us -> 6.76 us
  local copies, waits for them, and re-layouts: 9.18 us -> 9.73 us
    reshape x0 -> x1, local copies, waits for them, and re-layouts: none -> 0.87 us  [pair_exchange(): chip_sum = (side_sums(core) + moved).reshape(chains * across, blocks, width)]
    add x1 -> x2, other arithmetic: 0.85 us -> 0.15 us  [side_sums(): wanted = ((owners + side) * blocks + slots).reshape(-1)]
    dot_general x1 -> x0, local copies, waits for them, and re-layouts: 0.61 us -> none  [gather_lateral(): jnp.einsum('gk,tkc->gtc', pick, runoff_t, precision=lax.Precision.HIGHEST)]
    dot_general x1 -> x2, matrix products: 0.7 us -> 1.04 us  [side_sums(): jnp.einsum('gk,tkc->gtc', pick, runoff_t, precision=lax.Precision.HIGHEST)]
where the time goes in v15:
time: 51.4 us; the launch traced here: 51 us
  waiting for transfers between devices  19.5 us (38%)
  starting transfers between devices  11.8 us (23%)
  local copies, waits for them, and re-layouts  9.73 us (19%)
  other arithmetic  6.76 us (13%)
  matrix products  2.17 us (4%)
  between operations  1.01 us (2%)
    all_to_all x1, waiting for transfers between devices, pair_exchange(): lax.all_to_all(chip_sum, ('basin', 'x'), split_axis=0, concat_axis=0, til...  10.6 us
    all_to_all x1, starting transfers between devices, pair_exchange(): lax.all_to_all(chip_sum, ('basin', 'x'), split_axis=0, concat_axis=0, til...  8.37 us
    all_to_all x1, waiting for transfers between devices, local(): lax.all_to_all(jnp.broadcast_to(tile[None], (shards,) + tile.shape), grid...  7.58 us
    unnamed x37, local copies, waits for them, and re-layouts  5.07 us
    all_to_all x1, starting transfers between devices, local(): lax.all_to_all(jnp.broadcast_to(tile[None], (shards,) + tile.shape), grid...  2.92 us
    ppermute x1, waiting for transfers between devices, pair_exchange(): moved = lax.ppermute(side_sums(1 - core), 'core', [(0, 1), (1, 0)])  1.37 us
    select_n x1, other arithmetic, local(): jnp.where(lane == sub_steps + offset, value, 0.0)  1.3 us
    add x4, other arithmetic, route_series(): flow = keep * flow + (1.0 - keep) * mixed[..., sub_step, :]  1.06 us
  transfers between devices with their start and end apart: 3, of which 3 were waited for; matrix products, arithmetic and copies ran while one was open for 8% of the time, Pallas kernels for 0%

profile of v15, /device:TPU:0, one launch (start us, length us, event | category | flops | bytes accessed | tf_op | source)
XLA Modules:
  0.0 51.0 jit_solution(1557326214295497425)
XLA Ops:
  0.7 1.3 %copy.178 = f32[192,8,128]{2,0,1:T(8,128)S(1)} copy(f32[192,8,128]{2,1,0:T(8,128)} %param.15) | data formatting | bytes 1572864 | tf_op args[0]
  2.0 0.9 %copy-done.1 = f32[192,128]{1,0:T(8,128)S(1)} copy-done((f32[192,128]{1,0:T(8,128)S(1)}, f32[192,128]{1,0:T(8,128)}, u32[]{:S(2)}) %copy-start.1) | copy-done | bytes 98328
  3.0 0.1 bitcast_dynamic-update-slice_fusion.5
  3.0 0.1 bitcast_dynamic-update-slice_fusion.4
  3.1 0.1 bitcast_dynamic-update-slice_fusion.3
  3.3 0.1 bitcast_dynamic-update-slice_fusion.1
  3.4 0.1 iota_add_fusion
  3.5 0.1 add.446
  3.7 0.6 %copy-done.8 = s32[192]{0:T(256)S(1)} copy-done((s32[192]{0:T(256)S(1)}, s32[192]{0:T(256)}, u32[]{:S(2)}) %copy-start.8) | copy-done | bytes 792
  4.3 0.5 %fusion.3 = f32[128,8,128]{2,0,1:T(8,128)S(1)} fusion(f32[8,192,128]{2,1,0:T(8,128)S(1)} %bitcast_dynamic-update-slice_fusion, s32[128]{0:T(128)S(1)} %add.446, s32[192]{0:T(256)S(1)} %multiply_add_fusion.9), kind=kOutput, calls=%fused_computation.41 | convolution fusion | flops 302014464 | bytes 1312000 | tf_op jit(solution)/shard_map/gk,tkc->gtc/dot_general | solution.py:102
  4.8 0.5 %collective-permute-start = (f32[128,8,128]{2,0,1:T(8,128)S(1)}, f32[128,8,128]{2,0,1:T(8,128)S(1)}, u32[]{:S(2)}, u32[]{:S(2)}) collective-permute-start(f32[128,8,128]{2,0,1:T(8,128)S(1)} %fusion.3), channel_id=1, source_target_pairs={{0,1},{1,0},{2,3},{3,2},{4,5},{5,4},{6,7},{7,6},{8,9},{9,8},{10,11... | collective-permute-start | bytes 1572872 | tf_op jit(solution)/shard_map/ppermute | solution.py:104
  5.4 0.1 iota_add_fusion.1
  5.4 0.1 add.440
  5.5 1.4 %collective-permute-done = f32[128,8,128]{2,0,1:T(8,128)S(1)} collective-permute-done((f32[128,8,128]{2,0,1:T(8,128)S(1)}, f32[128,8,128]{2,0,1:T(8,128)S(1)}, u32[]{:S(2)}, u32[]{:S(2)}) %collective-permute-start) | collective-permute-done | bytes 524320 | tf_op jit(solution)/shard_map/ppermute | solution.py:104
  6.9 0.5 %convolution_add_fusion = f32[128,8,128]{2,0,1:T(8,128)S(1)} fusion(f32[128,8,128]{2,0,1:T(8,128)S(1)} %collective-permute-done, f32[8,192,128]{2,1,0:T(8,128)S(1)} %bitcast_dynamic-update-slice_fusion, s32[128]{0:T(128)S(1)} %add.440, s32[192]{0:T(256)S(1)} %multiply_add_fusion.9), kind=kOutput, calls=%fused_computation | convolution fusion | flops 302145536 | bytes 1836288 | tf_op jit(solution)/shard_map/gk,tkc->gtc/dot_general | solution.py:102
  7.4 0.3 copy.134
  7.7 0.9 %reshape.339 = f32[16,8,1024]{2,1,0:T(8,128)} reshape(f32[128,8,128]{2,1,0:T(8,128)S(1)} %copy.134) | data formatting | bytes 1048576 | tf_op jit(solution)/shard_map/reshape | solution.py:105
  8.6 8.4 %all-to-all-start = ((f32[16,8,1024]{2,1,0:T(8,128)}), f32[16,8,1024]{2,1,0:T(8,128)S(1)}, u32[]{:S(2)}, u32[]{:S(2)}) async-start(f32[16,8,1024]{2,1,0:T(8,128)} %reshape.339), calls=%async_computation | async-start | bytes 1048576 | tf_op jit(solution)/shard_map/all_to_all | solution.py:106
  17.0 0.1 reshape_squeeze.4
  17.1 0.6 %copy-done.11 = f32[1,1,128]{2,1,0:T(1,128)S(1)} copy-done((f32[1,1,128]{2,1,0:T(1,128)S(1)}, f32[1,1,128]{2,1,0:T(1,128)}, u32[]{:S(2)}) %copy-start.11) | copy-done | bytes 536
  17.8 0.6 %slice.191 = f32[1,1,1]{2,1,0:T(1,128)} slice(f32[1,1,128]{2,1,0:T(1,128)S(1)} %copy-done.11), slice={[0:1], [0:1], [127:128]} | slice | bytes 8 | tf_op jit(solution)/shard_map/slice | solution.py:164
  18.4 0.1 copy-done.10
  18.4 0.6 %slice.190 = f32[1,1,1]{2,1,0:T(1,128)} slice(f32[1,1,128]{2,1,0:T(1,128)S(1)} %copy-done.10), slice={[0:1], [0:1], [127:128]} | slice | bytes 8 | tf_op jit(solution)/shard_map/slice | solution.py:163
  19.0 0.1 copy-done.12
  19.1 0.7 %copy-done.13 = s32[8]{0:T(128)S(1)} copy-done((s32[8]{0:T(128)S(1)}, s32[8]{0:T(128)}, u32[]{:S(2)}) %copy-start.13) | copy-done | bytes 56
  19.8 1.3 %compare_select_fusion = (f32[128]{0:T(128)S(1)}, f32[128]{0:T(128)S(1)}) fusion(f32[]{:T(128)} %bitcast.41, f32[]{:T(128)} %bitcast.40), kind=kLoop, calls=%fused_computation.150 | loop fusion | flops 512 | bytes 1032 | tf_op jit(solution)/shard_map/jit(_where)/select_n | solution.py:171
  21.1 0.7 %add_subtract_fusion = f32[192,128]{1,0:T(8,128)} fusion(f32[8,192,128]{2,1,0:T(8,128)S(1)} %bitcast.445, f32[192,128]{1,0:T(8,128)S(1)} %copy-done.1, f32[192,128]{1,0:T(8,128)S(1)} %copy-done, f32[192,128]{1,0:T(8,128)S(1)} %get-tuple-element.34), kind=kLoop, calls=%fused_computation.26 | loop fusion | flops 319488 | bytes 589824 | tf_op jit(solution)/shard_map/sub | solution.py:24
  21.8 10.6 %all-to-all-done = f32[16,8,1024]{2,1,0:T(8,128)S(1)} async-done(((f32[16,8,1024]{2,1,0:T(8,128)}), f32[16,8,1024]{2,1,0:T(8,128)S(1)}, u32[]{:S(2)}, u32[]{:S(2)}) %all-to-all-start) | async-done | bytes 524320 | tf_op jit(solution)/shard_map/all_to_all | solution.py:106
  32.4 0.9 %fusion.14 = f32[8,8,128]{2,1,0:T(8,128)S(1)} fusion(f32[8,128,128]{2,1,0:T(8,128)S(1)} %copy-done.3, f32[1,8,8,128]{3,1,2,0:T(8,128)S(1)} %bitcast.450), kind=kOutput, calls=%fused_computation.61 | convolution fusion | flops 12582912 | bytes 589824 | tf_op jit(solution)/shard_map/brc,btc->btr/dot_general | solution.py:141
  33.4 0.1 fusion.16
  33.5 0.1 fusion.37
  33.6 0.3 fusion.36
  33.9 0.1 copy.150
  34.0 0.1 add_add_fusion
  34.1 0.6 %broadcast_in_dim.98 = f32[32,8,128]{2,1,0:T(8,128)} broadcast(f32[8,128]{1,0:T(8,128)S(1)} %add_add_fusion), dimensions={1,2} | broadcast | bytes 135168 | tf_op jit(solution)/shard_map/broadcast_in_dim | solution.py:174
  34.7 2.9 %all-to-all-start.1 = ((f32[32,8,128]{2,1,0:T(8,128)}), f32[32,8,128]{2,1,0:T(8,128)S(1)}, u32[]{:S(2)}, u32[]{:S(2)}) async-start(f32[32,8,128]{2,1,0:T(8,128)} %broadcast_in_dim.98), calls=%async_computation.1 | async-start | bytes 262144 | tf_op jit(solution)/shard_map/all_to_all | solution.py:173
  37.7 0.6 %multiply_add_fusion.8 = f32[8,128]{1,0:T(8,128)} fusion(f32[8,128]{1,0:T(8,128)S(1)} %bitcast.463, f32[8,128]{1,0:T(8,128)S(1)} %copy-done.5, f32[8,128]{1,0:T(8,128)S(1)} %bitcast.464, f32[8,128]{1,0:T(8,128)S(1)} %bitcast.462, f32[8,128]{1,0:T(8,128)S(1)} %bitcast.461, f32[8,128]{1,0:T(8,128)S(1)} %bitcast.460, f32[8,128]{1,0:T(8,128)S(1)} %bitcast.459, ...), kind=kLoop, calls=%fused_computation.128 | loop fusion | flops 25600 | bytes 45056 | tf_op jit(solution)/shard_map/add | solution.py:33
  38.3 7.6 %all-to-all-done.1 = f32[32,8,128]{2,1,0:T(8,128)S(1)} async-done(((f32[32,8,128]{2,1,0:T(8,128)}), f32[32,8,128]{2,1,0:T(8,128)S(1)}, u32[]{:S(2)}, u32[]{:S(2)}) %all-to-all-start.1) | async-done | bytes 131104 | tf_op jit(solution)/shard_map/all_to_all | solution.py:173
  45.9 0.2 slice_reduce_fusion
  46.1 0.1 eq.110
  46.2 0.7 %fusion.2 = pred[32,8]{1,0:T(8,128)(4,1)S(1)} fusion(f32[32,8,128]{2,1,0:T(8,128)S(1)} %all-to-all-done.1, f32[]{:T(128)S(6)} %convert_element_type.38), kind=kLoop, calls=%fused_computation.8 | loop fusion | flops 256 | bytes 1284 | tf_op jit(solution)/shard_map/eq | solution.py:220
  46.9 0.1 eq.109
  47.0 0.1 slice.234
  47.0 0.1 reshape.342
  47.1 0.1 copy.170
  47.2 0.1 copy.152
  47.3 0.2 multiply_reduce_fusion.2
  47.5 0.1 fusion.1
  47.7 0.3 multiply_reduce_fusion
  48.0 0.1 multiply_reduce_fusion.1
  48.1 0.1 multiply_select_fusion
  48.2 0.6 %copy-done.7 = f32[1,8]{1,0:T(1,128)S(1)} copy-done((f32[1,8]{1,0:T(1,128)S(1)}, f32[1,8]{1,0:T(1,128)}, u32[]{:S(2)}) %copy-start.7) | copy-done | bytes 56
  48.9 0.1 fusion.19
  49.0 0.1 multiply_add_fusion
  49.1 0.1 stack.94
  49.2 0.1 fusion.21
  49.3 0.1 fusion.23
  49.4 0.1 fusion.25
  49.6 0.1 fusion.27
  49.7 0.1 fusion.29
  49.8 0.1 fusion.31
  50.0 0.1 fusion.33
  50.1 0.2 fusion.8
  50.4 0.6 %stack.95 = f32[8,128]{1,0:T(8,128)} concatenate(f32[1,128]{1,0:T(1,128)S(1)} %get-tuple-element.20, f32[1,128]{1,0:T(1,128)S(1)} %get-tuple-element.19, f32[1,128]{1,0:T(1,128)S(1)} %get-tuple-element.18, f32[1,128]{1,0:T(1,128)S(1)} %get-tuple-element.17, f32[1,128]{1,0:T(1,128)S(1)} %get-tuple-element.16, f32[1,128]{1,0:T(1,128)S(1)} %get-tuple-element.15, ...), dimensions={0} | concatenate | bytes 8192 | tf_op jit(solution)/shard_map/stack | solution.py:35
  (56 shorter events, 0.6 us)
Async XLA Ops:
  0.6 1.3 %copy-start = (f32[192,128]{1,0:T(8,128)S(1)}, f32[192,128]{1,0:T(8,128)}, u32[]{:S(2)}) copy-start(f32[192,128]{1,0:T(8,128)} %param.17) | copy-start | bytes 294916
  0.6 1.3 %copy-start.2 = (f32[192,128]{1,0:T(8,128)S(1)}, f32[192,128]{1,0:T(8,128)}, u32[]{:S(2)}) copy-start(f32[192,128]{1,0:T(8,128)} %param.16) | copy-start | bytes 294916
  2.0 0.9 %copy-start.1 = (f32[192,128]{1,0:T(8,128)S(1)}, f32[192,128]{1,0:T(8,128)}, u32[]{:S(2)}) copy-start(f32[192,128]{1,0:T(8,128)} %param.18) | copy-start | bytes 294916
  3.6 0.7 %copy-start.8 = (s32[192]{0:T(256)S(1)}, s32[192]{0:T(256)}, u32[]{:S(2)}) copy-start(s32[192]{0:T(256)} %param.20) | copy-start | bytes 2308
  3.6 0.7 %copy-start.9 = (s32[192]{0:T(256)S(1)}, s32[192]{0:T(256)}, u32[]{:S(2)}) copy-start(s32[192]{0:T(256)} %param.19) | copy-start | bytes 2308
  4.8 2.1 %collective-permute-start = (f32[128,8,128]{2,0,1:T(8,128)S(1)}, f32[128,8,128]{2,0,1:T(8,128)S(1)}, u32[]{:S(2)}, u32[]{:S(2)}) collective-permute-start(f32[128,8,128]{2,0,1:T(8,128)S(1)} %fusion.3), channel_id=1, source_target_pairs={{0,1},{1,0},{2,3},{3,2},{4,5},{5,4},{6,7},{7,6},{8,9},{9,8},{10,11... | collective-permute-start | bytes 1572872 | tf_op jit(solution)/shard_map/ppermute | solution.py:104
  8.6 8.4 %copy-start.4 = (f32[1,1,128,128]{3,2,1,0:T(8,128)S(1)}, f32[1,1,128,128]{3,2,1,0:T(8,128)}, u32[]{:S(2)}) copy-start(f32[1,1,128,128]{3,2,1,0:T(8,128)} %param.26) | copy-start | bytes 196612
  8.6 8.5 %copy-start.3 = (f32[8,128,128]{2,1,0:T(8,128)S(1)}, f32[8,128,128]{2,1,0:T(8,128)}, u32[]{:S(2)}) copy-start(f32[8,128,128]{2,1,0:T(8,128)} %param.21) | copy-start | bytes 1572868
  8.6 23.8 %all-to-all-start = ((f32[16,8,1024]{2,1,0:T(8,128)}), f32[16,8,1024]{2,1,0:T(8,128)S(1)}, u32[]{:S(2)}, u32[]{:S(2)}) async-start(f32[16,8,1024]{2,1,0:T(8,128)} %reshape.339), calls=%async_computation | async-start | bytes 1048576 | tf_op jit(solution)/shard_map/all_to_all | solution.py:106
  17.1 0.7 %copy-start.11 = (f32[1,1,128]{2,1,0:T(1,128)S(1)}, f32[1,1,128]{2,1,0:T(1,128)}, u32[]{:S(2)}) copy-start(f32[1,1,128]{2,1,0:T(1,128)} %param.28) | copy-start | bytes 1540
  17.8 0.7 %copy-start.10 = (f32[1,1,128]{2,1,0:T(1,128)S(1)}, f32[1,1,128]{2,1,0:T(1,128)}, u32[]{:S(2)}) copy-start(f32[1,1,128]{2,1,0:T(1,128)} %param.27) | copy-start | bytes 1540
  18.4 0.7 %copy-start.12 = (s32[8]{0:T(128)S(1)}, s32[8]{0:T(128)}, u32[]{:S(2)}) copy-start(s32[8]{0:T(128)} %param.25) | copy-start | bytes 100
  19.1 0.7 %copy-start.13 = (s32[8]{0:T(128)S(1)}, s32[8]{0:T(128)}, u32[]{:S(2)}) copy-start(s32[8]{0:T(128)} %param.24) | copy-start | bytes 100
  32.4 1.0 %copy-start.5 = (f32[8,128]{1,0:T(8,128)S(1)}, f32[8,128]{1,0:T(8,128)}, u32[]{:S(2)}) copy-start(f32[8,128]{1,0:T(8,128)} %param.22) | copy-start | bytes 12292
  32.4 1.0 %copy-start.6 = (f32[8,128]{1,0:T(8,128)S(1)}, f32[8,128]{1,0:T(8,128)}, u32[]{:S(2)}) copy-start(f32[8,128]{1,0:T(8,128)} %param.23) | copy-start | bytes 12292
  34.7 11.2 %all-to-all-start.1 = ((f32[32,8,128]{2,1,0:T(8,128)}), f32[32,8,128]{2,1,0:T(8,128)S(1)}, u32[]{:S(2)}, u32[]{:S(2)}) async-start(f32[32,8,128]{2,1,0:T(8,128)} %broadcast_in_dim.98), calls=%async_computation.1 | async-start | bytes 262144 | tf_op jit(solution)/shard_map/all_to_all | solution.py:173
  48.2 0.7 %copy-start.7 = (f32[1,8]{1,0:T(1,128)S(1)}, f32[1,8]{1,0:T(1,128)}, u32[]{:S(2)}) copy-start(f32[1,8]{1,0:T(1,128)} %param.29) | copy-start | bytes 100

commit v16 on v13

--- a/solution.py
+++ b/solution.py
@@ -131,13 +131,6 @@
 
     runoff_t, water = land_update_t(jnp.transpose(precip, (1, 0, 2)), soil_water, capacity, evap_rate)
     lateral = gather_lateral(runoff_t, tile_dest, tile_block, blocks, shards)
-    trib_mixed = jnp.einsum(
-        "brc,btc->btr",
-        trib_op,
-        lateral.reshape(blocks, sub_steps, reaches),
-        precision=lax.Precision.HIGHEST,
-    )
-    trib_flows = route_series(trib_mixed, trib_keep, trib_prev)
     exit_mixed = jnp.sum(
         lateral.reshape(blocks, sub_steps, reaches) * trib_op[:, reaches - 1][:, None, :], axis=2
     )
@@ -163,9 +156,8 @@
         for offset, value in enumerate(columns):
             static_tile = static_tile + jnp.where(lane == sub_steps + offset, value, 0.0)
         tile = jnp.pad(outlet, ((0, 0), (0, reaches - sub_steps))) + static_tile
-        every = lax.all_to_all(
-            jnp.broadcast_to(tile[None], (shards,) + tile.shape), grid, split_axis=0, concat_axis=0, tiled=True
-        )
+        outgoing = jnp.broadcast_to(tile[None], (shards,) + tile.shape)
+        every = lax.all_to_all(outgoing, grid, split_axis=0, concat_axis=0, tiled=True)
         outlets = every[:, :, :sub_steps].reshape(chains, rivers * blocks, sub_steps)
         river_of = every[:, :, sub_steps].reshape(chains, rivers * blocks)
         reach_of = every[:, :, sub_steps + 1].reshape(chains, rivers * blocks)
@@ -189,9 +181,8 @@
         width = payload.shape[0]
         padded = -(-width // 128) * 128
         payload = jnp.pad(payload, (0, padded - width))
-        every = lax.all_to_all(
-            jnp.broadcast_to(payload[None], (shards, padded)), grid, split_axis=0, concat_axis=0, tiled=True
-        )
+        outgoing = jnp.broadcast_to(payload[None], (shards, padded))
+        every = lax.all_to_all(outgoing, grid, split_axis=0, concat_axis=0, tiled=True)
         at = 0
         outlets = every[:, at : at + blocks * sub_steps].reshape(chains, rivers * blocks, sub_steps)
         at += blocks * sub_steps
@@ -209,6 +200,15 @@
         starts = lax.dynamic_index_in_dim(
             every[:, at + 1].reshape(chains, rivers), mine, axis=1, keepdims=False
         )
+
+    lateral_late, _ = lax.optimization_barrier((lateral, outgoing))
+    trib_mixed = jnp.einsum(
+        "brc,btc->btr",
+        trib_op,
+        lateral_late.reshape(blocks, sub_steps, reaches),
+        precision=lax.Precision.HIGHEST,
+    )
+    trib_flows = route_series(trib_mixed, trib_keep, trib_prev)
 
     joins = (river_of == mine.astype(jnp.float32))[:, :, None] & (
         reach_of[:, :, None] == jnp.arange(reaches, dtype=jnp.float32)[None, None, :]

time: 51.4 us -> 51.2 us (level)
  waiting for transfers between devices: 19.7 us -> 18.8 us
  local copies, waits for them, and re-layouts: 9.18 us -> 9.87 us
    all_to_all x1, waiting for transfers between devices: 7.58 us -> 6.65 us  [local(): lax.all_to_all(outgoing, grid, split_axis=0, concat_axis=0, tiled=True)]
    unnamed x37, local copies, waits for them, and re-layouts: 5.07 us -> 5.67 us
  transfers between devices with their start and end apart: 3 -> 3, of which waited for: 3 -> 3; matrix products, arithmetic and copies ran while one was open for 8% -> 10% of each run, Pallas kernels for 0% -> 0%
where the time goes in v16:
time: 51.2 us; the launch traced here: 50.7 us
  waiting for transfers between devices  18.8 us (37%)
  starting transfers between devices  11.8 us (23%)
  local copies, waits for them, and re-layouts  9.87 us (19%)
  other arithmetic  7.43 us (15%)
  matrix products  1.83 us (4%)
  between operations  1 us (2%)
    all_to_all x1, waiting for transfers between devices, pair_exchange(): lax.all_to_all(chip_sum.reshape(chains * across, blocks, width), ('basin'...  10.6 us
    all_to_all x1, starting transfers between devices, pair_exchange(): lax.all_to_all(chip_sum.reshape(chains * across, blocks, width), ('basin'...  8.37 us
    all_to_all x1, waiting for transfers between devices, local(): lax.all_to_all(outgoing, grid, split_axis=0, concat_axis=0, tiled=True)  6.65 us
    unnamed x37, local copies, waits for them, and re-layouts  5.67 us
    all_to_all x1, starting transfers between devices, local(): lax.all_to_all(outgoing, grid, split_axis=0, concat_axis=0, tiled=True)  2.92 us
    ppermute x1, waiting for transfers between devices, pair_exchange(): chip_sum = keep_side + lax.ppermute(give_side, 'core', [(0, 1), (1, 0)])  1.54 us
    select_n x1, other arithmetic, local(): jnp.where(lane == sub_steps + offset, value, 0.0)  1.3 us
    add x4, other arithmetic, route_series(): flow = keep * flow + (1.0 - keep) * mixed[..., sub_step, :]  1.06 us
  transfers between devices with their start and end apart: 3, of which 3 were waited for; matrix products, arithmetic and copies ran while one was open for 10% of the time, Pallas kernels for 0%

profile of v16, /device:TPU:0, one launch (start us, length us, event | category | flops | bytes accessed | tf_op | source)
XLA Modules:
  0.0 50.7 jit_solution(13135230861917658372)
XLA Ops:
  0.7 1.3 %copy.202 = f32[192,8,128]{2,0,1:T(8,128)S(1)} copy(f32[192,8,128]{2,1,0:T(8,128)} %param.15) | data formatting | bytes 1572864 | tf_op args[0]
  2.0 0.9 %copy-done.1 = f32[192,128]{1,0:T(8,128)S(1)} copy-done((f32[192,128]{1,0:T(8,128)S(1)}, f32[192,128]{1,0:T(8,128)}, u32[]{:S(2)}) %copy-start.1) | copy-done | bytes 98328
  2.9 0.1 bitcast_dynamic-update-slice_fusion.6
  3.0 0.1 bitcast_dynamic-update-slice_fusion.5
  3.0 0.1 bitcast_dynamic-update-slice_fusion.4
  3.1 0.1 bitcast_dynamic-update-slice_fusion.3
  3.3 0.1 bitcast_dynamic-update-slice_fusion.1
  3.5 0.6 %copy-done.8 = s32[192]{0:T(256)S(1)} copy-done((s32[192]{0:T(256)S(1)}, s32[192]{0:T(256)}, u32[]{:S(2)}) %copy-start.8) | copy-done | bytes 792
  4.1 0.7 %fusion.1 = f32[256,8,128]{2,0,1:T(8,128)S(1)} fusion(f32[8,192,128]{2,1,0:T(8,128)S(1)} %bitcast_dynamic-update-slice_fusion, s32[192]{0:T(256)S(1)} %multiply_add_fusion.9), kind=kOutput, calls=%fused_computation.6 | convolution fusion | flops 604028928 | bytes 1835776 | tf_op jit(solution)/shard_map/gk,tkc->gtc/dot_general | solution.py:63
  4.8 0.6 %copy.158 = f32[256,8,128]{2,1,0:T(8,128)S(1)} copy(f32[256,8,128]{2,0,1:T(8,128)S(1)} %fusion.1) | data formatting | bytes 2097152 | tf_op jit(solution)/shard_map/gk,tkc->gtc/dot_general | solution.py:63
  5.5 0.2 reshape_reshape.3
  5.7 0.5 %collective-permute-start = (f32[8,2,8,1024]{3,2,1,0:T(8,128)S(1)}, f32[8,2,8,1024]{3,2,1,0:T(8,128)S(1)}, u32[]{:S(2)}, u32[]{:S(2)}) collective-permute-start(f32[8,2,8,1024]{3,2,1,0:T(8,128)S(1)} %dynamic-slice_bitcast_fusion), channel_id=1, source_target_pairs={{0,1},{1,0},{2,3},{3,2},{4,5},{5,4},{6,7},{7,6},{8,9},{9,8},{10,11... | collective-permute-start | bytes 1572872 | tf_op jit(solution)/shard_map/ppermute | solution.py:96
  6.2 1.5 %collective-permute-done = f32[8,2,8,1024]{3,2,1,0:T(8,128)S(1)} collective-permute-done((f32[8,2,8,1024]{3,2,1,0:T(8,128)S(1)}, f32[8,2,8,1024]{3,2,1,0:T(8,128)S(1)}, u32[]{:S(2)}, u32[]{:S(2)}) %collective-permute-start) | collective-permute-done | bytes 524320 | tf_op jit(solution)/shard_map/ppermute | solution.py:96
  7.7 0.8 %bitcast_add_fusion = f32[8,2,8,1024]{3,2,1,0:T(8,128)} fusion(f32[8,2,8,1024]{3,2,1,0:T(8,128)S(1)} %collective-permute-done, f32[8,2,2,8,1024]{4,3,2,1,0:T(8,128)S(1)} %reshape_reshape.3, s32[]{:T(128)S(6)} %select_n.173), kind=kLoop, calls=%fused_computation.2 | loop fusion | flops 131072 | bytes 1572868 | tf_op jit(solution)/shard_map/add | solution.py:96
  8.6 8.4 %all-to-all-start = ((f32[16,8,1024]{2,1,0:T(8,128)}), f32[16,8,1024]{2,1,0:T(8,128)S(1)}, u32[]{:S(2)}, u32[]{:S(2)}) async-start(f32[16,8,1024]{2,1,0:T(8,128)} %bitcast.20), calls=%async_computation | async-start | bytes 1048576 | tf_op jit(solution)/shard_map/all_to_all | solution.py:97
  17.0 0.1 reshape_squeeze.4
  17.1 0.6 %copy-done.11 = f32[1,1,128]{2,1,0:T(1,128)S(1)} copy-done((f32[1,1,128]{2,1,0:T(1,128)S(1)}, f32[1,1,128]{2,1,0:T(1,128)}, u32[]{:S(2)}) %copy-start.11) | copy-done | bytes 536
  17.8 0.6 %slice.183 = f32[1,1,1]{2,1,0:T(1,128)} slice(f32[1,1,128]{2,1,0:T(1,128)S(1)} %copy-done.11), slice={[0:1], [0:1], [127:128]} | slice | bytes 8 | tf_op jit(solution)/shard_map/slice | solution.py:150
  18.3 0.1 copy-done.10
  18.4 0.6 %slice.182 = f32[1,1,1]{2,1,0:T(1,128)} slice(f32[1,1,128]{2,1,0:T(1,128)S(1)} %copy-done.10), slice={[0:1], [0:1], [127:128]} | slice | bytes 8 | tf_op jit(solution)/shard_map/slice | solution.py:149
  19.0 0.1 copy-done.12
  19.1 0.7 %copy-done.13 = s32[8]{0:T(128)S(1)} copy-done((s32[8]{0:T(128)S(1)}, s32[8]{0:T(128)}, u32[]{:S(2)}) %copy-start.13) | copy-done | bytes 56
  19.8 1.3 %compare_select_fusion = (f32[128]{0:T(128)S(1)}, f32[128]{0:T(128)S(1)}) fusion(f32[]{:T(128)} %bitcast.34, f32[]{:T(128)} %bitcast.33), kind=kLoop, calls=%fused_computation.144 | loop fusion | flops 512 | bytes 1032 | tf_op jit(solution)/shard_map/jit(_where)/select_n | solution.py:157
  21.1 0.7 %add_subtract_fusion = f32[192,128]{1,0:T(8,128)} fusion(f32[8,192,128]{2,1,0:T(8,128)S(1)} %bitcast.447, f32[192,128]{1,0:T(8,128)S(1)} %copy-done.1, f32[192,128]{1,0:T(8,128)S(1)} %copy-done, f32[192,128]{1,0:T(8,128)S(1)} %get-tuple-element.36), kind=kLoop, calls=%fused_computation.31 | loop fusion | flops 319488 | bytes 589824 | tf_op jit(solution)/shard_map/sub | solution.py:24
  21.8 10.6 %all-to-all-done = f32[16,8,1024]{2,1,0:T(8,128)S(1)} async-done(((f32[16,8,1024]{2,1,0:T(8,128)}), f32[16,8,1024]{2,1,0:T(8,128)S(1)}, u32[]{:S(2)}, u32[]{:S(2)}) %all-to-all-start) | async-done | bytes 524320 | tf_op jit(solution)/shard_map/all_to_all | solution.py:97
  32.4 0.1 fusion.12
  32.5 0.1 copy.159
  32.6 0.6 %copy-done.5 = f32[8,128]{1,0:T(8,128)S(1)} copy-done((f32[8,128]{1,0:T(8,128)S(1)}, f32[8,128]{1,0:T(8,128)}, u32[]{:S(2)}) %copy-start.5) | copy-done | bytes 4120
  33.2 0.1 fusion.32
  33.3 0.3 fusion.31
  33.7 0.1 copy.168
  33.7 0.1 add_add_fusion
  33.8 0.6 %broadcast_in_dim.96 = f32[32,8,128]{2,1,0:T(8,128)} broadcast(f32[8,128]{1,0:T(8,128)S(1)} %add_add_fusion), dimensions={1,2} | broadcast | bytes 135168 | tf_op jit(solution)/shard_map/broadcast_in_dim | solution.py:159
  34.5 2.9 %all-to-all-start.1 = ((f32[32,8,128]{2,1,0:T(8,128)}), f32[32,8,128]{2,1,0:T(8,128)S(1)}, u32[]{:S(2)}, u32[]{:S(2)}) async-start(f32[32,8,128]{2,1,0:T(8,128)} %broadcast_in_dim.96), calls=%async_computation.1 | async-start | bytes 262144 | tf_op jit(solution)/shard_map/all_to_all | solution.py:160
  37.4 0.9 %fusion.9 = f32[8,8,128]{2,1,0:T(8,128)S(1)} fusion(f32[8,128,128]{2,1,0:T(8,128)S(1)} %copy-done.3, f32[1,8,8,128]{3,1,2,0:T(8,128)S(1)} %bitcast.452), kind=kOutput, calls=%fused_computation.56 | convolution fusion | flops 12582912 | bytes 589824 | tf_op jit(solution)/shard_map/brc,btc->btr/dot_general | solution.py:205
  38.4 0.6 %multiply_add_fusion.8 = f32[8,128]{1,0:T(8,128)} fusion(f32[8,128]{1,0:T(8,128)S(1)} %bitcast.464, f32[8,128]{1,0:T(8,128)S(1)} %copy-done.5, f32[8,128]{1,0:T(8,128)S(1)} %bitcast.465, f32[8,128]{1,0:T(8,128)S(1)} %bitcast.463, f32[8,128]{1,0:T(8,128)S(1)} %bitcast.462, f32[8,128]{1,0:T(8,128)S(1)} %bitcast.461, f32[8,128]{1,0:T(8,128)S(1)} %bitcast.460, ...), kind=kLoop, calls=%fused_computation.121 | loop fusion | flops 25600 | bytes 45056 | tf_op jit(solution)/shard_map/add | solution.py:33
  39.0 6.7 %all-to-all-done.1 = f32[32,8,128]{2,1,0:T(8,128)S(1)} async-done(((f32[32,8,128]{2,1,0:T(8,128)}), f32[32,8,128]{2,1,0:T(8,128)S(1)}, u32[]{:S(2)}, u32[]{:S(2)}) %all-to-all-start.1) | async-done | bytes 131104 | tf_op jit(solution)/shard_map/all_to_all | solution.py:160
  45.6 0.2 slice_reduce_fusion
  45.8 0.1 eq.97
  45.9 0.7 %fusion.5 = pred[32,8]{1,0:T(8,128)(4,1)S(1)} fusion(f32[32,8,128]{2,1,0:T(8,128)S(1)} %all-to-all-done.1, f32[]{:T(128)S(6)} %convert_element_type.37), kind=kLoop, calls=%fused_computation.12 | loop fusion | flops 256 | bytes 1284 | tf_op jit(solution)/shard_map/eq | solution.py:213
  46.6 0.1 eq.96
  46.7 0.1 slice.234
  46.8 0.1 reshape.303
  46.8 0.1 copy.195
  46.9 0.1 copy.177
  47.0 0.2 multiply_reduce_fusion.2
  47.2 0.1 fusion.4
  47.4 0.3 multiply_reduce_fusion
  47.7 0.1 multiply_reduce_fusion.1
  47.8 0.1 multiply_select_fusion
  48.0 0.6 %copy-done.7 = f32[1,8]{1,0:T(1,128)S(1)} copy-done((f32[1,8]{1,0:T(1,128)S(1)}, f32[1,8]{1,0:T(1,128)}, u32[]{:S(2)}) %copy-start.7) | copy-done | bytes 56
  48.6 0.1 fusion.14
  48.7 0.1 multiply_add_fusion
  48.8 0.1 stack.94
  48.9 0.1 fusion.16
  49.0 0.1 fusion.18
  49.2 0.1 fusion.20
  49.3 0.1 fusion.22
  49.4 0.1 fusion.24
  49.5 0.1 fusion.26
  49.7 0.1 fusion.28
  49.8 0.2 fusion.7
  50.0 0.1 fusion.66
  50.1 0.6 %stack.95 = f32[8,128]{1,0:T(8,128)} concatenate(f32[1,128]{1,0:T(1,128)S(1)} %get-tuple-element.22, f32[1,128]{1,0:T(1,128)S(1)} %get-tuple-element.21, f32[1,128]{1,0:T(1,128)S(1)} %get-tuple-element.20, f32[1,128]{1,0:T(1,128)S(1)} %get-tuple-element.19, f32[1,128]{1,0:T(1,128)S(1)} %get-tuple-element.18, f32[1,128]{1,0:T(1,128)S(1)} %get-tuple-element.17, ...), dimensions={0} | concatenate | bytes 8192 | tf_op jit(solution)/shard_map/stack | solution.py:35
  (52 shorter events, 0.5 us)
Async XLA Ops:
  0.6 1.3 %copy-start = (f32[192,128]{1,0:T(8,128)S(1)}, f32[192,128]{1,0:T(8,128)}, u32[]{:S(2)}) copy-start(f32[192,128]{1,0:T(8,128)} %param.17) | copy-start | bytes 294916
  0.6 1.3 %copy-start.2 = (f32[192,128]{1,0:T(8,128)S(1)}, f32[192,128]{1,0:T(8,128)}, u32[]{:S(2)}) copy-start(f32[192,128]{1,0:T(8,128)} %param.16) | copy-start | bytes 294916
  2.0 0.9 %copy-start.1 = (f32[192,128]{1,0:T(8,128)S(1)}, f32[192,128]{1,0:T(8,128)}, u32[]{:S(2)}) copy-start(f32[192,128]{1,0:T(8,128)} %param.18) | copy-start | bytes 294916
  3.4 0.7 %copy-start.8 = (s32[192]{0:T(256)S(1)}, s32[192]{0:T(256)}, u32[]{:S(2)}) copy-start(s32[192]{0:T(256)} %param.20) | copy-start | bytes 2308
  3.4 0.7 %copy-start.9 = (s32[192]{0:T(256)S(1)}, s32[192]{0:T(256)}, u32[]{:S(2)}) copy-start(s32[192]{0:T(256)} %param.19) | copy-start | bytes 2308
  5.7 2.1 %collective-permute-start = (f32[8,2,8,1024]{3,2,1,0:T(8,128)S(1)}, f32[8,2,8,1024]{3,2,1,0:T(8,128)S(1)}, u32[]{:S(2)}, u32[]{:S(2)}) collective-permute-start(f32[8,2,8,1024]{3,2,1,0:T(8,128)S(1)} %dynamic-slice_bitcast_fusion), channel_id=1, source_target_pairs={{0,1},{1,0},{2,3},{3,2},{4,5},{5,4},{6,7},{7,6},{8,9},{9,8},{10,11... | collective-permute-start | bytes 1572872 | tf_op jit(solution)/shard_map/ppermute | solution.py:96
  8.6 8.4 %copy-start.4 = (f32[1,1,128,128]{3,2,1,0:T(8,128)S(1)}, f32[1,1,128,128]{3,2,1,0:T(8,128)}, u32[]{:S(2)}) copy-start(f32[1,1,128,128]{3,2,1,0:T(8,128)} %param.26) | copy-start | bytes 196612
  8.6 8.5 %copy-start.3 = (f32[8,128,128]{2,1,0:T(8,128)S(1)}, f32[8,128,128]{2,1,0:T(8,128)}, u32[]{:S(2)}) copy-start(f32[8,128,128]{2,1,0:T(8,128)} %param.21) | copy-start | bytes 1572868
  8.6 23.8 %all-to-all-start = ((f32[16,8,1024]{2,1,0:T(8,128)}), f32[16,8,1024]{2,1,0:T(8,128)S(1)}, u32[]{:S(2)}, u32[]{:S(2)}) async-start(f32[16,8,1024]{2,1,0:T(8,128)} %bitcast.20), calls=%async_computation | async-start | bytes 1048576 | tf_op jit(solution)/shard_map/all_to_all | solution.py:97
  17.1 0.7 %copy-start.11 = (f32[1,1,128]{2,1,0:T(1,128)S(1)}, f32[1,1,128]{2,1,0:T(1,128)}, u32[]{:S(2)}) copy-start(f32[1,1,128]{2,1,0:T(1,128)} %param.28) | copy-start | bytes 1540
  17.8 0.7 %copy-start.10 = (f32[1,1,128]{2,1,0:T(1,128)S(1)}, f32[1,1,128]{2,1,0:T(1,128)}, u32[]{:S(2)}) copy-start(f32[1,1,128]{2,1,0:T(1,128)} %param.27) | copy-start | bytes 1540
  18.4 0.7 %copy-start.12 = (s32[8]{0:T(128)S(1)}, s32[8]{0:T(128)}, u32[]{:S(2)}) copy-start(s32[8]{0:T(128)} %param.25) | copy-start | bytes 100
  19.1 0.7 %copy-start.13 = (s32[8]{0:T(128)S(1)}, s32[8]{0:T(128)}, u32[]{:S(2)}) copy-start(s32[8]{0:T(128)} %param.24) | copy-start | bytes 100
  32.5 0.7 %copy-start.5 = (f32[8,128]{1,0:T(8,128)S(1)}, f32[8,128]{1,0:T(8,128)}, u32[]{:S(2)}) copy-start(f32[8,128]{1,0:T(8,128)} %param.22) | copy-start | bytes 12292
  32.5 0.7 %copy-start.6 = (f32[8,128]{1,0:T(8,128)S(1)}, f32[8,128]{1,0:T(8,128)}, u32[]{:S(2)}) copy-start(f32[8,128]{1,0:T(8,128)} %param.23) | copy-start | bytes 12292
  34.5 11.2 %all-to-all-start.1 = ((f32[32,8,128]{2,1,0:T(8,128)}), f32[32,8,128]{2,1,0:T(8,128)S(1)}, u32[]{:S(2)}, u32[]{:S(2)}) async-start(f32[32,8,128]{2,1,0:T(8,128)} %broadcast_in_dim.96), calls=%async_computation.1 | async-start | bytes 262144 | tf_op jit(solution)/shard_map/all_to_all | solution.py:160
  47.9 0.7 %copy-start.7 = (f32[1,8]{1,0:T(1,128)S(1)}, f32[1,8]{1,0:T(1,128)}, u32[]{:S(2)}) copy-start(f32[1,8]{1,0:T(1,128)} %param.29) | copy-start | bytes 100

commit v17 on v16

--- a/solution.py
+++ b/solution.py
@@ -60,15 +60,13 @@
         pick = (
             block_ids[None, :] == jnp.arange(shards * blocks, dtype=jnp.int32)[:, None]
         ).astype(jnp.float32)
-        dense = jnp.einsum(
-            "gk,tkc->gtc", pick, runoff_t, precision=lax.Precision.HIGHEST
-        ).reshape(shards * blocks, width)
+        dense = jnp.einsum("gk,tkc->gtc", pick, runoff_t, precision=lax.Precision.HIGHEST)
         if not PAIRED or blocks % 2:
             arrived = lax.all_to_all(
                 dense.reshape(shards, blocks, width), grid, split_axis=0, concat_axis=0, tiled=True
             )
             return jnp.sum(arrived, axis=0)
-        return pair_exchange(dense, blocks, shards)
+        return pair_exchange(dense, blocks, shards).reshape(blocks, width)
     runoff = jnp.transpose(runoff_t, (1, 0, 2)).reshape(tile_count, width)
     buffer, slot_labels = pack_slots(runoff, tile_block, tile_dest, shards, tile_cap)
     arrived = lax.all_to_all(
@@ -88,14 +86,14 @@
 def pair_exchange(dense, blocks, shards):
     chains = lax.axis_size("basin")
     across = lax.axis_size("x")
-    width = dense.shape[1]
+    tail = dense.shape[1:]
     core = lax.axis_index("core")
-    parts = dense.reshape(chains, across, 2, blocks, width)
+    parts = dense.reshape((chains, across, 2, blocks) + tail)
     keep_side = lax.dynamic_index_in_dim(parts, core, axis=2, keepdims=False)
     give_side = lax.dynamic_index_in_dim(parts, 1 - core, axis=2, keepdims=False)
     chip_sum = keep_side + lax.ppermute(give_side, "core", [(0, 1), (1, 0)])
     arrived = lax.all_to_all(
-        chip_sum.reshape(chains * across, blocks, width), ("basin", "x"), split_axis=0, concat_axis=0, tiled=True
+        chip_sum.reshape((chains * across, blocks) + tail), ("basin", "x"), split_axis=0, concat_axis=0, tiled=True
     )
     return jnp.sum(arrived, axis=0)
 

time: 51.2 us -> 51.1 us (level)
  local copies, waits for them, and re-layouts: 9.87 us -> 10.4 us
  other arithmetic: 7.43 us -> 6.91 us
    reshape x0 -> x1, local copies, waits for them, and re-layouts: none -> 0.88 us  [pair_exchange(): chip_sum.reshape((chains * across, blocks) + tail)]
    dot_general x1 -> x0, local copies, waits for them, and re-layouts: 0.61 us -> none  [gather_lateral(): jnp.einsum('gk,tkc->gtc', pick, runoff_t, precision=lax.Precision.HIGHEST)]
    add x1, other arithmetic: 0.85 us -> 0.33 us  [pair_exchange(): chip_sum = keep_side + lax.ppermute(give_side, 'core', [(0, 1), (1, 0)])]
    unnamed x37 -> x38, local copies, waits for them, and re-layouts: 5.67 us -> 5.98 us
where the time goes in v17:
time: 51.1 us; the launch traced here: 50.7 us
  waiting for transfers between devices  18.8 us (37%)
  starting transfers between devices  11.8 us (23%)
  local copies, waits for them, and re-layouts  10.4 us (20%)
  other arithmetic  6.91 us (14%)
  matrix products  1.84 us (4%)
  between operations  1 us (2%)
    all_to_all x1, waiting for transfers between devices, pair_exchange(): lax.all_to_all(chip_sum.reshape((chains * across, blocks) + tail), ('basi...  10.6 us
    all_to_all x1, starting transfers between devices, pair_exchange(): lax.all_to_all(chip_sum.reshape((chains * across, blocks) + tail), ('basi...  8.36 us
    all_to_all x1, waiting for transfers between devices, local(): lax.all_to_all(outgoing, grid, split_axis=0, concat_axis=0, tiled=True)  6.65 us
    unnamed x38, local copies, waits for them, and re-layouts  5.98 us
    all_to_all x1, starting transfers between devices, local(): lax.all_to_all(outgoing, grid, split_axis=0, concat_axis=0, tiled=True)  2.92 us
    ppermute x1, waiting for transfers between devices, pair_exchange(): chip_sum = keep_side + lax.ppermute(give_side, 'core', [(0, 1), (1, 0)])  1.54 us
    select_n x1, other arithmetic, local(): jnp.where(lane == sub_steps + offset, value, 0.0)  1.3 us
    add x4, other arithmetic, route_series(): flow = keep * flow + (1.0 - keep) * mixed[..., sub_step, :]  1.06 us
  transfers between devices with their start and end apart: 3, of which 3 were waited for; matrix products, arithmetic and copies ran while one was open for 10% of the time, Pallas kernels for 0%

profile of v17, /device:TPU:0, one launch (start us, length us, event | category | flops | bytes accessed | tf_op | source)
XLA Modules:
  0.0 50.7 jit_solution(4784482207283233291)
XLA Ops:
  0.7 1.3 %copy.233 = f32[192,8,128]{2,0,1:T(8,128)S(1)} copy(f32[192,8,128]{2,1,0:T(8,128)} %param.15) | data formatting | bytes 1572864 | tf_op args[0]
  2.0 0.9 %copy-done.1 = f32[192,128]{1,0:T(8,128)S(1)} copy-done((f32[192,128]{1,0:T(8,128)S(1)}, f32[192,128]{1,0:T(8,128)}, u32[]{:S(2)}) %copy-start.1) | copy-done | bytes 98328
  3.0 0.1 bitcast_dynamic-update-slice_fusion.5
  3.0 0.1 bitcast_dynamic-update-slice_fusion.4
  3.1 0.1 bitcast_dynamic-update-slice_fusion.3
  3.3 0.1 bitcast_dynamic-update-slice_fusion.1
  3.5 0.6 %copy-done.8 = s32[192]{0:T(256)S(1)} copy-done((s32[192]{0:T(256)S(1)}, s32[192]{0:T(256)}, u32[]{:S(2)}) %copy-start.8) | copy-done | bytes 792
  4.1 0.7 %fusion.2 = f32[256,8,128]{2,0,1:T(8,128)S(1)} fusion(f32[8,192,128]{2,1,0:T(8,128)S(1)} %bitcast_dynamic-update-slice_fusion, s32[192]{0:T(256)S(1)} %multiply_add_fusion.9), kind=kOutput, calls=%fused_computation.7 | convolution fusion | flops 604028928 | bytes 1835776 | tf_op jit(solution)/shard_map/gk,tkc->gtc/dot_general | solution.py:63
  4.8 0.1 constant_dynamic-slice_fusion.1
  5.0 0.3 copy.234
  5.3 0.5 %collective-permute-start = (f32[8,2,8,8,128]{4,3,2,1,0:T(8,128)S(1)}, f32[8,2,8,8,128]{4,3,2,1,0:T(8,128)S(1)}, u32[]{:S(2)}, u32[]{:S(2)}) collective-permute-start(f32[8,2,8,8,128]{4,3,2,1,0:T(8,128)S(1)} %bitcast.455), channel_id=1, source_target_pairs={{0,1},{1,0},{2,3},{3,2},{4,5},{5,4},{6,7},{7,6},{8,9},{9,8},{10,11... | collective-permute-start | bytes 1572872 | tf_op jit(solution)/shard_map/ppermute | solution.py:94
  5.8 1.5 %collective-permute-done = f32[8,2,8,8,128]{4,3,2,1,0:T(8,128)S(1)} collective-permute-done((f32[8,2,8,8,128]{4,3,2,1,0:T(8,128)S(1)}, f32[8,2,8,8,128]{4,3,2,1,0:T(8,128)S(1)}, u32[]{:S(2)}, u32[]{:S(2)}) %collective-permute-start) | collective-permute-done | bytes 524320 | tf_op jit(solution)/shard_map/ppermute | solution.py:94
  7.3 0.3 fusion
  7.7 0.9 %copy.183 = f32[16,8,8,128]{3,1,2,0:T(8,128)} copy(f32[16,8,8,128]{3,2,1,0:T(8,128)S(1)} %bitcast.452) | data formatting | bytes 1048576 | tf_op jit(solution)/shard_map/reshape | solution.py:96
  8.6 8.4 %all-to-all-start = ((f32[16,8,8,128]{3,1,2,0:T(8,128)}), f32[16,8,8,128]{3,1,2,0:T(8,128)S(1)}, u32[]{:S(2)}, u32[]{:S(2)}) async-start(f32[16,8,8,128]{3,1,2,0:T(8,128)} %copy.183), calls=%async_computation | async-start | bytes 1048576 | tf_op jit(solution)/shard_map/all_to_all | solution.py:95
  17.0 0.1 reshape_squeeze.4
  17.1 0.6 %copy-done.11 = f32[1,1,128]{2,1,0:T(1,128)S(1)} copy-done((f32[1,1,128]{2,1,0:T(1,128)S(1)}, f32[1,1,128]{2,1,0:T(1,128)}, u32[]{:S(2)}) %copy-start.11) | copy-done | bytes 536
  17.7 0.6 %slice.183 = f32[1,1,1]{2,1,0:T(1,128)} slice(f32[1,1,128]{2,1,0:T(1,128)S(1)} %copy-done.11), slice={[0:1], [0:1], [127:128]} | slice | bytes 8 | tf_op jit(solution)/shard_map/slice | solution.py:148
  18.3 0.1 copy-done.10
  18.4 0.6 %slice.182 = f32[1,1,1]{2,1,0:T(1,128)} slice(f32[1,1,128]{2,1,0:T(1,128)S(1)} %copy-done.10), slice={[0:1], [0:1], [127:128]} | slice | bytes 8 | tf_op jit(solution)/shard_map/slice | solution.py:147
  19.0 0.1 copy-done.12
  19.0 0.7 %copy-done.13 = s32[8]{0:T(128)S(1)} copy-done((s32[8]{0:T(128)S(1)}, s32[8]{0:T(128)}, u32[]{:S(2)}) %copy-start.13) | copy-done | bytes 56
  19.7 1.3 %compare_select_fusion = (f32[128]{0:T(128)S(1)}, f32[128]{0:T(128)S(1)}) fusion(f32[]{:T(128)} %bitcast.35, f32[]{:T(128)} %bitcast.34), kind=kLoop, calls=%fused_computation.144 | loop fusion | flops 512 | bytes 1032 | tf_op jit(solution)/shard_map/jit(_where)/select_n | solution.py:155
  21.0 0.7 %add_subtract_fusion = f32[192,128]{1,0:T(8,128)} fusion(f32[8,192,128]{2,1,0:T(8,128)S(1)} %bitcast.448, f32[192,128]{1,0:T(8,128)S(1)} %copy-done.1, f32[192,128]{1,0:T(8,128)S(1)} %copy-done, f32[192,128]{1,0:T(8,128)S(1)} %get-tuple-element.36), kind=kLoop, calls=%fused_computation.32 | loop fusion | flops 319488 | bytes 589824 | tf_op jit(solution)/shard_map/sub | solution.py:24
  21.7 10.6 %all-to-all-done = f32[16,8,8,128]{3,1,2,0:T(8,128)S(1)} async-done(((f32[16,8,8,128]{3,1,2,0:T(8,128)}), f32[16,8,8,128]{3,1,2,0:T(8,128)S(1)}, u32[]{:S(2)}, u32[]{:S(2)}) %all-to-all-start) | async-done | bytes 524320 | tf_op jit(solution)/shard_map/all_to_all | solution.py:95
  32.4 0.1 multiply_reduce_fusion.2
  32.5 0.1 copy.184
  32.5 0.6 %copy-done.5 = f32[8,128]{1,0:T(8,128)S(1)} copy-done((f32[8,128]{1,0:T(8,128)S(1)}, f32[8,128]{1,0:T(8,128)}, u32[]{:S(2)}) %copy-start.5) | copy-done | bytes 4120
  33.2 0.1 fusion.32
  33.2 0.3 fusion.31
  33.6 0.1 copy.193
  33.7 0.1 add_add_fusion
  33.8 0.6 %broadcast_in_dim.96 = f32[32,8,128]{2,1,0:T(8,128)} broadcast(f32[8,128]{1,0:T(8,128)S(1)} %add_add_fusion), dimensions={1,2} | broadcast | bytes 135168 | tf_op jit(solution)/shard_map/broadcast_in_dim | solution.py:157
  34.4 2.9 %all-to-all-start.1 = ((f32[32,8,128]{2,1,0:T(8,128)}), f32[32,8,128]{2,1,0:T(8,128)S(1)}, u32[]{:S(2)}, u32[]{:S(2)}) async-start(f32[32,8,128]{2,1,0:T(8,128)} %broadcast_in_dim.96), calls=%async_computation.1 | async-start | bytes 262144 | tf_op jit(solution)/shard_map/all_to_all | solution.py:158
  37.4 0.9 %fusion.10 = f32[8,8,128]{2,1,0:T(8,128)S(1)} fusion(f32[8,128,128]{2,1,0:T(8,128)S(1)} %copy-done.3, f32[1,8,8,128]{3,1,2,0:T(8,128)S(1)} %bitcast.456), kind=kOutput, calls=%fused_computation.57 | convolution fusion | flops 12582912 | bytes 589824 | tf_op jit(solution)/shard_map/brc,btc->btr/dot_general | solution.py:203
  38.3 0.6 %multiply_add_fusion.8 = f32[8,128]{1,0:T(8,128)} fusion(f32[8,128]{1,0:T(8,128)S(1)} %bitcast.468, f32[8,128]{1,0:T(8,128)S(1)} %copy-done.5, f32[8,128]{1,0:T(8,128)S(1)} %bitcast.469, f32[8,128]{1,0:T(8,128)S(1)} %bitcast.467, f32[8,128]{1,0:T(8,128)S(1)} %bitcast.466, f32[8,128]{1,0:T(8,128)S(1)} %bitcast.465, f32[8,128]{1,0:T(8,128)S(1)} %bitcast.464, ...), kind=kLoop, calls=%fused_computation.121 | loop fusion | flops 25600 | bytes 45056 | tf_op jit(solution)/shard_map/add | solution.py:33
  38.9 6.7 %all-to-all-done.1 = f32[32,8,128]{2,1,0:T(8,128)S(1)} async-done(((f32[32,8,128]{2,1,0:T(8,128)}), f32[32,8,128]{2,1,0:T(8,128)S(1)}, u32[]{:S(2)}, u32[]{:S(2)}) %all-to-all-start.1) | async-done | bytes 131104 | tf_op jit(solution)/shard_map/all_to_all | solution.py:158
  45.6 0.2 slice_reduce_fusion
  45.8 0.1 eq.97
  45.8 0.7 %fusion.6 = pred[32,8]{1,0:T(8,128)(4,1)S(1)} fusion(f32[32,8,128]{2,1,0:T(8,128)S(1)} %all-to-all-done.1, f32[]{:T(128)S(6)} %convert_element_type.37), kind=kLoop, calls=%fused_computation.13 | loop fusion | flops 256 | bytes 1284 | tf_op jit(solution)/shard_map/eq | solution.py:211
  46.5 0.1 eq.96
  46.6 0.1 slice.234
  46.7 0.1 reshape.307
  46.8 0.1 copy.222
  46.9 0.1 copy.202
  47.0 0.2 multiply_reduce_fusion.3
  47.2 0.1 fusion.5
  47.4 0.3 multiply_reduce_fusion
  47.7 0.1 multiply_reduce_fusion.1
  47.8 0.1 multiply_select_fusion
  47.9 0.6 %copy-done.7 = f32[1,8]{1,0:T(1,128)S(1)} copy-done((f32[1,8]{1,0:T(1,128)S(1)}, f32[1,8]{1,0:T(1,128)}, u32[]{:S(2)}) %copy-start.7) | copy-done | bytes 56
  48.6 0.1 fusion.14
  48.7 0.1 multiply_add_fusion
  48.8 0.1 stack.94
  48.9 0.1 fusion.16
  49.0 0.1 fusion.18
  49.1 0.1 fusion.20
  49.3 0.1 fusion.22
  49.4 0.1 fusion.24
  49.5 0.1 fusion.26
  49.6 0.1 fusion.28
  49.8 0.2 fusion.8
  50.0 0.1 fusion.66
  50.1 0.6 %stack.95 = f32[8,128]{1,0:T(8,128)} concatenate(f32[1,128]{1,0:T(1,128)S(1)} %get-tuple-element.22, f32[1,128]{1,0:T(1,128)S(1)} %get-tuple-element.21, f32[1,128]{1,0:T(1,128)S(1)} %get-tuple-element.20, f32[1,128]{1,0:T(1,128)S(1)} %get-tuple-element.19, f32[1,128]{1,0:T(1,128)S(1)} %get-tuple-element.18, f32[1,128]{1,0:T(1,128)S(1)} %get-tuple-element.17, ...), dimensions={0} | concatenate | bytes 8192 | tf_op jit(solution)/shard_map/stack | solution.py:35
  (52 shorter events, 0.5 us)
Async XLA Ops:
  0.6 1.3 %copy-start = (f32[192,128]{1,0:T(8,128)S(1)}, f32[192,128]{1,0:T(8,128)}, u32[]{:S(2)}) copy-start(f32[192,128]{1,0:T(8,128)} %param.17) | copy-start | bytes 294916
  0.6 1.3 %copy-start.2 = (f32[192,128]{1,0:T(8,128)S(1)}, f32[192,128]{1,0:T(8,128)}, u32[]{:S(2)}) copy-start(f32[192,128]{1,0:T(8,128)} %param.16) | copy-start | bytes 294916
  2.0 0.9 %copy-start.1 = (f32[192,128]{1,0:T(8,128)S(1)}, f32[192,128]{1,0:T(8,128)}, u32[]{:S(2)}) copy-start(f32[192,128]{1,0:T(8,128)} %param.18) | copy-start | bytes 294916
  3.4 0.7 %copy-start.8 = (s32[192]{0:T(256)S(1)}, s32[192]{0:T(256)}, u32[]{:S(2)}) copy-start(s32[192]{0:T(256)} %param.20) | copy-start | bytes 2308
  3.4 0.7 %copy-start.9 = (s32[192]{0:T(256)S(1)}, s32[192]{0:T(256)}, u32[]{:S(2)}) copy-start(s32[192]{0:T(256)} %param.19) | copy-start | bytes 2308
  5.3 2.1 %collective-permute-start = (f32[8,2,8,8,128]{4,3,2,1,0:T(8,128)S(1)}, f32[8,2,8,8,128]{4,3,2,1,0:T(8,128)S(1)}, u32[]{:S(2)}, u32[]{:S(2)}) collective-permute-start(f32[8,2,8,8,128]{4,3,2,1,0:T(8,128)S(1)} %bitcast.455), channel_id=1, source_target_pairs={{0,1},{1,0},{2,3},{3,2},{4,5},{5,4},{6,7},{7,6},{8,9},{9,8},{10,11... | collective-permute-start | bytes 1572872 | tf_op jit(solution)/shard_map/ppermute | solution.py:94
  8.6 8.4 %copy-start.4 = (f32[1,1,128,128]{3,2,1,0:T(8,128)S(1)}, f32[1,1,128,128]{3,2,1,0:T(8,128)}, u32[]{:S(2)}) copy-start(f32[1,1,128,128]{3,2,1,0:T(8,128)} %param.26) | copy-start | bytes 196612
  8.6 8.5 %copy-start.3 = (f32[8,128,128]{2,1,0:T(8,128)S(1)}, f32[8,128,128]{2,1,0:T(8,128)}, u32[]{:S(2)}) copy-start(f32[8,128,128]{2,1,0:T(8,128)} %param.21) | copy-start | bytes 1572868
  8.6 23.8 %all-to-all-start = ((f32[16,8,8,128]{3,1,2,0:T(8,128)}), f32[16,8,8,128]{3,1,2,0:T(8,128)S(1)}, u32[]{:S(2)}, u32[]{:S(2)}) async-start(f32[16,8,8,128]{3,1,2,0:T(8,128)} %copy.183), calls=%async_computation | async-start | bytes 1048576 | tf_op jit(solution)/shard_map/all_to_all | solution.py:95
  17.1 0.7 %copy-start.11 = (f32[1,1,128]{2,1,0:T(1,128)S(1)}, f32[1,1,128]{2,1,0:T(1,128)}, u32[]{:S(2)}) copy-start(f32[1,1,128]{2,1,0:T(1,128)} %param.28) | copy-start | bytes 1540
  17.7 0.7 %copy-start.10 = (f32[1,1,128]{2,1,0:T(1,128)S(1)}, f32[1,1,128]{2,1,0:T(1,128)}, u32[]{:S(2)}) copy-start(f32[1,1,128]{2,1,0:T(1,128)} %param.27) | copy-start | bytes 1540
  18.4 0.7 %copy-start.12 = (s32[8]{0:T(128)S(1)}, s32[8]{0:T(128)}, u32[]{:S(2)}) copy-start(s32[8]{0:T(128)} %param.25) | copy-start | bytes 100
  19.0 0.7 %copy-start.13 = (s32[8]{0:T(128)S(1)}, s32[8]{0:T(128)}, u32[]{:S(2)}) copy-start(s32[8]{0:T(128)} %param.24) | copy-start | bytes 100
  32.4 0.7 %copy-start.5 = (f32[8,128]{1,0:T(8,128)S(1)}, f32[8,128]{1,0:T(8,128)}, u32[]{:S(2)}) copy-start(f32[8,128]{1,0:T(8,128)} %param.22) | copy-start | bytes 12292
  32.5 0.7 %copy-start.6 = (f32[8,128]{1,0:T(8,128)S(1)}, f32[8,128]{1,0:T(8,128)}, u32[]{:S(2)}) copy-start(f32[8,128]{1,0:T(8,128)} %param.23) | copy-start | bytes 12292
  34.4 11.2 %all-to-all-start.1 = ((f32[32,8,128]{2,1,0:T(8,128)}), f32[32,8,128]{2,1,0:T(8,128)S(1)}, u32[]{:S(2)}, u32[]{:S(2)}) async-start(f32[32,8,128]{2,1,0:T(8,128)} %broadcast_in_dim.96), calls=%async_computation.1 | async-start | bytes 262144 | tf_op jit(solution)/shard_map/all_to_all | solution.py:158
  47.9 0.7 %copy-start.7 = (f32[1,8]{1,0:T(1,128)S(1)}, f32[1,8]{1,0:T(1,128)}, u32[]{:S(2)}) copy-start(f32[1,8]{1,0:T(1,128)} %param.29) | copy-start | bytes 100

commit v18 on v16

--- a/solution.py
+++ b/solution.py
@@ -61,7 +61,7 @@
             block_ids[None, :] == jnp.arange(shards * blocks, dtype=jnp.int32)[:, None]
         ).astype(jnp.float32)
         dense = jnp.einsum(
-            "gk,tkc->gtc", pick, runoff_t, precision=lax.Precision.HIGHEST
+            "gk,tkc->gtc", pick, runoff_t, precision=lax.Precision.HIGH
         ).reshape(shards * blocks, width)
         if not PAIRED or blocks % 2:
             arrived = lax.all_to_all(

time: 51.2 us -> 51 us (level)
  no operation moved by 1% of the time
where the time goes in v18:
time: 51 us; the launch traced here: 50.6 us
  waiting for transfers between devices  18.8 us (37%)
  starting transfers between devices  11.8 us (23%)
  local copies, waits for them, and re-layouts  9.87 us (19%)
  other arithmetic  7.43 us (15%)
  matrix products  1.69 us (3%)
  between operations  1 us (2%)
    all_to_all x1, waiting for transfers between devices, pair_exchange(): lax.all_to_all(chip_sum.reshape(chains * across, blocks, width), ('basin'...  10.6 us
    all_to_all x1, starting transfers between devices, pair_exchange(): lax.all_to_all(chip_sum.reshape(chains * across, blocks, width), ('basin'...  8.37 us
    all_to_all x1, waiting for transfers between devices, local(): lax.all_to_all(outgoing, grid, split_axis=0, concat_axis=0, tiled=True)  6.65 us
    unnamed x37, local copies, waits for them, and re-layouts  5.67 us
    all_to_all x1, starting transfers between devices, local(): lax.all_to_all(outgoing, grid, split_axis=0, concat_axis=0, tiled=True)  2.92 us
    ppermute x1, waiting for transfers between devices, pair_exchange(): chip_sum = keep_side + lax.ppermute(give_side, 'core', [(0, 1), (1, 0)])  1.54 us
    select_n x1, other arithmetic, local(): jnp.where(lane == sub_steps + offset, value, 0.0)  1.3 us
    add x4, other arithmetic, route_series(): flow = keep * flow + (1.0 - keep) * mixed[..., sub_step, :]  1.06 us
  transfers between devices with their start and end apart: 3, of which 3 were waited for; matrix products, arithmetic and copies ran while one was open for 10% of the time, Pallas kernels for 0%

profile of v18, /device:TPU:0, one launch (start us, length us, event | category | flops | bytes accessed | tf_op | source)
XLA Modules:
  0.0 50.6 jit_solution(12212385978175633907)
XLA Ops:
  0.7 1.3 %copy.202 = f32[192,8,128]{2,0,1:T(8,128)S(1)} copy(f32[192,8,128]{2,1,0:T(8,128)} %param.15) | data formatting | bytes 1572864 | tf_op args[0]
  2.0 0.9 %copy-done.1 = f32[192,128]{1,0:T(8,128)S(1)} copy-done((f32[192,128]{1,0:T(8,128)S(1)}, f32[192,128]{1,0:T(8,128)}, u32[]{:S(2)}) %copy-start.1) | copy-done | bytes 98328
  2.9 0.1 bitcast_dynamic-update-slice_fusion.6
  3.0 0.1 bitcast_dynamic-update-slice_fusion.5
  3.0 0.1 bitcast_dynamic-update-slice_fusion.4
  3.1 0.1 bitcast_dynamic-update-slice_fusion.3
  3.3 0.1 bitcast_dynamic-update-slice_fusion.1
  3.5 0.6 %copy-done.8 = s32[192]{0:T(256)S(1)} copy-done((s32[192]{0:T(256)S(1)}, s32[192]{0:T(256)}, u32[]{:S(2)}) %copy-start.8) | copy-done | bytes 792
  4.1 0.6 %fusion.1 = f32[256,8,128]{2,0,1:T(8,128)S(1)} fusion(f32[8,192,128]{2,1,0:T(8,128)S(1)} %bitcast_dynamic-update-slice_fusion, s32[192]{0:T(256)S(1)} %multiply_add_fusion.9), kind=kOutput, calls=%fused_computation.6 | convolution fusion | flops 302039040 | bytes 1835776 | tf_op jit(solution)/shard_map/gk,tkc->gtc/dot_general | solution.py:63
  4.7 0.6 %copy.158 = f32[256,8,128]{2,1,0:T(8,128)S(1)} copy(f32[256,8,128]{2,0,1:T(8,128)S(1)} %fusion.1) | data formatting | bytes 2097152 | tf_op jit(solution)/shard_map/gk,tkc->gtc/dot_general | solution.py:63
  5.3 0.2 reshape_reshape.3
  5.5 0.5 %collective-permute-start = (f32[8,2,8,1024]{3,2,1,0:T(8,128)S(1)}, f32[8,2,8,1024]{3,2,1,0:T(8,128)S(1)}, u32[]{:S(2)}, u32[]{:S(2)}) collective-permute-start(f32[8,2,8,1024]{3,2,1,0:T(8,128)S(1)} %dynamic-slice_bitcast_fusion), channel_id=1, source_target_pairs={{0,1},{1,0},{2,3},{3,2},{4,5},{5,4},{6,7},{7,6},{8,9},{9,8},{10,11... | collective-permute-start | bytes 1572872 | tf_op jit(solution)/shard_map/ppermute | solution.py:96
  6.1 1.5 %collective-permute-done = f32[8,2,8,1024]{3,2,1,0:T(8,128)S(1)} collective-permute-done((f32[8,2,8,1024]{3,2,1,0:T(8,128)S(1)}, f32[8,2,8,1024]{3,2,1,0:T(8,128)S(1)}, u32[]{:S(2)}, u32[]{:S(2)}) %collective-permute-start) | collective-permute-done | bytes 524320 | tf_op jit(solution)/shard_map/ppermute | solution.py:96
  7.6 0.8 %bitcast_add_fusion = f32[8,2,8,1024]{3,2,1,0:T(8,128)} fusion(f32[8,2,8,1024]{3,2,1,0:T(8,128)S(1)} %collective-permute-done, f32[8,2,2,8,1024]{4,3,2,1,0:T(8,128)S(1)} %reshape_reshape.3, s32[]{:T(128)S(6)} %select_n.173), kind=kLoop, calls=%fused_computation.2 | loop fusion | flops 131072 | bytes 1572868 | tf_op jit(solution)/shard_map/add | solution.py:96
  8.4 8.4 %all-to-all-start = ((f32[16,8,1024]{2,1,0:T(8,128)}), f32[16,8,1024]{2,1,0:T(8,128)S(1)}, u32[]{:S(2)}, u32[]{:S(2)}) async-start(f32[16,8,1024]{2,1,0:T(8,128)} %bitcast.20), calls=%async_computation | async-start | bytes 1048576 | tf_op jit(solution)/shard_map/all_to_all | solution.py:97
  16.9 0.1 reshape_squeeze.4
  17.0 0.6 %copy-done.11 = f32[1,1,128]{2,1,0:T(1,128)S(1)} copy-done((f32[1,1,128]{2,1,0:T(1,128)S(1)}, f32[1,1,128]{2,1,0:T(1,128)}, u32[]{:S(2)}) %copy-start.11) | copy-done | bytes 536
  17.6 0.6 %slice.183 = f32[1,1,1]{2,1,0:T(1,128)} slice(f32[1,1,128]{2,1,0:T(1,128)S(1)} %copy-done.11), slice={[0:1], [0:1], [127:128]} | slice | bytes 8 | tf_op jit(solution)/shard_map/slice | solution.py:150
  18.2 0.1 copy-done.10
  18.3 0.6 %slice.182 = f32[1,1,1]{2,1,0:T(1,128)} slice(f32[1,1,128]{2,1,0:T(1,128)S(1)} %copy-done.10), slice={[0:1], [0:1], [127:128]} | slice | bytes 8 | tf_op jit(solution)/shard_map/slice | solution.py:149
  18.9 0.1 copy-done.12
  18.9 0.7 %copy-done.13 = s32[8]{0:T(128)S(1)} copy-done((s32[8]{0:T(128)S(1)}, s32[8]{0:T(128)}, u32[]{:S(2)}) %copy-start.13) | copy-done | bytes 56
  19.6 1.3 %compare_select_fusion = (f32[128]{0:T(128)S(1)}, f32[128]{0:T(128)S(1)}) fusion(f32[]{:T(128)} %bitcast.34, f32[]{:T(128)} %bitcast.33), kind=kLoop, calls=%fused_computation.144 | loop fusion | flops 512 | bytes 1032 | tf_op jit(solution)/shard_map/jit(_where)/select_n | solution.py:157
  20.9 0.7 %add_subtract_fusion = f32[192,128]{1,0:T(8,128)} fusion(f32[8,192,128]{2,1,0:T(8,128)S(1)} %bitcast.447, f32[192,128]{1,0:T(8,128)S(1)} %copy-done.1, f32[192,128]{1,0:T(8,128)S(1)} %copy-done, f32[192,128]{1,0:T(8,128)S(1)} %get-tuple-element.36), kind=kLoop, calls=%fused_computation.31 | loop fusion | flops 319488 | bytes 589824 | tf_op jit(solution)/shard_map/sub | solution.py:24
  21.6 10.6 %all-to-all-done = f32[16,8,1024]{2,1,0:T(8,128)S(1)} async-done(((f32[16,8,1024]{2,1,0:T(8,128)}), f32[16,8,1024]{2,1,0:T(8,128)S(1)}, u32[]{:S(2)}, u32[]{:S(2)}) %all-to-all-start) | async-done | bytes 524320 | tf_op jit(solution)/shard_map/all_to_all | solution.py:97
  32.2 0.1 fusion.12
  32.4 0.1 copy.159
  32.4 0.6 %copy-done.5 = f32[8,128]{1,0:T(8,128)S(1)} copy-done((f32[8,128]{1,0:T(8,128)S(1)}, f32[8,128]{1,0:T(8,128)}, u32[]{:S(2)}) %copy-start.5) | copy-done | bytes 4120
  33.0 0.1 fusion.32
  33.1 0.3 fusion.31
  33.5 0.1 copy.168
  33.6 0.1 add_add_fusion
  33.7 0.6 %broadcast_in_dim.96 = f32[32,8,128]{2,1,0:T(8,128)} broadcast(f32[8,128]{1,0:T(8,128)S(1)} %add_add_fusion), dimensions={1,2} | broadcast | bytes 135168 | tf_op jit(solution)/shard_map/broadcast_in_dim | solution.py:159
  34.3 2.9 %all-to-all-start.1 = ((f32[32,8,128]{2,1,0:T(8,128)}), f32[32,8,128]{2,1,0:T(8,128)S(1)}, u32[]{:S(2)}, u32[]{:S(2)}) async-start(f32[32,8,128]{2,1,0:T(8,128)} %broadcast_in_dim.96), calls=%async_computation.1 | async-start | bytes 262144 | tf_op jit(solution)/shard_map/all_to_all | solution.py:160
  37.3 0.9 %fusion.9 = f32[8,8,128]{2,1,0:T(8,128)S(1)} fusion(f32[8,128,128]{2,1,0:T(8,128)S(1)} %copy-done.3, f32[1,8,8,128]{3,1,2,0:T(8,128)S(1)} %bitcast.452), kind=kOutput, calls=%fused_computation.56 | convolution fusion | flops 12582912 | bytes 589824 | tf_op jit(solution)/shard_map/brc,btc->btr/dot_general | solution.py:205
  38.2 0.6 %multiply_add_fusion.8 = f32[8,128]{1,0:T(8,128)} fusion(f32[8,128]{1,0:T(8,128)S(1)} %bitcast.464, f32[8,128]{1,0:T(8,128)S(1)} %copy-done.5, f32[8,128]{1,0:T(8,128)S(1)} %bitcast.465, f32[8,128]{1,0:T(8,128)S(1)} %bitcast.463, f32[8,128]{1,0:T(8,128)S(1)} %bitcast.462, f32[8,128]{1,0:T(8,128)S(1)} %bitcast.461, f32[8,128]{1,0:T(8,128)S(1)} %bitcast.460, ...), kind=kLoop, calls=%fused_computation.121 | loop fusion | flops 25600 | bytes 45056 | tf_op jit(solution)/shard_map/add | solution.py:33
  38.8 6.7 %all-to-all-done.1 = f32[32,8,128]{2,1,0:T(8,128)S(1)} async-done(((f32[32,8,128]{2,1,0:T(8,128)}), f32[32,8,128]{2,1,0:T(8,128)S(1)}, u32[]{:S(2)}, u32[]{:S(2)}) %all-to-all-start.1) | async-done | bytes 131104 | tf_op jit(solution)/shard_map/all_to_all | solution.py:160
  45.5 0.2 slice_reduce_fusion
  45.7 0.1 eq.97
  45.7 0.7 %fusion.5 = pred[32,8]{1,0:T(8,128)(4,1)S(1)} fusion(f32[32,8,128]{2,1,0:T(8,128)S(1)} %all-to-all-done.1, f32[]{:T(128)S(6)} %convert_element_type.37), kind=kLoop, calls=%fused_computation.12 | loop fusion | flops 256 | bytes 1284 | tf_op jit(solution)/shard_map/eq | solution.py:213
  46.4 0.1 eq.96
  46.5 0.1 slice.234
  46.6 0.1 reshape.303
  46.7 0.1 copy.195
  46.8 0.1 copy.177
  46.9 0.2 multiply_reduce_fusion.2
  47.1 0.1 fusion.4
  47.3 0.3 multiply_reduce_fusion
  47.6 0.1 multiply_reduce_fusion.1
  47.7 0.1 multiply_select_fusion
  47.8 0.6 %copy-done.7 = f32[1,8]{1,0:T(1,128)S(1)} copy-done((f32[1,8]{1,0:T(1,128)S(1)}, f32[1,8]{1,0:T(1,128)}, u32[]{:S(2)}) %copy-start.7) | copy-done | bytes 56
  48.5 0.1 fusion.14
  48.6 0.1 multiply_add_fusion
  48.7 0.1 stack.94
  48.8 0.1 fusion.16
  48.9 0.1 fusion.18
  49.0 0.1 fusion.20
  49.1 0.1 fusion.22
  49.3 0.1 fusion.24
  49.4 0.1 fusion.26
  49.5 0.1 fusion.28
  49.7 0.2 fusion.7
  49.9 0.1 fusion.66
  50.0 0.6 %stack.95 = f32[8,128]{1,0:T(8,128)} concatenate(f32[1,128]{1,0:T(1,128)S(1)} %get-tuple-element.22, f32[1,128]{1,0:T(1,128)S(1)} %get-tuple-element.21, f32[1,128]{1,0:T(1,128)S(1)} %get-tuple-element.20, f32[1,128]{1,0:T(1,128)S(1)} %get-tuple-element.19, f32[1,128]{1,0:T(1,128)S(1)} %get-tuple-element.18, f32[1,128]{1,0:T(1,128)S(1)} %get-tuple-element.17, ...), dimensions={0} | concatenate | bytes 8192 | tf_op jit(solution)/shard_map/stack | solution.py:35
  (52 shorter events, 0.5 us)
Async XLA Ops:
  0.6 1.3 %copy-start = (f32[192,128]{1,0:T(8,128)S(1)}, f32[192,128]{1,0:T(8,128)}, u32[]{:S(2)}) copy-start(f32[192,128]{1,0:T(8,128)} %param.17) | copy-start | bytes 294916
  0.6 1.3 %copy-start.2 = (f32[192,128]{1,0:T(8,128)S(1)}, f32[192,128]{1,0:T(8,128)}, u32[]{:S(2)}) copy-start(f32[192,128]{1,0:T(8,128)} %param.16) | copy-start | bytes 294916
  2.0 0.9 %copy-start.1 = (f32[192,128]{1,0:T(8,128)S(1)}, f32[192,128]{1,0:T(8,128)}, u32[]{:S(2)}) copy-start(f32[192,128]{1,0:T(8,128)} %param.18) | copy-start | bytes 294916
  3.4 0.7 %copy-start.8 = (s32[192]{0:T(256)S(1)}, s32[192]{0:T(256)}, u32[]{:S(2)}) copy-start(s32[192]{0:T(256)} %param.20) | copy-start | bytes 2308
  3.4 0.7 %copy-start.9 = (s32[192]{0:T(256)S(1)}, s32[192]{0:T(256)}, u32[]{:S(2)}) copy-start(s32[192]{0:T(256)} %param.19) | copy-start | bytes 2308
  5.5 2.1 %collective-permute-start = (f32[8,2,8,1024]{3,2,1,0:T(8,128)S(1)}, f32[8,2,8,1024]{3,2,1,0:T(8,128)S(1)}, u32[]{:S(2)}, u32[]{:S(2)}) collective-permute-start(f32[8,2,8,1024]{3,2,1,0:T(8,128)S(1)} %dynamic-slice_bitcast_fusion), channel_id=1, source_target_pairs={{0,1},{1,0},{2,3},{3,2},{4,5},{5,4},{6,7},{7,6},{8,9},{9,8},{10,11... | collective-permute-start | bytes 1572872 | tf_op jit(solution)/shard_map/ppermute | solution.py:96
  8.4 8.4 %copy-start.4 = (f32[1,1,128,128]{3,2,1,0:T(8,128)S(1)}, f32[1,1,128,128]{3,2,1,0:T(8,128)}, u32[]{:S(2)}) copy-start(f32[1,1,128,128]{3,2,1,0:T(8,128)} %param.26) | copy-start | bytes 196612
  8.4 8.5 %copy-start.3 = (f32[8,128,128]{2,1,0:T(8,128)S(1)}, f32[8,128,128]{2,1,0:T(8,128)}, u32[]{:S(2)}) copy-start(f32[8,128,128]{2,1,0:T(8,128)} %param.21) | copy-start | bytes 1572868
  8.4 23.8 %all-to-all-start = ((f32[16,8,1024]{2,1,0:T(8,128)}), f32[16,8,1024]{2,1,0:T(8,128)S(1)}, u32[]{:S(2)}, u32[]{:S(2)}) async-start(f32[16,8,1024]{2,1,0:T(8,128)} %bitcast.20), calls=%async_computation | async-start | bytes 1048576 | tf_op jit(solution)/shard_map/all_to_all | solution.py:97
  17.0 0.7 %copy-start.11 = (f32[1,1,128]{2,1,0:T(1,128)S(1)}, f32[1,1,128]{2,1,0:T(1,128)}, u32[]{:S(2)}) copy-start(f32[1,1,128]{2,1,0:T(1,128)} %param.28) | copy-start | bytes 1540
  17.6 0.7 %copy-start.10 = (f32[1,1,128]{2,1,0:T(1,128)S(1)}, f32[1,1,128]{2,1,0:T(1,128)}, u32[]{:S(2)}) copy-start(f32[1,1,128]{2,1,0:T(1,128)} %param.27) | copy-start | bytes 1540
  18.3 0.7 %copy-start.12 = (s32[8]{0:T(128)S(1)}, s32[8]{0:T(128)}, u32[]{:S(2)}) copy-start(s32[8]{0:T(128)} %param.25) | copy-start | bytes 100
  18.9 0.7 %copy-start.13 = (s32[8]{0:T(128)S(1)}, s32[8]{0:T(128)}, u32[]{:S(2)}) copy-start(s32[8]{0:T(128)} %param.24) | copy-start | bytes 100
  32.3 0.7 %copy-start.5 = (f32[8,128]{1,0:T(8,128)S(1)}, f32[8,128]{1,0:T(8,128)}, u32[]{:S(2)}) copy-start(f32[8,128]{1,0:T(8,128)} %param.22) | copy-start | bytes 12292
  32.3 0.7 %copy-start.6 = (f32[8,128]{1,0:T(8,128)S(1)}, f32[8,128]{1,0:T(8,128)}, u32[]{:S(2)}) copy-start(f32[8,128]{1,0:T(8,128)} %param.23) | copy-start | bytes 12292
  34.3 11.2 %all-to-all-start.1 = ((f32[32,8,128]{2,1,0:T(8,128)}), f32[32,8,128]{2,1,0:T(8,128)S(1)}, u32[]{:S(2)}, u32[]{:S(2)}) async-start(f32[32,8,128]{2,1,0:T(8,128)} %broadcast_in_dim.96), calls=%async_computation.1 | async-start | bytes 262144 | tf_op jit(solution)/shard_map/all_to_all | solution.py:160
  47.8 0.7 %copy-start.7 = (f32[1,8]{1,0:T(1,128)S(1)}, f32[1,8]{1,0:T(1,128)}, u32[]{:S(2)}) copy-start(f32[1,8]{1,0:T(1,128)} %param.29) | copy-start | bytes 100
